TPU v7x, 128 devices: a whole 4x4x4 slice. The times are simulated.
128 devices in a mesh: section: 4 (over x), sample: 8 (over z, y_lo), tensor: 4 (over y_hi, core).
Axes of the slice: x: 4, y: 4 (y_hi: 2, y_lo: 2; y = y_hi * 2 + y_lo), z: 4, core: 2. Of those that a mesh axis runs over, the one named last changes fastest.
Arguments:
- queries: bfloat16 [4, 1024, 8192], P('section', 'sample', 'tensor'), may hold values from -4.5 to 4.5
- suffix_keys: bfloat16 [4, 1024, 1024], P('section', 'sample', 'tensor'), may hold values from -4.5 to 4.5
- suffix_values: bfloat16 [4, 1024, 1024], P('section', 'sample', 'tensor'), may hold values from -4.5 to 4.5
- output_grad: bfloat16 [4, 1024, 8192], P('section', 'sample', 'tensor'), may hold values from -192 to 192
- prefix_keys: bfloat16 [4, 4096, 1024], P('section', ('sample', 'tensor')), may hold values from -4.5 to 4.5
- prefix_values: bfloat16 [4, 4096, 1024], P('section', ('sample', 'tensor')), may hold values from -4.5 to 4.5
- kv_weight: bfloat16 [4, 8192, 2, 1024], P('section', None, None, 'tensor'), may hold values from -0.0625 to 0.0625
- prefix_states: bfloat16 [4, 4096, 8192], P('section', ('sample', 'tensor')), may hold values from -6 to 6
- norm_gain: bfloat16 [4, 8192], P('section'), may hold values from 0.099609375 to 1.8984375
- segment_ids: int32 [8, 128], P('sample'), may hold values from 0 to 1, never falling along the last dimension, each value on 1 to 96 neighbouring positions
- segment_prompt: int32 [8, 2], P('sample'), may hold values from 0 to 2
- block_table: int32 [3, 16], replicated, may hold values from 0 to 31, as said below
Outputs:
- query_grad: bfloat16 [4, 1024, 8192], P('section', 'sample', 'tensor')
- rollout_key_gradient: bfloat16 [4, 1024, 1024], P('section', 'sample', 'tensor')
- suffix_value_grad: bfloat16 [4, 1024, 1024], P('section', 'sample', 'tensor')
- prefix_key_grad: float32 [4, 4096, 1024], P('section', ('sample', 'tensor'))
- prefix_value_grad: float32 [4, 4096, 1024], P('section', ('sample', 'tensor'))
- prefix_state_gradient: float32 [4, 4096, 8192], P('section', ('sample', 'tensor'))
Inputs may be any that keep to these rules, and one draw needn't show every extreme that they name: `block_table`: each row lists 16 distinct pages; its first 8 entries are the same pages in every row, and every page of the pool appears in some row.
All inputs are finite; a program needn't handle non-finite values.
Results may differ from a plain program's by a relative error of at most 0.024.
Values may be sent and summed in bfloat16 or wider, within the bound.
No kernel may reach another device: no remote copies, remote signals or barrier semaphores. Data moves between devices by JAX's collectives and lax.ppermute only.
A program may use at most 192 MiB of HBM per device.

v0:
```python
import jax
import jax.numpy as jnp
from jax import lax
from jax.sharding import PartitionSpec as P

HEAD_SIZE = 128
PAGE = 128


MASKED_SCORE = -1e30
EPSILON = 1e-05


def visible_keys(seg_row, prompt_row, table, pooled_rows):
    tok_count = seg_row.shape[0]
    seg_hot = seg_row[:, None] == jnp.arange(prompt_row.shape[0], dtype=jnp.int32)[None, :]
    prompt_tok = jnp.sum(jnp.where(seg_hot, prompt_row[None, :], 0), axis=1)
    page_ids = jnp.arange(pooled_rows // PAGE, dtype=jnp.int32)
    member = jnp.any(table[:, :, None] == page_ids[None, None, :], axis=1)
    prompt_hot = prompt_tok[:, None] == jnp.arange(table.shape[0], dtype=jnp.int32)[None, :]
    member_tok = jnp.any(prompt_hot[:, :, None] & member[None, :, :], axis=1)
    prefix_seen = jnp.repeat(member_tok, PAGE, axis=1)
    position = jnp.arange(tok_count, dtype=jnp.int32)
    suffix_seen = (seg_row[:, None] == seg_row[None, :]) & (position[None, :] <= position[:, None])
    return jnp.concatenate([prefix_seen, suffix_seen], axis=1)


def attend_group(query_grp, grad_grp, key_rows, value_rows, visible):
    inv_root = query_grp.shape[-1] ** (-0.5)
    scores = (
        jnp.einsum("rgd,kd->rgk", query_grp, key_rows, preferred_element_type=jnp.float32)
        * inv_root
    )
    scores = jnp.where(visible[:, None, :], scores, MASKED_SCORE)
    row_max = jnp.max(scores, axis=2, keepdims=True)
    exponent = jnp.exp(scores - row_max)
    softmax_w = exponent / jnp.sum(exponent, axis=2, keepdims=True)
    weights_low = softmax_w.astype(jnp.bfloat16)
    attended = jnp.einsum(
        "rgk,kd->rgd", weights_low, value_rows, preferred_element_type=jnp.float32
    )
    delta_row = jnp.sum(grad_grp.astype(jnp.float32) * attended, axis=2, keepdims=True)
    weight_grad = jnp.einsum(
        "rgd,kd->rgk", grad_grp, value_rows, preferred_element_type=jnp.float32
    )
    score_grad = (softmax_w * (weight_grad - delta_row)).astype(jnp.bfloat16)
    query_out = (
        jnp.einsum("rgk,kd->rgd", score_grad, key_rows, preferred_element_type=jnp.float32)
        * inv_root
    )
    key_result = (
        jnp.einsum("rgk,rgd->kd", score_grad, query_grp, preferred_element_type=jnp.float32)
        * inv_root
    )
    value_out = jnp.einsum("rgk,rgd->kd", weights_low, grad_grp, preferred_element_type=jnp.float32)
    return (query_out, key_result, value_out)


def make_body(n_sec, n_smp, n_ten):
    def on_device(
        queries,
        suffix_keys,
        suffix_values,
        output_grad,
        prefix_keys,
        prefix_values,
        kv_weight,
        prefix_states,
        norm_gain,
        segment_ids,
        segment_prompt,
        block_table,
    ):
        head_width = suffix_keys.shape[2]
        kv_local = head_width // HEAD_SIZE
        rows_local = prefix_keys.shape[1]
        pooled_rows = rows_local * n_smp * n_ten
        block_rows = rows_local * n_ten
        tok_count = queries.shape[1]
        group_size = queries.shape[2] // head_width
        visible = visible_keys(segment_ids[0], segment_prompt[0], block_table, pooled_rows)
        query_rows = queries[0].reshape(tok_count, kv_local, group_size, HEAD_SIZE)
        grad_rows = output_grad[0].reshape(tok_count, kv_local, group_size, HEAD_SIZE)
        own_keys = suffix_keys[0]
        own_values = suffix_values[0]
        pk = prefix_keys[0].reshape(rows_local, n_ten, kv_local, 1, HEAD_SIZE)
        pv = prefix_values[0].reshape(rows_local, n_ten, kv_local, 1, HEAD_SIZE)
        send = jnp.concatenate([pk, pv], axis=3).reshape(rows_local, n_ten, -1).transpose(1, 0, 2)
        got_all = lax.all_to_all(send, "tensor", 0, 0, tiled=True)
        got_all = got_all.reshape(block_rows, kv_local, 2 * HEAD_SIZE)

        query_pieces, suffix_key_pieces, suffix_value_pieces, reduced_pieces = [], [], [], []
        for head_index in range(kv_local):
            low_col = head_index * HEAD_SIZE
            got = got_all[:, head_index]
            if head_index % 2 == 0:
                spread = jnp.broadcast_to(got[None], (n_smp,) + got.shape)
                pool = lax.all_to_all(spread, "sample", 0, 0, tiled=True).reshape(pooled_rows, -1)
            else:
                pool = lax.all_gather(got, "sample", axis=0, tiled=True)
            key_rows = jnp.concatenate(
                [pool[:, :HEAD_SIZE], own_keys[:, low_col : low_col + HEAD_SIZE]], axis=0
            )
            value_rows = jnp.concatenate(
                [pool[:, HEAD_SIZE:], own_values[:, low_col : low_col + HEAD_SIZE]], axis=0
            )
            query_out, key_result, value_out = attend_group(
                query_rows[:, head_index], grad_rows[:, head_index], key_rows, value_rows, visible
            )
            query_pieces.append(query_out)
            suffix_key_pieces.append(key_result[pooled_rows:])
            suffix_value_pieces.append(value_out[pooled_rows:])
            pool_grad = jnp.concatenate(
                [key_result[:pooled_rows], value_out[:pooled_rows]], axis=1
            ).astype(jnp.bfloat16)
            pool_grad = pool_grad.reshape(n_smp, block_rows, 2 * HEAD_SIZE)
            parts = lax.all_to_all(pool_grad, "sample", 0, 0, tiled=False)
            reduced_pieces.append(jnp.sum(parts.astype(jnp.float32), axis=0))
        query_grad = jnp.stack(query_pieces, axis=1).reshape(tok_count, -1).astype(jnp.bfloat16)
        rollout_key_gradient = jnp.concatenate(suffix_key_pieces, axis=1).astype(jnp.bfloat16)
        suffix_value_grad = jnp.concatenate(suffix_value_pieces, axis=1).astype(jnp.bfloat16)

        reduced = jnp.concatenate(reduced_pieces, axis=1).astype(jnp.bfloat16)
        home_send = reduced.reshape(n_ten, rows_local, kv_local * 2 * HEAD_SIZE)
        home = lax.all_to_all(home_send, "tensor", 0, 0, tiled=True)
        home = home.reshape(n_ten, rows_local, kv_local, 2, HEAD_SIZE).transpose(3, 1, 0, 2, 4)
        home = home.reshape(2, rows_local, n_ten * kv_local * HEAD_SIZE).astype(jnp.float32)
        key_home = home[0]
        value_home = home[1]

        grad_cols = reduced.reshape(block_rows, kv_local, 2, HEAD_SIZE).transpose(0, 2, 1, 3)
        grad_cols = grad_cols.reshape(block_rows, 2, kv_local * HEAD_SIZE)
        group_term = lax.dot_general(
            grad_cols, kv_weight[0], (((1, 2), (1, 2)), ((), ())), preferred_element_type=jnp.float32
        ).astype(jnp.bfloat16)
        key_home, value_home, group_term = lax.optimization_barrier((key_home, value_home, group_term))
        width = group_term.shape[1]
        t_idx = lax.axis_index("tensor")
        core = t_idx % 2
        hi = t_idx // 2
        term4 = group_term.reshape(2, 2, rows_local, width)
        keep = lax.dynamic_index_in_dim(term4, core, 1, False)
        give = lax.dynamic_index_in_dim(term4, 1 - core, 1, False)
        core_pairs = [(i, i ^ 1) for i in range(n_ten)]
        chip_pairs = [(i, i ^ 2) for i in range(n_ten)]
        states_all = prefix_states[0]
        gain_wide = norm_gain[0].astype(jnp.float32)[None, :]
        sec = lax.axis_index("section")
        n_chunks = 2
        step = rows_local // n_chunks
        outs = []
        for c in range(n_chunks):
            rows = slice(c * step, (c + 1) * step)
            got1 = lax.ppermute(give[:, rows], "tensor", core_pairs)
            partial = keep[:, rows].astype(jnp.float32) + got1.astype(jnp.float32)
            mine = lax.dynamic_index_in_dim(partial, hi, 0, False)
            other = lax.dynamic_index_in_dim(partial, 1 - hi, 0, False)
            got2 = lax.ppermute(other.astype(jnp.bfloat16), "tensor", chip_pairs)
            normed_grad = mine + got2.astype(jnp.float32)

            states = states_all[rows].astype(jnp.float32)
            inv_rms = lax.rsqrt(jnp.mean(states * states, axis=1, keepdims=True) + EPSILON)
            gained = gain_wide * normed_grad
            layer_term = inv_rms * gained - states * inv_rms**3 * jnp.mean(
                states * gained, axis=1, keepdims=True
            )
            term_low = layer_term.astype(jnp.bfloat16)
            if n_sec == 4:
                down = lax.ppermute(term_low, "section", [(3, 2), (2, 1)])
                wrap = lax.ppermute(term_low, "section", [(3, 0)])
                carry = (
                    jnp.where(sec == 1, layer_term, 0.0)
                    + down.astype(jnp.float32)
                    + wrap.astype(jnp.float32)
                )
                last = lax.ppermute(carry.astype(jnp.bfloat16), "section", [(1, 0), (0, 1)])
                outs.append(
                    layer_term
                    + down.astype(jnp.float32)
                    + wrap.astype(jnp.float32)
                    + last.astype(jnp.float32)
                )
            else:
                terms = lax.all_gather(term_low, "section")
                above = jnp.arange(n_sec) > sec
                outs.append(
                    layer_term
                    + jnp.sum(jnp.where(above[:, None, None], terms.astype(jnp.float32), 0.0), axis=0)
                )
        prefix_state_gradient = jnp.concatenate(outs, axis=0)
        return (
            query_grad[None],
            rollout_key_gradient[None],
            suffix_value_grad[None],
            key_home[None],
            value_home[None],
            prefix_state_gradient[None],
        )

    return on_device


def solution(mesh):
    placed = (
        P("section", "sample", "tensor"),
        P("section", "sample", "tensor"),
        P("section", "sample", "tensor"),
        P("section", "sample", "tensor"),
        P("section", ("sample", "tensor"), None),
        P("section", ("sample", "tensor"), None),
        P("section", None, None, "tensor"),
        P("section", ("sample", "tensor"), None),
        P("section", None),
        P("sample", None),
        P("sample", None),
        P(),
    )
    body = make_body(mesh.shape["section"], mesh.shape["sample"], mesh.shape["tensor"])
    return jax.shard_map(
        body,
        mesh=mesh,
        in_specs=placed,
        out_specs=(
            P("section", "sample", "tensor"),
            P("section", "sample", "tensor"),
            P("section", "sample", "tensor"),
            P("section", ("sample", "tensor"), None),
            P("section", ("sample", "tensor"), None),
            P("section", ("sample", "tensor"), None),
        ),
        check_vma=False,
    )
```

profile of v0, /device:TPU:0, one launch (start us, length us, event | category | flops | bytes accessed | tf_op | source)
XLA Modules:
  0.0 398.4 jit_solution(17685371777089666462)
XLA Ops:
  7.2 1.2 copy.83
  8.4 1.1 copy.84
  10.3 4.6 %all-to-all-start = ((bf16[4,128,512]{1,2,0:T(8,128)(2,1)}), bf16[4,128,512]{1,2,0:T(8,128)(2,1)S(1)}, u32[]{:S(2)}, u32[]{:S(2)}) async-start(bf16[4,128,512]{1,2,0:T(8,128)(2,1)} %bitcast.6), calls=%async_computation | async-start | bytes 1048576 | tf_op jit(solution)/shard_map/all_to_all | solution.py:89
  15.2 10.0 %all-to-all-done = bf16[4,128,512]{1,2,0:T(8,128)(2,1)S(1)} async-done(((bf16[4,128,512]{1,2,0:T(8,128)(2,1)}), bf16[4,128,512]{1,2,0:T(8,128)(2,1)S(1)}, u32[]{:S(2)}, u32[]{:S(2)}) %all-to-all-start) | async-done | bytes 524320 | tf_op jit(solution)/shard_map/all_to_all | solution.py:89
  26.4 1.5 broadcast_in_dim.85
  27.8 5.6 %all-to-all-start.1 = ((bf16[8,512,256]{2,1,0:T(8,128)(2,1)}), bf16[8,512,256]{2,1,0:T(8,128)(2,1)}, u32[]{:S(2)}, u32[]{:S(2)}) async-start(bf16[8,512,256]{2,1,0:T(8,128)(2,1)} %broadcast_in_dim.85), calls=%async_computation.1 | async-start | bytes 4194304 | tf_op jit(solution)/shard_map/all_to_all | solution.py:98
  37.2 34.4 %all-to-all-done.1 = bf16[8,512,256]{2,1,0:T(8,128)(2,1)} async-done(((bf16[8,512,256]{2,1,0:T(8,128)(2,1)}), bf16[8,512,256]{2,1,0:T(8,128)(2,1)}, u32[]{:S(2)}, u32[]{:S(2)}) %all-to-all-start.1) | async-done | bytes 2097184 | tf_op jit(solution)/shard_map/all_to_all | solution.py:98
  71.6 2.7 fusion.73
  75.2 2.4 fusion.44
  77.6 10.2 %fusion.81 = (f32[128,8]{0,1:T(8,128)S(1)}, f32[128,8,4224]{0,2,1:T(8,128)}) fusion(f32[4224,128,8]{1,0,2:T(8,128)S(1)} %fusion.44, pred[128,4224]{0,1:T(8,128)(4,1)S(1)} %pad_add_fusion), kind=kOutput, calls=%fused_computation.150 | output fusion | flops 17305728 | bytes 35147776 | tf_op jit(solution)/shard_map/sub | solution.py:36
  87.9 7.5 %fusion.13 = bf16[128,8,4224]{0,2,1:T(8,128)(2,1)S(1)} fusion(f32[128,8,4224]{0,2,1:T(8,128)} %get-tuple-element.73, f32[128,8]{0,1:T(8,128)S(1)} %get-tuple-element.72), kind=kLoop, calls=%fused_computation.22 | loop fusion | flops 8650752 | bytes 25956352 | tf_op jit(solution)/shard_map/convert_element_type | solution.py:38
  95.5 4.4 %copy-done.7 = bf16[128,8,4224]{0,2,1:T(8,128)(2,1)} copy-done((bf16[128,8,4224]{0,2,1:T(8,128)(2,1)}, bf16[128,8,4224]{0,2,1:T(8,128)(2,1)S(1)}, u32[]{:S(2)}) %copy-start.7) | copy-done | bytes 8650776
  99.8 2.5 fusion.37
  102.5 16.9 %fusion.3 = bf16[128,8,4224]{0,2,1:T(8,128)(2,1)} fusion(f32[128,8]{0,1:T(8,128)S(1)} %fusion.37, f32[128,8,4224]{0,2,1:T(8,128)S(1)} %bitcast.196, f32[128,8]{0,1:T(8,128)S(1)} %get-tuple-element.72, bf16[128,128]{1,0:T(8,128)(2,1)} %get-tuple-element.62, bf16[4096,128]{1,0:T(8,128)(2,1)} %get-tuple-element.52, bf16[128,2,8,128]{0,3,2,1:T(8,128)(2,1)S(1)} %bitcast.211), kind=kOutput, calls=%fused_computation.6 | convolution fusion | flops 1126760448 | bytes 27303936 | tf_op jit(solution)/shard_map/rgd,kd->rgk/dot_general | solution.py:43
  119.4 6.0 %fusion.17 = bf16[4224,128]{1,0:T(8,128)(2,1)S(1)} fusion(bf16[128,8,4224]{0,2,1:T(8,128)(2,1)} %fusion.3, bf16[128,2,8,128]{0,3,2,1:T(8,128)(2,1)S(1)} %bitcast.206), kind=kOutput, calls=%fused_computation.30 | convolution fusion | flops 1108377600 | bytes 9994240 | tf_op jit(solution)/shard_map/rgk,rgd->kd/dot_general | solution.py:52
  126.5 2.5 fusion.19
  130.0 1.5 pad_maximum_fusion
  131.6 4.4 %all-to-all-start.2 = ((bf16[8,512,256]{2,1,0:T(8,128)(2,1)}), bf16[8,512,256]{2,1,0:T(8,128)(2,1)}, u32[]{:S(2)}, u32[]{:S(2)}) async-start(bf16[8,512,256]{2,1,0:T(8,128)(2,1)} %pad_maximum_fusion), calls=%async_computation.2 | async-start | bytes 4194304 | tf_op jit(solution)/shard_map/all_to_all | solution.py:117
  136.0 2.6 fusion.74
  139.6 2.4 fusion.43
  142.0 10.2 %fusion.80 = (f32[128,8]{0,1:T(8,128)S(1)}, f32[128,8,4224]{0,2,1:T(8,128)}) fusion(f32[4224,128,8]{1,0,2:T(8,128)S(1)} %fusion.43, pred[128,4224]{0,1:T(8,128)(4,1)S(1)} %pad_add_fusion), kind=kOutput, calls=%fused_computation.149 | output fusion | flops 17305728 | bytes 35147776 | tf_op jit(solution)/shard_map/sub | solution.py:36
  152.3 7.5 %fusion.14 = bf16[128,8,4224]{0,2,1:T(8,128)(2,1)S(1)} fusion(f32[128,8,4224]{0,2,1:T(8,128)} %get-tuple-element.71, f32[128,8]{0,1:T(8,128)S(1)} %get-tuple-element.70), kind=kLoop, calls=%fused_computation.23 | loop fusion | flops 8650752 | bytes 25956352 | tf_op jit(solution)/shard_map/convert_element_type | solution.py:38
  159.8 4.4 %copy-done.5 = bf16[128,8,4224]{0,2,1:T(8,128)(2,1)} copy-done((bf16[128,8,4224]{0,2,1:T(8,128)(2,1)}, bf16[128,8,4224]{0,2,1:T(8,128)(2,1)S(1)}, u32[]{:S(2)}) %copy-start.5) | copy-done | bytes 8650776
  164.2 2.5 fusion.38
  166.8 6.5 %fusion.2 = bf16[128,8,4224]{0,2,1:T(8,128)(2,1)} fusion(f32[128,8]{0,1:T(8,128)S(1)} %fusion.38, f32[128,8,4224]{0,2,1:T(8,128)S(1)} %bitcast.194, f32[128,8]{0,1:T(8,128)S(1)} %get-tuple-element.70, bf16[128,128]{1,0:T(8,128)(2,1)S(1)} %copy-done.29, bf16[4096,128]{1,0:T(8,128)(2,1)} %get-tuple-element.54, bf16[128,2,8,128]{0,3,2,1:T(8,128)(2,1)S(1)} %bitcast.213), kind=kOutput, calls=%fused_computation.3 | convolution fusion | flops 1126760448 | bytes 27303936 | tf_op jit(solution)/shard_map/rgd,kd->rgk/dot_general | solution.py:43
  173.3 6.0 %fusion.18 = bf16[4224,128]{1,0:T(8,128)(2,1)S(1)} fusion(bf16[128,8,4224]{0,2,1:T(8,128)(2,1)} %fusion.2, bf16[128,2,8,128]{0,3,2,1:T(8,128)(2,1)S(1)} %bitcast.208), kind=kOutput, calls=%fused_computation.31 | convolution fusion | flops 1108377600 | bytes 9994240 | tf_op jit(solution)/shard_map/rgk,rgd->kd/dot_general | solution.py:52
  180.4 2.5 fusion.20
  183.9 1.6 pad_maximum_fusion.1
  185.5 5.6 %all-to-all-start.3 = ((bf16[8,512,256]{2,1,0:T(8,128)(2,1)}), bf16[8,512,256]{2,1,0:T(8,128)(2,1)S(1)}, u32[]{:S(2)}, u32[]{:S(2)}) async-start(bf16[8,512,256]{2,1,0:T(8,128)(2,1)} %pad_maximum_fusion.1), calls=%async_computation.3 | async-start | bytes 4194304 | tf_op jit(solution)/shard_map/all_to_all | solution.py:117
  191.0 2.0 reduce
  193.2 19.8 %all-to-all-done.3 = bf16[8,512,256]{2,1,0:T(8,128)(2,1)S(1)} async-done(((bf16[8,512,256]{2,1,0:T(8,128)(2,1)}), bf16[8,512,256]{2,1,0:T(8,128)(2,1)S(1)}, u32[]{:S(2)}, u32[]{:S(2)}) %all-to-all-start.3) | async-done | bytes 2097184 | tf_op jit(solution)/shard_map/all_to_all | solution.py:117
  214.3 3.5 all-to-all-start.4
  218.6 10.1 %bitcast_convert_fusion = bf16[512,8192]{1,0:T(8,128)(2,1)} fusion(bf16[512,2,256]{2,0,1:T(8,128)(2,1)S(1)} %reshape.213, bf16[8192,2,256]{2,1,0:T(2,128)(2,1)} %bitcast.232), kind=kOutput, calls=%fused_computation.10 | convolution fusion | flops 4299161600 | bytes 17301504 | tf_op jit(solution)/shard_map/dot_general | solution.py:133
  229.0 1.0 fusion.75
  230.0 6.2 %dynamic-slice_bitcast_fusion.1 = (bf16[2,128,8192]{2,1,0:T(8,128)(2,1)}, bf16[2,128,8192]{2,1,0:T(8,128)(2,1)S(1)}) fusion(bf16[2,2,128,8192]{3,2,1,0:T(8,128)(2,1)} %bitcast.197, s32[]{:T(128)S(6)} %select_n.54, s32[]{:T(128)S(6)} %select_n.55), kind=kLoop, calls=%fused_computation.38 | loop fusion | bytes 16777224 | tf_op jit(solution)/shard_map/jit(dynamic_index_in_dim)/squeeze | solution.py:142
  236.2 1.7 fusion.72
  238.6 3.9 collective-permute-done.5
  242.5 3.0 collective-permute-done
  245.5 4.9 %convert_add_fusion = (f32[2,64,8192]{2,1,0:T(8,128)S(1)}, f32[2,64,8192]{2,1,0:T(8,128)S(1)}) fusion(bf16[2,64,8192]{2,1,0:T(8,128)(2,1)} %collective-permute-done.5, bf16[2,128,8192]{2,1,0:T(8,128)(2,1)} %get-tuple-element.44, bf16[2,64,8192]{2,1,0:T(8,128)(2,1)} %collective-permute-done), kind=kLoop, calls=%fused_computation.35 | loop fusion | flops 6291456 | bytes 16777216 | tf_op jit(solution)/shard_map/add | solution.py:155
  250.5 2.0 copy-done
  252.5 1.6 fusion.42
  254.0 1.1 fusion.41
  255.1 3.4 collective-permute-start.1
  258.8 5.0 %fusion.40 = bf16[128,1,8,128]{0,3,2,1:T(8,128)(2,1)S(1)} fusion(bf16[128,8,4224]{0,2,1:T(8,128)(2,1)} %fusion.3, bf16[128,128]{1,0:T(8,128)(2,1)S(1)} %copy-done.25, bf16[4096,128]{1,0:T(8,128)(2,1)S(1)} %copy-done.14), kind=kOutput, calls=%fused_computation.83 | convolution fusion | flops 1109721088 | bytes 9994240 | tf_op jit(solution)/shard_map/rgk,kd->rgd/dot_general | solution.py:48
  263.8 19.1 %collective-permute-done.1 = bf16[64,8192]{1,0:T(8,128)(2,1)S(1)} collective-permute-done((bf16[64,8192]{1,0:T(8,128)(2,1)}, bf16[64,8192]{1,0:T(8,128)(2,1)S(1)}, u32[]{:S(2)}, u32[]{:S(2)}) %collective-permute-start.1) | collective-permute-done | bytes 1048608 | tf_op jit(solution)/shard_map/ppermute | solution.py:158
  282.9 21.9 %collective-permute-done.6 = bf16[64,8192]{1,0:T(8,128)(2,1)S(1)} collective-permute-done((bf16[64,8192]{1,0:T(8,128)(2,1)}, bf16[64,8192]{1,0:T(8,128)(2,1)S(1)}, u32[]{:S(2)}, u32[]{:S(2)}) %collective-permute-start.6) | collective-permute-done | bytes 1048608 | tf_op jit(solution)/shard_map/ppermute | solution.py:158
  304.8 1.2 fusion.28
  306.1 4.7 %fusion.68 = (bf16[64,8192]{1,0:T(8,128)(2,1)}, f32[64,8192]{1,0:T(8,128)}, bf16[64,8192]{1,0:T(8,128)(2,1)}, f32[64,8192]{1,0:T(8,128)S(1)}) fusion(f32[64]{0:T(128)S(1)} %get-tuple-element.81, f32[64]{0:T(128)S(1)} %get-tuple-element.78, bf16[1,128,8192]{2,1,0:T(8,128)(2,1)S(1)} %copy-done.9, bf16[64,8192]{1,0:T(8,128)(2,1)S(1)} %collective-permute-done.1, ...), kind=kLoop, calls=%fused_computation.139 | loop fusion | flops 9437184 | bytes 14714372 | tf_op jit(solution)/shard_map/convert_element_type | solution.py:167
  310.8 1.3 collective-permute-start.3
  312.1 1.6 collective-permute-start.2
  313.7 1.4 fusion.39
  316.0 2.0 copy.110
  320.9 2.0 copy.108
  322.9 2.0 copy.109
  324.9 1.3 collective-permute-start.8
  327.0 13.1 %collective-permute-done.3 = bf16[64,8192]{1,0:T(8,128)(2,1)S(1)} collective-permute-done((bf16[64,8192]{1,0:T(8,128)(2,1)}, bf16[64,8192]{1,0:T(8,128)(2,1)S(1)}, u32[]{:S(2)}, u32[]{:S(2)}) %collective-permute-start.3) | collective-permute-done | bytes 1048608 | tf_op jit(solution)/shard_map/ppermute | solution.py:170
  340.1 1.6 fusion.22
  341.7 3.7 collective-permute-start.4
  345.5 15.7 %collective-permute-done.8 = bf16[64,8192]{1,0:T(8,128)(2,1)S(1)} collective-permute-done((bf16[64,8192]{1,0:T(8,128)(2,1)}, bf16[64,8192]{1,0:T(8,128)(2,1)S(1)}, u32[]{:S(2)}, u32[]{:S(2)}) %collective-permute-start.8) | collective-permute-done | bytes 1048608 | tf_op jit(solution)/shard_map/ppermute | solution.py:170
  361.6 3.1 collective-permute-start.9
  364.7 2.5 collective-permute-done.4
  367.1 1.7 fusion.21
  368.8 19.6 %collective-permute-done.9 = bf16[64,8192]{1,0:T(8,128)(2,1)S(1)} collective-permute-done((bf16[64,8192]{1,0:T(8,128)(2,1)S(1)}, bf16[64,8192]{1,0:T(8,128)(2,1)S(1)}, u32[]{:S(2)}, u32[]{:S(2)}) %collective-permute-start.9) | collective-permute-done | bytes 1048608 | tf_op jit(solution)/shard_map/ppermute | solution.py:176
  388.9 2.4 maximum_bitcast_fusion
  (147 shorter events, 21.1 us)
Async XLA Ops:
  7.2 7.7 %copy-start.21 = (bf16[1,128,2048]{2,1,0:T(8,128)(2,1)S(1)}, bf16[1,128,2048]{2,1,0:T(8,128)(2,1)}, u32[]{:S(2)}) copy-start(bf16[1,128,2048]{2,1,0:T(8,128)(2,1)} %param.15) | copy-start | bytes 1572868
  10.3 14.9 %all-to-all-start = ((bf16[4,128,512]{1,2,0:T(8,128)(2,1)}), bf16[4,128,512]{1,2,0:T(8,128)(2,1)S(1)}, u32[]{:S(2)}, u32[]{:S(2)}) async-start(bf16[4,128,512]{1,2,0:T(8,128)(2,1)} %bitcast.6), calls=%async_computation | async-start | bytes 1048576 | tf_op jit(solution)/shard_map/all_to_all | solution.py:89
  27.8 6.1 %copy-start.22 = (bf16[1,128,2048]{2,1,0:T(8,128)(2,1)S(1)}, bf16[1,128,2048]{2,1,0:T(8,128)(2,1)}, u32[]{:S(2)}) copy-start(bf16[1,128,2048]{2,1,0:T(8,128)(2,1)} %param.12) | copy-start | bytes 1572868
  27.8 43.8 %all-to-all-start.1 = ((bf16[8,512,256]{2,1,0:T(8,128)(2,1)}), bf16[8,512,256]{2,1,0:T(8,128)(2,1)}, u32[]{:S(2)}, u32[]{:S(2)}) async-start(bf16[8,512,256]{2,1,0:T(8,128)(2,1)} %broadcast_in_dim.85), calls=%async_computation.1 | async-start | bytes 4194304 | tf_op jit(solution)/shard_map/all_to_all | solution.py:98
  33.4 1.2 copy-start.31
  33.4 1.2 copy-start.33
  33.4 1.3 copy-start.32
  33.4 1.5 copy-start.26
  33.4 2.2 copy-start.27
  33.4 102.6 %all-gather.3.cloned.1.call-start = ((), (), s32[]{:S(2)}) async-start(), calls=%async_computation.5 | async-start | bytes 2359296 | tf_op jit(solution)/shard_map/all_gather | solution.py:100
  71.6 3.6 copy-start.24
  74.3 1.0 copy-start.13
  87.9 12.0 %copy-start.20 = (bf16[4096,128]{1,0:T(8,128)(2,1)S(1)}, bf16[4096,128]{1,0:T(8,128)(2,1)}, u32[]{:S(2)}) copy-start(bf16[4096,128]{1,0:T(8,128)(2,1)} %get-tuple-element.52) | copy-start | bytes 3145732
  87.9 12.0 %copy-start.30 = (bf16[128,128]{1,0:T(8,128)(2,1)S(1)}, bf16[128,128]{1,0:T(8,128)(2,1)}, u32[]{:S(2)}) copy-start(bf16[128,128]{1,0:T(8,128)(2,1)} %get-tuple-element.62) | copy-start | bytes 98308
  87.9 14.5 %slice-start.5 = ((s8[17301504]{0:T(1024)(128)(4,1)}), s8[4194304]{0:T(1024)(128)(4,1)S(1)}, s32[]{:S(2)}) async-start(s8[17301504]{0:T(1024)(128)(4,1)} %bitcast.195), calls=%async_computation.11 | async-start | bytes 8388608
  87.9 14.5 %slice-start.6 = ((s8[17301504]{0:T(1024)(128)(4,1)}), s8[4194304]{0:T(1024)(128)(4,1)S(1)}, s32[]{:S(2)}) async-start(s8[17301504]{0:T(1024)(128)(4,1)} %bitcast.195), calls=%async_computation.12 | async-start | bytes 8388608
  87.9 14.5 %slice-start.7 = ((s8[17301504]{0:T(1024)(128)(4,1)}), s8[4194304]{0:T(1024)(128)(4,1)S(1)}, s32[]{:S(2)}) async-start(s8[17301504]{0:T(1024)(128)(4,1)} %bitcast.195), calls=%async_computation.13 | async-start | bytes 8388608
  87.9 14.5 %slice-start.8 = ((s8[17301504]{0:T(1024)(128)(4,1)}), s8[4194304]{0:T(1024)(128)(4,1)S(1)}, s32[]{:S(2)}) async-start(s8[17301504]{0:T(1024)(128)(4,1)} %bitcast.195), calls=%async_computation.14 | async-start | bytes 8388608
  95.4 4.4 %copy-start.7 = (bf16[128,8,4224]{0,2,1:T(8,128)(2,1)}, bf16[128,8,4224]{0,2,1:T(8,128)(2,1)S(1)}, u32[]{:S(2)}) copy-start(bf16[128,8,4224]{0,2,1:T(8,128)(2,1)S(1)} %fusion.13) | copy-start | bytes 25952260
  99.8 2.7 slice-start.9
  119.4 7.1 %copy-start.8 = (bf16[128,8,4224]{0,2,1:T(8,128)(2,1)S(1)}, bf16[128,8,4224]{0,2,1:T(8,128)(2,1)}, u32[]{:S(2)}) copy-start(bf16[128,8,4224]{0,2,1:T(8,128)(2,1)} %copy-done.7) | copy-start | bytes 25952260
  125.4 1.0 copy-start.16
  128.9 1.0 copy-start.15
  131.6 53.9 %all-to-all-start.2 = ((bf16[8,512,256]{2,1,0:T(8,128)(2,1)}), bf16[8,512,256]{2,1,0:T(8,128)(2,1)}, u32[]{:S(2)}, u32[]{:S(2)}) async-start(bf16[8,512,256]{2,1,0:T(8,128)(2,1)} %pad_maximum_fusion), calls=%async_computation.2 | async-start | bytes 4194304 | tf_op jit(solution)/shard_map/all_to_all | solution.py:117
  136.0 3.7 copy-start.23
  138.6 1.0 copy-start.11
  152.3 11.9 %copy-start.19 = (bf16[4096,128]{1,0:T(8,128)(2,1)S(1)}, bf16[4096,128]{1,0:T(8,128)(2,1)}, u32[]{:S(2)}) copy-start(bf16[4096,128]{1,0:T(8,128)(2,1)} %get-tuple-element.54) | copy-start | bytes 3145732
  152.3 11.9 %copy-start.29 = (bf16[128,128]{1,0:T(8,128)(2,1)S(1)}, bf16[128,128]{1,0:T(8,128)(2,1)}, u32[]{:S(2)}) copy-start(bf16[128,128]{1,0:T(8,128)(2,1)} %get-tuple-element.63) | copy-start | bytes 98308
  152.3 14.4 %slice-start = ((s8[17301504]{0:T(1024)(128)(4,1)}), s8[4194304]{0:T(1024)(128)(4,1)S(1)}, s32[]{:S(2)}) async-start(s8[17301504]{0:T(1024)(128)(4,1)} %bitcast.193), calls=%async_computation.6 | async-start | bytes 8388608
  152.3 14.4 %slice-start.1 = ((s8[17301504]{0:T(1024)(128)(4,1)}), s8[4194304]{0:T(1024)(128)(4,1)S(1)}, s32[]{:S(2)}) async-start(s8[17301504]{0:T(1024)(128)(4,1)} %bitcast.193), calls=%async_computation.7 | async-start | bytes 8388608
  152.3 14.4 %slice-start.2 = ((s8[17301504]{0:T(1024)(128)(4,1)}), s8[4194304]{0:T(1024)(128)(4,1)S(1)}, s32[]{:S(2)}) async-start(s8[17301504]{0:T(1024)(128)(4,1)} %bitcast.193), calls=%async_computation.8 | async-start | bytes 8388608
  152.3 14.4 %slice-start.3 = ((s8[17301504]{0:T(1024)(128)(4,1)}), s8[4194304]{0:T(1024)(128)(4,1)S(1)}, s32[]{:S(2)}) async-start(s8[17301504]{0:T(1024)(128)(4,1)} %bitcast.193), calls=%async_computation.9 | async-start | bytes 8388608
  159.8 4.4 %copy-start.5 = (bf16[128,8,4224]{0,2,1:T(8,128)(2,1)}, bf16[128,8,4224]{0,2,1:T(8,128)(2,1)S(1)}, u32[]{:S(2)}) copy-start(bf16[128,8,4224]{0,2,1:T(8,128)(2,1)S(1)} %fusion.14) | copy-start | bytes 25952260
  164.2 2.6 slice-start.4
  173.3 7.1 %copy-start.6 = (bf16[128,8,4224]{0,2,1:T(8,128)(2,1)S(1)}, bf16[128,8,4224]{0,2,1:T(8,128)(2,1)}, u32[]{:S(2)}) copy-start(bf16[128,8,4224]{0,2,1:T(8,128)(2,1)} %copy-done.5) | copy-start | bytes 25952260
  179.3 1.0 copy-start.18
  182.9 1.0 copy-start.17
  185.5 27.5 %all-to-all-start.3 = ((bf16[8,512,256]{2,1,0:T(8,128)(2,1)}), bf16[8,512,256]{2,1,0:T(8,128)(2,1)S(1)}, u32[]{:S(2)}, u32[]{:S(2)}) async-start(bf16[8,512,256]{2,1,0:T(8,128)(2,1)} %pad_maximum_fusion.1), calls=%async_computation.3 | async-start | bytes 4194304 | tf_op jit(solution)/shard_map/all_to_all | solution.py:117
  214.3 14.4 %all-to-all-start.4 = ((bf16[4,128,512]{2,1,0:T(8,128)(2,1)}), bf16[4,128,512]{2,1,0:T(8,128)(2,1)S(1)}, u32[]{:S(2)}, u32[]{:S(2)}) async-start(bf16[4,128,512]{2,1,0:T(8,128)(2,1)} %pad_maximum_fusion.4), calls=%async_computation.4 | async-start | bytes 1048576 | tf_op jit(solution)/shard_map/all_to_all | solution.py:125
  237.9 4.6 %collective-permute-start.5 = (bf16[2,64,8192]{2,1,0:T(8,128)(2,1)}, bf16[2,64,8192]{2,1,0:T(8,128)(2,1)}, u32[]{:S(2)}, u32[]{:S(2)}) collective-permute-start(bf16[2,64,8192]{2,1,0:T(8,128)(2,1)} %get-tuple-element.48), channel_id=1, source_target_pairs={{0,1},{1,0},{2,3},{3,2},{4,5},{5,4},{6,7},{7,6},{8,9},{9,8},{10,11... | collective-permute-start | bytes 6291464 | tf_op jit(solution)/shard_map/ppermute | solution.py:154
  238.4 7.1 %collective-permute-start = (bf16[2,64,8192]{2,1,0:T(8,128)(2,1)S(1)}, bf16[2,64,8192]{2,1,0:T(8,128)(2,1)}, u32[]{:S(2)}, u32[]{:S(2)}) collective-permute-start(bf16[2,64,8192]{2,1,0:T(8,128)(2,1)S(1)} %get-tuple-element.49), channel_id=1, source_target_pairs={{0,1},{1,0},{2,3},{3,2},{4,5},{5,4},{6,7},{7,6},{8,9},{9,8},{10,11... | collective-permute-start | bytes 6291464 | tf_op jit(solution)/shard_map/ppermute | solution.py:154
  250.4 2.1 copy-start
  250.4 3.6 copy-start.2
  250.4 8.2 %copy-start.28 = (bf16[1,8192]{1,0:T(2,128)(2,1)S(1)}, bf16[1,8192]{1,0:T(2,128)(2,1)}, u32[]{:S(2)}) copy-start(bf16[1,8192]{1,0:T(2,128)(2,1)} %param.20) | copy-start | bytes 49156
  250.4 8.3 %copy-start.14 = (bf16[4096,128]{1,0:T(8,128)(2,1)S(1)}, bf16[4096,128]{1,0:T(8,128)(2,1)}, u32[]{:S(2)}) copy-start(bf16[4096,128]{1,0:T(8,128)(2,1)} %copy-done.13) | copy-start | bytes 3145732
  250.4 8.3 %copy-start.25 = (bf16[128,128]{1,0:T(8,128)(2,1)S(1)}, bf16[128,128]{1,0:T(8,128)(2,1)}, u32[]{:S(2)}) copy-start(bf16[128,128]{1,0:T(8,128)(2,1)} %get-tuple-element.64) | copy-start | bytes 98308
  255.1 27.7 %collective-permute-start.1 = (bf16[64,8192]{1,0:T(8,128)(2,1)}, bf16[64,8192]{1,0:T(8,128)(2,1)S(1)}, u32[]{:S(2)}, u32[]{:S(2)}) collective-permute-start(bf16[64,8192]{1,0:T(8,128)(2,1)} %fusion.41), channel_id=1, source_target_pairs={{0,2},{1,3},{2,0},{3,1},{4,6},{5,7},{6,4},{7,5},{8,10},{9,11},{10,... | collective-permute-start | bytes 3145736 | tf_op jit(solution)/shard_map/ppermute | solution.py:158
  258.5 46.2 %collective-permute-start.6 = (bf16[64,8192]{1,0:T(8,128)(2,1)}, bf16[64,8192]{1,0:T(8,128)(2,1)S(1)}, u32[]{:S(2)}, u32[]{:S(2)}) collective-permute-start(bf16[64,8192]{1,0:T(8,128)(2,1)} %fusion.42), channel_id=1, source_target_pairs={{0,2},{1,3},{2,0},{3,1},{4,6},{5,7},{6,4},{7,5},{8,10},{9,11},{10,... | collective-permute-start | bytes 3145736 | tf_op jit(solution)/shard_map/ppermute | solution.py:158
  258.7 46.0 %copy-start.1 = (f32[2,64,8192]{2,1,0:T(8,128)S(1)}, f32[2,64,8192]{2,1,0:T(8,128)}, u32[]{:S(2)}) copy-start(f32[2,64,8192]{2,1,0:T(8,128)} %copy-done) | copy-start | bytes 12582916
  258.7 46.0 %copy-start.3 = (f32[2,64,8192]{2,1,0:T(8,128)S(1)}, f32[2,64,8192]{2,1,0:T(8,128)}, u32[]{:S(2)}) copy-start(f32[2,64,8192]{2,1,0:T(8,128)} %copy-done.2) | copy-start | bytes 12582916
  258.8 46.0 %copy-start.9 = (bf16[1,128,8192]{2,1,0:T(8,128)(2,1)S(1)}, bf16[1,128,8192]{2,1,0:T(8,128)(2,1)}, u32[]{:S(2)}) copy-start(bf16[1,128,8192]{2,1,0:T(8,128)(2,1)} %param.19) | copy-start | bytes 6291460
  304.8 1.3 copy-start.10
  304.8 8.9 %slice-start.10 = ((s8[8650752]{0:T(1024)(128)(4,1)}), s8[4194304]{0:T(1024)(128)(4,1)S(1)}, s32[]{:S(2)}) async-start(s8[8650752]{0:T(1024)(128)(4,1)} %bitcast.234), calls=%async_computation.16 | async-start | bytes 8388608
  304.8 8.9 %slice-start.11 = ((s8[8650752]{0:T(1024)(128)(4,1)}), s8[4194304]{0:T(1024)(128)(4,1)S(1)}, s32[]{:S(2)}) async-start(s8[8650752]{0:T(1024)(128)(4,1)} %bitcast.234), calls=%async_computation.17 | async-start | bytes 8388608
  306.1 7.7 %copy-start.12 = (bf16[4096,128]{1,0:T(8,128)(2,1)S(1)}, bf16[4096,128]{1,0:T(8,128)(2,1)}, u32[]{:S(2)}) copy-start(bf16[4096,128]{1,0:T(8,128)(2,1)} %copy-done.11) | copy-start | bytes 3145732
  306.1 7.6 %slice-start.12 = ((s8[8650752]{0:T(1024)(128)(4,1)}), s8[262144]{0:T(1024)(128)(4,1)S(1)}, s32[]{:S(2)}) async-start(s8[8650752]{0:T(1024)(128)(4,1)} %bitcast.234), calls=%async_computation.18 | async-start | bytes 524288
  310.8 29.3 %collective-permute-start.3 = (bf16[64,8192]{1,0:T(8,128)(2,1)}, bf16[64,8192]{1,0:T(8,128)(2,1)S(1)}, u32[]{:S(2)}, u32[]{:S(2)}) collective-permute-start(bf16[64,8192]{1,0:T(8,128)(2,1)} %get-tuple-element.40), channel_id=1, source_target_pairs={{96,0},{97,1},{98,2},{99,3},{100,4},{101,5},{102,6},{103,7},{104,8... | collective-permute-start | bytes 3145736 | tf_op jit(solution)/shard_map/ppermute | solution.py:170
  312.1 28.0 %collective-permute-start.2 = (bf16[64,8192]{1,0:T(8,128)(2,1)}, bf16[64,8192]{1,0:T(8,128)(2,1)}, u32[]{:S(2)}, u32[]{:S(2)}) collective-permute-start(bf16[64,8192]{1,0:T(8,128)(2,1)} %get-tuple-element.40), channel_id=1, source_target_pairs={{96,64},{64,32},{97,65},{65,33},{98,66},{66,34},{99,67},{67,35},{1... | collective-permute-start | bytes 3145736 | tf_op jit(solution)/shard_map/ppermute | solution.py:169
  324.9 36.2 %collective-permute-start.8 = (bf16[64,8192]{1,0:T(8,128)(2,1)}, bf16[64,8192]{1,0:T(8,128)(2,1)S(1)}, u32[]{:S(2)}, u32[]{:S(2)}) collective-permute-start(bf16[64,8192]{1,0:T(8,128)(2,1)} %get-tuple-element.50), channel_id=1, source_target_pairs={{96,0},{97,1},{98,2},{99,3},{100,4},{101,5},{102,6},{103,7},{104,8... | collective-permute-start | bytes 3145736 | tf_op jit(solution)/shard_map/ppermute | solution.py:170
  326.2 34.9 %collective-permute-start.7 = (bf16[64,8192]{1,0:T(8,128)(2,1)}, bf16[64,8192]{1,0:T(8,128)(2,1)S(1)}, u32[]{:S(2)}, u32[]{:S(2)}) collective-permute-start(bf16[64,8192]{1,0:T(8,128)(2,1)} %get-tuple-element.50), channel_id=1, source_target_pairs={{96,64},{64,32},{97,65},{65,33},{98,66},{66,34},{99,67},{67,35},{1... | collective-permute-start | bytes 3145736 | tf_op jit(solution)/shard_map/ppermute | solution.py:169
  341.7 25.4 %collective-permute-start.4 = (bf16[64,8192]{1,0:T(8,128)(2,1)S(1)}, bf16[64,8192]{1,0:T(8,128)(2,1)S(1)}, u32[]{:S(2)}, u32[]{:S(2)}) collective-permute-start(bf16[64,8192]{1,0:T(8,128)(2,1)S(1)} %fusion.22), channel_id=1, source_target_pairs={{32,0},{0,32},{33,1},{1,33},{34,2},{2,34},{35,3},{3,35},{36,4},{4,... | collective-permute-start | bytes 3145736 | tf_op jit(solution)/shard_map/ppermute | solution.py:176
  361.1 6.0 %copy-start.4 = (f32[64,8192]{1,0:T(8,128)S(1)}, f32[64,8192]{1,0:T(8,128)}, u32[]{:S(2)}) copy-start(f32[64,8192]{1,0:T(8,128)} %get-tuple-element.41) | copy-start | bytes 6291460
  361.6 26.9 %collective-permute-start.9 = (bf16[64,8192]{1,0:T(8,128)(2,1)S(1)}, bf16[64,8192]{1,0:T(8,128)(2,1)S(1)}, u32[]{:S(2)}, u32[]{:S(2)}) collective-permute-start(bf16[64,8192]{1,0:T(8,128)(2,1)S(1)} %fusion.24), channel_id=1, source_target_pairs={{32,0},{0,32},{33,1},{1,33},{34,2},{2,34},{35,3},{3,35},{36,4},{4,... | collective-permute-start | bytes 3145736 | tf_op jit(solution)/shard_map/ppermute | solution.py:176
Sparse Core Ops, SparseCore 0:
  37.3 61.9 all-gather.2
where the time goes:
time: 397 us; the launch traced here: 398 us
  waiting for transfers between devices  163 us (41%)
  matrix products  66.7 us (17%)
  other arithmetic  62.6 us (16%)
  local copies, waits for them, and re-layouts  51.1 us (13%)
  starting transfers between devices  39.9 us (10%)
  between operations  15 us (4%)
    ppermute x2, waiting for transfers between devices, on_device(): got2 = lax.ppermute(other.astype(jnp.bfloat16), 'tensor', chip_pairs)  41 us
    all_to_all x1, waiting for transfers between devices, on_device(): lax.all_to_all(spread, 'sample', 0, 0, tiled=True).reshape(pooled_rows, -1)  34.4 us
    ppermute x2, waiting for transfers between devices, on_device(): wrap = lax.ppermute(term_low, 'section', [(3, 0)])  28.8 us
    dot_general x2, matrix products, attend_group(): jnp.einsum('rgd,kd->rgk', grad_grp, value_rows, preferred_element_type=jn...  23.4 us
    unnamed x103, local copies, waits for them, and re-layouts  23.1 us
    ppermute x2, waiting for transfers between devices, on_device(): last = lax.ppermute(carry.astype(jnp.bfloat16), 'section', [(1, 0), (0, 1)])  22.1 us
    sub x2, other arithmetic, attend_group(): exponent = jnp.exp(scores - row_max)  20.4 us
    all_to_all x2, waiting for transfers between devices, on_device(): parts = lax.all_to_all(pool_grad, 'sample', 0, 0, tiled=False)  19.8 us
  transfers between devices with their start and end apart: 16, of which 11 were waited for; matrix products, arithmetic and copies ran while one was open for 33% of the time, Pallas kernels for 0%

commit v1 on v0

--- a/solution.py
+++ b/solution.py
@@ -146,17 +146,21 @@
         states_all = prefix_states[0]
         gain_wide = norm_gain[0].astype(jnp.float32)[None, :]
         sec = lax.axis_index("section")
-        n_chunks = 2
+        got1 = lax.ppermute(give, "tensor", core_pairs)
+        partial = keep.astype(jnp.float32) + got1.astype(jnp.float32)
+        mine_all = lax.dynamic_index_in_dim(partial, hi, 0, False)
+        other_all = lax.dynamic_index_in_dim(partial, 1 - hi, 0, False).astype(jnp.bfloat16)
+        n_chunks = 4
         step = rows_local // n_chunks
         outs = []
+        previous = None
         for c in range(n_chunks):
             rows = slice(c * step, (c + 1) * step)
-            got1 = lax.ppermute(give[:, rows], "tensor", core_pairs)
-            partial = keep[:, rows].astype(jnp.float32) + got1.astype(jnp.float32)
-            mine = lax.dynamic_index_in_dim(partial, hi, 0, False)
-            other = lax.dynamic_index_in_dim(partial, 1 - hi, 0, False)
-            got2 = lax.ppermute(other.astype(jnp.bfloat16), "tensor", chip_pairs)
-            normed_grad = mine + got2.astype(jnp.float32)
+            other = other_all[rows]
+            if previous is not None:
+                other, previous = lax.optimization_barrier((other, previous))
+            got2 = lax.ppermute(other, "tensor", chip_pairs)
+            normed_grad = mine_all[rows] + got2.astype(jnp.float32)
 
             states = states_all[rows].astype(jnp.float32)
             inv_rms = lax.rsqrt(jnp.mean(states * states, axis=1, keepdims=True) + EPSILON)
@@ -165,6 +169,7 @@
                 states * gained, axis=1, keepdims=True
             )
             term_low = layer_term.astype(jnp.bfloat16)
+            previous = term_low
             if n_sec == 4:
                 down = lax.ppermute(term_low, "section", [(3, 2), (2, 1)])
                 wrap = lax.ppermute(term_low, "section", [(3, 0)])

time: 397 us -> 364 us (0.917); the launches traced: 398 us -> 360 us
  waiting for transfers between devices: 163 us -> 117 us
  starting transfers between devices: 39.9 us -> 56.8 us
  matrix products: 66.7 us -> 61.7 us
  local copies, waits for them, and re-layouts: 51.1 us -> 46.7 us
    ppermute x2 -> x4, waiting for transfers between devices: 28.8 us -> 8.68 us  [on_device(): wrap = lax.ppermute(term_low, 'section', [(3, 0)])]
    ppermute x4 -> x5, waiting for transfers between devices: 47.9 us -> 34.7 us  [the longest x4 34.7 us: on_device(): got2 = lax.ppermute(other, 'tensor', chip_pairs)]
    ppermute x2 -> x4, waiting for transfers between devices: 22.1 us -> 9.88 us  [on_device(): last = lax.ppermute(carry.astype(jnp.bfloat16), 'section', [(1, 0), (0, 1)])]
    ppermute x4 -> x5, starting transfers between devices: 4.19 us -> 13.8 us  [the longest x4 13.1 us: on_device(): got2 = lax.ppermute(other, 'tensor', chip_pairs)]
    dot_general x2, matrix products: 23.4 us -> 13.8 us  [attend_group(): jnp.einsum('rgd,kd->rgk', grad_grp, value_rows, preferred_element_type=jn...]
    ppermute x2 -> x4, starting transfers between devices: 6.82 us -> 11.3 us  [on_device(): last = lax.ppermute(carry.astype(jnp.bfloat16), 'section', [(1, 0), (0, 1)])]
    unnamed x103 -> x99, local copies, waits for them, and re-layouts: 23.1 us -> 23.5 us
  transfers between devices with their start and end apart: 16 -> 23, of which waited for: 11 -> 9; matrix products, arithmetic and copies ran while one was open for 33% -> 35% of each run, Pallas kernels for 0% -> 0%
where the time goes in v1:
time: 364 us; the launch traced here: 360 us
  waiting for transfers between devices  117 us (32%)
  other arithmetic  62.5 us (17%)
  matrix products  61.7 us (17%)
  starting transfers between devices  56.8 us (16%)
  local copies, waits for them, and re-layouts  46.7 us (13%)
  between operations  15.2 us (4%)
    all_to_all x1, waiting for transfers between devices, on_device(): lax.all_to_all(spread, 'sample', 0, 0, tiled=True).reshape(pooled_rows, -1)  36 us
    ppermute x4, waiting for transfers between devices, on_device(): got2 = lax.ppermute(other, 'tensor', chip_pairs)  34.7 us
    unnamed x99, local copies, waits for them, and re-layouts  23.5 us
    sub x2, other arithmetic, attend_group(): exponent = jnp.exp(scores - row_max)  20.4 us
    all_to_all x2, waiting for transfers between devices, on_device(): parts = lax.all_to_all(pool_grad, 'sample', 0, 0, tiled=False)  19.1 us
    convert_element_type x2, other arithmetic, attend_group(): weights_low = softmax_w.astype(jnp.bfloat16)  15 us
    dot_general x2, matrix products, attend_group(): jnp.einsum('rgd,kd->rgk', grad_grp, value_rows, preferred_element_type=jn...  13.8 us
    ppermute x4, starting transfers between devices, on_device(): got2 = lax.ppermute(other, 'tensor', chip_pairs)  13.1 us
  transfers between devices with their start and end apart: 23, of which 9 were waited for; matrix products, arithmetic and copies ran while one was open for 35% of the time, Pallas kernels for 0%

profile of v1, /device:TPU:0, one launch (start us, length us, event | category | flops | bytes accessed | tf_op | source)
XLA Modules:
  0.0 360.3 jit_solution(4281739896269567818)
XLA Ops:
  7.2 1.1 copy.86
  8.3 1.1 copy.87
  10.3 4.6 %all-to-all-start = ((bf16[4,128,512]{1,2,0:T(8,128)(2,1)}), bf16[4,128,512]{1,2,0:T(8,128)(2,1)S(1)}, u32[]{:S(2)}, u32[]{:S(2)}) async-start(bf16[4,128,512]{1,2,0:T(8,128)(2,1)} %bitcast.6), calls=%async_computation | async-start | bytes 1048576 | tf_op jit(solution)/shard_map/all_to_all | solution.py:89
  14.8 1.3 copy.91
  16.2 9.0 %all-to-all-done = bf16[4,128,512]{1,2,0:T(8,128)(2,1)S(1)} async-done(((bf16[4,128,512]{1,2,0:T(8,128)(2,1)}), bf16[4,128,512]{1,2,0:T(8,128)(2,1)S(1)}, u32[]{:S(2)}, u32[]{:S(2)}) %all-to-all-start) | async-done | bytes 524320 | tf_op jit(solution)/shard_map/all_to_all | solution.py:89
  26.3 1.5 broadcast_in_dim.91
  27.8 5.6 %all-to-all-start.1 = ((bf16[8,512,256]{2,1,0:T(8,128)(2,1)}), bf16[8,512,256]{2,1,0:T(8,128)(2,1)}, u32[]{:S(2)}, u32[]{:S(2)}) async-start(bf16[8,512,256]{2,1,0:T(8,128)(2,1)} %broadcast_in_dim.91), calls=%async_computation.1 | async-start | bytes 4194304 | tf_op jit(solution)/shard_map/all_to_all | solution.py:98
  36.4 36.0 %all-to-all-done.1 = bf16[8,512,256]{2,1,0:T(8,128)(2,1)} async-done(((bf16[8,512,256]{2,1,0:T(8,128)(2,1)}), bf16[8,512,256]{2,1,0:T(8,128)(2,1)}, u32[]{:S(2)}, u32[]{:S(2)}) %all-to-all-start.1) | async-done | bytes 2097184 | tf_op jit(solution)/shard_map/all_to_all | solution.py:98
  72.4 2.7 fusion.92
  76.0 2.4 fusion.60
  78.4 10.2 %fusion.100 = (f32[128,8]{0,1:T(8,128)S(1)}, f32[128,8,4224]{0,2,1:T(8,128)}) fusion(f32[4224,128,8]{1,0,2:T(8,128)S(1)} %fusion.60, pred[128,4224]{0,1:T(8,128)(4,1)S(1)} %pad_add_fusion), kind=kOutput, calls=%fused_computation.190 | output fusion | flops 17305728 | bytes 35147776 | tf_op jit(solution)/shard_map/sub | solution.py:36
  88.6 7.5 %fusion.13 = bf16[128,8,4224]{0,2,1:T(8,128)(2,1)S(1)} fusion(f32[128,8,4224]{0,2,1:T(8,128)} %get-tuple-element.84, f32[128,8]{0,1:T(8,128)S(1)} %get-tuple-element.83), kind=kLoop, calls=%fused_computation.23 | loop fusion | flops 8650752 | bytes 25956352 | tf_op jit(solution)/shard_map/convert_element_type | solution.py:38
  96.2 4.4 %copy-done.5 = bf16[128,8,4224]{0,2,1:T(8,128)(2,1)} copy-done((bf16[128,8,4224]{0,2,1:T(8,128)(2,1)}, bf16[128,8,4224]{0,2,1:T(8,128)(2,1)S(1)}, u32[]{:S(2)}) %copy-start.5) | copy-done | bytes 8650776
  100.6 2.5 fusion.23
  103.3 6.5 %fusion.3 = bf16[128,8,4224]{0,2,1:T(8,128)(2,1)} fusion(f32[128,8]{0,1:T(8,128)S(1)} %fusion.23, f32[128,8,4224]{0,2,1:T(8,128)S(1)} %bitcast.241, f32[128,8]{0,1:T(8,128)S(1)} %get-tuple-element.83, bf16[128,128]{1,0:T(8,128)(2,1)S(1)} %get-tuple-element.69, bf16[4096,128]{1,0:T(8,128)(2,1)} %get-tuple-element.59, bf16[128,2,8,128]{0,3,2,1:T(8,128)(2,1)S(1)} %bitcast.267), kind=kOutput, calls=%fused_computation.6 | convolution fusion | flops 1126760448 | bytes 27303936 | tf_op jit(solution)/shard_map/rgd,kd->rgk/dot_general | solution.py:43
  109.8 6.0 %fusion.17 = bf16[4224,128]{1,0:T(8,128)(2,1)S(1)} fusion(bf16[128,8,4224]{0,2,1:T(8,128)(2,1)} %fusion.3, bf16[128,2,8,128]{0,3,2,1:T(8,128)(2,1)S(1)} %bitcast.262), kind=kOutput, calls=%fused_computation.31 | convolution fusion | flops 1108377600 | bytes 9994240 | tf_op jit(solution)/shard_map/rgk,rgd->kd/dot_general | solution.py:52
  117.0 2.5 fusion.19
  120.5 1.5 pad_maximum_fusion
  122.0 4.4 %all-to-all-start.2 = ((bf16[8,512,256]{2,1,0:T(8,128)(2,1)}), bf16[8,512,256]{2,1,0:T(8,128)(2,1)}, u32[]{:S(2)}, u32[]{:S(2)}) async-start(bf16[8,512,256]{2,1,0:T(8,128)(2,1)} %pad_maximum_fusion), calls=%async_computation.2 | async-start | bytes 4194304 | tf_op jit(solution)/shard_map/all_to_all | solution.py:117
  126.4 2.6 fusion.93
  129.0 3.3 fusion.59
  132.4 10.2 %fusion.99 = (f32[128,8]{0,1:T(8,128)S(1)}, f32[128,8,4224]{0,2,1:T(8,128)}) fusion(f32[4224,128,8]{1,0,2:T(8,128)S(1)} %fusion.59, pred[128,4224]{0,1:T(8,128)(4,1)S(1)} %pad_add_fusion), kind=kOutput, calls=%fused_computation.189 | output fusion | flops 17305728 | bytes 35147776 | tf_op jit(solution)/shard_map/sub | solution.py:36
  142.6 7.5 %fusion.14 = bf16[128,8,4224]{0,2,1:T(8,128)(2,1)S(1)} fusion(f32[128,8,4224]{0,2,1:T(8,128)} %get-tuple-element.82, f32[128,8]{0,1:T(8,128)S(1)} %get-tuple-element.81), kind=kLoop, calls=%fused_computation.24 | loop fusion | flops 8650752 | bytes 25956352 | tf_op jit(solution)/shard_map/convert_element_type | solution.py:38
  150.1 4.4 %copy-done.3 = bf16[128,8,4224]{0,2,1:T(8,128)(2,1)} copy-done((bf16[128,8,4224]{0,2,1:T(8,128)(2,1)}, bf16[128,8,4224]{0,2,1:T(8,128)(2,1)S(1)}, u32[]{:S(2)}) %copy-start.3) | copy-done | bytes 8650776
  154.5 2.5 fusion.24
  157.1 7.3 %fusion.2 = bf16[128,8,4224]{0,2,1:T(8,128)(2,1)} fusion(f32[128,8]{0,1:T(8,128)S(1)} %fusion.24, f32[128,8,4224]{0,2,1:T(8,128)S(1)} %bitcast.239, f32[128,8]{0,1:T(8,128)S(1)} %get-tuple-element.81, bf16[128,128]{1,0:T(8,128)(2,1)S(1)} %get-tuple-element.70, bf16[4096,128]{1,0:T(8,128)(2,1)} %get-tuple-element.61, bf16[128,2,8,128]{0,3,2,1:T(8,128)(2,1)} %bitcast.269), kind=kOutput, calls=%fused_computation.3 | convolution fusion | flops 1126760448 | bytes 27303936 | tf_op jit(solution)/shard_map/rgd,kd->rgk/dot_general | solution.py:43
  164.4 6.0 %fusion.18 = bf16[4224,128]{1,0:T(8,128)(2,1)S(1)} fusion(bf16[128,8,4224]{0,2,1:T(8,128)(2,1)} %fusion.2, bf16[128,2,8,128]{0,3,2,1:T(8,128)(2,1)S(1)} %bitcast.264), kind=kOutput, calls=%fused_computation.32 | convolution fusion | flops 1108377600 | bytes 9994240 | tf_op jit(solution)/shard_map/rgk,rgd->kd/dot_general | solution.py:52
  171.5 2.5 fusion.20
  175.0 1.6 pad_maximum_fusion.1
  176.6 5.6 %all-to-all-start.3 = ((bf16[8,512,256]{2,1,0:T(8,128)(2,1)}), bf16[8,512,256]{2,1,0:T(8,128)(2,1)S(1)}, u32[]{:S(2)}, u32[]{:S(2)}) async-start(bf16[8,512,256]{2,1,0:T(8,128)(2,1)} %pad_maximum_fusion.1), calls=%async_computation.3 | async-start | bytes 4194304 | tf_op jit(solution)/shard_map/all_to_all | solution.py:117
  182.2 2.0 reduce
  185.0 19.1 %all-to-all-done.3 = bf16[8,512,256]{2,1,0:T(8,128)(2,1)S(1)} async-done(((bf16[8,512,256]{2,1,0:T(8,128)(2,1)}), bf16[8,512,256]{2,1,0:T(8,128)(2,1)S(1)}, u32[]{:S(2)}, u32[]{:S(2)}) %all-to-all-start.3) | async-done | bytes 2097184 | tf_op jit(solution)/shard_map/all_to_all | solution.py:117
  206.2 1.8 pad_maximum_fusion.4
  208.0 3.5 all-to-all-start.4
  213.3 10.1 %bitcast_convert_fusion = bf16[512,8192]{1,0:T(8,128)(2,1)} fusion(bf16[512,2,256]{2,0,1:T(8,128)(2,1)S(1)} %reshape.264, bf16[8192,2,256]{2,1,0:T(2,128)(2,1)} %bitcast.286), kind=kOutput, calls=%fused_computation.10 | convolution fusion | flops 4299161600 | bytes 17301504 | tf_op jit(solution)/shard_map/dot_general | solution.py:133
  224.7 4.7 %dynamic-slice_bitcast_fusion = bf16[2,128,8192]{2,1,0:T(8,128)(2,1)} fusion(bf16[2,2,128,8192]{3,2,1,0:T(8,128)(2,1)} %bitcast.242, s32[]{:T(128)S(6)} %select_n.61), kind=kLoop, calls=%fused_computation.37 | loop fusion | bytes 8388612 | tf_op jit(solution)/shard_map/jit(dynamic_index_in_dim)/squeeze | solution.py:143
  230.2 5.0 %fusion.26 = bf16[128,1,8,128]{0,3,2,1:T(8,128)(2,1)S(1)} fusion(bf16[128,8,4224]{0,2,1:T(8,128)(2,1)} %fusion.3, bf16[128,128]{1,0:T(8,128)(2,1)S(1)} %copy-done.26, bf16[4096,128]{1,0:T(8,128)(2,1)S(1)} %copy-done.8), kind=kOutput, calls=%fused_computation.78 | convolution fusion | flops 1109721088 | bytes 9994240 | tf_op jit(solution)/shard_map/rgk,kd->rgd/dot_general | solution.py:48
  236.1 5.1 %fusion.25 = bf16[128,1,8,128]{0,3,2,1:T(8,128)(2,1)S(1)} fusion(bf16[128,8,4224]{0,2,1:T(8,128)(2,1)} %fusion.2, bf16[128,128]{1,0:T(8,128)(2,1)S(1)} %get-tuple-element.72, bf16[4096,128]{1,0:T(8,128)(2,1)S(1)} %get-tuple-element.62), kind=kOutput, calls=%fused_computation.77 | convolution fusion | flops 1109721088 | bytes 9994240 | tf_op jit(solution)/shard_map/rgk,kd->rgd/dot_general | solution.py:48
  241.3 3.6 convert_add_fusion
  245.2 1.3 slice_bitcast_fusion.3
  246.5 2.8 copy-done
  249.2 3.1 collective-permute-start.1
  255.5 2.0 copy.111
  258.5 6.6 %collective-permute-done.1 = bf16[32,8192]{1,0:T(8,128)(2,1)} collective-permute-done((bf16[32,8192]{1,0:T(8,128)(2,1)}, bf16[32,8192]{1,0:T(8,128)(2,1)}, u32[]{:S(2)}, u32[]{:S(2)}) %collective-permute-start.1) | collective-permute-done | bytes 524320 | tf_op jit(solution)/shard_map/ppermute | solution.py:162
  265.2 2.3 fusion.47
  267.5 2.3 fusion.90
  269.8 1.3 collective-permute-start.3
  271.8 3.3 collective-permute-start.5
  275.1 11.6 %collective-permute-done.5 = bf16[32,8192]{1,0:T(8,128)(2,1)S(1)} collective-permute-done((bf16[32,8192]{1,0:T(8,128)(2,1)S(1)}, bf16[32,8192]{1,0:T(8,128)(2,1)S(1)}, u32[]{:S(2)}, u32[]{:S(2)}) %collective-permute-start.5) | collective-permute-done | bytes 524320 | tf_op jit(solution)/shard_map/ppermute | solution.py:162
  286.7 1.5 fusion.42
  288.6 1.3 collective-permute-start.7
  290.7 3.3 collective-permute-start.9
  294.2 3.5 collective-permute-start.4
  297.7 7.0 %collective-permute-done.9 = bf16[32,8192]{1,0:T(8,128)(2,1)S(1)} collective-permute-done((bf16[32,8192]{1,0:T(8,128)(2,1)S(1)}, bf16[32,8192]{1,0:T(8,128)(2,1)S(1)}, u32[]{:S(2)}, u32[]{:S(2)}) %collective-permute-start.9) | collective-permute-done | bytes 524320 | tf_op jit(solution)/shard_map/ppermute | solution.py:162
  305.5 1.3 collective-permute-start.11
  307.7 3.4 collective-permute-start.8
  311.1 3.3 collective-permute-start.13
  314.7 9.4 %collective-permute-done.13 = bf16[32,8192]{1,0:T(8,128)(2,1)S(1)} collective-permute-done((bf16[32,8192]{1,0:T(8,128)(2,1)S(1)}, bf16[32,8192]{1,0:T(8,128)(2,1)S(1)}, u32[]{:S(2)}, u32[]{:S(2)}) %collective-permute-start.13) | collective-permute-done | bytes 524320 | tf_op jit(solution)/shard_map/ppermute | solution.py:162
  324.8 1.3 collective-permute-start.15
  327.0 2.4 collective-permute-start.12
  329.7 8.7 %collective-permute-done.15 = bf16[32,8192]{1,0:T(8,128)(2,1)S(1)} collective-permute-done((bf16[32,8192]{1,0:T(8,128)(2,1)S(1)}, bf16[32,8192]{1,0:T(8,128)(2,1)S(1)}, u32[]{:S(2)}, u32[]{:S(2)}) %collective-permute-start.15) | collective-permute-done | bytes 524320 | tf_op jit(solution)/shard_map/ppermute | solution.py:175
  338.6 1.9 collective-permute-start.16
  340.8 9.9 %collective-permute-done.16 = bf16[32,8192]{1,0:T(8,128)(2,1)S(1)} collective-permute-done((bf16[32,8192]{1,0:T(8,128)(2,1)S(1)}, bf16[32,8192]{1,0:T(8,128)(2,1)S(1)}, u32[]{:S(2)}, u32[]{:S(2)}) %collective-permute-start.16) | collective-permute-done | bytes 524320 | tf_op jit(solution)/shard_map/ppermute | solution.py:181
  350.9 2.4 maximum_bitcast_fusion
  (171 shorter events, 28.7 us)
Async XLA Ops:
  10.3 14.9 %all-to-all-start = ((bf16[4,128,512]{1,2,0:T(8,128)(2,1)}), bf16[4,128,512]{1,2,0:T(8,128)(2,1)S(1)}, u32[]{:S(2)}, u32[]{:S(2)}) async-start(bf16[4,128,512]{1,2,0:T(8,128)(2,1)} %bitcast.6), calls=%async_computation | async-start | bytes 1048576 | tf_op jit(solution)/shard_map/all_to_all | solution.py:89
  16.2 100.8 %copy-start.11 = (bf16[1,128,2048]{1,2,0:T(8,128)(2,1)}, bf16[1,128,2048]{1,2,0:T(8,128)(2,1)S(1)}, u32[]{:S(2)}) copy-start(bf16[1,128,2048]{1,2,0:T(8,128)(2,1)S(1)} %copy.91) | copy-start | bytes 1572868
  26.2 7.4 %copy-start.20 = (bf16[1,128,2048]{2,1,0:T(8,128)(2,1)S(1)}, bf16[1,128,2048]{2,1,0:T(8,128)(2,1)}, u32[]{:S(2)}) copy-start(bf16[1,128,2048]{2,1,0:T(8,128)(2,1)} %param.12) | copy-start | bytes 1572868
  27.8 7.2 %copy-start.30 = (s32[1,128]{1,0:T(1,128)S(1)}, s32[1,128]{1,0:T(1,128)}, u32[]{:S(2)}) copy-start(s32[1,128]{1,0:T(1,128)} %param.21) | copy-start | bytes 1540
  27.8 7.2 %copy-start.32 = (s32[1,2]{1,0:T(1,128)S(1)}, s32[1,2]{1,0:T(1,128)}, u32[]{:S(2)}) copy-start(s32[1,2]{1,0:T(1,128)} %param.22) | copy-start | bytes 28
  27.8 7.3 %copy-start.31 = (s32[3,16]{1,0:T(4,128)S(1)}, s32[3,16]{1,0:T(4,128)}, u32[]{:S(2)}) copy-start(s32[3,16]{1,0:T(4,128)} %param.23) | copy-start | bytes 580
  27.8 7.6 %copy-start.27 = (bf16[1,128,256]{2,1,0:T(8,128)(2,1)S(1)}, bf16[1,128,256]{2,1,0:T(8,128)(2,1)}, u32[]{:S(2)}) copy-start(bf16[1,128,256]{2,1,0:T(8,128)(2,1)} %param.13) | copy-start | bytes 196612
  27.8 7.6 %copy-start.28 = (bf16[1,128,256]{2,1,0:T(8,128)(2,1)S(1)}, bf16[1,128,256]{2,1,0:T(8,128)(2,1)}, u32[]{:S(2)}) copy-start(bf16[1,128,256]{2,1,0:T(8,128)(2,1)} %param.14) | copy-start | bytes 196612
  27.8 44.6 %all-to-all-start.1 = ((bf16[8,512,256]{2,1,0:T(8,128)(2,1)}), bf16[8,512,256]{2,1,0:T(8,128)(2,1)}, u32[]{:S(2)}, u32[]{:S(2)}) async-start(bf16[8,512,256]{2,1,0:T(8,128)(2,1)} %broadcast_in_dim.91), calls=%async_computation.1 | async-start | bytes 4194304 | tf_op jit(solution)/shard_map/all_to_all | solution.py:98
  33.4 93.0 %all-gather.3.cloned.1.call-start = ((), (), s32[]{:S(2)}) async-start(), calls=%async_computation.5 | async-start | bytes 2359296 | tf_op jit(solution)/shard_map/all_gather | solution.py:100
  33.9 75.9 %copy-start.9 = (bf16[1,128,2048]{1,2,0:T(8,128)(2,1)}, bf16[1,128,2048]{1,2,0:T(8,128)(2,1)S(1)}, u32[]{:S(2)}) copy-start(bf16[1,128,2048]{1,2,0:T(8,128)(2,1)S(1)} %copy.89) | copy-start | bytes 1572868
  35.4 43.0 %copy-start.25 = (bf16[128,128]{1,0:T(8,128)(2,1)}, bf16[128,128]{1,0:T(8,128)(2,1)S(1)}, u32[]{:S(2)}) copy-start(bf16[128,128]{1,0:T(8,128)(2,1)S(1)} %get-tuple-element.71) | copy-start | bytes 98308
  88.6 12.0 %copy-start.19 = (bf16[4096,128]{1,0:T(8,128)(2,1)S(1)}, bf16[4096,128]{1,0:T(8,128)(2,1)}, u32[]{:S(2)}) copy-start(bf16[4096,128]{1,0:T(8,128)(2,1)} %get-tuple-element.59) | copy-start | bytes 3145732
  88.6 12.0 %copy-start.24 = (bf16[128,1,8,128]{3,0,2,1:T(8,128)(2,1)S(1)}, bf16[128,1,8,128]{3,0,2,1:T(8,128)(2,1)}, u32[]{:S(2)}) copy-start(bf16[128,1,8,128]{3,0,2,1:T(8,128)(2,1)} %copy.131) | copy-start | bytes 786436
  88.6 14.5 %slice-start.5 = ((s8[17301504]{0:T(1024)(128)(4,1)}), s8[4194304]{0:T(1024)(128)(4,1)S(1)}, s32[]{:S(2)}) async-start(s8[17301504]{0:T(1024)(128)(4,1)} %bitcast.240), calls=%async_computation.11 | async-start | bytes 8388608
  88.6 14.5 %slice-start.6 = ((s8[17301504]{0:T(1024)(128)(4,1)}), s8[4194304]{0:T(1024)(128)(4,1)S(1)}, s32[]{:S(2)}) async-start(s8[17301504]{0:T(1024)(128)(4,1)} %bitcast.240), calls=%async_computation.12 | async-start | bytes 8388608
  88.6 14.5 %slice-start.7 = ((s8[17301504]{0:T(1024)(128)(4,1)}), s8[4194304]{0:T(1024)(128)(4,1)S(1)}, s32[]{:S(2)}) async-start(s8[17301504]{0:T(1024)(128)(4,1)} %bitcast.240), calls=%async_computation.13 | async-start | bytes 8388608
  88.6 14.5 %slice-start.8 = ((s8[17301504]{0:T(1024)(128)(4,1)}), s8[4194304]{0:T(1024)(128)(4,1)S(1)}, s32[]{:S(2)}) async-start(s8[17301504]{0:T(1024)(128)(4,1)} %bitcast.240), calls=%async_computation.14 | async-start | bytes 8388608
  96.2 4.4 %copy-start.5 = (bf16[128,8,4224]{0,2,1:T(8,128)(2,1)}, bf16[128,8,4224]{0,2,1:T(8,128)(2,1)S(1)}, u32[]{:S(2)}) copy-start(bf16[128,8,4224]{0,2,1:T(8,128)(2,1)S(1)} %fusion.13) | copy-start | bytes 25952260
  100.6 2.7 slice-start.9
  109.8 7.1 %copy-start.6 = (bf16[128,8,4224]{0,2,1:T(8,128)(2,1)S(1)}, bf16[128,8,4224]{0,2,1:T(8,128)(2,1)}, u32[]{:S(2)}) copy-start(bf16[128,8,4224]{0,2,1:T(8,128)(2,1)} %copy-done.5) | copy-start | bytes 25952260
  115.9 1.0 copy-start.15
  122.0 54.6 %all-to-all-start.2 = ((bf16[8,512,256]{2,1,0:T(8,128)(2,1)}), bf16[8,512,256]{2,1,0:T(8,128)(2,1)}, u32[]{:S(2)}, u32[]{:S(2)}) async-start(bf16[8,512,256]{2,1,0:T(8,128)(2,1)} %pad_maximum_fusion), calls=%async_computation.2 | async-start | bytes 4194304 | tf_op jit(solution)/shard_map/all_to_all | solution.py:117
  142.6 11.9 %copy-start.18 = (bf16[4096,128]{1,0:T(8,128)(2,1)S(1)}, bf16[4096,128]{1,0:T(8,128)(2,1)}, u32[]{:S(2)}) copy-start(bf16[4096,128]{1,0:T(8,128)(2,1)} %get-tuple-element.61) | copy-start | bytes 3145732
  142.6 14.4 %slice-start = ((s8[17301504]{0:T(1024)(128)(4,1)}), s8[4194304]{0:T(1024)(128)(4,1)S(1)}, s32[]{:S(2)}) async-start(s8[17301504]{0:T(1024)(128)(4,1)} %bitcast.238), calls=%async_computation.6 | async-start | bytes 8388608
  142.6 14.4 %slice-start.1 = ((s8[17301504]{0:T(1024)(128)(4,1)}), s8[4194304]{0:T(1024)(128)(4,1)S(1)}, s32[]{:S(2)}) async-start(s8[17301504]{0:T(1024)(128)(4,1)} %bitcast.238), calls=%async_computation.7 | async-start | bytes 8388608
  142.6 14.4 %slice-start.2 = ((s8[17301504]{0:T(1024)(128)(4,1)}), s8[4194304]{0:T(1024)(128)(4,1)S(1)}, s32[]{:S(2)}) async-start(s8[17301504]{0:T(1024)(128)(4,1)} %bitcast.238), calls=%async_computation.8 | async-start | bytes 8388608
  142.6 14.4 %slice-start.3 = ((s8[17301504]{0:T(1024)(128)(4,1)}), s8[4194304]{0:T(1024)(128)(4,1)S(1)}, s32[]{:S(2)}) async-start(s8[17301504]{0:T(1024)(128)(4,1)} %bitcast.238), calls=%async_computation.9 | async-start | bytes 8388608
  150.1 4.4 %copy-start.3 = (bf16[128,8,4224]{0,2,1:T(8,128)(2,1)}, bf16[128,8,4224]{0,2,1:T(8,128)(2,1)S(1)}, u32[]{:S(2)}) copy-start(bf16[128,8,4224]{0,2,1:T(8,128)(2,1)S(1)} %fusion.14) | copy-start | bytes 25952260
  154.5 2.6 slice-start.4
  157.1 7.3 %copy-start.10 = (bf16[1,128,2048]{1,2,0:T(8,128)(2,1)S(1)}, bf16[1,128,2048]{1,2,0:T(8,128)(2,1)}, u32[]{:S(2)}) copy-start(bf16[1,128,2048]{1,2,0:T(8,128)(2,1)} %copy-done.9) | copy-start | bytes 1572868
  164.4 7.1 %copy-start.4 = (bf16[128,8,4224]{0,2,1:T(8,128)(2,1)S(1)}, bf16[128,8,4224]{0,2,1:T(8,128)(2,1)}, u32[]{:S(2)}) copy-start(bf16[128,8,4224]{0,2,1:T(8,128)(2,1)} %copy-done.3) | copy-start | bytes 25952260
  164.4 7.1 %copy-start.12 = (bf16[1,128,2048]{1,2,0:T(8,128)(2,1)S(1)}, bf16[1,128,2048]{1,2,0:T(8,128)(2,1)}, u32[]{:S(2)}) copy-start(bf16[1,128,2048]{1,2,0:T(8,128)(2,1)} %copy-done.11) | copy-start | bytes 1572868
  176.6 27.5 %all-to-all-start.3 = ((bf16[8,512,256]{2,1,0:T(8,128)(2,1)}), bf16[8,512,256]{2,1,0:T(8,128)(2,1)S(1)}, u32[]{:S(2)}, u32[]{:S(2)}) async-start(bf16[8,512,256]{2,1,0:T(8,128)(2,1)} %pad_maximum_fusion.1), calls=%async_computation.3 | async-start | bytes 4194304 | tf_op jit(solution)/shard_map/all_to_all | solution.py:117
  208.0 15.4 %all-to-all-start.4 = ((bf16[4,128,512]{2,1,0:T(8,128)(2,1)}), bf16[4,128,512]{2,1,0:T(8,128)(2,1)S(1)}, u32[]{:S(2)}, u32[]{:S(2)}) async-start(bf16[4,128,512]{2,1,0:T(8,128)(2,1)} %pad_maximum_fusion.4), calls=%async_computation.4 | async-start | bytes 1048576 | tf_op jit(solution)/shard_map/all_to_all | solution.py:125
  224.7 5.4 %copy-start.29 = (bf16[1,8192]{1,0:T(2,128)(2,1)S(1)}, bf16[1,8192]{1,0:T(2,128)(2,1)}, u32[]{:S(2)}) copy-start(bf16[1,8192]{1,0:T(2,128)(2,1)} %param.20) | copy-start | bytes 49156
  224.7 5.5 %copy-start.8 = (bf16[4096,128]{1,0:T(8,128)(2,1)S(1)}, bf16[4096,128]{1,0:T(8,128)(2,1)}, u32[]{:S(2)}) copy-start(bf16[4096,128]{1,0:T(8,128)(2,1)} %copy-done.7) | copy-start | bytes 3145732
  224.7 5.5 %copy-start.26 = (bf16[128,128]{1,0:T(8,128)(2,1)S(1)}, bf16[128,128]{1,0:T(8,128)(2,1)}, u32[]{:S(2)}) copy-start(bf16[128,128]{1,0:T(8,128)(2,1)} %copy-done.25) | copy-start | bytes 98308
  229.4 11.8 %collective-permute-start = (bf16[2,128,8192]{2,1,0:T(8,128)(2,1)}, bf16[2,128,8192]{2,1,0:T(8,128)(2,1)}, u32[]{:S(2)}, u32[]{:S(2)}) collective-permute-start(bf16[2,128,8192]{2,1,0:T(8,128)(2,1)} %dynamic-slice_bitcast_fusion), channel_id=1, source_target_pairs={{0,1},{1,0},{2,3},{3,2},{4,5},{5,4},{6,7},{7,6},{8,9},{9,8},{10,11... | collective-permute-start | bytes 12582920 | tf_op jit(solution)/shard_map/ppermute | solution.py:149
  230.1 11.1 %slice-start.10 = ((s8[8388608]{0:T(1024)(128)(4,1)}), s8[4194304]{0:T(1024)(128)(4,1)S(1)}, s32[]{:S(2)}) async-start(s8[8388608]{0:T(1024)(128)(4,1)} %bitcast.243), calls=%async_computation.16 | async-start | bytes 8388608
  235.2 6.1 %slice-start.11 = ((s8[8388608]{0:T(1024)(128)(4,1)}), s8[4194304]{0:T(1024)(128)(4,1)S(1)}, s32[]{:S(2)}) async-start(s8[8388608]{0:T(1024)(128)(4,1)} %bitcast.243), calls=%async_computation.17 | async-start | bytes 8388608
  244.9 4.4 %copy-start = (f32[2,128,8192]{2,1,0:T(8,128)}, f32[2,128,8192]{2,1,0:T(8,128)S(1)}, u32[]{:S(2)}) copy-start(f32[2,128,8192]{2,1,0:T(8,128)S(1)} %convert_add_fusion) | copy-start | bytes 25165828
  245.1 12.4 %copy-start.13 = (f32[1,128,4,2,128]{1,4,0,3,2:T(8,128)S(1)}, f32[1,128,4,2,128]{1,4,0,3,2:T(8,128)}, u32[]{:S(2)}) copy-start(f32[1,128,4,2,128]{1,4,0,3,2:T(8,128)} %get-tuple-element.63) | copy-start | bytes 1572868
  245.1 20.0 %copy-start.2 = (bf16[1,128,8192]{2,1,0:T(8,128)(2,1)S(1)}, bf16[1,128,8192]{2,1,0:T(8,128)(2,1)}, u32[]{:S(2)}) copy-start(bf16[1,128,8192]{2,1,0:T(8,128)(2,1)} %param.19) | copy-start | bytes 6291460
  249.2 15.9 %collective-permute-start.1 = (bf16[32,8192]{1,0:T(8,128)(2,1)}, bf16[32,8192]{1,0:T(8,128)(2,1)}, u32[]{:S(2)}, u32[]{:S(2)}) collective-permute-start(bf16[32,8192]{1,0:T(8,128)(2,1)} %get-tuple-element.55), channel_id=1, source_target_pairs={{0,2},{1,3},{2,0},{3,1},{4,6},{5,7},{6,4},{7,5},{8,10},{9,11},{10,... | collective-permute-start | bytes 1572872 | tf_op jit(solution)/shard_map/ppermute | solution.py:162
  257.5 14.2 %copy-start.23 = (bf16[32,8192]{1,0:T(8,128)(2,1)S(1)}, bf16[32,8192]{1,0:T(8,128)(2,1)}, u32[]{:S(2)}) copy-start(bf16[32,8192]{1,0:T(8,128)(2,1)} %get-tuple-element.15) | copy-start | bytes 1572868
  265.2 23.1 %copy-start.1 = (f32[2,128,8192]{2,1,0:T(8,128)S(1)}, f32[2,128,8192]{2,1,0:T(8,128)}, u32[]{:S(2)}) copy-start(f32[2,128,8192]{2,1,0:T(8,128)} %copy-done) | copy-start | bytes 25165828
  267.5 23.2 %copy-start.22 = (bf16[32,8192]{1,0:T(8,128)(2,1)S(1)}, bf16[32,8192]{1,0:T(8,128)(2,1)}, u32[]{:S(2)}) copy-start(bf16[32,8192]{1,0:T(8,128)(2,1)} %get-tuple-element.16) | copy-start | bytes 1572868
  269.8 24.2 %collective-permute-start.3 = (bf16[32,8192]{1,0:T(8,128)(2,1)S(1)}, bf16[32,8192]{1,0:T(8,128)(2,1)S(1)}, u32[]{:S(2)}, u32[]{:S(2)}) collective-permute-start(bf16[32,8192]{1,0:T(8,128)(2,1)S(1)} %get-tuple-element.53), channel_id=1, source_target_pairs={{96,0},{97,1},{98,2},{99,3},{100,4},{101,5},{102,6},{103,7},{104,8... | collective-permute-start | bytes 1572872 | tf_op jit(solution)/shard_map/ppermute | solution.py:175
  271.1 22.9 %collective-permute-start.2 = (bf16[32,8192]{1,0:T(8,128)(2,1)S(1)}, bf16[32,8192]{1,0:T(8,128)(2,1)S(1)}, u32[]{:S(2)}, u32[]{:S(2)}) collective-permute-start(bf16[32,8192]{1,0:T(8,128)(2,1)S(1)} %get-tuple-element.53), channel_id=1, source_target_pairs={{96,64},{64,32},{97,65},{65,33},{98,66},{66,34},{99,67},{67,35},{1... | collective-permute-start | bytes 1572872 | tf_op jit(solution)/shard_map/ppermute | solution.py:174
  271.8 15.0 %collective-permute-start.5 = (bf16[32,8192]{1,0:T(8,128)(2,1)S(1)}, bf16[32,8192]{1,0:T(8,128)(2,1)S(1)}, u32[]{:S(2)}, u32[]{:S(2)}) collective-permute-start(bf16[32,8192]{1,0:T(8,128)(2,1)S(1)} %copy-done.23), channel_id=1, source_target_pairs={{0,2},{1,3},{2,0},{3,1},{4,6},{5,7},{6,4},{7,5},{8,10},{9,11},{10,... | collective-permute-start | bytes 1572872 | tf_op jit(solution)/shard_map/ppermute | solution.py:162
  288.6 18.8 %collective-permute-start.7 = (bf16[32,8192]{1,0:T(8,128)(2,1)S(1)}, bf16[32,8192]{1,0:T(8,128)(2,1)S(1)}, u32[]{:S(2)}, u32[]{:S(2)}) collective-permute-start(bf16[32,8192]{1,0:T(8,128)(2,1)S(1)} %get-tuple-element.51), channel_id=1, source_target_pairs={{96,0},{97,1},{98,2},{99,3},{100,4},{101,5},{102,6},{103,7},{104,8... | collective-permute-start | bytes 1572872 | tf_op jit(solution)/shard_map/ppermute | solution.py:175
  289.9 17.5 %collective-permute-start.6 = (bf16[32,8192]{1,0:T(8,128)(2,1)S(1)}, bf16[32,8192]{1,0:T(8,128)(2,1)S(1)}, u32[]{:S(2)}, u32[]{:S(2)}) collective-permute-start(bf16[32,8192]{1,0:T(8,128)(2,1)S(1)} %get-tuple-element.51), channel_id=1, source_target_pairs={{96,64},{64,32},{97,65},{65,33},{98,66},{66,34},{99,67},{67,35},{1... | collective-permute-start | bytes 1572872 | tf_op jit(solution)/shard_map/ppermute | solution.py:174
  290.7 14.1 %collective-permute-start.9 = (bf16[32,8192]{1,0:T(8,128)(2,1)S(1)}, bf16[32,8192]{1,0:T(8,128)(2,1)S(1)}, u32[]{:S(2)}, u32[]{:S(2)}) collective-permute-start(bf16[32,8192]{1,0:T(8,128)(2,1)S(1)} %copy-done.22), channel_id=1, source_target_pairs={{0,2},{1,3},{2,0},{3,1},{4,6},{5,7},{6,4},{7,5},{8,10},{9,11},{10,... | collective-permute-start | bytes 1572872 | tf_op jit(solution)/shard_map/ppermute | solution.py:162
  294.2 16.9 %copy-start.21 = (bf16[32,8192]{1,0:T(8,128)(2,1)S(1)}, bf16[32,8192]{1,0:T(8,128)(2,1)}, u32[]{:S(2)}) copy-start(bf16[32,8192]{1,0:T(8,128)(2,1)} %get-tuple-element.17) | copy-start | bytes 1572868
  294.2 20.3 %collective-permute-start.4 = (bf16[32,8192]{1,0:T(8,128)(2,1)S(1)}, bf16[32,8192]{1,0:T(8,128)(2,1)S(1)}, u32[]{:S(2)}, u32[]{:S(2)}) collective-permute-start(bf16[32,8192]{1,0:T(8,128)(2,1)S(1)} %fusion.28), channel_id=1, source_target_pairs={{32,0},{0,32},{33,1},{1,33},{34,2},{2,34},{35,3},{3,35},{36,4},{4,... | collective-permute-start | bytes 1572872 | tf_op jit(solution)/shard_map/ppermute | solution.py:181
  305.5 21.3 %collective-permute-start.11 = (bf16[32,8192]{1,0:T(8,128)(2,1)S(1)}, bf16[32,8192]{1,0:T(8,128)(2,1)S(1)}, u32[]{:S(2)}, u32[]{:S(2)}) collective-permute-start(bf16[32,8192]{1,0:T(8,128)(2,1)S(1)} %get-tuple-element.49), channel_id=1, source_target_pairs={{96,0},{97,1},{98,2},{99,3},{100,4},{101,5},{102,6},{103,7},{104,8... | collective-permute-start | bytes 1572872 | tf_op jit(solution)/shard_map/ppermute | solution.py:175
  306.8 20.0 %collective-permute-start.10 = (bf16[32,8192]{1,0:T(8,128)(2,1)S(1)}, bf16[32,8192]{1,0:T(8,128)(2,1)S(1)}, u32[]{:S(2)}, u32[]{:S(2)}) collective-permute-start(bf16[32,8192]{1,0:T(8,128)(2,1)S(1)} %get-tuple-element.49), channel_id=1, source_target_pairs={{96,64},{64,32},{97,65},{65,33},{98,66},{66,34},{99,67},{67,35},{1... | collective-permute-start | bytes 1572872 | tf_op jit(solution)/shard_map/ppermute | solution.py:174
  307.7 21.8 %collective-permute-start.8 = (bf16[32,8192]{1,0:T(8,128)(2,1)S(1)}, bf16[32,8192]{1,0:T(8,128)(2,1)S(1)}, u32[]{:S(2)}, u32[]{:S(2)}) collective-permute-start(bf16[32,8192]{1,0:T(8,128)(2,1)S(1)} %fusion.30), channel_id=1, source_target_pairs={{32,0},{0,32},{33,1},{1,33},{34,2},{2,34},{35,3},{3,35},{36,4},{4,... | collective-permute-start | bytes 1572872 | tf_op jit(solution)/shard_map/ppermute | solution.py:181
  311.1 13.0 %collective-permute-start.13 = (bf16[32,8192]{1,0:T(8,128)(2,1)S(1)}, bf16[32,8192]{1,0:T(8,128)(2,1)S(1)}, u32[]{:S(2)}, u32[]{:S(2)}) collective-permute-start(bf16[32,8192]{1,0:T(8,128)(2,1)S(1)} %copy-done.21), channel_id=1, source_target_pairs={{0,2},{1,3},{2,0},{3,1},{4,6},{5,7},{6,4},{7,5},{8,10},{9,11},{10,... | collective-permute-start | bytes 1572872 | tf_op jit(solution)/shard_map/ppermute | solution.py:162
  324.8 13.6 %collective-permute-start.15 = (bf16[32,8192]{1,0:T(8,128)(2,1)S(1)}, bf16[32,8192]{1,0:T(8,128)(2,1)S(1)}, u32[]{:S(2)}, u32[]{:S(2)}) collective-permute-start(bf16[32,8192]{1,0:T(8,128)(2,1)S(1)} %get-tuple-element.47), channel_id=1, source_target_pairs={{96,0},{97,1},{98,2},{99,3},{100,4},{101,5},{102,6},{103,7},{104,8... | collective-permute-start | bytes 1572872 | tf_op jit(solution)/shard_map/ppermute | solution.py:175
  326.1 12.3 %collective-permute-start.14 = (bf16[32,8192]{1,0:T(8,128)(2,1)S(1)}, bf16[32,8192]{1,0:T(8,128)(2,1)S(1)}, u32[]{:S(2)}, u32[]{:S(2)}) collective-permute-start(bf16[32,8192]{1,0:T(8,128)(2,1)S(1)} %get-tuple-element.47), channel_id=1, source_target_pairs={{96,64},{64,32},{97,65},{65,33},{98,66},{66,34},{99,67},{67,35},{1... | collective-permute-start | bytes 1572872 | tf_op jit(solution)/shard_map/ppermute | solution.py:174
  327.0 13.5 %collective-permute-start.12 = (bf16[32,8192]{1,0:T(8,128)(2,1)S(1)}, bf16[32,8192]{1,0:T(8,128)(2,1)S(1)}, u32[]{:S(2)}, u32[]{:S(2)}) collective-permute-start(bf16[32,8192]{1,0:T(8,128)(2,1)S(1)} %fusion.32), channel_id=1, source_target_pairs={{32,0},{0,32},{33,1},{1,33},{34,2},{2,34},{35,3},{3,35},{36,4},{4,... | collective-permute-start | bytes 1572872 | tf_op jit(solution)/shard_map/ppermute | solution.py:181
  338.6 12.1 %collective-permute-start.16 = (bf16[32,8192]{1,0:T(8,128)(2,1)S(1)}, bf16[32,8192]{1,0:T(8,128)(2,1)S(1)}, u32[]{:S(2)}, u32[]{:S(2)}) collective-permute-start(bf16[32,8192]{1,0:T(8,128)(2,1)S(1)} %fusion.34), channel_id=1, source_target_pairs={{32,0},{0,32},{33,1},{1,33},{34,2},{2,34},{35,3},{3,35},{36,4},{4,... | collective-permute-start | bytes 1572872 | tf_op jit(solution)/shard_map/ppermute | solution.py:181
  (4 other events, 3.9 us)
Sparse Core Ops, SparseCore 0:
  36.5 62.7 all-gather.2

commit v2 on v1

--- a/solution.py
+++ b/solution.py
@@ -129,38 +129,46 @@
         value_home = home[1]
 
         grad_cols = reduced.reshape(block_rows, kv_local, 2, HEAD_SIZE).transpose(0, 2, 1, 3)
-        grad_cols = grad_cols.reshape(block_rows, 2, kv_local * HEAD_SIZE)
-        group_term = lax.dot_general(
-            grad_cols, kv_weight[0], (((1, 2), (1, 2)), ((), ())), preferred_element_type=jnp.float32
-        ).astype(jnp.bfloat16)
-        key_home, value_home, group_term = lax.optimization_barrier((key_home, value_home, group_term))
-        width = group_term.shape[1]
+        grad_cols = grad_cols.reshape(n_ten, rows_local, 2, kv_local * HEAD_SIZE)
+        weight_local = kv_weight[0]
+        width = weight_local.shape[0]
         t_idx = lax.axis_index("tensor")
         core = t_idx % 2
         hi = t_idx // 2
-        term4 = group_term.reshape(2, 2, rows_local, width)
-        keep = lax.dynamic_index_in_dim(term4, core, 1, False)
-        give = lax.dynamic_index_in_dim(term4, 1 - core, 1, False)
         core_pairs = [(i, i ^ 1) for i in range(n_ten)]
         chip_pairs = [(i, i ^ 2) for i in range(n_ten)]
         states_all = prefix_states[0]
         gain_wide = norm_gain[0].astype(jnp.float32)[None, :]
         sec = lax.axis_index("section")
-        got1 = lax.ppermute(give, "tensor", core_pairs)
-        partial = keep.astype(jnp.float32) + got1.astype(jnp.float32)
-        mine_all = lax.dynamic_index_in_dim(partial, hi, 0, False)
-        other_all = lax.dynamic_index_in_dim(partial, 1 - hi, 0, False).astype(jnp.bfloat16)
         n_chunks = 4
         step = rows_local // n_chunks
         outs = []
         previous = None
         for c in range(n_chunks):
             rows = slice(c * step, (c + 1) * step)
-            other = other_all[rows]
+            grad_rows_c = grad_cols[:, rows]
+            if c > 0:
+                grad_rows_c, sent = lax.optimization_barrier((grad_rows_c, sent))
+            group_term = lax.dot_general(
+                grad_rows_c, weight_local, (((2, 3), (1, 2)), ((), ())),
+                preferred_element_type=jnp.float32,
+            ).astype(jnp.bfloat16)
+            if c == 0:
+                key_home, value_home, group_term = lax.optimization_barrier(
+                    (key_home, value_home, group_term)
+                )
+            term4 = group_term.reshape(2, 2, step, width)
+            keep = lax.dynamic_index_in_dim(term4, core, 1, False)
+            give = lax.dynamic_index_in_dim(term4, 1 - core, 1, False)
+            got1 = lax.ppermute(give, "tensor", core_pairs)
+            partial = keep.astype(jnp.float32) + got1.astype(jnp.float32)
+            mine = lax.dynamic_index_in_dim(partial, hi, 0, False)
+            other = lax.dynamic_index_in_dim(partial, 1 - hi, 0, False).astype(jnp.bfloat16)
             if previous is not None:
                 other, previous = lax.optimization_barrier((other, previous))
+            sent = other
             got2 = lax.ppermute(other, "tensor", chip_pairs)
-            normed_grad = mine_all[rows] + got2.astype(jnp.float32)
+            normed_grad = mine + got2.astype(jnp.float32)
 
             states = states_all[rows].astype(jnp.float32)
             inv_rms = lax.rsqrt(jnp.mean(states * states, axis=1, keepdims=True) + EPSILON)

time: 364 us -> 356 us (0.978)
  matrix products: 61.7 us -> 71 us
  other arithmetic: 62.5 us -> 55.2 us
  local copies, waits for them, and re-layouts: 46.7 us -> 40.1 us
  starting transfers between devices: 56.8 us -> 50.7 us
    ppermute x4, waiting for transfers between devices: 34.7 us -> 20.3 us  [on_device(): got2 = lax.ppermute(other, 'tensor', chip_pairs)]
    ppermute x4, waiting for transfers between devices: 9.88 us -> 21.2 us  [on_device(): last = lax.ppermute(carry.astype(jnp.bfloat16), 'section', [(1, 0), (0, 1)])]
    dot_general x1 -> x4, matrix products: 10.1 us -> 19.8 us  [on_device(): lax.dot_general(grad_rows_c, weight_local, (((2, 3), (1, 2)), ((), ())),...]
    ppermute x4, waiting for transfers between devices: 8.68 us -> 17.7 us  [on_device(): wrap = lax.ppermute(term_low, 'section', [(3, 0)])]
    all_to_all x2, waiting for transfers between devices: 19.1 us -> 13.2 us  [on_device(): parts = lax.all_to_all(pool_grad, 'sample', 0, 0, tiled=False)]
    ppermute x4, starting transfers between devices: 13.1 us -> 7.28 us  [on_device(): got2 = lax.ppermute(other, 'tensor', chip_pairs)]
    unnamed x99 -> x97, local copies, waits for them, and re-layouts: 23.5 us -> 20.6 us
  transfers between devices with their start and end apart: 23 -> 26, of which waited for: 9 -> 12; matrix products, arithmetic and copies ran while one was open for 35% -> 38% of each run, Pallas kernels for 0% -> 0%
where the time goes in v2:
time: 356 us; the launch traced here: 353 us
  waiting for transfers between devices  120 us (34%)
  matrix products  71 us (20%)
  other arithmetic  55.2 us (16%)
  starting transfers between devices  50.7 us (14%)
  local copies, waits for them, and re-layouts  40.1 us (11%)
  between operations  15.4 us (4%)
    all_to_all x1, waiting for transfers between devices, on_device(): lax.all_to_all(spread, 'sample', 0, 0, tiled=True).reshape(pooled_rows, -1)  35.9 us
    ppermute x4, waiting for transfers between devices, on_device(): last = lax.ppermute(carry.astype(jnp.bfloat16), 'section', [(1, 0), (0, 1)])  21.2 us
    unnamed x97, local copies, waits for them, and re-layouts  20.6 us
    sub x2, other arithmetic, attend_group(): exponent = jnp.exp(scores - row_max)  20.4 us
    ppermute x4, waiting for transfers between devices, on_device(): got2 = lax.ppermute(other, 'tensor', chip_pairs)  20.3 us
    dot_general x4, matrix products, on_device(): lax.dot_general(grad_rows_c, weight_local, (((2, 3), (1, 2)), ((), ())),...  19.8 us
    ppermute x4, waiting for transfers between devices, on_device(): wrap = lax.ppermute(term_low, 'section', [(3, 0)])  17.7 us
    convert_element_type x2, other arithmetic, attend_group(): weights_low = softmax_w.astype(jnp.bfloat16)  15 us
  transfers between devices with their start and end apart: 26, of which 12 were waited for; matrix products, arithmetic and copies ran while one was open for 38% of the time, Pallas kernels for 0%

profile of v2, /device:TPU:0, one launch (start us, length us, event | category | flops | bytes accessed | tf_op | source)
XLA Modules:
  0.0 352.5 jit_solution(4396307207459906739)
XLA Ops:
  7.2 1.2 copy.108
  8.4 1.1 copy.109
  10.3 4.6 %all-to-all-start = ((bf16[4,128,512]{1,2,0:T(8,128)(2,1)}), bf16[4,128,512]{1,2,0:T(8,128)(2,1)S(1)}, u32[]{:S(2)}, u32[]{:S(2)}) async-start(bf16[4,128,512]{1,2,0:T(8,128)(2,1)} %bitcast.6), calls=%async_computation | async-start | bytes 1048576 | tf_op jit(solution)/shard_map/all_to_all | solution.py:89
  15.2 10.0 %all-to-all-done = bf16[4,128,512]{1,2,0:T(8,128)(2,1)S(1)} async-done(((bf16[4,128,512]{1,2,0:T(8,128)(2,1)}), bf16[4,128,512]{1,2,0:T(8,128)(2,1)S(1)}, u32[]{:S(2)}, u32[]{:S(2)}) %all-to-all-start) | async-done | bytes 524320 | tf_op jit(solution)/shard_map/all_to_all | solution.py:89
  26.4 1.5 broadcast_in_dim.91
  27.8 5.6 %all-to-all-start.1 = ((bf16[8,512,256]{2,1,0:T(8,128)(2,1)}), bf16[8,512,256]{2,1,0:T(8,128)(2,1)}, u32[]{:S(2)}, u32[]{:S(2)}) async-start(bf16[8,512,256]{2,1,0:T(8,128)(2,1)} %broadcast_in_dim.91), calls=%async_computation.1 | async-start | bytes 4194304 | tf_op jit(solution)/shard_map/all_to_all | solution.py:98
  36.5 35.9 %all-to-all-done.1 = bf16[8,512,256]{2,1,0:T(8,128)(2,1)} async-done(((bf16[8,512,256]{2,1,0:T(8,128)(2,1)}), bf16[8,512,256]{2,1,0:T(8,128)(2,1)}, u32[]{:S(2)}, u32[]{:S(2)}) %all-to-all-start.1) | async-done | bytes 2097184 | tf_op jit(solution)/shard_map/all_to_all | solution.py:98
  72.3 2.7 fusion.101
  75.9 2.4 fusion.64
  78.3 10.2 %fusion.110 = (f32[128,8]{0,1:T(8,128)S(1)}, f32[128,8,4224]{0,2,1:T(8,128)}) fusion(f32[4224,128,8]{1,0,2:T(8,128)S(1)} %fusion.64, pred[128,4224]{0,1:T(8,128)(4,1)S(1)} %pad_add_fusion), kind=kOutput, calls=%fused_computation.208 | output fusion | flops 17305728 | bytes 35147776 | tf_op jit(solution)/shard_map/sub | solution.py:36
  88.6 7.5 %fusion.18 = bf16[128,8,4224]{0,2,1:T(8,128)(2,1)S(1)} fusion(f32[128,8,4224]{0,2,1:T(8,128)} %get-tuple-element.89, f32[128,8]{0,1:T(8,128)S(1)} %get-tuple-element.88), kind=kLoop, calls=%fused_computation.30 | loop fusion | flops 8650752 | bytes 25956352 | tf_op jit(solution)/shard_map/convert_element_type | solution.py:38
  96.2 4.4 %copy-done.3 = bf16[128,8,4224]{0,2,1:T(8,128)(2,1)} copy-done((bf16[128,8,4224]{0,2,1:T(8,128)(2,1)}, bf16[128,8,4224]{0,2,1:T(8,128)(2,1)S(1)}, u32[]{:S(2)}) %copy-start.3) | copy-done | bytes 8650776
  100.5 2.5 fusion.31
  103.2 6.5 %fusion.3 = bf16[128,8,4224]{0,2,1:T(8,128)(2,1)} fusion(f32[128,8]{0,1:T(8,128)S(1)} %fusion.31, f32[128,8,4224]{0,2,1:T(8,128)S(1)} %bitcast.285, f32[128,8]{0,1:T(8,128)S(1)} %get-tuple-element.88, bf16[128,128]{1,0:T(8,128)(2,1)S(1)} %get-tuple-element.74, bf16[4096,128]{1,0:T(8,128)(2,1)} %get-tuple-element.61, bf16[128,2,8,128]{0,3,2,1:T(8,128)(2,1)S(1)} %bitcast.315), kind=kOutput, calls=%fused_computation.6 | convolution fusion | flops 1126760448 | bytes 27303936 | tf_op jit(solution)/shard_map/rgd,kd->rgk/dot_general | solution.py:43
  109.8 6.0 %fusion.25 = bf16[4224,128]{1,0:T(8,128)(2,1)S(1)} fusion(bf16[128,8,4224]{0,2,1:T(8,128)(2,1)} %fusion.3, bf16[128,2,8,128]{0,3,2,1:T(8,128)(2,1)S(1)} %bitcast.302), kind=kOutput, calls=%fused_computation.41 | convolution fusion | flops 1108377600 | bytes 9994240 | tf_op jit(solution)/shard_map/rgk,rgd->kd/dot_general | solution.py:52
  116.9 2.5 fusion.27
  120.4 1.5 pad_maximum_fusion
  122.0 4.4 %all-to-all-start.2 = ((bf16[8,512,256]{2,1,0:T(8,128)(2,1)}), bf16[8,512,256]{2,1,0:T(8,128)(2,1)}, u32[]{:S(2)}, u32[]{:S(2)}) async-start(bf16[8,512,256]{2,1,0:T(8,128)(2,1)} %pad_maximum_fusion), calls=%async_computation.2 | async-start | bytes 4194304 | tf_op jit(solution)/shard_map/all_to_all | solution.py:117
  126.4 2.7 fusion.102
  129.1 2.4 fusion.63
  131.5 10.2 %fusion.109 = (f32[128,8]{0,1:T(8,128)S(1)}, f32[128,8,4224]{0,2,1:T(8,128)}) fusion(f32[4224,128,8]{1,0,2:T(8,128)S(1)} %fusion.63, pred[128,4224]{0,1:T(8,128)(4,1)S(1)} %pad_add_fusion), kind=kOutput, calls=%fused_computation.207 | output fusion | flops 17305728 | bytes 35147776 | tf_op jit(solution)/shard_map/sub | solution.py:36
  141.7 7.5 %fusion.19 = bf16[128,8,4224]{0,2,1:T(8,128)(2,1)S(1)} fusion(f32[128,8,4224]{0,2,1:T(8,128)} %get-tuple-element.87, f32[128,8]{0,1:T(8,128)S(1)} %get-tuple-element.86), kind=kLoop, calls=%fused_computation.31 | loop fusion | flops 8650752 | bytes 25956352 | tf_op jit(solution)/shard_map/convert_element_type | solution.py:38
  149.2 4.4 %copy-done.1 = bf16[128,8,4224]{0,2,1:T(8,128)(2,1)} copy-done((bf16[128,8,4224]{0,2,1:T(8,128)(2,1)}, bf16[128,8,4224]{0,2,1:T(8,128)(2,1)S(1)}, u32[]{:S(2)}) %copy-start.1) | copy-done | bytes 8650776
  153.6 2.5 fusion.32
  156.2 7.2 %fusion.2 = bf16[128,8,4224]{0,2,1:T(8,128)(2,1)} fusion(f32[128,8]{0,1:T(8,128)S(1)} %fusion.32, f32[128,8,4224]{0,2,1:T(8,128)S(1)} %bitcast.283, f32[128,8]{0,1:T(8,128)S(1)} %get-tuple-element.86, bf16[128,128]{1,0:T(8,128)(2,1)S(1)} %get-tuple-element.75, bf16[4096,128]{1,0:T(8,128)(2,1)} %get-tuple-element.63, bf16[128,2,8,128]{0,3,2,1:T(8,128)(2,1)} %bitcast.317), kind=kOutput, calls=%fused_computation.3 | convolution fusion | flops 1126760448 | bytes 27303936 | tf_op jit(solution)/shard_map/rgd,kd->rgk/dot_general | solution.py:43
  163.5 6.0 %fusion.26 = bf16[4224,128]{1,0:T(8,128)(2,1)S(1)} fusion(bf16[128,8,4224]{0,2,1:T(8,128)(2,1)} %fusion.2, bf16[128,2,8,128]{0,3,2,1:T(8,128)(2,1)S(1)} %bitcast.304), kind=kOutput, calls=%fused_computation.42 | convolution fusion | flops 1108377600 | bytes 9994240 | tf_op jit(solution)/shard_map/rgk,rgd->kd/dot_general | solution.py:52
  170.6 2.4 fusion.28
  174.1 1.6 pad_maximum_fusion.1
  175.6 5.7 %all-to-all-start.3 = ((bf16[8,512,256]{2,1,0:T(8,128)(2,1)}), bf16[8,512,256]{2,1,0:T(8,128)(2,1)S(1)}, u32[]{:S(2)}, u32[]{:S(2)}) async-start(bf16[8,512,256]{2,1,0:T(8,128)(2,1)} %pad_maximum_fusion.1), calls=%async_computation.3 | async-start | bytes 4194304 | tf_op jit(solution)/shard_map/all_to_all | solution.py:117
  181.4 5.9 %fusion.34 = bf16[128,1,8,128]{0,3,2,1:T(8,128)(2,1)} fusion(bf16[128,8,4224]{0,2,1:T(8,128)(2,1)} %fusion.3, bf16[128,128]{1,0:T(8,128)(2,1)S(1)} %get-tuple-element.76, bf16[4096,128]{1,0:T(8,128)(2,1)} %copy-done.5), kind=kOutput, calls=%fused_computation.90 | convolution fusion | flops 1109721088 | bytes 9994240 | tf_op jit(solution)/shard_map/rgk,kd->rgd/dot_general | solution.py:48
  187.3 2.0 reduce
  190.1 13.2 %all-to-all-done.3 = bf16[8,512,256]{2,1,0:T(8,128)(2,1)S(1)} async-done(((bf16[8,512,256]{2,1,0:T(8,128)(2,1)}), bf16[8,512,256]{2,1,0:T(8,128)(2,1)S(1)}, u32[]{:S(2)}, u32[]{:S(2)}) %all-to-all-start.3) | async-done | bytes 2097184 | tf_op jit(solution)/shard_map/all_to_all | solution.py:117
  204.3 1.1 copy.130
  205.4 1.8 pad_maximum_fusion.4
  207.2 3.5 all-to-all-start.4
  211.6 7.7 %fusion.9 = bf16[4,32,8192]{2,1,0:T(8,128)(2,1)} fusion(bf16[8192,2,256]{2,1,0:T(2,128)(2,1)} %bitcast.334, bf16[4,128,2,256]{3,1,0,2:T(8,128)(2,1)S(1)} %reshape.274), kind=kOutput, calls=%fused_computation.19 | convolution fusion | flops 1074790400 | bytes 10616832 | tf_op jit(solution)/shard_map/dot_general | solution.py:152
  219.3 1.7 all-to-all-done.4
  224.5 4.9 %fusion.33 = bf16[128,1,8,128]{0,3,2,1:T(8,128)(2,1)S(1)} fusion(bf16[128,8,4224]{0,2,1:T(8,128)(2,1)} %fusion.2, bf16[128,128]{1,0:T(8,128)(2,1)S(1)} %get-tuple-element.77, bf16[4096,128]{1,0:T(8,128)(2,1)S(1)} %get-tuple-element.64), kind=kOutput, calls=%fused_computation.89 | convolution fusion | flops 1109721088 | bytes 9994240 | tf_op jit(solution)/shard_map/rgk,kd->rgd/dot_general | solution.py:48
  234.3 2.0 copy.134
  237.4 1.4 convert_add_fusion.3
  238.9 2.0 collective-permute-start.1
  240.8 6.4 %fusion.6 = bf16[4,32,8192]{2,1,0:T(8,128)(2,1)S(1)} fusion(bf16[4,32,2,256]{3,1,0,2:T(8,128)(2,1)S(1)} %get-tuple-element.18, bf16[8192,2,256,1]{2,1,0,3:T(2,128)(2,1)} %bitcast.335), kind=kOutput, calls=%fused_computation.16 | convolution fusion | flops 1074790400 | bytes 10616832 | tf_op jit(solution)/shard_map/dot_general | solution.py:152
  247.5 7.3 %collective-permute-done.1 = bf16[32,8192]{1,0:T(8,128)(2,1)S(1)} collective-permute-done((bf16[32,8192]{1,0:T(8,128)(2,1)S(1)}, bf16[32,8192]{1,0:T(8,128)(2,1)S(1)}, u32[]{:S(2)}, u32[]{:S(2)}) %collective-permute-start.1) | collective-permute-done | bytes 524320 | tf_op jit(solution)/shard_map/ppermute | solution.py:170
  255.9 1.3 collective-permute-start.3
  258.2 1.9 collective-permute-start.6
  260.1 2.8 fusion.7
  263.1 9.3 %collective-permute-done.3 = bf16[32,8192]{1,0:T(8,128)(2,1)S(1)} collective-permute-done((bf16[32,8192]{1,0:T(8,128)(2,1)S(1)}, bf16[32,8192]{1,0:T(8,128)(2,1)S(1)}, u32[]{:S(2)}, u32[]{:S(2)}) %collective-permute-start.3) | collective-permute-done | bytes 524320 | tf_op jit(solution)/shard_map/ppermute | solution.py:183
  272.6 2.9 collective-permute-start.4
  276.2 1.3 collective-permute-start.8
  278.2 8.9 %collective-permute-done.4 = bf16[32,8192]{1,0:T(8,128)(2,1)S(1)} collective-permute-done((bf16[32,8192]{1,0:T(8,128)(2,1)S(1)}, bf16[32,8192]{1,0:T(8,128)(2,1)S(1)}, u32[]{:S(2)}, u32[]{:S(2)}) %collective-permute-start.4) | collective-permute-done | bytes 524320 | tf_op jit(solution)/shard_map/ppermute | solution.py:189
  287.6 1.9 collective-permute-start.11
  289.5 2.8 fusion.8
  292.8 2.9 collective-permute-start.9
  295.7 5.5 %collective-permute-done.11 = bf16[32,8192]{1,0:T(8,128)(2,1)S(1)} collective-permute-done((bf16[32,8192]{1,0:T(8,128)(2,1)S(1)}, bf16[32,8192]{1,0:T(8,128)(2,1)S(1)}, u32[]{:S(2)}, u32[]{:S(2)}) %collective-permute-start.11) | collective-permute-done | bytes 524320 | tf_op jit(solution)/shard_map/ppermute | solution.py:170
  301.9 1.3 collective-permute-start.13
  304.2 1.6 collective-permute-start.16
  305.7 3.2 collective-permute-done.9
  309.2 7.5 %collective-permute-done.16 = bf16[32,8192]{1,0:T(8,128)(2,1)S(1)} collective-permute-done((bf16[32,8192]{1,0:T(8,128)(2,1)S(1)}, bf16[32,8192]{1,0:T(8,128)(2,1)S(1)}, u32[]{:S(2)}, u32[]{:S(2)}) %collective-permute-start.16) | collective-permute-done | bytes 524320 | tf_op jit(solution)/shard_map/ppermute | solution.py:170
  317.4 1.3 collective-permute-start.18
  319.6 2.9 collective-permute-start.14
  322.5 8.4 %collective-permute-done.18 = bf16[32,8192]{1,0:T(8,128)(2,1)S(1)} collective-permute-done((bf16[32,8192]{1,0:T(8,128)(2,1)S(1)}, bf16[32,8192]{1,0:T(8,128)(2,1)S(1)}, u32[]{:S(2)}, u32[]{:S(2)}) %collective-permute-start.18) | collective-permute-done | bytes 524320 | tf_op jit(solution)/shard_map/ppermute | solution.py:183
  331.1 2.4 collective-permute-start.19
  333.7 9.0 %collective-permute-done.19 = bf16[32,8192]{1,0:T(8,128)(2,1)S(1)} collective-permute-done((bf16[32,8192]{1,0:T(8,128)(2,1)S(1)}, bf16[32,8192]{1,0:T(8,128)(2,1)S(1)}, u32[]{:S(2)}, u32[]{:S(2)}) %collective-permute-start.19) | collective-permute-done | bytes 524320 | tf_op jit(solution)/shard_map/ppermute | solution.py:189
  343.0 2.4 maximum_bitcast_fusion
  (187 shorter events, 31.8 us)
Async XLA Ops:
  7.2 7.7 %copy-start.22 = (bf16[1,128,2048]{2,1,0:T(8,128)(2,1)S(1)}, bf16[1,128,2048]{2,1,0:T(8,128)(2,1)}, u32[]{:S(2)}) copy-start(bf16[1,128,2048]{2,1,0:T(8,128)(2,1)} %param.15) | copy-start | bytes 1572868
  10.3 14.9 %all-to-all-start = ((bf16[4,128,512]{1,2,0:T(8,128)(2,1)}), bf16[4,128,512]{1,2,0:T(8,128)(2,1)S(1)}, u32[]{:S(2)}, u32[]{:S(2)}) async-start(bf16[4,128,512]{1,2,0:T(8,128)(2,1)} %bitcast.6), calls=%async_computation | async-start | bytes 1048576 | tf_op jit(solution)/shard_map/all_to_all | solution.py:89
  15.2 101.7 %copy-start.11 = (bf16[1,128,2048]{1,2,0:T(8,128)(2,1)}, bf16[1,128,2048]{1,2,0:T(8,128)(2,1)S(1)}, u32[]{:S(2)}) copy-start(bf16[1,128,2048]{1,2,0:T(8,128)(2,1)S(1)} %copy.113) | copy-start | bytes 1572868
  27.8 5.9 %copy-start.23 = (bf16[1,128,2048]{2,1,0:T(8,128)(2,1)S(1)}, bf16[1,128,2048]{2,1,0:T(8,128)(2,1)}, u32[]{:S(2)}) copy-start(bf16[1,128,2048]{2,1,0:T(8,128)(2,1)} %param.12) | copy-start | bytes 1572868
  27.8 44.5 %all-to-all-start.1 = ((bf16[8,512,256]{2,1,0:T(8,128)(2,1)}), bf16[8,512,256]{2,1,0:T(8,128)(2,1)}, u32[]{:S(2)}, u32[]{:S(2)}) async-start(bf16[8,512,256]{2,1,0:T(8,128)(2,1)} %broadcast_in_dim.91), calls=%async_computation.1 | async-start | bytes 4194304 | tf_op jit(solution)/shard_map/all_to_all | solution.py:98
  33.4 1.7 copy-start.31
  33.4 1.8 copy-start.30
  33.4 2.0 copy-start.26
  33.4 2.1 copy-start.27
  33.4 92.9 %all-gather.3.cloned.1.call-start = ((), (), s32[]{:S(2)}) async-start(), calls=%async_computation.5 | async-start | bytes 2359296 | tf_op jit(solution)/shard_map/all_gather | solution.py:100
  34.0 75.8 %copy-start.6 = (bf16[1,128,2048]{1,2,0:T(8,128)(2,1)}, bf16[1,128,2048]{1,2,0:T(8,128)(2,1)S(1)}, u32[]{:S(2)}) copy-start(bf16[1,128,2048]{1,2,0:T(8,128)(2,1)S(1)} %copy.111) | copy-start | bytes 1572868
  88.6 12.0 %copy-start.21 = (bf16[4096,128]{1,0:T(8,128)(2,1)S(1)}, bf16[4096,128]{1,0:T(8,128)(2,1)}, u32[]{:S(2)}) copy-start(bf16[4096,128]{1,0:T(8,128)(2,1)} %get-tuple-element.61) | copy-start | bytes 3145732
  88.6 12.0 %copy-start.24 = (bf16[128,1,8,128]{3,0,2,1:T(8,128)(2,1)S(1)}, bf16[128,1,8,128]{3,0,2,1:T(8,128)(2,1)}, u32[]{:S(2)}) copy-start(bf16[128,1,8,128]{3,0,2,1:T(8,128)(2,1)} %copy.170) | copy-start | bytes 786436
  88.6 14.5 %slice-start.5 = ((s8[17301504]{0:T(1024)(128)(4,1)}), s8[4194304]{0:T(1024)(128)(4,1)S(1)}, s32[]{:S(2)}) async-start(s8[17301504]{0:T(1024)(128)(4,1)} %bitcast.284), calls=%async_computation.11 | async-start | bytes 8388608
  88.6 14.5 %slice-start.6 = ((s8[17301504]{0:T(1024)(128)(4,1)}), s8[4194304]{0:T(1024)(128)(4,1)S(1)}, s32[]{:S(2)}) async-start(s8[17301504]{0:T(1024)(128)(4,1)} %bitcast.284), calls=%async_computation.12 | async-start | bytes 8388608
  88.6 14.5 %slice-start.7 = ((s8[17301504]{0:T(1024)(128)(4,1)}), s8[4194304]{0:T(1024)(128)(4,1)S(1)}, s32[]{:S(2)}) async-start(s8[17301504]{0:T(1024)(128)(4,1)} %bitcast.284), calls=%async_computation.13 | async-start | bytes 8388608
  88.6 14.5 %slice-start.8 = ((s8[17301504]{0:T(1024)(128)(4,1)}), s8[4194304]{0:T(1024)(128)(4,1)S(1)}, s32[]{:S(2)}) async-start(s8[17301504]{0:T(1024)(128)(4,1)} %bitcast.284), calls=%async_computation.14 | async-start | bytes 8388608
  96.1 4.4 %copy-start.3 = (bf16[128,8,4224]{0,2,1:T(8,128)(2,1)}, bf16[128,8,4224]{0,2,1:T(8,128)(2,1)S(1)}, u32[]{:S(2)}) copy-start(bf16[128,8,4224]{0,2,1:T(8,128)(2,1)S(1)} %fusion.18) | copy-start | bytes 25952260
  100.5 2.7 slice-start.9
  109.8 7.1 %copy-start.4 = (bf16[128,8,4224]{0,2,1:T(8,128)(2,1)S(1)}, bf16[128,8,4224]{0,2,1:T(8,128)(2,1)}, u32[]{:S(2)}) copy-start(bf16[128,8,4224]{0,2,1:T(8,128)(2,1)} %copy-done.3) | copy-start | bytes 25952260
  122.0 53.7 %all-to-all-start.2 = ((bf16[8,512,256]{2,1,0:T(8,128)(2,1)}), bf16[8,512,256]{2,1,0:T(8,128)(2,1)}, u32[]{:S(2)}, u32[]{:S(2)}) async-start(bf16[8,512,256]{2,1,0:T(8,128)(2,1)} %pad_maximum_fusion), calls=%async_computation.2 | async-start | bytes 4194304 | tf_op jit(solution)/shard_map/all_to_all | solution.py:117
  126.4 2.7 copy-start.7
  141.7 11.9 %copy-start.20 = (bf16[4096,128]{1,0:T(8,128)(2,1)S(1)}, bf16[4096,128]{1,0:T(8,128)(2,1)}, u32[]{:S(2)}) copy-start(bf16[4096,128]{1,0:T(8,128)(2,1)} %get-tuple-element.63) | copy-start | bytes 3145732
  141.7 14.4 %slice-start = ((s8[17301504]{0:T(1024)(128)(4,1)}), s8[4194304]{0:T(1024)(128)(4,1)S(1)}, s32[]{:S(2)}) async-start(s8[17301504]{0:T(1024)(128)(4,1)} %bitcast.282), calls=%async_computation.6 | async-start | bytes 8388608
  141.7 14.4 %slice-start.1 = ((s8[17301504]{0:T(1024)(128)(4,1)}), s8[4194304]{0:T(1024)(128)(4,1)S(1)}, s32[]{:S(2)}) async-start(s8[17301504]{0:T(1024)(128)(4,1)} %bitcast.282), calls=%async_computation.7 | async-start | bytes 8388608
  141.7 14.4 %slice-start.2 = ((s8[17301504]{0:T(1024)(128)(4,1)}), s8[4194304]{0:T(1024)(128)(4,1)S(1)}, s32[]{:S(2)}) async-start(s8[17301504]{0:T(1024)(128)(4,1)} %bitcast.282), calls=%async_computation.8 | async-start | bytes 8388608
  141.7 14.4 %slice-start.3 = ((s8[17301504]{0:T(1024)(128)(4,1)}), s8[4194304]{0:T(1024)(128)(4,1)S(1)}, s32[]{:S(2)}) async-start(s8[17301504]{0:T(1024)(128)(4,1)} %bitcast.282), calls=%async_computation.9 | async-start | bytes 8388608
  149.2 4.4 %copy-start.1 = (bf16[128,8,4224]{0,2,1:T(8,128)(2,1)}, bf16[128,8,4224]{0,2,1:T(8,128)(2,1)S(1)}, u32[]{:S(2)}) copy-start(bf16[128,8,4224]{0,2,1:T(8,128)(2,1)S(1)} %fusion.19) | copy-start | bytes 25952260
  153.6 2.6 slice-start.4
  156.2 7.3 %copy-start.8 = (bf16[1,128,2048]{1,2,0:T(8,128)(2,1)S(1)}, bf16[1,128,2048]{1,2,0:T(8,128)(2,1)}, u32[]{:S(2)}) copy-start(bf16[1,128,2048]{1,2,0:T(8,128)(2,1)} %copy-done.6) | copy-start | bytes 1572868
  163.5 7.1 %copy-start.2 = (bf16[128,8,4224]{0,2,1:T(8,128)(2,1)S(1)}, bf16[128,8,4224]{0,2,1:T(8,128)(2,1)}, u32[]{:S(2)}) copy-start(bf16[128,8,4224]{0,2,1:T(8,128)(2,1)} %copy-done.1) | copy-start | bytes 25952260
  163.5 7.1 %copy-start.12 = (bf16[1,128,2048]{1,2,0:T(8,128)(2,1)S(1)}, bf16[1,128,2048]{1,2,0:T(8,128)(2,1)}, u32[]{:S(2)}) copy-start(bf16[1,128,2048]{1,2,0:T(8,128)(2,1)} %copy-done.11) | copy-start | bytes 1572868
  175.6 5.7 %copy-start.28 = (bf16[1,8192]{1,0:T(2,128)(2,1)S(1)}, bf16[1,8192]{1,0:T(2,128)(2,1)}, u32[]{:S(2)}) copy-start(bf16[1,8192]{1,0:T(2,128)(2,1)} %param.20) | copy-start | bytes 49156
  175.6 27.6 %all-to-all-start.3 = ((bf16[8,512,256]{2,1,0:T(8,128)(2,1)}), bf16[8,512,256]{2,1,0:T(8,128)(2,1)S(1)}, u32[]{:S(2)}, u32[]{:S(2)}) async-start(bf16[8,512,256]{2,1,0:T(8,128)(2,1)} %pad_maximum_fusion.1), calls=%async_computation.3 | async-start | bytes 4194304 | tf_op jit(solution)/shard_map/all_to_all | solution.py:117
  204.3 6.4 %copy-start.19 = (bf16[512,256]{0,1:T(8,128)(2,1)S(1)}, bf16[512,256]{0,1:T(8,128)(2,1)}, u32[]{:S(2)}) copy-start(bf16[512,256]{0,1:T(8,128)(2,1)} %copy.129) | copy-start | bytes 786436
  207.2 13.8 %all-to-all-start.4 = ((bf16[4,128,512]{2,1,0:T(8,128)(2,1)}), bf16[4,128,512]{2,1,0:T(8,128)(2,1)S(1)}, u32[]{:S(2)}, u32[]{:S(2)}) async-start(bf16[4,128,512]{2,1,0:T(8,128)(2,1)} %pad_maximum_fusion.4), calls=%async_computation.4 | async-start | bytes 1048576 | tf_op jit(solution)/shard_map/all_to_all | solution.py:125
  211.5 7.7 %copy-start.14 = (bf16[4,128,2,256]{3,1,0,2:T(8,128)(2,1)}, bf16[4,128,2,256]{3,1,0,2:T(8,128)(2,1)S(1)}, u32[]{:S(2)}) copy-start(bf16[4,128,2,256]{3,1,0,2:T(8,128)(2,1)S(1)} %reshape.274) | copy-start | bytes 1572868
  221.2 2.0 copy-start.9
  224.2 5.1 %copy-start.25 = (bf16[128,1,8,128]{0,3,2,1:T(8,128)(2,1)S(1)}, bf16[128,1,8,128]{0,3,2,1:T(8,128)(2,1)}, u32[]{:S(2)}) copy-start(bf16[128,1,8,128]{0,3,2,1:T(8,128)(2,1)} %fusion.34) | copy-start | bytes 786436
  224.2 13.1 %collective-permute-start = (bf16[2,32,8192]{2,1,0:T(8,128)(2,1)}, bf16[2,32,8192]{2,1,0:T(8,128)(2,1)}, u32[]{:S(2)}, u32[]{:S(2)}) collective-permute-start(bf16[2,32,8192]{2,1,0:T(8,128)(2,1)} %dynamic-slice_bitcast_fusion.3), channel_id=1, source_target_pairs={{0,1},{1,0},{2,3},{3,2},{4,5},{5,4},{6,7},{7,6},{8,9},{9,8},{10,11... | collective-permute-start | bytes 3145736 | tf_op jit(solution)/shard_map/ppermute | solution.py:163
  229.3 7.0 %copy-start.13 = (f32[1,128,4,2,128]{1,4,0,3,2:T(8,128)S(1)}, f32[1,128,4,2,128]{1,4,0,3,2:T(8,128)}, u32[]{:S(2)}) copy-start(f32[1,128,4,2,128]{1,4,0,3,2:T(8,128)} %get-tuple-element.65) | copy-start | bytes 1572868
  229.4 8.0 %copy-start.10 = (bf16[4,32,8192]{2,1,0:T(8,128)(2,1)S(1)}, bf16[4,32,8192]{2,1,0:T(8,128)(2,1)}, u32[]{:S(2)}) copy-start(bf16[4,32,8192]{2,1,0:T(8,128)(2,1)} %fusion.9) | copy-start | bytes 6291460
  238.9 15.9 %collective-permute-start.1 = (bf16[32,8192]{1,0:T(8,128)(2,1)S(1)}, bf16[32,8192]{1,0:T(8,128)(2,1)S(1)}, u32[]{:S(2)}, u32[]{:S(2)}) collective-permute-start(bf16[32,8192]{1,0:T(8,128)(2,1)S(1)} %fusion.65), channel_id=1, source_target_pairs={{0,2},{1,3},{2,0},{3,1},{4,6},{5,7},{6,4},{7,5},{8,10},{9,11},{10,... | collective-permute-start | bytes 1572872 | tf_op jit(solution)/shard_map/ppermute | solution.py:170
  240.8 19.2 %slice-start.10 = ((s8[8388608]{0:T(1024)(128)(4,1)}), s8[4194304]{0:T(1024)(128)(4,1)S(1)}, s32[]{:S(2)}) async-start(s8[8388608]{0:T(1024)(128)(4,1)} %bitcast.336), calls=%async_computation.16 | async-start | bytes 8388608
  247.2 7.6 %copy-start = (bf16[1,128,8192]{2,1,0:T(8,128)(2,1)S(1)}, bf16[1,128,8192]{2,1,0:T(8,128)(2,1)}, u32[]{:S(2)}) copy-start(bf16[1,128,8192]{2,1,0:T(8,128)(2,1)} %param.19) | copy-start | bytes 6291460
  247.2 12.8 %slice-start.11 = ((s8[8388608]{0:T(1024)(128)(4,1)}), s8[4194304]{0:T(1024)(128)(4,1)S(1)}, s32[]{:S(2)}) async-start(s8[8388608]{0:T(1024)(128)(4,1)} %bitcast.336), calls=%async_computation.17 | async-start | bytes 8388608
  247.3 10.6 %collective-permute-start.5 = (bf16[2,32,8192]{2,1,0:T(8,128)(2,1)S(1)}, bf16[2,32,8192]{2,1,0:T(8,128)(2,1)S(1)}, u32[]{:S(2)}, u32[]{:S(2)}) collective-permute-start(bf16[2,32,8192]{2,1,0:T(8,128)(2,1)S(1)} %dynamic-slice_bitcast_fusion.2), channel_id=1, source_target_pairs={{0,1},{1,0},{2,3},{3,2},{4,5},{5,4},{6,7},{7,6},{8,9},{9,8},{10,11... | collective-permute-start | bytes 3145736 | tf_op jit(solution)/shard_map/ppermute | solution.py:163
  255.9 16.6 %collective-permute-start.3 = (bf16[32,8192]{1,0:T(8,128)(2,1)S(1)}, bf16[32,8192]{1,0:T(8,128)(2,1)S(1)}, u32[]{:S(2)}, u32[]{:S(2)}) collective-permute-start(bf16[32,8192]{1,0:T(8,128)(2,1)S(1)} %get-tuple-element.59), channel_id=1, source_target_pairs={{96,0},{97,1},{98,2},{99,3},{100,4},{101,5},{102,6},{103,7},{104,8... | collective-permute-start | bytes 1572872 | tf_op jit(solution)/shard_map/ppermute | solution.py:183
  257.2 15.3 %collective-permute-start.2 = (bf16[32,8192]{1,0:T(8,128)(2,1)S(1)}, bf16[32,8192]{1,0:T(8,128)(2,1)S(1)}, u32[]{:S(2)}, u32[]{:S(2)}) collective-permute-start(bf16[32,8192]{1,0:T(8,128)(2,1)S(1)} %get-tuple-element.59), channel_id=1, source_target_pairs={{96,64},{64,32},{97,65},{65,33},{98,66},{66,34},{99,67},{67,35},{1... | collective-permute-start | bytes 1572872 | tf_op jit(solution)/shard_map/ppermute | solution.py:182
  258.2 17.3 %collective-permute-start.6 = (bf16[32,8192]{1,0:T(8,128)(2,1)S(1)}, bf16[32,8192]{1,0:T(8,128)(2,1)S(1)}, u32[]{:S(2)}, u32[]{:S(2)}) collective-permute-start(bf16[32,8192]{1,0:T(8,128)(2,1)S(1)} %fusion.66), channel_id=1, source_target_pairs={{0,2},{1,3},{2,0},{3,1},{4,6},{5,7},{6,4},{7,5},{8,10},{9,11},{10,... | collective-permute-start | bytes 1572872 | tf_op jit(solution)/shard_map/ppermute | solution.py:170
  263.0 24.4 %collective-permute-start.10 = (bf16[2,32,8192]{2,1,0:T(8,128)(2,1)S(1)}, bf16[2,32,8192]{2,1,0:T(8,128)(2,1)S(1)}, u32[]{:S(2)}, u32[]{:S(2)}) collective-permute-start(bf16[2,32,8192]{2,1,0:T(8,128)(2,1)S(1)} %dynamic-slice_bitcast_fusion.1), channel_id=1, source_target_pairs={{0,1},{1,0},{2,3},{3,2},{4,5},{5,4},{6,7},{7,6},{8,9},{9,8},{10,11... | collective-permute-start | bytes 3145736 | tf_op jit(solution)/shard_map/ppermute | solution.py:163
  272.6 14.5 %collective-permute-start.4 = (bf16[32,8192]{1,0:T(8,128)(2,1)S(1)}, bf16[32,8192]{1,0:T(8,128)(2,1)S(1)}, u32[]{:S(2)}, u32[]{:S(2)}) collective-permute-start(bf16[32,8192]{1,0:T(8,128)(2,1)S(1)} %fusion.36), channel_id=1, source_target_pairs={{32,0},{0,32},{33,1},{1,33},{34,2},{2,34},{35,3},{3,35},{36,4},{4,... | collective-permute-start | bytes 1572872 | tf_op jit(solution)/shard_map/ppermute | solution.py:189
  276.2 16.4 %collective-permute-start.8 = (bf16[32,8192]{1,0:T(8,128)(2,1)S(1)}, bf16[32,8192]{1,0:T(8,128)(2,1)S(1)}, u32[]{:S(2)}, u32[]{:S(2)}) collective-permute-start(bf16[32,8192]{1,0:T(8,128)(2,1)S(1)} %get-tuple-element.57), channel_id=1, source_target_pairs={{96,0},{97,1},{98,2},{99,3},{100,4},{101,5},{102,6},{103,7},{104,8... | collective-permute-start | bytes 1572872 | tf_op jit(solution)/shard_map/ppermute | solution.py:183
  277.5 15.1 %collective-permute-start.7 = (bf16[32,8192]{1,0:T(8,128)(2,1)S(1)}, bf16[32,8192]{1,0:T(8,128)(2,1)S(1)}, u32[]{:S(2)}, u32[]{:S(2)}) collective-permute-start(bf16[32,8192]{1,0:T(8,128)(2,1)S(1)} %get-tuple-element.57), channel_id=1, source_target_pairs={{96,64},{64,32},{97,65},{65,33},{98,66},{66,34},{99,67},{67,35},{1... | collective-permute-start | bytes 1572872 | tf_op jit(solution)/shard_map/ppermute | solution.py:182
  287.6 13.6 %collective-permute-start.11 = (bf16[32,8192]{1,0:T(8,128)(2,1)S(1)}, bf16[32,8192]{1,0:T(8,128)(2,1)S(1)}, u32[]{:S(2)}, u32[]{:S(2)}) collective-permute-start(bf16[32,8192]{1,0:T(8,128)(2,1)S(1)} %fusion.67), channel_id=1, source_target_pairs={{0,2},{1,3},{2,0},{3,1},{4,6},{5,7},{6,4},{7,5},{8,10},{9,11},{10,... | collective-permute-start | bytes 1572872 | tf_op jit(solution)/shard_map/ppermute | solution.py:170
  292.5 11.4 %collective-permute-start.15 = (bf16[2,32,8192]{2,1,0:T(8,128)(2,1)S(1)}, bf16[2,32,8192]{2,1,0:T(8,128)(2,1)S(1)}, u32[]{:S(2)}, u32[]{:S(2)}) collective-permute-start(bf16[2,32,8192]{2,1,0:T(8,128)(2,1)S(1)} %dynamic-slice_bitcast_fusion), channel_id=1, source_target_pairs={{0,1},{1,0},{2,3},{3,2},{4,5},{5,4},{6,7},{7,6},{8,9},{9,8},{10,11... | collective-permute-start | bytes 3145736 | tf_op jit(solution)/shard_map/ppermute | solution.py:163
  292.8 16.2 %collective-permute-start.9 = (bf16[32,8192]{1,0:T(8,128)(2,1)S(1)}, bf16[32,8192]{1,0:T(8,128)(2,1)S(1)}, u32[]{:S(2)}, u32[]{:S(2)}) collective-permute-start(bf16[32,8192]{1,0:T(8,128)(2,1)S(1)} %fusion.38), channel_id=1, source_target_pairs={{32,0},{0,32},{33,1},{1,33},{34,2},{2,34},{35,3},{3,35},{36,4},{4,... | collective-permute-start | bytes 1572872 | tf_op jit(solution)/shard_map/ppermute | solution.py:189
  301.9 17.5 %collective-permute-start.13 = (bf16[32,8192]{1,0:T(8,128)(2,1)S(1)}, bf16[32,8192]{1,0:T(8,128)(2,1)S(1)}, u32[]{:S(2)}, u32[]{:S(2)}) collective-permute-start(bf16[32,8192]{1,0:T(8,128)(2,1)S(1)} %get-tuple-element.55), channel_id=1, source_target_pairs={{96,0},{97,1},{98,2},{99,3},{100,4},{101,5},{102,6},{103,7},{104,8... | collective-permute-start | bytes 1572872 | tf_op jit(solution)/shard_map/ppermute | solution.py:183
  303.2 16.2 %collective-permute-start.12 = (bf16[32,8192]{1,0:T(8,128)(2,1)S(1)}, bf16[32,8192]{1,0:T(8,128)(2,1)S(1)}, u32[]{:S(2)}, u32[]{:S(2)}) collective-permute-start(bf16[32,8192]{1,0:T(8,128)(2,1)S(1)} %get-tuple-element.55), channel_id=1, source_target_pairs={{96,64},{64,32},{97,65},{65,33},{98,66},{66,34},{99,67},{67,35},{1... | collective-permute-start | bytes 1572872 | tf_op jit(solution)/shard_map/ppermute | solution.py:182
  304.2 12.5 %collective-permute-start.16 = (bf16[32,8192]{1,0:T(8,128)(2,1)S(1)}, bf16[32,8192]{1,0:T(8,128)(2,1)S(1)}, u32[]{:S(2)}, u32[]{:S(2)}) collective-permute-start(bf16[32,8192]{1,0:T(8,128)(2,1)S(1)} %fusion.68), channel_id=1, source_target_pairs={{0,2},{1,3},{2,0},{3,1},{4,6},{5,7},{6,4},{7,5},{8,10},{9,11},{10,... | collective-permute-start | bytes 1572872 | tf_op jit(solution)/shard_map/ppermute | solution.py:170
  317.4 13.5 %collective-permute-start.18 = (bf16[32,8192]{1,0:T(8,128)(2,1)S(1)}, bf16[32,8192]{1,0:T(8,128)(2,1)S(1)}, u32[]{:S(2)}, u32[]{:S(2)}) collective-permute-start(bf16[32,8192]{1,0:T(8,128)(2,1)S(1)} %get-tuple-element.53), channel_id=1, source_target_pairs={{96,0},{97,1},{98,2},{99,3},{100,4},{101,5},{102,6},{103,7},{104,8... | collective-permute-start | bytes 1572872 | tf_op jit(solution)/shard_map/ppermute | solution.py:183
  318.7 12.2 %collective-permute-start.17 = (bf16[32,8192]{1,0:T(8,128)(2,1)S(1)}, bf16[32,8192]{1,0:T(8,128)(2,1)S(1)}, u32[]{:S(2)}, u32[]{:S(2)}) collective-permute-start(bf16[32,8192]{1,0:T(8,128)(2,1)S(1)} %get-tuple-element.53), channel_id=1, source_target_pairs={{96,64},{64,32},{97,65},{65,33},{98,66},{66,34},{99,67},{67,35},{1... | collective-permute-start | bytes 1572872 | tf_op jit(solution)/shard_map/ppermute | solution.py:182
  319.6 13.9 %collective-permute-start.14 = (bf16[32,8192]{1,0:T(8,128)(2,1)S(1)}, bf16[32,8192]{1,0:T(8,128)(2,1)S(1)}, u32[]{:S(2)}, u32[]{:S(2)}) collective-permute-start(bf16[32,8192]{1,0:T(8,128)(2,1)S(1)} %fusion.40), channel_id=1, source_target_pairs={{32,0},{0,32},{33,1},{1,33},{34,2},{2,34},{35,3},{3,35},{36,4},{4,... | collective-permute-start | bytes 1572872 | tf_op jit(solution)/shard_map/ppermute | solution.py:189
  331.1 11.7 %collective-permute-start.19 = (bf16[32,8192]{1,0:T(8,128)(2,1)S(1)}, bf16[32,8192]{1,0:T(8,128)(2,1)S(1)}, u32[]{:S(2)}, u32[]{:S(2)}) collective-permute-start(bf16[32,8192]{1,0:T(8,128)(2,1)S(1)} %fusion.42), channel_id=1, source_target_pairs={{32,0},{0,32},{33,1},{1,33},{34,2},{2,34},{35,3},{3,35},{36,4},{4,... | collective-permute-start | bytes 1572872 | tf_op jit(solution)/shard_map/ppermute | solution.py:189
  (6 other events, 6.6 us)
Sparse Core Ops, SparseCore 0:
  36.6 62.6 all-gather.2

commit v3 on v2

--- a/solution.py
+++ b/solution.py
@@ -44,16 +44,12 @@
         "rgd,kd->rgk", grad_grp, value_rows, preferred_element_type=jnp.float32
     )
     score_grad = (softmax_w * (weight_grad - delta_row)).astype(jnp.bfloat16)
-    query_out = (
-        jnp.einsum("rgk,kd->rgd", score_grad, key_rows, preferred_element_type=jnp.float32)
-        * inv_root
-    )
     key_result = (
         jnp.einsum("rgk,rgd->kd", score_grad, query_grp, preferred_element_type=jnp.float32)
         * inv_root
     )
     value_out = jnp.einsum("rgk,rgd->kd", weights_low, grad_grp, preferred_element_type=jnp.float32)
-    return (query_out, key_result, value_out)
+    return (score_grad, key_result, value_out)
 
 
 def make_body(n_sec, n_smp, n_ten):
@@ -97,6 +93,7 @@
                 spread = jnp.broadcast_to(got[None], (n_smp,) + got.shape)
                 pool = lax.all_to_all(spread, "sample", 0, 0, tiled=True).reshape(pooled_rows, -1)
             else:
+                got, _ = lax.optimization_barrier((got, pool))
                 pool = lax.all_gather(got, "sample", axis=0, tiled=True)
             key_rows = jnp.concatenate(
                 [pool[:, :HEAD_SIZE], own_keys[:, low_col : low_col + HEAD_SIZE]], axis=0
@@ -104,16 +101,20 @@
             value_rows = jnp.concatenate(
                 [pool[:, HEAD_SIZE:], own_values[:, low_col : low_col + HEAD_SIZE]], axis=0
             )
-            query_out, key_result, value_out = attend_group(
+            score_grad, key_result, value_out = attend_group(
                 query_rows[:, head_index], grad_rows[:, head_index], key_rows, value_rows, visible
             )
-            query_pieces.append(query_out)
             suffix_key_pieces.append(key_result[pooled_rows:])
             suffix_value_pieces.append(value_out[pooled_rows:])
             pool_grad = jnp.concatenate(
                 [key_result[:pooled_rows], value_out[:pooled_rows]], axis=1
             ).astype(jnp.bfloat16)
             pool_grad = pool_grad.reshape(n_smp, block_rows, 2 * HEAD_SIZE)
+            score_grad, pool_grad = lax.optimization_barrier((score_grad, pool_grad))
+            query_pieces.append(
+                jnp.einsum("rgk,kd->rgd", score_grad, key_rows, preferred_element_type=jnp.float32)
+                * HEAD_SIZE ** (-0.5)
+            )
             parts = lax.all_to_all(pool_grad, "sample", 0, 0, tiled=False)
             reduced_pieces.append(jnp.sum(parts.astype(jnp.float32), axis=0))
         query_grad = jnp.stack(query_pieces, axis=1).reshape(tok_count, -1).astype(jnp.bfloat16)

time: 356 us -> 350 us (0.983)
  waiting for transfers between devices: 120 us -> 111 us
  local copies, waits for them, and re-layouts: 40.1 us -> 33.7 us
  matrix products: 71 us -> 75.9 us
    all_to_all x1, waiting for transfers between devices: 35.9 us -> 22.1 us  [on_device(): lax.all_to_all(spread, 'sample', 0, 0, tiled=True).reshape(pooled_rows, -1)]
    unnamed x97 -> x105, local copies, waits for them, and re-layouts: 20.6 us -> 12.1 us
    dot_general x2, matrix products: 5.03 us -> 9.37 us  [attend_group(): jnp.einsum('rgk,kd->rgd', weights_low, value_rows, preferred_element_type...]
    dot_general x2, matrix products: 12 us -> 8.41 us  [attend_group(): jnp.einsum('rgk,rgd->kd', score_grad, query_grp, preferred_element_type=j...]
  transfers between devices with their start and end apart: 26 -> 26, of which waited for: 12 -> 13; matrix products, arithmetic and copies ran while one was open for 38% -> 41% of each run, Pallas kernels for 0% -> 0%
where the time goes in v3:
time: 350 us; the launch traced here: 344 us
  waiting for transfers between devices  111 us (32%)
  matrix products  75.9 us (22%)
  other arithmetic  58.1 us (17%)
  starting transfers between devices  49.5 us (14%)
  local copies, waits for them, and re-layouts  33.7 us (10%)
  between operations  15.3 us (4%)
    all_to_all x1, waiting for transfers between devices, on_device(): lax.all_to_all(spread, 'sample', 0, 0, tiled=True).reshape(pooled_rows, -1)  22.1 us
    ppermute x4, waiting for transfers between devices, on_device(): last = lax.ppermute(carry.astype(jnp.bfloat16), 'section', [(1, 0), (0, 1)])  21.3 us
    sub x2, other arithmetic, attend_group(): exponent = jnp.exp(scores - row_max)  21 us
    ppermute x4, waiting for transfers between devices, on_device(): got2 = lax.ppermute(other, 'tensor', chip_pairs)  20.3 us
    dot_general x4, matrix products, on_device(): lax.dot_general(grad_rows_c, weight_local, (((2, 3), (1, 2)), ((), ())),...  19.8 us
    ppermute x4, waiting for transfers between devices, on_device(): wrap = lax.ppermute(term_low, 'section', [(3, 0)])  17.8 us
    convert_element_type x2, other arithmetic, attend_group(): weights_low = softmax_w.astype(jnp.bfloat16)  17.1 us
    all_to_all x2, waiting for transfers between devices, on_device(): parts = lax.all_to_all(pool_grad, 'sample', 0, 0, tiled=False)  16.4 us
  transfers between devices with their start and end apart: 26, of which 13 were waited for; matrix products, arithmetic and copies ran while one was open for 41% of the time, Pallas kernels for 0%

profile of v3, /device:TPU:0, one launch (start us, length us, event | category | flops | bytes accessed | tf_op | source)
XLA Modules:
  0.0 343.8 jit_solution(2399927756102489936)
XLA Ops:
  7.2 1.2 copy.108
  8.4 1.1 copy.109
  10.3 4.6 %all-to-all-start = ((bf16[4,128,512]{1,2,0:T(8,128)(2,1)}), bf16[4,128,512]{1,2,0:T(8,128)(2,1)S(1)}, u32[]{:S(2)}, u32[]{:S(2)}) async-start(bf16[4,128,512]{1,2,0:T(8,128)(2,1)} %bitcast.6), calls=%async_computation | async-start | bytes 1048576 | tf_op jit(solution)/shard_map/all_to_all | solution.py:85
  15.2 10.0 %all-to-all-done = bf16[4,128,512]{1,2,0:T(8,128)(2,1)S(1)} async-done(((bf16[4,128,512]{1,2,0:T(8,128)(2,1)}), bf16[4,128,512]{1,2,0:T(8,128)(2,1)S(1)}, u32[]{:S(2)}, u32[]{:S(2)}) %all-to-all-start) | async-done | bytes 524320 | tf_op jit(solution)/shard_map/all_to_all | solution.py:85
  26.4 1.5 broadcast_in_dim.91
  27.8 5.6 %all-to-all-start.1 = ((bf16[8,512,256]{2,1,0:T(8,128)(2,1)}), bf16[8,512,256]{2,1,0:T(8,128)(2,1)}, u32[]{:S(2)}, u32[]{:S(2)}) async-start(bf16[8,512,256]{2,1,0:T(8,128)(2,1)} %broadcast_in_dim.91), calls=%async_computation.1 | async-start | bytes 4194304 | tf_op jit(solution)/shard_map/all_to_all | solution.py:94
  38.1 22.1 %all-to-all-done.1 = bf16[8,512,256]{2,1,0:T(8,128)(2,1)} async-done(((bf16[8,512,256]{2,1,0:T(8,128)(2,1)}), bf16[8,512,256]{2,1,0:T(8,128)(2,1)}, u32[]{:S(2)}, u32[]{:S(2)}) %all-to-all-start.1) | async-done | bytes 2097184 | tf_op jit(solution)/shard_map/all_to_all | solution.py:94
  60.2 2.6 fusion.101
  62.9 3.2 fusion.64
  66.0 10.8 %fusion.110 = (f32[128,8]{0,1:T(8,128)S(1)}, f32[128,8,4224]{0,2,1:T(8,128)}) fusion(f32[4224,128,8]{1,0,2:T(8,128)S(1)} %fusion.64, pred[128,4224]{0,1:T(8,128)(4,1)S(1)} %pad_add_fusion), kind=kOutput, calls=%fused_computation.209 | output fusion | flops 17305728 | bytes 35147776 | tf_op jit(solution)/shard_map/sub | solution.py:36
  76.8 6.8 %fusion.18 = bf16[128,8,4224]{0,2,1:T(8,128)(2,1)S(1)} fusion(f32[128,8,4224]{0,2,1:T(8,128)} %get-tuple-element.99, f32[128,8]{0,1:T(8,128)S(1)} %get-tuple-element.98), kind=kLoop, calls=%fused_computation.30 | loop fusion | flops 8650752 | bytes 25956352 | tf_op jit(solution)/shard_map/convert_element_type | solution.py:38
  83.7 2.4 fusion.26
  86.2 2.5 fusion.31
  89.2 1.3 slice-done.3
  90.5 7.2 %fusion.3 = bf16[128,8,4224]{0,2,1:T(8,128)(2,1)} fusion(f32[128,8]{0,1:T(8,128)S(1)} %fusion.31, f32[128,8,4224]{0,2,1:T(8,128)S(1)} %bitcast.285, f32[128,8]{0,1:T(8,128)S(1)} %get-tuple-element.98, bf16[128,128]{1,0:T(8,128)(2,1)S(1)} %copy-done.31, bf16[4096,128]{1,0:T(8,128)(2,1)} %get-tuple-element.71, bf16[128,2,8,128]{0,3,2,1:T(8,128)(2,1)} %bitcast.316), kind=kOutput, calls=%fused_computation.6 | convolution fusion | flops 1126760448 | bytes 27303936 | tf_op jit(solution)/shard_map/rgd,kd->rgk/dot_general | solution.py:43
  97.8 5.9 %fusion.25 = bf16[4224,128]{1,0:T(8,128)(2,1)S(1)} fusion(bf16[128,8,4224]{0,2,1:T(8,128)(2,1)} %fusion.3, bf16[128,2,8,128]{0,3,2,1:T(8,128)(2,1)} %bitcast.304), kind=kOutput, calls=%fused_computation.41 | convolution fusion | flops 1108377600 | bytes 9994240 | tf_op jit(solution)/shard_map/rgk,rgd->kd/dot_general | solution.py:48
  104.8 1.2 slice-done.10
  105.9 1.5 pad_maximum_fusion
  107.5 4.3 %all-to-all-start.2 = ((bf16[8,512,256]{2,1,0:T(8,128)(2,1)}), bf16[8,512,256]{2,1,0:T(8,128)(2,1)}, u32[]{:S(2)}, u32[]{:S(2)}) async-start(bf16[8,512,256]{2,1,0:T(8,128)(2,1)} %pad_maximum_fusion), calls=%async_computation.2 | async-start | bytes 4194304 | tf_op jit(solution)/shard_map/all_to_all | solution.py:118
  111.8 1.5 all-gather.2.cloned.1.call-done
  113.4 2.7 fusion.102
  116.1 2.4 fusion.63
  118.5 10.2 %fusion.109 = (f32[128,8]{0,1:T(8,128)S(1)}, f32[128,8,4224]{0,2,1:T(8,128)}) fusion(f32[4224,128,8]{1,0,2:T(8,128)S(1)} %fusion.63, pred[128,4224]{0,1:T(8,128)(4,1)S(1)} %pad_add_fusion), kind=kOutput, calls=%fused_computation.208 | output fusion | flops 17305728 | bytes 35147776 | tf_op jit(solution)/shard_map/sub | solution.py:36
  128.8 10.2 %fusion.19 = bf16[128,8,4224]{0,2,1:T(8,128)(2,1)} fusion(f32[128,8,4224]{0,2,1:T(8,128)} %get-tuple-element.97, f32[128,8]{0,1:T(8,128)S(1)} %get-tuple-element.96), kind=kLoop, calls=%fused_computation.31 | loop fusion | flops 8650752 | bytes 25956352 | tf_op jit(solution)/shard_map/convert_element_type | solution.py:38
  139.0 6.8 %fusion.32 = f32[128,8]{0,1:T(8,128)S(1)} fusion(bf16[128,8,4224]{0,2,1:T(8,128)(2,1)} %fusion.19, bf16[128,128]{1,0:T(8,128)(2,1)S(1)} %copy-done.30, bf16[4096,128]{1,0:T(8,128)(2,1)S(1)} %copy-done.19, bf16[128,1,8,128]{3,0,2,1:T(8,128)(2,1)S(1)} %copy-done.22), kind=kOutput, calls=%fused_computation.88 | convolution fusion | flops 1109851136 | bytes 9998336 | tf_op jit(solution)/shard_map/rgk,kd->rgd/dot_general | solution.py:39
  145.9 6.4 %fusion.2 = bf16[128,8,4224]{0,2,1:T(8,128)(2,1)} fusion(f32[128,8]{0,1:T(8,128)S(1)} %fusion.32, f32[128,8,4224]{0,2,1:T(8,128)S(1)} %bitcast.287, f32[128,8]{0,1:T(8,128)S(1)} %get-tuple-element.96, bf16[128,128]{1,0:T(8,128)(2,1)S(1)} %copy-done.30, bf16[4096,128]{1,0:T(8,128)(2,1)} %get-tuple-element.73, bf16[128,2,8,128]{0,3,2,1:T(8,128)(2,1)S(1)} %bitcast.318), kind=kOutput, calls=%fused_computation.3 | convolution fusion | flops 1126760448 | bytes 27303936 | tf_op jit(solution)/shard_map/rgd,kd->rgk/dot_general | solution.py:43
  152.3 6.0 %fusion.28 = bf16[4224,128]{1,0:T(8,128)(2,1)S(1)} fusion(bf16[128,8,4224]{0,2,1:T(8,128)(2,1)} %fusion.19, bf16[128,2,8,128]{0,3,2,1:T(8,128)(2,1)S(1)} %bitcast.319), kind=kOutput, calls=%fused_computation.44 | convolution fusion | flops 1107836928 | bytes 9994240 | tf_op jit(solution)/shard_map/rgk,rgd->kd/dot_general | solution.py:51
  159.5 2.5 fusion.27
  163.0 1.5 pad_maximum_fusion.1
  164.5 4.2 %all-to-all-start.3 = ((bf16[8,512,256]{2,1,0:T(8,128)(2,1)}), bf16[8,512,256]{2,1,0:T(8,128)(2,1)S(1)}, u32[]{:S(2)}, u32[]{:S(2)}) async-start(bf16[8,512,256]{2,1,0:T(8,128)(2,1)} %pad_maximum_fusion.1), calls=%async_computation.3 | async-start | bytes 4194304 | tf_op jit(solution)/shard_map/all_to_all | solution.py:118
  169.6 5.9 %fusion.34 = bf16[128,1,8,128]{0,3,2,1:T(8,128)(2,1)} fusion(bf16[128,8,4224]{0,2,1:T(8,128)(2,1)} %fusion.3, bf16[128,128]{1,0:T(8,128)(2,1)S(1)} %copy-done.26, bf16[4096,128]{1,0:T(8,128)(2,1)} %copy-done.1), kind=kOutput, calls=%fused_computation.90 | convolution fusion | flops 1109721088 | bytes 9994240 | tf_op jit(solution)/shard_map/rgk,kd->rgd/dot_general | solution.py:115
  175.4 2.0 reduce
  178.3 16.4 %all-to-all-done.3 = bf16[8,512,256]{2,1,0:T(8,128)(2,1)S(1)} async-done(((bf16[8,512,256]{2,1,0:T(8,128)(2,1)}), bf16[8,512,256]{2,1,0:T(8,128)(2,1)S(1)}, u32[]{:S(2)}, u32[]{:S(2)}) %all-to-all-start.3) | async-done | bytes 2097184 | tf_op jit(solution)/shard_map/all_to_all | solution.py:118
  195.7 1.1 copy.130
  196.9 1.8 pad_maximum_fusion.4
  198.7 4.0 %all-to-all-start.4 = ((bf16[4,128,512]{2,1,0:T(8,128)(2,1)}), bf16[4,128,512]{2,1,0:T(8,128)(2,1)S(1)}, u32[]{:S(2)}, u32[]{:S(2)}) async-start(bf16[4,128,512]{2,1,0:T(8,128)(2,1)} %pad_maximum_fusion.4), calls=%async_computation.4 | async-start | bytes 1048576 | tf_op jit(solution)/shard_map/all_to_all | solution.py:126
  203.5 7.7 %fusion.9 = bf16[4,32,8192]{2,1,0:T(8,128)(2,1)} fusion(bf16[8192,2,256]{2,1,0:T(2,128)(2,1)} %bitcast.336, bf16[4,128,2,256]{3,1,0,2:T(8,128)(2,1)S(1)} %reshape.274), kind=kOutput, calls=%fused_computation.19 | convolution fusion | flops 1074790400 | bytes 10616832 | tf_op jit(solution)/shard_map/dot_general | solution.py:153
  211.2 1.8 all-to-all-done.4
  216.6 4.9 %fusion.33 = bf16[128,1,8,128]{0,3,2,1:T(8,128)(2,1)S(1)} fusion(bf16[128,8,4224]{0,2,1:T(8,128)(2,1)} %fusion.2, bf16[128,128]{1,0:T(8,128)(2,1)S(1)} %copy-done.25, bf16[4096,128]{1,0:T(8,128)(2,1)S(1)} %get-tuple-element.74), kind=kOutput, calls=%fused_computation.89 | convolution fusion | flops 1109721088 | bytes 9994240 | tf_op jit(solution)/shard_map/rgk,kd->rgd/dot_general | solution.py:115
  228.5 1.7 convert_add_fusion.3
  230.3 2.0 collective-permute-start.1
  232.2 6.4 %fusion.6 = bf16[4,32,8192]{2,1,0:T(8,128)(2,1)S(1)} fusion(bf16[4,32,2,256]{3,1,0,2:T(8,128)(2,1)S(1)} %get-tuple-element.28, bf16[8192,2,256,1]{2,1,0,3:T(2,128)(2,1)} %bitcast.337), kind=kOutput, calls=%fused_computation.16 | convolution fusion | flops 1074790400 | bytes 10616832 | tf_op jit(solution)/shard_map/dot_general | solution.py:153
  238.9 7.3 %collective-permute-done.1 = bf16[32,8192]{1,0:T(8,128)(2,1)S(1)} collective-permute-done((bf16[32,8192]{1,0:T(8,128)(2,1)S(1)}, bf16[32,8192]{1,0:T(8,128)(2,1)S(1)}, u32[]{:S(2)}, u32[]{:S(2)}) %collective-permute-start.1) | collective-permute-done | bytes 524320 | tf_op jit(solution)/shard_map/ppermute | solution.py:171
  247.3 1.3 collective-permute-start.3
  249.6 1.9 collective-permute-start.6
  251.5 2.8 fusion.7
  254.5 9.3 %collective-permute-done.3 = bf16[32,8192]{1,0:T(8,128)(2,1)S(1)} collective-permute-done((bf16[32,8192]{1,0:T(8,128)(2,1)S(1)}, bf16[32,8192]{1,0:T(8,128)(2,1)S(1)}, u32[]{:S(2)}, u32[]{:S(2)}) %collective-permute-start.3) | collective-permute-done | bytes 524320 | tf_op jit(solution)/shard_map/ppermute | solution.py:184
  264.0 2.9 collective-permute-start.4
  267.6 1.3 collective-permute-start.8
  269.6 9.0 %collective-permute-done.4 = bf16[32,8192]{1,0:T(8,128)(2,1)S(1)} collective-permute-done((bf16[32,8192]{1,0:T(8,128)(2,1)S(1)}, bf16[32,8192]{1,0:T(8,128)(2,1)S(1)}, u32[]{:S(2)}, u32[]{:S(2)}) %collective-permute-start.4) | collective-permute-done | bytes 524320 | tf_op jit(solution)/shard_map/ppermute | solution.py:190
  279.0 1.8 collective-permute-start.11
  280.9 2.8 fusion.8
  284.1 2.9 collective-permute-start.9
  287.0 5.6 %collective-permute-done.11 = bf16[32,8192]{1,0:T(8,128)(2,1)S(1)} collective-permute-done((bf16[32,8192]{1,0:T(8,128)(2,1)S(1)}, bf16[32,8192]{1,0:T(8,128)(2,1)S(1)}, u32[]{:S(2)}, u32[]{:S(2)}) %collective-permute-start.11) | collective-permute-done | bytes 524320 | tf_op jit(solution)/shard_map/ppermute | solution.py:171
  293.2 1.3 collective-permute-start.13
  295.5 1.6 collective-permute-start.16
  297.1 3.2 collective-permute-done.9
  300.5 7.5 %collective-permute-done.16 = bf16[32,8192]{1,0:T(8,128)(2,1)S(1)} collective-permute-done((bf16[32,8192]{1,0:T(8,128)(2,1)S(1)}, bf16[32,8192]{1,0:T(8,128)(2,1)S(1)}, u32[]{:S(2)}, u32[]{:S(2)}) %collective-permute-start.16) | collective-permute-done | bytes 524320 | tf_op jit(solution)/shard_map/ppermute | solution.py:171
  308.7 1.3 collective-permute-start.18
  310.9 2.9 collective-permute-start.14
  313.8 8.4 %collective-permute-done.18 = bf16[32,8192]{1,0:T(8,128)(2,1)S(1)} collective-permute-done((bf16[32,8192]{1,0:T(8,128)(2,1)S(1)}, bf16[32,8192]{1,0:T(8,128)(2,1)S(1)}, u32[]{:S(2)}, u32[]{:S(2)}) %collective-permute-start.18) | collective-permute-done | bytes 524320 | tf_op jit(solution)/shard_map/ppermute | solution.py:184
  322.4 2.3 collective-permute-start.19
  325.0 9.1 %collective-permute-done.19 = bf16[32,8192]{1,0:T(8,128)(2,1)S(1)} collective-permute-done((bf16[32,8192]{1,0:T(8,128)(2,1)S(1)}, bf16[32,8192]{1,0:T(8,128)(2,1)S(1)}, u32[]{:S(2)}, u32[]{:S(2)}) %collective-permute-start.19) | collective-permute-done | bytes 524320 | tf_op jit(solution)/shard_map/ppermute | solution.py:190
  334.3 2.4 maximum_bitcast_fusion
  (197 shorter events, 33.7 us)
Async XLA Ops:
  7.2 7.7 %copy-start.20 = (bf16[1,128,2048]{2,1,0:T(8,128)(2,1)S(1)}, bf16[1,128,2048]{2,1,0:T(8,128)(2,1)}, u32[]{:S(2)}) copy-start(bf16[1,128,2048]{2,1,0:T(8,128)(2,1)} %param.15) | copy-start | bytes 1572868
  10.3 14.9 %all-to-all-start = ((bf16[4,128,512]{1,2,0:T(8,128)(2,1)}), bf16[4,128,512]{1,2,0:T(8,128)(2,1)S(1)}, u32[]{:S(2)}, u32[]{:S(2)}) async-start(bf16[4,128,512]{1,2,0:T(8,128)(2,1)} %bitcast.6), calls=%async_computation | async-start | bytes 1048576 | tf_op jit(solution)/shard_map/all_to_all | solution.py:85
  15.2 18.3 %copy-start.8 = (bf16[1,128,2048]{1,2,0:T(8,128)(2,1)}, bf16[1,128,2048]{1,2,0:T(8,128)(2,1)S(1)}, u32[]{:S(2)}) copy-start(bf16[1,128,2048]{1,2,0:T(8,128)(2,1)S(1)} %copy.113) | copy-start | bytes 1572868
  27.8 5.7 %copy-start.21 = (bf16[1,128,2048]{2,1,0:T(8,128)(2,1)S(1)}, bf16[1,128,2048]{2,1,0:T(8,128)(2,1)}, u32[]{:S(2)}) copy-start(bf16[1,128,2048]{2,1,0:T(8,128)(2,1)} %param.12) | copy-start | bytes 1572868
  27.8 32.4 %all-to-all-start.1 = ((bf16[8,512,256]{2,1,0:T(8,128)(2,1)}), bf16[8,512,256]{2,1,0:T(8,128)(2,1)}, u32[]{:S(2)}, u32[]{:S(2)}) async-start(bf16[8,512,256]{2,1,0:T(8,128)(2,1)} %broadcast_in_dim.91), calls=%async_computation.1 | async-start | bytes 4194304 | tf_op jit(solution)/shard_map/all_to_all | solution.py:94
  33.4 2.5 copy-start.27
  33.4 3.1 copy-start.28
  33.4 79.9 %all-gather.2.cloned.1.call-start = ((), (), s32[]{:S(2)}) async-start(), calls=%async_computation.5 | async-start | bytes 2359296 | tf_op jit(solution)/shard_map/all_gather | solution.py:97
  33.8 29.0 %copy-start.4 = (bf16[1,128,2048]{1,2,0:T(8,128)(2,1)}, bf16[1,128,2048]{1,2,0:T(8,128)(2,1)S(1)}, u32[]{:S(2)}) copy-start(bf16[1,128,2048]{1,2,0:T(8,128)(2,1)S(1)} %copy.111) | copy-start | bytes 1572868
  62.8 3.2 copy-start.1
  76.8 6.8 %copy-start.9 = (bf16[1,128,2048]{1,2,0:T(8,128)(2,1)S(1)}, bf16[1,128,2048]{1,2,0:T(8,128)(2,1)}, u32[]{:S(2)}) copy-start(bf16[1,128,2048]{1,2,0:T(8,128)(2,1)} %copy-done.8) | copy-start | bytes 1572868
  83.7 5.1 %slice-start = ((s8[17301504]{0:T(1024)(128)(4,1)}), s8[4194304]{0:T(1024)(128)(4,1)S(1)}, s32[]{:S(2)}) async-start(s8[17301504]{0:T(1024)(128)(4,1)} %bitcast.284), calls=%async_computation.6 | async-start | bytes 8388608
  83.7 5.1 %slice-start.1 = ((s8[17301504]{0:T(1024)(128)(4,1)}), s8[4194304]{0:T(1024)(128)(4,1)S(1)}, s32[]{:S(2)}) async-start(s8[17301504]{0:T(1024)(128)(4,1)} %bitcast.284), calls=%async_computation.7 | async-start | bytes 8388608
  83.7 5.5 %slice-start.2 = ((s8[17301504]{0:T(1024)(128)(4,1)}), s8[4194304]{0:T(1024)(128)(4,1)S(1)}, s32[]{:S(2)}) async-start(s8[17301504]{0:T(1024)(128)(4,1)} %bitcast.284), calls=%async_computation.8 | async-start | bytes 8388608
  86.1 2.6 copy-start.2
  86.2 4.3 %slice-start.3 = ((s8[17301504]{0:T(1024)(128)(4,1)}), s8[4194304]{0:T(1024)(128)(4,1)S(1)}, s32[]{:S(2)}) async-start(s8[17301504]{0:T(1024)(128)(4,1)} %bitcast.284), calls=%async_computation.9 | async-start | bytes 8388608
  86.2 4.3 %slice-start.4 = ((s8[17301504]{0:T(1024)(128)(4,1)}), s8[524288]{0:T(1024)(128)(4,1)S(1)}, s32[]{:S(2)}) async-start(s8[17301504]{0:T(1024)(128)(4,1)} %bitcast.284), calls=%async_computation.10 | async-start | bytes 1048576
  107.5 57.1 %all-to-all-start.2 = ((bf16[8,512,256]{2,1,0:T(8,128)(2,1)}), bf16[8,512,256]{2,1,0:T(8,128)(2,1)}, u32[]{:S(2)}, u32[]{:S(2)}) async-start(bf16[8,512,256]{2,1,0:T(8,128)(2,1)} %pad_maximum_fusion), calls=%async_computation.2 | async-start | bytes 4194304 | tf_op jit(solution)/shard_map/all_to_all | solution.py:118
  111.8 4.3 %copy-start.25 = (bf16[128,128]{1,0:T(8,128)(2,1)S(1)}, bf16[128,128]{1,0:T(8,128)(2,1)}, u32[]{:S(2)}) copy-start(bf16[128,128]{1,0:T(8,128)(2,1)} %get-tuple-element.87) | copy-start | bytes 98308
  113.4 2.7 copy-start.5
  128.7 10.3 %copy-start.19 = (bf16[4096,128]{1,0:T(8,128)(2,1)S(1)}, bf16[4096,128]{1,0:T(8,128)(2,1)}, u32[]{:S(2)}) copy-start(bf16[4096,128]{1,0:T(8,128)(2,1)} %get-tuple-element.73) | copy-start | bytes 3145732
  128.7 10.3 %copy-start.22 = (bf16[128,1,8,128]{3,0,2,1:T(8,128)(2,1)S(1)}, bf16[128,1,8,128]{3,0,2,1:T(8,128)(2,1)}, u32[]{:S(2)}) copy-start(bf16[128,1,8,128]{3,0,2,1:T(8,128)(2,1)} %copy.173) | copy-start | bytes 786436
  128.7 10.3 %copy-start.30 = (bf16[128,128]{1,0:T(8,128)(2,1)S(1)}, bf16[128,128]{1,0:T(8,128)(2,1)}, u32[]{:S(2)}) copy-start(bf16[128,128]{1,0:T(8,128)(2,1)} %get-tuple-element.85) | copy-start | bytes 98308
  128.7 17.1 %slice-start.5 = ((s8[17301504]{0:T(1024)(128)(4,1)}), s8[4194304]{0:T(1024)(128)(4,1)S(1)}, s32[]{:S(2)}) async-start(s8[17301504]{0:T(1024)(128)(4,1)} %bitcast.286), calls=%async_computation.11 | async-start | bytes 8388608
  128.7 17.2 %slice-start.6 = ((s8[17301504]{0:T(1024)(128)(4,1)}), s8[4194304]{0:T(1024)(128)(4,1)S(1)}, s32[]{:S(2)}) async-start(s8[17301504]{0:T(1024)(128)(4,1)} %bitcast.286), calls=%async_computation.12 | async-start | bytes 8388608
  128.7 17.2 %slice-start.7 = ((s8[17301504]{0:T(1024)(128)(4,1)}), s8[4194304]{0:T(1024)(128)(4,1)S(1)}, s32[]{:S(2)}) async-start(s8[17301504]{0:T(1024)(128)(4,1)} %bitcast.286), calls=%async_computation.13 | async-start | bytes 8388608
  128.8 17.2 %slice-start.8 = ((s8[17301504]{0:T(1024)(128)(4,1)}), s8[4194304]{0:T(1024)(128)(4,1)S(1)}, s32[]{:S(2)}) async-start(s8[17301504]{0:T(1024)(128)(4,1)} %bitcast.286), calls=%async_computation.14 | async-start | bytes 8388608
  139.0 6.9 %slice-start.9 = ((s8[17301504]{0:T(1024)(128)(4,1)}), s8[524288]{0:T(1024)(128)(4,1)S(1)}, s32[]{:S(2)}) async-start(s8[17301504]{0:T(1024)(128)(4,1)} %bitcast.286), calls=%async_computation.15 | async-start | bytes 1048576
  139.0 6.9 %copy-start.10 = (bf16[1,128,2048]{1,2,0:T(8,128)(2,1)S(1)}, bf16[1,128,2048]{1,2,0:T(8,128)(2,1)}, u32[]{:S(2)}) copy-start(bf16[1,128,2048]{1,2,0:T(8,128)(2,1)} %copy-done.8) | copy-start | bytes 1572868
  152.3 7.1 %copy-start.6 = (bf16[1,128,2048]{1,2,0:T(8,128)(2,1)S(1)}, bf16[1,128,2048]{1,2,0:T(8,128)(2,1)}, u32[]{:S(2)}) copy-start(bf16[1,128,2048]{1,2,0:T(8,128)(2,1)} %copy-done.4) | copy-start | bytes 1572868
  152.3 7.1 %copy-start.35 = (bf16[128,8,4224]{0,2,1:T(8,128)(2,1)S(1)}, bf16[128,8,4224]{0,2,1:T(8,128)(2,1)}, u32[]{:S(2)}) copy-start(bf16[128,8,4224]{0,2,1:T(8,128)(2,1)} %fusion.2) | copy-start | bytes 25952260
  164.5 4.2 %copy-start.29 = (bf16[1,8192]{1,0:T(2,128)(2,1)S(1)}, bf16[1,8192]{1,0:T(2,128)(2,1)}, u32[]{:S(2)}) copy-start(bf16[1,8192]{1,0:T(2,128)(2,1)} %param.20) | copy-start | bytes 49156
  164.5 5.0 %copy-start.26 = (bf16[128,128]{1,0:T(8,128)(2,1)S(1)}, bf16[128,128]{1,0:T(8,128)(2,1)}, u32[]{:S(2)}) copy-start(bf16[128,128]{1,0:T(8,128)(2,1)} %get-tuple-element.86) | copy-start | bytes 98308
  164.5 30.1 %all-to-all-start.3 = ((bf16[8,512,256]{2,1,0:T(8,128)(2,1)}), bf16[8,512,256]{2,1,0:T(8,128)(2,1)S(1)}, u32[]{:S(2)}, u32[]{:S(2)}) async-start(bf16[8,512,256]{2,1,0:T(8,128)(2,1)} %pad_maximum_fusion.1), calls=%async_computation.3 | async-start | bytes 4194304 | tf_op jit(solution)/shard_map/all_to_all | solution.py:118
  195.7 6.9 %copy-start.17 = (bf16[512,256]{0,1:T(8,128)(2,1)S(1)}, bf16[512,256]{0,1:T(8,128)(2,1)}, u32[]{:S(2)}) copy-start(bf16[512,256]{0,1:T(8,128)(2,1)} %copy.129) | copy-start | bytes 786436
  198.7 14.3 %all-to-all-start.4 = ((bf16[4,128,512]{2,1,0:T(8,128)(2,1)}), bf16[4,128,512]{2,1,0:T(8,128)(2,1)S(1)}, u32[]{:S(2)}, u32[]{:S(2)}) async-start(bf16[4,128,512]{2,1,0:T(8,128)(2,1)} %pad_maximum_fusion.4), calls=%async_computation.4 | async-start | bytes 1048576 | tf_op jit(solution)/shard_map/all_to_all | solution.py:126
  203.5 7.7 %copy-start.13 = (bf16[4,128,2,256]{3,1,0,2:T(8,128)(2,1)}, bf16[4,128,2,256]{3,1,0,2:T(8,128)(2,1)S(1)}, u32[]{:S(2)}) copy-start(bf16[4,128,2,256]{3,1,0,2:T(8,128)(2,1)S(1)} %reshape.274) | copy-start | bytes 1572868
  216.2 5.3 %copy-start.24 = (bf16[128,1,8,128]{0,3,2,1:T(8,128)(2,1)S(1)}, bf16[128,1,8,128]{0,3,2,1:T(8,128)(2,1)}, u32[]{:S(2)}) copy-start(bf16[128,1,8,128]{0,3,2,1:T(8,128)(2,1)} %fusion.34) | copy-start | bytes 786436
  216.2 6.4 %copy-start.3 = (bf16[4224,128]{1,0:T(8,128)(2,1)S(1)}, bf16[4224,128]{1,0:T(8,128)(2,1)}, u32[]{:S(2)}) copy-start(bf16[4224,128]{1,0:T(8,128)(2,1)} %copy-done.2) | copy-start | bytes 3244036
  216.2 12.3 %collective-permute-start = (bf16[2,32,8192]{2,1,0:T(8,128)(2,1)}, bf16[2,32,8192]{2,1,0:T(8,128)(2,1)}, u32[]{:S(2)}, u32[]{:S(2)}) collective-permute-start(bf16[2,32,8192]{2,1,0:T(8,128)(2,1)} %dynamic-slice_bitcast_fusion.3), channel_id=1, source_target_pairs={{0,1},{1,0},{2,3},{3,2},{4,5},{5,4},{6,7},{7,6},{8,9},{9,8},{10,11... | collective-permute-start | bytes 3145736 | tf_op jit(solution)/shard_map/ppermute | solution.py:164
  221.5 5.0 %copy-start.12 = (f32[1,128,4,2,128]{1,4,0,3,2:T(8,128)S(1)}, f32[1,128,4,2,128]{1,4,0,3,2:T(8,128)}, u32[]{:S(2)}) copy-start(f32[1,128,4,2,128]{1,4,0,3,2:T(8,128)} %get-tuple-element.76) | copy-start | bytes 1572868
  221.5 6.0 %copy-start.11 = (f32[1,128,4,2,128]{1,4,0,3,2:T(8,128)S(1)}, f32[1,128,4,2,128]{1,4,0,3,2:T(8,128)}, u32[]{:S(2)}) copy-start(f32[1,128,4,2,128]{1,4,0,3,2:T(8,128)} %get-tuple-element.75) | copy-start | bytes 1572868
  230.3 15.9 %collective-permute-start.1 = (bf16[32,8192]{1,0:T(8,128)(2,1)S(1)}, bf16[32,8192]{1,0:T(8,128)(2,1)S(1)}, u32[]{:S(2)}, u32[]{:S(2)}) collective-permute-start(bf16[32,8192]{1,0:T(8,128)(2,1)S(1)} %fusion.65), channel_id=1, source_target_pairs={{0,2},{1,3},{2,0},{3,1},{4,6},{5,7},{6,4},{7,5},{8,10},{9,11},{10,... | collective-permute-start | bytes 1572872 | tf_op jit(solution)/shard_map/ppermute | solution.py:171
  232.2 19.2 %slice-start.11 = ((s8[8388608]{0:T(1024)(128)(4,1)}), s8[4194304]{0:T(1024)(128)(4,1)S(1)}, s32[]{:S(2)}) async-start(s8[8388608]{0:T(1024)(128)(4,1)} %bitcast.338), calls=%async_computation.17 | async-start | bytes 8388608
  238.6 7.6 %copy-start = (bf16[1,128,8192]{2,1,0:T(8,128)(2,1)S(1)}, bf16[1,128,8192]{2,1,0:T(8,128)(2,1)}, u32[]{:S(2)}) copy-start(bf16[1,128,8192]{2,1,0:T(8,128)(2,1)} %param.19) | copy-start | bytes 6291460
  238.6 12.8 %slice-start.12 = ((s8[8388608]{0:T(1024)(128)(4,1)}), s8[4194304]{0:T(1024)(128)(4,1)S(1)}, s32[]{:S(2)}) async-start(s8[8388608]{0:T(1024)(128)(4,1)} %bitcast.338), calls=%async_computation.18 | async-start | bytes 8388608
  238.7 10.6 %collective-permute-start.5 = (bf16[2,32,8192]{2,1,0:T(8,128)(2,1)S(1)}, bf16[2,32,8192]{2,1,0:T(8,128)(2,1)S(1)}, u32[]{:S(2)}, u32[]{:S(2)}) collective-permute-start(bf16[2,32,8192]{2,1,0:T(8,128)(2,1)S(1)} %dynamic-slice_bitcast_fusion.2), channel_id=1, source_target_pairs={{0,1},{1,0},{2,3},{3,2},{4,5},{5,4},{6,7},{7,6},{8,9},{9,8},{10,11... | collective-permute-start | bytes 3145736 | tf_op jit(solution)/shard_map/ppermute | solution.py:164
  247.3 16.6 %collective-permute-start.3 = (bf16[32,8192]{1,0:T(8,128)(2,1)S(1)}, bf16[32,8192]{1,0:T(8,128)(2,1)S(1)}, u32[]{:S(2)}, u32[]{:S(2)}) collective-permute-start(bf16[32,8192]{1,0:T(8,128)(2,1)S(1)} %get-tuple-element.69), channel_id=1, source_target_pairs={{96,0},{97,1},{98,2},{99,3},{100,4},{101,5},{102,6},{103,7},{104,8... | collective-permute-start | bytes 1572872 | tf_op jit(solution)/shard_map/ppermute | solution.py:184
  248.6 15.3 %collective-permute-start.2 = (bf16[32,8192]{1,0:T(8,128)(2,1)S(1)}, bf16[32,8192]{1,0:T(8,128)(2,1)S(1)}, u32[]{:S(2)}, u32[]{:S(2)}) collective-permute-start(bf16[32,8192]{1,0:T(8,128)(2,1)S(1)} %get-tuple-element.69), channel_id=1, source_target_pairs={{96,64},{64,32},{97,65},{65,33},{98,66},{66,34},{99,67},{67,35},{1... | collective-permute-start | bytes 1572872 | tf_op jit(solution)/shard_map/ppermute | solution.py:183
  249.6 17.3 %collective-permute-start.6 = (bf16[32,8192]{1,0:T(8,128)(2,1)S(1)}, bf16[32,8192]{1,0:T(8,128)(2,1)S(1)}, u32[]{:S(2)}, u32[]{:S(2)}) collective-permute-start(bf16[32,8192]{1,0:T(8,128)(2,1)S(1)} %fusion.66), channel_id=1, source_target_pairs={{0,2},{1,3},{2,0},{3,1},{4,6},{5,7},{6,4},{7,5},{8,10},{9,11},{10,... | collective-permute-start | bytes 1572872 | tf_op jit(solution)/shard_map/ppermute | solution.py:171
  254.4 24.4 %collective-permute-start.10 = (bf16[2,32,8192]{2,1,0:T(8,128)(2,1)S(1)}, bf16[2,32,8192]{2,1,0:T(8,128)(2,1)S(1)}, u32[]{:S(2)}, u32[]{:S(2)}) collective-permute-start(bf16[2,32,8192]{2,1,0:T(8,128)(2,1)S(1)} %dynamic-slice_bitcast_fusion.1), channel_id=1, source_target_pairs={{0,1},{1,0},{2,3},{3,2},{4,5},{5,4},{6,7},{7,6},{8,9},{9,8},{10,11... | collective-permute-start | bytes 3145736 | tf_op jit(solution)/shard_map/ppermute | solution.py:164
  264.0 14.5 %collective-permute-start.4 = (bf16[32,8192]{1,0:T(8,128)(2,1)S(1)}, bf16[32,8192]{1,0:T(8,128)(2,1)S(1)}, u32[]{:S(2)}, u32[]{:S(2)}) collective-permute-start(bf16[32,8192]{1,0:T(8,128)(2,1)S(1)} %fusion.36), channel_id=1, source_target_pairs={{32,0},{0,32},{33,1},{1,33},{34,2},{2,34},{35,3},{3,35},{36,4},{4,... | collective-permute-start | bytes 1572872 | tf_op jit(solution)/shard_map/ppermute | solution.py:190
  267.6 16.3 %collective-permute-start.8 = (bf16[32,8192]{1,0:T(8,128)(2,1)S(1)}, bf16[32,8192]{1,0:T(8,128)(2,1)S(1)}, u32[]{:S(2)}, u32[]{:S(2)}) collective-permute-start(bf16[32,8192]{1,0:T(8,128)(2,1)S(1)} %get-tuple-element.67), channel_id=1, source_target_pairs={{96,0},{97,1},{98,2},{99,3},{100,4},{101,5},{102,6},{103,7},{104,8... | collective-permute-start | bytes 1572872 | tf_op jit(solution)/shard_map/ppermute | solution.py:184
  268.9 15.0 %collective-permute-start.7 = (bf16[32,8192]{1,0:T(8,128)(2,1)S(1)}, bf16[32,8192]{1,0:T(8,128)(2,1)S(1)}, u32[]{:S(2)}, u32[]{:S(2)}) collective-permute-start(bf16[32,8192]{1,0:T(8,128)(2,1)S(1)} %get-tuple-element.67), channel_id=1, source_target_pairs={{96,64},{64,32},{97,65},{65,33},{98,66},{66,34},{99,67},{67,35},{1... | collective-permute-start | bytes 1572872 | tf_op jit(solution)/shard_map/ppermute | solution.py:183
  279.0 13.5 %collective-permute-start.11 = (bf16[32,8192]{1,0:T(8,128)(2,1)S(1)}, bf16[32,8192]{1,0:T(8,128)(2,1)S(1)}, u32[]{:S(2)}, u32[]{:S(2)}) collective-permute-start(bf16[32,8192]{1,0:T(8,128)(2,1)S(1)} %fusion.67), channel_id=1, source_target_pairs={{0,2},{1,3},{2,0},{3,1},{4,6},{5,7},{6,4},{7,5},{8,10},{9,11},{10,... | collective-permute-start | bytes 1572872 | tf_op jit(solution)/shard_map/ppermute | solution.py:171
  283.8 11.4 %collective-permute-start.15 = (bf16[2,32,8192]{2,1,0:T(8,128)(2,1)S(1)}, bf16[2,32,8192]{2,1,0:T(8,128)(2,1)S(1)}, u32[]{:S(2)}, u32[]{:S(2)}) collective-permute-start(bf16[2,32,8192]{2,1,0:T(8,128)(2,1)S(1)} %dynamic-slice_bitcast_fusion), channel_id=1, source_target_pairs={{0,1},{1,0},{2,3},{3,2},{4,5},{5,4},{6,7},{7,6},{8,9},{9,8},{10,11... | collective-permute-start | bytes 3145736 | tf_op jit(solution)/shard_map/ppermute | solution.py:164
  284.1 16.2 %collective-permute-start.9 = (bf16[32,8192]{1,0:T(8,128)(2,1)S(1)}, bf16[32,8192]{1,0:T(8,128)(2,1)S(1)}, u32[]{:S(2)}, u32[]{:S(2)}) collective-permute-start(bf16[32,8192]{1,0:T(8,128)(2,1)S(1)} %fusion.38), channel_id=1, source_target_pairs={{32,0},{0,32},{33,1},{1,33},{34,2},{2,34},{35,3},{3,35},{36,4},{4,... | collective-permute-start | bytes 1572872 | tf_op jit(solution)/shard_map/ppermute | solution.py:190
  293.2 17.5 %collective-permute-start.13 = (bf16[32,8192]{1,0:T(8,128)(2,1)S(1)}, bf16[32,8192]{1,0:T(8,128)(2,1)S(1)}, u32[]{:S(2)}, u32[]{:S(2)}) collective-permute-start(bf16[32,8192]{1,0:T(8,128)(2,1)S(1)} %get-tuple-element.65), channel_id=1, source_target_pairs={{96,0},{97,1},{98,2},{99,3},{100,4},{101,5},{102,6},{103,7},{104,8... | collective-permute-start | bytes 1572872 | tf_op jit(solution)/shard_map/ppermute | solution.py:184
  294.5 16.2 %collective-permute-start.12 = (bf16[32,8192]{1,0:T(8,128)(2,1)S(1)}, bf16[32,8192]{1,0:T(8,128)(2,1)S(1)}, u32[]{:S(2)}, u32[]{:S(2)}) collective-permute-start(bf16[32,8192]{1,0:T(8,128)(2,1)S(1)} %get-tuple-element.65), channel_id=1, source_target_pairs={{96,64},{64,32},{97,65},{65,33},{98,66},{66,34},{99,67},{67,35},{1... | collective-permute-start | bytes 1572872 | tf_op jit(solution)/shard_map/ppermute | solution.py:183
  295.5 12.5 %collective-permute-start.16 = (bf16[32,8192]{1,0:T(8,128)(2,1)S(1)}, bf16[32,8192]{1,0:T(8,128)(2,1)S(1)}, u32[]{:S(2)}, u32[]{:S(2)}) collective-permute-start(bf16[32,8192]{1,0:T(8,128)(2,1)S(1)} %fusion.68), channel_id=1, source_target_pairs={{0,2},{1,3},{2,0},{3,1},{4,6},{5,7},{6,4},{7,5},{8,10},{9,11},{10,... | collective-permute-start | bytes 1572872 | tf_op jit(solution)/shard_map/ppermute | solution.py:171
  308.7 13.5 %collective-permute-start.18 = (bf16[32,8192]{1,0:T(8,128)(2,1)S(1)}, bf16[32,8192]{1,0:T(8,128)(2,1)S(1)}, u32[]{:S(2)}, u32[]{:S(2)}) collective-permute-start(bf16[32,8192]{1,0:T(8,128)(2,1)S(1)} %get-tuple-element.63), channel_id=1, source_target_pairs={{96,0},{97,1},{98,2},{99,3},{100,4},{101,5},{102,6},{103,7},{104,8... | collective-permute-start | bytes 1572872 | tf_op jit(solution)/shard_map/ppermute | solution.py:184
  310.0 12.2 %collective-permute-start.17 = (bf16[32,8192]{1,0:T(8,128)(2,1)S(1)}, bf16[32,8192]{1,0:T(8,128)(2,1)S(1)}, u32[]{:S(2)}, u32[]{:S(2)}) collective-permute-start(bf16[32,8192]{1,0:T(8,128)(2,1)S(1)} %get-tuple-element.63), channel_id=1, source_target_pairs={{96,64},{64,32},{97,65},{65,33},{98,66},{66,34},{99,67},{67,35},{1... | collective-permute-start | bytes 1572872 | tf_op jit(solution)/shard_map/ppermute | solution.py:183
  310.9 13.8 %collective-permute-start.14 = (bf16[32,8192]{1,0:T(8,128)(2,1)S(1)}, bf16[32,8192]{1,0:T(8,128)(2,1)S(1)}, u32[]{:S(2)}, u32[]{:S(2)}) collective-permute-start(bf16[32,8192]{1,0:T(8,128)(2,1)S(1)} %fusion.40), channel_id=1, source_target_pairs={{32,0},{0,32},{33,1},{1,33},{34,2},{2,34},{35,3},{3,35},{36,4},{4,... | collective-permute-start | bytes 1572872 | tf_op jit(solution)/shard_map/ppermute | solution.py:190
  322.4 11.7 %collective-permute-start.19 = (bf16[32,8192]{1,0:T(8,128)(2,1)S(1)}, bf16[32,8192]{1,0:T(8,128)(2,1)S(1)}, u32[]{:S(2)}, u32[]{:S(2)}) collective-permute-start(bf16[32,8192]{1,0:T(8,128)(2,1)S(1)} %fusion.42), channel_id=1, source_target_pairs={{32,0},{0,32},{33,1},{1,33},{34,2},{2,34},{35,3},{3,35},{36,4},{4,... | collective-permute-start | bytes 1572872 | tf_op jit(solution)/shard_map/ppermute | solution.py:190
  (11 other events, 20.2 us)
Sparse Core Ops, SparseCore 0:
  63.0 50.3 all-gather.1

commit v4 on v3

--- a/solution.py
+++ b/solution.py
@@ -141,12 +141,14 @@
         states_all = prefix_states[0]
         gain_wide = norm_gain[0].astype(jnp.float32)[None, :]
         sec = lax.axis_index("section")
-        n_chunks = 4
-        step = rows_local // n_chunks
+        unit = rows_local // 8
+        sizes = [3 * unit, 2 * unit, 2 * unit, unit]
+        starts = [sum(sizes[:i]) for i in range(len(sizes))]
         outs = []
         previous = None
-        for c in range(n_chunks):
-            rows = slice(c * step, (c + 1) * step)
+        for c in range(len(sizes)):
+            step = sizes[c]
+            rows = slice(starts[c], starts[c] + step)
             grad_rows_c = grad_cols[:, rows]
             if c > 0:
                 grad_rows_c, sent = lax.optimization_barrier((grad_rows_c, sent))

time: 350 us -> 349 us (level)
  waiting for transfers between devices: 111 us -> 107 us
    ppermute x4, waiting for transfers between devices: 21.3 us -> 14.9 us  [on_device(): last = lax.ppermute(carry.astype(jnp.bfloat16), 'section', [(1, 0), (0, 1)])]
    ppermute x4, waiting for transfers between devices: 20.3 us -> 26.2 us  [on_device(): got2 = lax.ppermute(other, 'tensor', chip_pairs)]
    unnamed x105 -> x103, local copies, waits for them, and re-layouts: 12.1 us -> 11.3 us
  transfers between devices with their start and end apart: 26 -> 26, of which waited for: 13 -> 16; matrix products, arithmetic and copies ran while one was open for 41% -> 41% of each run, Pallas kernels for 0% -> 0%
where the time goes in v4:
time: 349 us; the launch traced here: 343 us
  waiting for transfers between devices  107 us (31%)
  matrix products  76 us (22%)
  other arithmetic  58.4 us (17%)
  starting transfers between devices  52 us (15%)
  local copies, waits for them, and re-layouts  34.3 us (10%)
  between operations  15.3 us (4%)
    ppermute x4, waiting for transfers between devices, on_device(): got2 = lax.ppermute(other, 'tensor', chip_pairs)  26.2 us
    all_to_all x1, waiting for transfers between devices, on_device(): lax.all_to_all(spread, 'sample', 0, 0, tiled=True).reshape(pooled_rows, -1)  22.1 us
    sub x2, other arithmetic, attend_group(): exponent = jnp.exp(scores - row_max)  21 us
    dot_general x4, matrix products, on_device(): lax.dot_general(grad_rows_c, weight_local, (((2, 3), (1, 2)), ((), ())),...  20 us
    convert_element_type x2, other arithmetic, attend_group(): weights_low = softmax_w.astype(jnp.bfloat16)  17.1 us
    all_to_all x2, waiting for transfers between devices, on_device(): parts = lax.all_to_all(pool_grad, 'sample', 0, 0, tiled=False)  16.5 us
    ppermute x4, waiting for transfers between devices, on_device(): last = lax.ppermute(carry.astype(jnp.bfloat16), 'section', [(1, 0), (0, 1)])  14.9 us
    ppermute x4, waiting for transfers between devices, on_device(): wrap = lax.ppermute(term_low, 'section', [(3, 0)])  14.7 us
  transfers between devices with their start and end apart: 26, of which 16 were waited for; matrix products, arithmetic and copies ran while one was open for 41% of the time, Pallas kernels for 0%

profile of v4, /device:TPU:0, one launch (start us, length us, event | category | flops | bytes accessed | tf_op | source)
XLA Modules:
  0.0 343.5 jit_solution(5823049345762756228)
XLA Ops:
  10.3 4.6 %all-to-all-start = ((bf16[4,128,512]{1,2,0:T(8,128)(2,1)}), bf16[4,128,512]{1,2,0:T(8,128)(2,1)S(1)}, u32[]{:S(2)}, u32[]{:S(2)}) async-start(bf16[4,128,512]{1,2,0:T(8,128)(2,1)} %bitcast.6), calls=%async_computation | async-start | bytes 1048576 | tf_op jit(solution)/shard_map/all_to_all | solution.py:85
  15.2 10.0 %all-to-all-done = bf16[4,128,512]{1,2,0:T(8,128)(2,1)S(1)} async-done(((bf16[4,128,512]{1,2,0:T(8,128)(2,1)}), bf16[4,128,512]{1,2,0:T(8,128)(2,1)S(1)}, u32[]{:S(2)}, u32[]{:S(2)}) %all-to-all-start) | async-done | bytes 524320 | tf_op jit(solution)/shard_map/all_to_all | solution.py:85
  26.4 1.5 broadcast_in_dim.97
  27.8 5.6 %all-to-all-start.1 = ((bf16[8,512,256]{2,1,0:T(8,128)(2,1)}), bf16[8,512,256]{2,1,0:T(8,128)(2,1)}, u32[]{:S(2)}, u32[]{:S(2)}) async-start(bf16[8,512,256]{2,1,0:T(8,128)(2,1)} %broadcast_in_dim.97), calls=%async_computation.1 | async-start | bytes 4194304 | tf_op jit(solution)/shard_map/all_to_all | solution.py:94
  38.1 22.1 %all-to-all-done.1 = bf16[8,512,256]{2,1,0:T(8,128)(2,1)} async-done(((bf16[8,512,256]{2,1,0:T(8,128)(2,1)}), bf16[8,512,256]{2,1,0:T(8,128)(2,1)}, u32[]{:S(2)}, u32[]{:S(2)}) %all-to-all-start.1) | async-done | bytes 2097184 | tf_op jit(solution)/shard_map/all_to_all | solution.py:94
  60.2 2.6 fusion.101
  62.9 3.2 fusion.58
  66.0 10.8 %fusion.110 = (f32[128,8]{0,1:T(8,128)S(1)}, f32[128,8,4224]{0,2,1:T(8,128)}) fusion(f32[4224,128,8]{1,0,2:T(8,128)S(1)} %fusion.58, pred[128,4224]{0,1:T(8,128)(4,1)S(1)} %pad_add_fusion), kind=kOutput, calls=%fused_computation.209 | output fusion | flops 17305728 | bytes 35147776 | tf_op jit(solution)/shard_map/sub | solution.py:36
  76.8 6.8 %fusion.18 = bf16[128,8,4224]{0,2,1:T(8,128)(2,1)S(1)} fusion(f32[128,8,4224]{0,2,1:T(8,128)} %get-tuple-element.100, f32[128,8]{0,1:T(8,128)S(1)} %get-tuple-element.99), kind=kLoop, calls=%fused_computation.30 | loop fusion | flops 8650752 | bytes 25956352 | tf_op jit(solution)/shard_map/convert_element_type | solution.py:38
  83.7 2.4 fusion.26
  86.2 2.5 fusion.38
  89.2 1.3 slice-done.3
  90.5 7.1 %fusion.3 = bf16[128,8,4224]{0,2,1:T(8,128)(2,1)} fusion(f32[128,8]{0,1:T(8,128)S(1)} %fusion.38, f32[128,8,4224]{0,2,1:T(8,128)S(1)} %bitcast.285, f32[128,8]{0,1:T(8,128)S(1)} %get-tuple-element.99, bf16[128,128]{1,0:T(8,128)(2,1)S(1)} %copy-done.30, bf16[4096,128]{1,0:T(8,128)(2,1)} %get-tuple-element.73, bf16[128,2,8,128]{0,3,2,1:T(8,128)(2,1)} %bitcast.314), kind=kOutput, calls=%fused_computation.6 | convolution fusion | flops 1126760448 | bytes 27303936 | tf_op jit(solution)/shard_map/rgd,kd->rgk/dot_general | solution.py:43
  97.7 5.9 %fusion.25 = bf16[4224,128]{1,0:T(8,128)(2,1)S(1)} fusion(bf16[128,8,4224]{0,2,1:T(8,128)(2,1)} %fusion.3, bf16[128,2,8,128]{0,3,2,1:T(8,128)(2,1)} %bitcast.306), kind=kOutput, calls=%fused_computation.41 | convolution fusion | flops 1108377600 | bytes 9994240 | tf_op jit(solution)/shard_map/rgk,rgd->kd/dot_general | solution.py:48
  105.8 1.5 pad_maximum_fusion
  107.4 4.3 %all-to-all-start.2 = ((bf16[8,512,256]{2,1,0:T(8,128)(2,1)}), bf16[8,512,256]{2,1,0:T(8,128)(2,1)}, u32[]{:S(2)}, u32[]{:S(2)}) async-start(bf16[8,512,256]{2,1,0:T(8,128)(2,1)} %pad_maximum_fusion), calls=%async_computation.2 | async-start | bytes 4194304 | tf_op jit(solution)/shard_map/all_to_all | solution.py:118
  111.7 1.7 all-gather.2.cloned.1.call-done
  113.4 2.7 fusion.102
  116.1 2.4 fusion.57
  118.5 10.2 %fusion.109 = (f32[128,8]{0,1:T(8,128)S(1)}, f32[128,8,4224]{0,2,1:T(8,128)}) fusion(f32[4224,128,8]{1,0,2:T(8,128)S(1)} %fusion.57, pred[128,4224]{0,1:T(8,128)(4,1)S(1)} %pad_add_fusion), kind=kOutput, calls=%fused_computation.208 | output fusion | flops 17305728 | bytes 35147776 | tf_op jit(solution)/shard_map/sub | solution.py:36
  128.8 10.2 %fusion.19 = bf16[128,8,4224]{0,2,1:T(8,128)(2,1)} fusion(f32[128,8,4224]{0,2,1:T(8,128)} %get-tuple-element.98, f32[128,8]{0,1:T(8,128)S(1)} %get-tuple-element.97), kind=kLoop, calls=%fused_computation.31 | loop fusion | flops 8650752 | bytes 25956352 | tf_op jit(solution)/shard_map/convert_element_type | solution.py:38
  139.0 6.8 %fusion.39 = f32[128,8]{0,1:T(8,128)S(1)} fusion(bf16[128,8,4224]{0,2,1:T(8,128)(2,1)} %fusion.19, bf16[128,128]{1,0:T(8,128)(2,1)S(1)} %copy-done.29, bf16[4096,128]{1,0:T(8,128)(2,1)S(1)} %copy-done.18, bf16[128,1,8,128]{3,0,2,1:T(8,128)(2,1)S(1)} %copy-done.21), kind=kOutput, calls=%fused_computation.90 | convolution fusion | flops 1109851136 | bytes 9998336 | tf_op jit(solution)/shard_map/rgk,kd->rgd/dot_general | solution.py:39
  145.9 6.4 %fusion.2 = bf16[128,8,4224]{0,2,1:T(8,128)(2,1)} fusion(f32[128,8]{0,1:T(8,128)S(1)} %fusion.39, f32[128,8,4224]{0,2,1:T(8,128)S(1)} %bitcast.287, f32[128,8]{0,1:T(8,128)S(1)} %get-tuple-element.97, bf16[128,128]{1,0:T(8,128)(2,1)S(1)} %copy-done.29, bf16[4096,128]{1,0:T(8,128)(2,1)} %get-tuple-element.75, bf16[128,2,8,128]{0,3,2,1:T(8,128)(2,1)S(1)} %bitcast.316), kind=kOutput, calls=%fused_computation.3 | convolution fusion | flops 1126760448 | bytes 27303936 | tf_op jit(solution)/shard_map/rgd,kd->rgk/dot_general | solution.py:43
  152.3 6.0 %fusion.28 = bf16[4224,128]{1,0:T(8,128)(2,1)S(1)} fusion(bf16[128,8,4224]{0,2,1:T(8,128)(2,1)} %fusion.19, bf16[128,2,8,128]{0,3,2,1:T(8,128)(2,1)S(1)} %bitcast.317), kind=kOutput, calls=%fused_computation.44 | convolution fusion | flops 1107836928 | bytes 9994240 | tf_op jit(solution)/shard_map/rgk,rgd->kd/dot_general | solution.py:51
  159.4 2.5 fusion.27
  163.0 1.5 pad_maximum_fusion.1
  164.6 4.1 %all-to-all-start.3 = ((bf16[8,512,256]{2,1,0:T(8,128)(2,1)}), bf16[8,512,256]{2,1,0:T(8,128)(2,1)S(1)}, u32[]{:S(2)}, u32[]{:S(2)}) async-start(bf16[8,512,256]{2,1,0:T(8,128)(2,1)} %pad_maximum_fusion.1), calls=%async_computation.3 | async-start | bytes 4194304 | tf_op jit(solution)/shard_map/all_to_all | solution.py:118
  169.5 5.9 %fusion.41 = bf16[128,1,8,128]{0,3,2,1:T(8,128)(2,1)} fusion(bf16[128,8,4224]{0,2,1:T(8,128)(2,1)} %fusion.3, bf16[128,128]{1,0:T(8,128)(2,1)S(1)} %copy-done.25, bf16[4096,128]{1,0:T(8,128)(2,1)} %copy-done.1), kind=kOutput, calls=%fused_computation.92 | convolution fusion | flops 1109721088 | bytes 9994240 | tf_op jit(solution)/shard_map/rgk,kd->rgd/dot_general | solution.py:115
  175.4 2.0 reduce
  178.2 16.5 %all-to-all-done.3 = bf16[8,512,256]{2,1,0:T(8,128)(2,1)S(1)} async-done(((bf16[8,512,256]{2,1,0:T(8,128)(2,1)}), bf16[8,512,256]{2,1,0:T(8,128)(2,1)S(1)}, u32[]{:S(2)}, u32[]{:S(2)}) %all-to-all-start.3) | async-done | bytes 2097184 | tf_op jit(solution)/shard_map/all_to_all | solution.py:118
  196.9 1.8 pad_maximum_fusion.4
  198.7 4.0 %all-to-all-start.4 = ((bf16[4,128,512]{2,1,0:T(8,128)(2,1)}), bf16[4,128,512]{2,1,0:T(8,128)(2,1)S(1)}, u32[]{:S(2)}, u32[]{:S(2)}) async-start(bf16[4,128,512]{2,1,0:T(8,128)(2,1)} %pad_maximum_fusion.4), calls=%async_computation.4 | async-start | bytes 1048576 | tf_op jit(solution)/shard_map/all_to_all | solution.py:126
  203.5 8.2 %fusion.6 = bf16[4,48,8192]{2,1,0:T(8,128)(2,1)} fusion(bf16[8192,2,256]{2,1,0:T(2,128)(2,1)} %bitcast.336, bf16[4,128,2,256]{3,1,0,2:T(8,128)(2,1)S(1)} %reshape.274), kind=kOutput, calls=%fused_computation.13 | convolution fusion | flops 1612185600 | bytes 11730944 | tf_op jit(solution)/shard_map/dot_general | solution.py:155
  211.7 1.3 all-to-all-done.4
  214.3 2.7 dynamic-slice_bitcast_fusion
  217.3 4.9 %fusion.40 = bf16[128,1,8,128]{0,3,2,1:T(8,128)(2,1)S(1)} fusion(bf16[128,8,4224]{0,2,1:T(8,128)(2,1)} %fusion.2, bf16[128,128]{1,0:T(8,128)(2,1)S(1)} %copy-done.24, bf16[4096,128]{1,0:T(8,128)(2,1)S(1)} %get-tuple-element.76), kind=kOutput, calls=%fused_computation.91 | convolution fusion | flops 1109721088 | bytes 9994240 | tf_op jit(solution)/shard_map/rgk,kd->rgd/dot_general | solution.py:115
  229.1 2.2 convert_add_fusion
  231.4 2.4 collective-permute-start.1
  233.8 6.4 %fusion.7 = bf16[4,32,8192]{2,1,0:T(8,128)(2,1)S(1)} fusion(bf16[4,32,2,256]{3,1,0,2:T(8,128)(2,1)S(1)} %get-tuple-element.28, bf16[8192,2,256,1]{2,1,0,3:T(2,128)(2,1)} %bitcast.337), kind=kOutput, calls=%fused_computation.16 | convolution fusion | flops 1074790400 | bytes 10616832 | tf_op jit(solution)/shard_map/dot_general | solution.py:155
  240.5 12.5 %collective-permute-done.1 = bf16[48,8192]{1,0:T(8,128)(2,1)S(1)} collective-permute-done((bf16[48,8192]{1,0:T(8,128)(2,1)S(1)}, bf16[48,8192]{1,0:T(8,128)(2,1)S(1)}, u32[]{:S(2)}, u32[]{:S(2)}) %collective-permute-start.1) | collective-permute-done | bytes 786464 | tf_op jit(solution)/shard_map/ppermute | solution.py:173
  254.0 1.3 collective-permute-start.3
  256.3 2.3 collective-permute-start.6
  258.6 2.8 fusion.8
  261.6 9.7 %collective-permute-done.6 = bf16[32,8192]{1,0:T(8,128)(2,1)S(1)} collective-permute-done((bf16[32,8192]{1,0:T(8,128)(2,1)S(1)}, bf16[32,8192]{1,0:T(8,128)(2,1)S(1)}, u32[]{:S(2)}, u32[]{:S(2)}) %collective-permute-start.6) | collective-permute-done | bytes 524320 | tf_op jit(solution)/shard_map/ppermute | solution.py:173
  272.2 1.3 collective-permute-start.8
  274.3 1.9 collective-permute-done.3
  276.5 3.0 collective-permute-start.4
  279.8 2.3 collective-permute-start.11
  282.2 2.6 fusion.9
  285.0 3.4 collective-permute-done.8
  288.6 2.8 collective-permute-start.9
  291.4 2.5 collective-permute-done.11
  294.8 2.1 collective-permute-start.16
  296.8 2.1 collective-permute-done.4
  299.2 1.3 collective-permute-start.13
  301.2 1.5 collective-permute-done.16
  303.2 1.3 collective-permute-start.18
  305.2 2.8 collective-permute-done.9
  308.2 9.3 %collective-permute-done.18 = bf16[16,8192]{1,0:T(8,128)(2,1)S(1)} collective-permute-done((bf16[16,8192]{1,0:T(8,128)(2,1)S(1)}, bf16[16,8192]{1,0:T(8,128)(2,1)S(1)}, u32[]{:S(2)}, u32[]{:S(2)}) %collective-permute-start.18) | collective-permute-done | bytes 262176 | tf_op jit(solution)/shard_map/ppermute | solution.py:186
  317.6 2.4 collective-permute-start.19
  320.3 3.5 %collective-permute-start.14 = (bf16[32,8192]{1,0:T(8,128)(2,1)S(1)}, bf16[32,8192]{1,0:T(8,128)(2,1)S(1)}, u32[]{:S(2)}, u32[]{:S(2)}) collective-permute-start(bf16[32,8192]{1,0:T(8,128)(2,1)S(1)} %fusion.45), channel_id=1, source_target_pairs={{32,0},{0,32},{33,1},{1,33},{34,2},{2,34},{35,3},{3,35},{36,4},{4,... | collective-permute-start | bytes 1572872 | tf_op jit(solution)/shard_map/ppermute | solution.py:192
  323.7 4.5 %collective-permute-done.19 = bf16[16,8192]{1,0:T(8,128)(2,1)S(1)} collective-permute-done((bf16[16,8192]{1,0:T(8,128)(2,1)S(1)}, bf16[16,8192]{1,0:T(8,128)(2,1)S(1)}, u32[]{:S(2)}, u32[]{:S(2)}) %collective-permute-start.19) | collective-permute-done | bytes 262176 | tf_op jit(solution)/shard_map/ppermute | solution.py:192
  328.4 5.5 %collective-permute-done.14 = bf16[32,8192]{1,0:T(8,128)(2,1)S(1)} collective-permute-done((bf16[32,8192]{1,0:T(8,128)(2,1)S(1)}, bf16[32,8192]{1,0:T(8,128)(2,1)S(1)}, u32[]{:S(2)}, u32[]{:S(2)}) %collective-permute-start.14) | collective-permute-done | bytes 524320 | tf_op jit(solution)/shard_map/ppermute | solution.py:192
  334.1 2.3 maximum_bitcast_fusion
  (197 shorter events, 36.1 us)
Async XLA Ops:
  7.2 7.7 %copy-start.19 = (bf16[1,128,2048]{2,1,0:T(8,128)(2,1)S(1)}, bf16[1,128,2048]{2,1,0:T(8,128)(2,1)}, u32[]{:S(2)}) copy-start(bf16[1,128,2048]{2,1,0:T(8,128)(2,1)} %param.15) | copy-start | bytes 1572868
  10.3 14.9 %all-to-all-start = ((bf16[4,128,512]{1,2,0:T(8,128)(2,1)}), bf16[4,128,512]{1,2,0:T(8,128)(2,1)S(1)}, u32[]{:S(2)}, u32[]{:S(2)}) async-start(bf16[4,128,512]{1,2,0:T(8,128)(2,1)} %bitcast.6), calls=%async_computation | async-start | bytes 1048576 | tf_op jit(solution)/shard_map/all_to_all | solution.py:85
  15.2 18.3 %copy-start.7 = (bf16[1,128,2048]{1,2,0:T(8,128)(2,1)}, bf16[1,128,2048]{1,2,0:T(8,128)(2,1)S(1)}, u32[]{:S(2)}) copy-start(bf16[1,128,2048]{1,2,0:T(8,128)(2,1)S(1)} %copy.113) | copy-start | bytes 1572868
  27.8 5.7 %copy-start.20 = (bf16[1,128,2048]{2,1,0:T(8,128)(2,1)S(1)}, bf16[1,128,2048]{2,1,0:T(8,128)(2,1)}, u32[]{:S(2)}) copy-start(bf16[1,128,2048]{2,1,0:T(8,128)(2,1)} %param.12) | copy-start | bytes 1572868
  27.8 32.3 %all-to-all-start.1 = ((bf16[8,512,256]{2,1,0:T(8,128)(2,1)}), bf16[8,512,256]{2,1,0:T(8,128)(2,1)}, u32[]{:S(2)}, u32[]{:S(2)}) async-start(bf16[8,512,256]{2,1,0:T(8,128)(2,1)} %broadcast_in_dim.97), calls=%async_computation.1 | async-start | bytes 4194304 | tf_op jit(solution)/shard_map/all_to_all | solution.py:94
  33.4 3.1 copy-start.27
  33.4 79.9 %all-gather.2.cloned.1.call-start = ((), (), s32[]{:S(2)}) async-start(), calls=%async_computation.5 | async-start | bytes 2359296 | tf_op jit(solution)/shard_map/all_gather | solution.py:97
  33.8 29.0 %copy-start.4 = (bf16[1,128,2048]{1,2,0:T(8,128)(2,1)}, bf16[1,128,2048]{1,2,0:T(8,128)(2,1)S(1)}, u32[]{:S(2)}) copy-start(bf16[1,128,2048]{1,2,0:T(8,128)(2,1)S(1)} %copy.111) | copy-start | bytes 1572868
  62.8 3.2 copy-start.1
  76.8 6.8 %copy-start.8 = (bf16[1,128,2048]{1,2,0:T(8,128)(2,1)S(1)}, bf16[1,128,2048]{1,2,0:T(8,128)(2,1)}, u32[]{:S(2)}) copy-start(bf16[1,128,2048]{1,2,0:T(8,128)(2,1)} %copy-done.7) | copy-start | bytes 1572868
  83.7 5.1 %slice-start = ((s8[17301504]{0:T(1024)(128)(4,1)}), s8[4194304]{0:T(1024)(128)(4,1)S(1)}, s32[]{:S(2)}) async-start(s8[17301504]{0:T(1024)(128)(4,1)} %bitcast.284), calls=%async_computation.6 | async-start | bytes 8388608
  83.7 5.1 %slice-start.1 = ((s8[17301504]{0:T(1024)(128)(4,1)}), s8[4194304]{0:T(1024)(128)(4,1)S(1)}, s32[]{:S(2)}) async-start(s8[17301504]{0:T(1024)(128)(4,1)} %bitcast.284), calls=%async_computation.7 | async-start | bytes 8388608
  83.7 5.5 %slice-start.2 = ((s8[17301504]{0:T(1024)(128)(4,1)}), s8[4194304]{0:T(1024)(128)(4,1)S(1)}, s32[]{:S(2)}) async-start(s8[17301504]{0:T(1024)(128)(4,1)} %bitcast.284), calls=%async_computation.8 | async-start | bytes 8388608
  86.1 2.6 copy-start.2
  86.2 4.3 %slice-start.3 = ((s8[17301504]{0:T(1024)(128)(4,1)}), s8[4194304]{0:T(1024)(128)(4,1)S(1)}, s32[]{:S(2)}) async-start(s8[17301504]{0:T(1024)(128)(4,1)} %bitcast.284), calls=%async_computation.9 | async-start | bytes 8388608
  86.2 4.3 %slice-start.4 = ((s8[17301504]{0:T(1024)(128)(4,1)}), s8[524288]{0:T(1024)(128)(4,1)S(1)}, s32[]{:S(2)}) async-start(s8[17301504]{0:T(1024)(128)(4,1)} %bitcast.284), calls=%async_computation.10 | async-start | bytes 1048576
  107.4 57.2 %all-to-all-start.2 = ((bf16[8,512,256]{2,1,0:T(8,128)(2,1)}), bf16[8,512,256]{2,1,0:T(8,128)(2,1)}, u32[]{:S(2)}, u32[]{:S(2)}) async-start(bf16[8,512,256]{2,1,0:T(8,128)(2,1)} %pad_maximum_fusion), calls=%async_computation.2 | async-start | bytes 4194304 | tf_op jit(solution)/shard_map/all_to_all | solution.py:118
  111.7 4.4 %copy-start.24 = (bf16[128,128]{1,0:T(8,128)(2,1)S(1)}, bf16[128,128]{1,0:T(8,128)(2,1)}, u32[]{:S(2)}) copy-start(bf16[128,128]{1,0:T(8,128)(2,1)} %get-tuple-element.88) | copy-start | bytes 98308
  113.4 2.7 copy-start.5
  128.7 10.3 %copy-start.18 = (bf16[4096,128]{1,0:T(8,128)(2,1)S(1)}, bf16[4096,128]{1,0:T(8,128)(2,1)}, u32[]{:S(2)}) copy-start(bf16[4096,128]{1,0:T(8,128)(2,1)} %get-tuple-element.75) | copy-start | bytes 3145732
  128.7 10.3 %copy-start.21 = (bf16[128,1,8,128]{3,0,2,1:T(8,128)(2,1)S(1)}, bf16[128,1,8,128]{3,0,2,1:T(8,128)(2,1)}, u32[]{:S(2)}) copy-start(bf16[128,1,8,128]{3,0,2,1:T(8,128)(2,1)} %copy.173) | copy-start | bytes 786436
  128.7 10.3 %copy-start.29 = (bf16[128,128]{1,0:T(8,128)(2,1)S(1)}, bf16[128,128]{1,0:T(8,128)(2,1)}, u32[]{:S(2)}) copy-start(bf16[128,128]{1,0:T(8,128)(2,1)} %get-tuple-element.86) | copy-start | bytes 98308
  128.7 17.2 %slice-start.5 = ((s8[17301504]{0:T(1024)(128)(4,1)}), s8[4194304]{0:T(1024)(128)(4,1)S(1)}, s32[]{:S(2)}) async-start(s8[17301504]{0:T(1024)(128)(4,1)} %bitcast.286), calls=%async_computation.11 | async-start | bytes 8388608
  128.7 17.2 %slice-start.6 = ((s8[17301504]{0:T(1024)(128)(4,1)}), s8[4194304]{0:T(1024)(128)(4,1)S(1)}, s32[]{:S(2)}) async-start(s8[17301504]{0:T(1024)(128)(4,1)} %bitcast.286), calls=%async_computation.12 | async-start | bytes 8388608
  128.7 17.2 %slice-start.7 = ((s8[17301504]{0:T(1024)(128)(4,1)}), s8[4194304]{0:T(1024)(128)(4,1)S(1)}, s32[]{:S(2)}) async-start(s8[17301504]{0:T(1024)(128)(4,1)} %bitcast.286), calls=%async_computation.13 | async-start | bytes 8388608
  128.7 17.2 %slice-start.8 = ((s8[17301504]{0:T(1024)(128)(4,1)}), s8[4194304]{0:T(1024)(128)(4,1)S(1)}, s32[]{:S(2)}) async-start(s8[17301504]{0:T(1024)(128)(4,1)} %bitcast.286), calls=%async_computation.14 | async-start | bytes 8388608
  139.0 6.9 %slice-start.9 = ((s8[17301504]{0:T(1024)(128)(4,1)}), s8[524288]{0:T(1024)(128)(4,1)S(1)}, s32[]{:S(2)}) async-start(s8[17301504]{0:T(1024)(128)(4,1)} %bitcast.286), calls=%async_computation.15 | async-start | bytes 1048576
  139.0 6.9 %copy-start.9 = (bf16[1,128,2048]{1,2,0:T(8,128)(2,1)S(1)}, bf16[1,128,2048]{1,2,0:T(8,128)(2,1)}, u32[]{:S(2)}) copy-start(bf16[1,128,2048]{1,2,0:T(8,128)(2,1)} %copy-done.7) | copy-start | bytes 1572868
  152.3 7.1 %copy-start.6 = (bf16[1,128,2048]{1,2,0:T(8,128)(2,1)S(1)}, bf16[1,128,2048]{1,2,0:T(8,128)(2,1)}, u32[]{:S(2)}) copy-start(bf16[1,128,2048]{1,2,0:T(8,128)(2,1)} %copy-done.4) | copy-start | bytes 1572868
  152.3 7.1 %copy-start.34 = (bf16[128,8,4224]{0,2,1:T(8,128)(2,1)S(1)}, bf16[128,8,4224]{0,2,1:T(8,128)(2,1)}, u32[]{:S(2)}) copy-start(bf16[128,8,4224]{0,2,1:T(8,128)(2,1)} %fusion.2) | copy-start | bytes 25952260
  164.6 4.1 %copy-start.28 = (bf16[1,8192]{1,0:T(2,128)(2,1)S(1)}, bf16[1,8192]{1,0:T(2,128)(2,1)}, u32[]{:S(2)}) copy-start(bf16[1,8192]{1,0:T(2,128)(2,1)} %param.20) | copy-start | bytes 49156
  164.6 4.9 %copy-start.25 = (bf16[128,128]{1,0:T(8,128)(2,1)S(1)}, bf16[128,128]{1,0:T(8,128)(2,1)}, u32[]{:S(2)}) copy-start(bf16[128,128]{1,0:T(8,128)(2,1)} %get-tuple-element.87) | copy-start | bytes 98308
  164.6 30.2 %all-to-all-start.3 = ((bf16[8,512,256]{2,1,0:T(8,128)(2,1)}), bf16[8,512,256]{2,1,0:T(8,128)(2,1)S(1)}, u32[]{:S(2)}, u32[]{:S(2)}) async-start(bf16[8,512,256]{2,1,0:T(8,128)(2,1)} %pad_maximum_fusion.1), calls=%async_computation.3 | async-start | bytes 4194304 | tf_op jit(solution)/shard_map/all_to_all | solution.py:118
  195.8 6.9 %copy-start.16 = (bf16[512,256]{0,1:T(8,128)(2,1)S(1)}, bf16[512,256]{0,1:T(8,128)(2,1)}, u32[]{:S(2)}) copy-start(bf16[512,256]{0,1:T(8,128)(2,1)} %copy.129) | copy-start | bytes 786436
  198.7 14.3 %all-to-all-start.4 = ((bf16[4,128,512]{2,1,0:T(8,128)(2,1)}), bf16[4,128,512]{2,1,0:T(8,128)(2,1)S(1)}, u32[]{:S(2)}, u32[]{:S(2)}) async-start(bf16[4,128,512]{2,1,0:T(8,128)(2,1)} %pad_maximum_fusion.4), calls=%async_computation.4 | async-start | bytes 1048576 | tf_op jit(solution)/shard_map/all_to_all | solution.py:126
  203.5 8.2 %copy-start.12 = (bf16[4,128,2,256]{3,1,0,2:T(8,128)(2,1)}, bf16[4,128,2,256]{3,1,0,2:T(8,128)(2,1)S(1)}, u32[]{:S(2)}) copy-start(bf16[4,128,2,256]{3,1,0,2:T(8,128)(2,1)S(1)} %reshape.274) | copy-start | bytes 1572868
  216.9 5.3 %copy-start.23 = (bf16[128,1,8,128]{0,3,2,1:T(8,128)(2,1)S(1)}, bf16[128,1,8,128]{0,3,2,1:T(8,128)(2,1)}, u32[]{:S(2)}) copy-start(bf16[128,1,8,128]{0,3,2,1:T(8,128)(2,1)} %fusion.41) | copy-start | bytes 786436
  216.9 6.4 %copy-start.3 = (bf16[4224,128]{1,0:T(8,128)(2,1)S(1)}, bf16[4224,128]{1,0:T(8,128)(2,1)}, u32[]{:S(2)}) copy-start(bf16[4224,128]{1,0:T(8,128)(2,1)} %copy-done.2) | copy-start | bytes 3244036
  216.9 12.2 %collective-permute-start = (bf16[2,48,8192]{2,1,0:T(8,128)(2,1)}, bf16[2,48,8192]{2,1,0:T(8,128)(2,1)}, u32[]{:S(2)}, u32[]{:S(2)}) collective-permute-start(bf16[2,48,8192]{2,1,0:T(8,128)(2,1)} %dynamic-slice_bitcast_fusion), channel_id=1, source_target_pairs={{0,1},{1,0},{2,3},{3,2},{4,5},{5,4},{6,7},{7,6},{8,9},{9,8},{10,11... | collective-permute-start | bytes 4718600 | tf_op jit(solution)/shard_map/ppermute | solution.py:166
  222.2 4.9 %copy-start.11 = (f32[1,128,4,2,128]{1,4,0,3,2:T(8,128)S(1)}, f32[1,128,4,2,128]{1,4,0,3,2:T(8,128)}, u32[]{:S(2)}) copy-start(f32[1,128,4,2,128]{1,4,0,3,2:T(8,128)} %get-tuple-element.78) | copy-start | bytes 1572868
  222.2 5.9 %copy-start.10 = (f32[1,128,4,2,128]{1,4,0,3,2:T(8,128)S(1)}, f32[1,128,4,2,128]{1,4,0,3,2:T(8,128)}, u32[]{:S(2)}) copy-start(f32[1,128,4,2,128]{1,4,0,3,2:T(8,128)} %get-tuple-element.77) | copy-start | bytes 1572868
  231.4 21.5 %collective-permute-start.1 = (bf16[48,8192]{1,0:T(8,128)(2,1)S(1)}, bf16[48,8192]{1,0:T(8,128)(2,1)S(1)}, u32[]{:S(2)}, u32[]{:S(2)}) collective-permute-start(bf16[48,8192]{1,0:T(8,128)(2,1)S(1)} %fusion.56), channel_id=1, source_target_pairs={{0,2},{1,3},{2,0},{3,1},{4,6},{5,7},{6,4},{7,5},{8,10},{9,11},{10,... | collective-permute-start | bytes 2359304 | tf_op jit(solution)/shard_map/ppermute | solution.py:173
  233.8 24.8 %slice-start.12 = ((s8[8388608]{0:T(1024)(128)(4,1)}), s8[4194304]{0:T(1024)(128)(4,1)S(1)}, s32[]{:S(2)}) async-start(s8[8388608]{0:T(1024)(128)(4,1)} %bitcast.338), calls=%async_computation.18 | async-start | bytes 8388608
  240.2 12.8 %copy-start = (bf16[1,128,8192]{2,1,0:T(8,128)(2,1)S(1)}, bf16[1,128,8192]{2,1,0:T(8,128)(2,1)}, u32[]{:S(2)}) copy-start(bf16[1,128,8192]{2,1,0:T(8,128)(2,1)} %param.19) | copy-start | bytes 6291460
  240.2 18.4 %slice-start.13 = ((s8[8388608]{0:T(1024)(128)(4,1)}), s8[4194304]{0:T(1024)(128)(4,1)S(1)}, s32[]{:S(2)}) async-start(s8[8388608]{0:T(1024)(128)(4,1)} %bitcast.338), calls=%async_computation.19 | async-start | bytes 8388608
  240.3 15.7 %collective-permute-start.5 = (bf16[2,32,8192]{2,1,0:T(8,128)(2,1)S(1)}, bf16[2,32,8192]{2,1,0:T(8,128)(2,1)S(1)}, u32[]{:S(2)}, u32[]{:S(2)}) collective-permute-start(bf16[2,32,8192]{2,1,0:T(8,128)(2,1)S(1)} %dynamic-slice_bitcast_fusion.2), channel_id=1, source_target_pairs={{0,1},{1,0},{2,3},{3,2},{4,5},{5,4},{6,7},{7,6},{8,9},{9,8},{10,11... | collective-permute-start | bytes 3145736 | tf_op jit(solution)/shard_map/ppermute | solution.py:166
  254.0 22.2 %collective-permute-start.3 = (bf16[48,8192]{1,0:T(8,128)(2,1)S(1)}, bf16[48,8192]{1,0:T(8,128)(2,1)S(1)}, u32[]{:S(2)}, u32[]{:S(2)}) collective-permute-start(bf16[48,8192]{1,0:T(8,128)(2,1)S(1)} %get-tuple-element.71), channel_id=1, source_target_pairs={{96,0},{97,1},{98,2},{99,3},{100,4},{101,5},{102,6},{103,7},{104,8... | collective-permute-start | bytes 2359304 | tf_op jit(solution)/shard_map/ppermute | solution.py:186
  255.3 20.9 %collective-permute-start.2 = (bf16[48,8192]{1,0:T(8,128)(2,1)S(1)}, bf16[48,8192]{1,0:T(8,128)(2,1)S(1)}, u32[]{:S(2)}, u32[]{:S(2)}) collective-permute-start(bf16[48,8192]{1,0:T(8,128)(2,1)S(1)} %get-tuple-element.71), channel_id=1, source_target_pairs={{96,64},{64,32},{97,65},{65,33},{98,66},{66,34},{99,67},{67,35},{1... | collective-permute-start | bytes 2359304 | tf_op jit(solution)/shard_map/ppermute | solution.py:185
  256.3 15.1 %collective-permute-start.6 = (bf16[32,8192]{1,0:T(8,128)(2,1)S(1)}, bf16[32,8192]{1,0:T(8,128)(2,1)S(1)}, u32[]{:S(2)}, u32[]{:S(2)}) collective-permute-start(bf16[32,8192]{1,0:T(8,128)(2,1)S(1)} %fusion.65), channel_id=1, source_target_pairs={{0,2},{1,3},{2,0},{3,1},{4,6},{5,7},{6,4},{7,5},{8,10},{9,11},{10,... | collective-permute-start | bytes 1572872 | tf_op jit(solution)/shard_map/ppermute | solution.py:173
  261.5 18.0 %collective-permute-start.10 = (bf16[2,32,8192]{2,1,0:T(8,128)(2,1)S(1)}, bf16[2,32,8192]{2,1,0:T(8,128)(2,1)S(1)}, u32[]{:S(2)}, u32[]{:S(2)}) collective-permute-start(bf16[2,32,8192]{2,1,0:T(8,128)(2,1)S(1)} %dynamic-slice_bitcast_fusion.1), channel_id=1, source_target_pairs={{0,1},{1,0},{2,3},{3,2},{4,5},{5,4},{6,7},{7,6},{8,9},{9,8},{10,11... | collective-permute-start | bytes 3145736 | tf_op jit(solution)/shard_map/ppermute | solution.py:166
  272.2 16.1 %collective-permute-start.8 = (bf16[32,8192]{1,0:T(8,128)(2,1)S(1)}, bf16[32,8192]{1,0:T(8,128)(2,1)S(1)}, u32[]{:S(2)}, u32[]{:S(2)}) collective-permute-start(bf16[32,8192]{1,0:T(8,128)(2,1)S(1)} %get-tuple-element.69), channel_id=1, source_target_pairs={{96,0},{97,1},{98,2},{99,3},{100,4},{101,5},{102,6},{103,7},{104,8... | collective-permute-start | bytes 1572872 | tf_op jit(solution)/shard_map/ppermute | solution.py:186
  273.5 14.8 %collective-permute-start.7 = (bf16[32,8192]{1,0:T(8,128)(2,1)S(1)}, bf16[32,8192]{1,0:T(8,128)(2,1)S(1)}, u32[]{:S(2)}, u32[]{:S(2)}) collective-permute-start(bf16[32,8192]{1,0:T(8,128)(2,1)S(1)} %get-tuple-element.69), channel_id=1, source_target_pairs={{96,64},{64,32},{97,65},{65,33},{98,66},{66,34},{99,67},{67,35},{1... | collective-permute-start | bytes 1572872 | tf_op jit(solution)/shard_map/ppermute | solution.py:185
  276.5 5.7 %slice-start.11 = ((bf16[4,128,2,256]{3,1,0,2:T(8,128)(2,1)}), bf16[4,16,2,256]{3,1,0,2:T(8,128)(2,1)S(1)}, s32[]{:S(2)}) async-start(bf16[4,128,2,256]{3,1,0,2:T(8,128)(2,1)} %copy-done.12), calls=%async_computation.17 | async-start | bytes 131072 | tf_op jit(solution)/shard_map/slice | solution.py:152
  276.5 22.4 %collective-permute-start.4 = (bf16[48,8192]{1,0:T(8,128)(2,1)S(1)}, bf16[48,8192]{1,0:T(8,128)(2,1)S(1)}, u32[]{:S(2)}, u32[]{:S(2)}) collective-permute-start(bf16[48,8192]{1,0:T(8,128)(2,1)S(1)} %fusion.30), channel_id=1, source_target_pairs={{32,0},{0,32},{33,1},{1,33},{34,2},{2,34},{35,3},{3,35},{36,4},{4,... | collective-permute-start | bytes 2359304 | tf_op jit(solution)/shard_map/ppermute | solution.py:192
  279.8 14.1 %collective-permute-start.11 = (bf16[32,8192]{1,0:T(8,128)(2,1)S(1)}, bf16[32,8192]{1,0:T(8,128)(2,1)S(1)}, u32[]{:S(2)}, u32[]{:S(2)}) collective-permute-start(bf16[32,8192]{1,0:T(8,128)(2,1)S(1)} %fusion.66), channel_id=1, source_target_pairs={{0,2},{1,3},{2,0},{3,1},{4,6},{5,7},{6,4},{7,5},{8,10},{9,11},{10,... | collective-permute-start | bytes 1572872 | tf_op jit(solution)/shard_map/ppermute | solution.py:173
  284.9 9.4 %collective-permute-start.15 = (bf16[2,16,8192]{2,1,0:T(8,128)(2,1)S(1)}, bf16[2,16,8192]{2,1,0:T(8,128)(2,1)S(1)}, u32[]{:S(2)}, u32[]{:S(2)}) collective-permute-start(bf16[2,16,8192]{2,1,0:T(8,128)(2,1)S(1)} %dynamic-slice_bitcast_fusion.3), channel_id=1, source_target_pairs={{0,1},{1,0},{2,3},{3,2},{4,5},{5,4},{6,7},{7,6},{8,9},{9,8},{10,11... | collective-permute-start | bytes 1572872 | tf_op jit(solution)/shard_map/ppermute | solution.py:166
  288.6 19.4 %collective-permute-start.9 = (bf16[32,8192]{1,0:T(8,128)(2,1)S(1)}, bf16[32,8192]{1,0:T(8,128)(2,1)S(1)}, u32[]{:S(2)}, u32[]{:S(2)}) collective-permute-start(bf16[32,8192]{1,0:T(8,128)(2,1)S(1)} %fusion.43), channel_id=1, source_target_pairs={{32,0},{0,32},{33,1},{1,33},{34,2},{2,34},{35,3},{3,35},{36,4},{4,... | collective-permute-start | bytes 1572872 | tf_op jit(solution)/shard_map/ppermute | solution.py:192
  294.8 8.0 %collective-permute-start.16 = (bf16[16,8192]{1,0:T(8,128)(2,1)S(1)}, bf16[16,8192]{1,0:T(8,128)(2,1)S(1)}, u32[]{:S(2)}, u32[]{:S(2)}) collective-permute-start(bf16[16,8192]{1,0:T(8,128)(2,1)S(1)} %fusion.68), channel_id=1, source_target_pairs={{0,2},{1,3},{2,0},{3,1},{4,6},{5,7},{6,4},{7,5},{8,10},{9,11},{10,... | collective-permute-start | bytes 786440 | tf_op jit(solution)/shard_map/ppermute | solution.py:173
  299.2 20.8 %collective-permute-start.13 = (bf16[32,8192]{1,0:T(8,128)(2,1)S(1)}, bf16[32,8192]{1,0:T(8,128)(2,1)S(1)}, u32[]{:S(2)}, u32[]{:S(2)}) collective-permute-start(bf16[32,8192]{1,0:T(8,128)(2,1)S(1)} %get-tuple-element.67), channel_id=1, source_target_pairs={{96,0},{97,1},{98,2},{99,3},{100,4},{101,5},{102,6},{103,7},{104,8... | collective-permute-start | bytes 1572872 | tf_op jit(solution)/shard_map/ppermute | solution.py:186
  300.5 19.5 %collective-permute-start.12 = (bf16[32,8192]{1,0:T(8,128)(2,1)S(1)}, bf16[32,8192]{1,0:T(8,128)(2,1)S(1)}, u32[]{:S(2)}, u32[]{:S(2)}) collective-permute-start(bf16[32,8192]{1,0:T(8,128)(2,1)S(1)} %get-tuple-element.67), channel_id=1, source_target_pairs={{96,64},{64,32},{97,65},{65,33},{98,66},{66,34},{99,67},{67,35},{1... | collective-permute-start | bytes 1572872 | tf_op jit(solution)/shard_map/ppermute | solution.py:185
  303.2 14.3 %collective-permute-start.18 = (bf16[16,8192]{1,0:T(8,128)(2,1)S(1)}, bf16[16,8192]{1,0:T(8,128)(2,1)S(1)}, u32[]{:S(2)}, u32[]{:S(2)}) collective-permute-start(bf16[16,8192]{1,0:T(8,128)(2,1)S(1)} %get-tuple-element.65), channel_id=1, source_target_pairs={{96,0},{97,1},{98,2},{99,3},{100,4},{101,5},{102,6},{103,7},{104,8... | collective-permute-start | bytes 786440 | tf_op jit(solution)/shard_map/ppermute | solution.py:186
  304.5 13.0 %collective-permute-start.17 = (bf16[16,8192]{1,0:T(8,128)(2,1)S(1)}, bf16[16,8192]{1,0:T(8,128)(2,1)S(1)}, u32[]{:S(2)}, u32[]{:S(2)}) collective-permute-start(bf16[16,8192]{1,0:T(8,128)(2,1)S(1)} %get-tuple-element.65), channel_id=1, source_target_pairs={{96,64},{64,32},{97,65},{65,33},{98,66},{66,34},{99,67},{67,35},{1... | collective-permute-start | bytes 786440 | tf_op jit(solution)/shard_map/ppermute | solution.py:185
  317.6 10.6 %collective-permute-start.19 = (bf16[16,8192]{1,0:T(8,128)(2,1)S(1)}, bf16[16,8192]{1,0:T(8,128)(2,1)S(1)}, u32[]{:S(2)}, u32[]{:S(2)}) collective-permute-start(bf16[16,8192]{1,0:T(8,128)(2,1)S(1)} %fusion.60), channel_id=1, source_target_pairs={{32,0},{0,32},{33,1},{1,33},{34,2},{2,34},{35,3},{3,35},{36,4},{4,... | collective-permute-start | bytes 786440 | tf_op jit(solution)/shard_map/ppermute | solution.py:192
  320.3 13.6 %collective-permute-start.14 = (bf16[32,8192]{1,0:T(8,128)(2,1)S(1)}, bf16[32,8192]{1,0:T(8,128)(2,1)S(1)}, u32[]{:S(2)}, u32[]{:S(2)}) collective-permute-start(bf16[32,8192]{1,0:T(8,128)(2,1)S(1)} %fusion.45), channel_id=1, source_target_pairs={{32,0},{0,32},{33,1},{1,33},{34,2},{2,34},{35,3},{3,35},{36,4},{4,... | collective-permute-start | bytes 1572872 | tf_op jit(solution)/shard_map/ppermute | solution.py:192
  (11 other events, 20.8 us)
Sparse Core Ops, SparseCore 0:
  63.0 50.3 all-gather.1

commit v5 on v3

--- a/solution.py
+++ b/solution.py
@@ -81,19 +81,22 @@
         own_values = suffix_values[0]
         pk = prefix_keys[0].reshape(rows_local, n_ten, kv_local, 1, HEAD_SIZE)
         pv = prefix_values[0].reshape(rows_local, n_ten, kv_local, 1, HEAD_SIZE)
-        send = jnp.concatenate([pk, pv], axis=3).reshape(rows_local, n_ten, -1).transpose(1, 0, 2)
-        got_all = lax.all_to_all(send, "tensor", 0, 0, tiled=True)
-        got_all = got_all.reshape(block_rows, kv_local, 2 * HEAD_SIZE)
+        send = jnp.concatenate([pk, pv], axis=3).reshape(rows_local, n_ten, kv_local, -1)
+        send = send.transpose(2, 1, 0, 3)
+        spread = jnp.broadcast_to(send[0][None], (n_smp,) + send[0].shape)
+        spread = spread.reshape((n_smp * n_ten,) + send[0].shape[1:])
+        first_pool = lax.all_to_all(spread, ("sample", "tensor"), 0, 0, tiled=True)
+        first_pool = first_pool.reshape(pooled_rows, 2 * HEAD_SIZE)
+        got_rest = lax.all_to_all(send[1:], "tensor", 1, 1, tiled=True)
 
         query_pieces, suffix_key_pieces, suffix_value_pieces, reduced_pieces = [], [], [], []
         for head_index in range(kv_local):
             low_col = head_index * HEAD_SIZE
-            got = got_all[:, head_index]
-            if head_index % 2 == 0:
-                spread = jnp.broadcast_to(got[None], (n_smp,) + got.shape)
-                pool = lax.all_to_all(spread, "sample", 0, 0, tiled=True).reshape(pooled_rows, -1)
+            if head_index == 0:
+                pool = first_pool
             else:
-                got, _ = lax.optimization_barrier((got, pool))
+                got = got_rest[head_index - 1].reshape(block_rows, 2 * HEAD_SIZE)
+                got, _ = lax.optimization_barrier((got, first_pool))
                 pool = lax.all_gather(got, "sample", axis=0, tiled=True)
             key_rows = jnp.concatenate(
                 [pool[:, :HEAD_SIZE], own_keys[:, low_col : low_col + HEAD_SIZE]], axis=0

time: 350 us -> 355 us (1.014)
  the two profiles are of different devices: /device:TPU:0 before, /device:TPU:24 now
where the time goes in v5:
time: 355 us; the launch traced here: 348 us
  waiting for transfers between devices  98.1 us (28%)
  matrix products  77.2 us (22%)
  starting transfers between devices  65.9 us (19%)
  other arithmetic  56.2 us (16%)
  local copies, waits for them, and re-layouts  34.8 us (10%)
  between operations  15.5 us (4%)
    ppermute x4, waiting for transfers between devices, on_device(): last = lax.ppermute(carry.astype(jnp.bfloat16), 'section', [(1, 0), (0, 1)])  26.4 us
    dot_general x4, matrix products, on_device(): lax.dot_general(grad_rows_c, weight_local, (((2, 3), (1, 2)), ((), ())),...  21.8 us
    all_to_all x1, waiting for transfers between devices, on_device(): first_pool = lax.all_to_all(spread, ('sample', 'tensor'), 0, 0, tiled=True)  21.8 us
    sub x2, other arithmetic, attend_group(): exponent = jnp.exp(scores - row_max)  20.6 us
    ppermute x4, waiting for transfers between devices, on_device(): wrap = lax.ppermute(term_low, 'section', [(3, 0)])  18.9 us
    all_to_all x2, waiting for transfers between devices, on_device(): parts = lax.all_to_all(pool_grad, 'sample', 0, 0, tiled=False)  17.5 us
    convert_element_type x2, other arithmetic, attend_group(): weights_low = softmax_w.astype(jnp.bfloat16)  17.1 us
    dot_general x2, matrix products, attend_group(): jnp.einsum('rgd,kd->rgk', grad_grp, value_rows, preferred_element_type=jn...  13.7 us
  transfers between devices with their start and end apart: 26, of which 12 were waited for; matrix products, arithmetic and copies ran while one was open for 42% of the time, Pallas kernels for 0%

profile of v5, /device:TPU:24, one launch (start us, length us, event | category | flops | bytes accessed | tf_op | source)
XLA Modules:
  0.0 347.7 jit_solution(10932183672329989995)
XLA Ops:
  7.2 1.1 reshape_squeeze.15
  8.7 1.1 reshape_squeeze.16
  10.2 1.2 pad_maximum_fusion.2
  12.5 1.6 broadcast_in_dim.91
  14.1 8.5 %all-to-all-start = ((bf16[32,128,256]{2,1,0:T(8,128)(2,1)}), bf16[32,128,256]{2,1,0:T(8,128)(2,1)}, u32[]{:S(2)}, u32[]{:S(2)}) async-start(bf16[32,128,256]{2,1,0:T(8,128)(2,1)} %bitcast.5), calls=%async_computation | async-start | bytes 4194304 | tf_op jit(solution)/shard_map/all_to_all | solution.py:88
  26.4 21.8 %all-to-all-done = bf16[32,128,256]{2,1,0:T(8,128)(2,1)} async-done(((bf16[32,128,256]{2,1,0:T(8,128)(2,1)}), bf16[32,128,256]{2,1,0:T(8,128)(2,1)}, u32[]{:S(2)}, u32[]{:S(2)}) %all-to-all-start) | async-done | bytes 2097184 | tf_op jit(solution)/shard_map/all_to_all | solution.py:88
  48.1 6.0 %all-to-all-start.1 = ((bf16[1,4,128,256]{3,2,0,1:T(8,128)(2,1)}), bf16[1,4,128,256]{3,2,0,1:T(8,128)(2,1)S(1)}, u32[]{:S(2)}, u32[]{:S(2)}) async-start(bf16[1,4,128,256]{3,2,0,1:T(8,128)(2,1)} %get-tuple-element.89), calls=%async_computation.1 | async-start | bytes 524288 | tf_op jit(solution)/shard_map/all_to_all | solution.py:90
  54.2 2.6 fusion.101
  56.8 1.7 all-to-all-done.1
  59.3 3.3 fusion.64
  62.6 10.4 %fusion.109 = (f32[128,8]{0,1:T(8,128)S(1)}, f32[128,8,4224]{0,2,1:T(8,128)}) fusion(f32[4224,128,8]{1,0,2:T(8,128)S(1)} %fusion.64, pred[128,4224]{0,1:T(8,128)(4,1)S(1)} %pad_add_fusion), kind=kOutput, calls=%fused_computation.207 | output fusion | flops 17305728 | bytes 35147776 | tf_op jit(solution)/shard_map/sub | solution.py:36
  73.0 6.8 %fusion.18 = bf16[128,8,4224]{0,2,1:T(8,128)(2,1)S(1)} fusion(f32[128,8,4224]{0,2,1:T(8,128)} %get-tuple-element.105, f32[128,8]{0,1:T(8,128)S(1)} %get-tuple-element.104), kind=kLoop, calls=%fused_computation.30 | loop fusion | flops 8650752 | bytes 25956352 | tf_op jit(solution)/shard_map/convert_element_type | solution.py:38
  79.9 2.4 fusion.26
  83.4 1.1 slice.150
  84.5 2.5 fusion.31
  87.2 7.4 %fusion.3 = bf16[128,8,4224]{0,2,1:T(8,128)(2,1)} fusion(f32[128,8]{0,1:T(8,128)S(1)} %fusion.31, f32[128,8,4224]{0,2,1:T(8,128)S(1)} %bitcast.281, f32[128,8]{0,1:T(8,128)S(1)} %get-tuple-element.104, bf16[128,128]{1,0:T(8,128)(2,1)S(1)} %get-tuple-element.90, bf16[4096,128]{1,0:T(8,128)(2,1)} %get-tuple-element.77, bf16[128,2,8,128]{0,3,2,1:T(8,128)(2,1)} %bitcast.312), kind=kOutput, calls=%fused_computation.6 | convolution fusion | flops 1126760448 | bytes 27303936 | tf_op jit(solution)/shard_map/rgd,kd->rgk/dot_general | solution.py:43
  94.7 5.9 %fusion.25 = bf16[4224,128]{1,0:T(8,128)(2,1)S(1)} fusion(bf16[128,8,4224]{0,2,1:T(8,128)(2,1)} %fusion.3, bf16[128,2,8,128]{0,3,2,1:T(8,128)(2,1)} %bitcast.300), kind=kOutput, calls=%fused_computation.41 | convolution fusion | flops 1108377600 | bytes 9994240 | tf_op jit(solution)/shard_map/rgk,rgd->kd/dot_general | solution.py:48
  101.6 1.2 copy-done.3
  102.8 1.5 pad_maximum_fusion
  104.3 5.0 %all-to-all-start.2 = ((bf16[8,512,256]{2,1,0:T(8,128)(2,1)}), bf16[8,512,256]{2,1,0:T(8,128)(2,1)}, u32[]{:S(2)}, u32[]{:S(2)}) async-start(bf16[8,512,256]{2,1,0:T(8,128)(2,1)} %pad_maximum_fusion), calls=%async_computation.2 | async-start | bytes 4194304 | tf_op jit(solution)/shard_map/all_to_all | solution.py:121
  109.7 2.7 fusion.102
  113.4 2.4 fusion.63
  115.8 10.2 %fusion.108 = (f32[128,8]{0,1:T(8,128)S(1)}, f32[128,8,4224]{0,2,1:T(8,128)}) fusion(f32[4224,128,8]{1,0,2:T(8,128)S(1)} %fusion.63, pred[128,4224]{0,1:T(8,128)(4,1)S(1)} %pad_add_fusion), kind=kOutput, calls=%fused_computation.206 | output fusion | flops 17305728 | bytes 35147776 | tf_op jit(solution)/shard_map/sub | solution.py:36
  126.0 10.2 %fusion.19 = bf16[128,8,4224]{0,2,1:T(8,128)(2,1)} fusion(f32[128,8,4224]{0,2,1:T(8,128)} %get-tuple-element.103, f32[128,8]{0,1:T(8,128)S(1)} %get-tuple-element.102), kind=kLoop, calls=%fused_computation.31 | loop fusion | flops 8650752 | bytes 25956352 | tf_op jit(solution)/shard_map/convert_element_type | solution.py:38
  136.3 6.8 %fusion.32 = f32[128,8]{0,1:T(8,128)S(1)} fusion(bf16[128,8,4224]{0,2,1:T(8,128)(2,1)} %fusion.19, bf16[128,128]{1,0:T(8,128)(2,1)S(1)} %get-tuple-element.91, bf16[4096,128]{1,0:T(8,128)(2,1)S(1)} %copy-done.17, bf16[128,1,8,128]{3,0,2,1:T(8,128)(2,1)S(1)} %copy-done.20), kind=kOutput, calls=%fused_computation.88 | convolution fusion | flops 1109851136 | bytes 9998336 | tf_op jit(solution)/shard_map/rgk,kd->rgd/dot_general | solution.py:39
  143.2 6.3 %fusion.2 = bf16[128,8,4224]{0,2,1:T(8,128)(2,1)} fusion(f32[128,8]{0,1:T(8,128)S(1)} %fusion.32, f32[128,8,4224]{0,2,1:T(8,128)S(1)} %bitcast.283, f32[128,8]{0,1:T(8,128)S(1)} %get-tuple-element.102, bf16[128,128]{1,0:T(8,128)(2,1)S(1)} %get-tuple-element.91, bf16[4096,128]{1,0:T(8,128)(2,1)} %get-tuple-element.79, bf16[128,2,8,128]{0,3,2,1:T(8,128)(2,1)S(1)} %bitcast.314), kind=kOutput, calls=%fused_computation.3 | convolution fusion | flops 1126760448 | bytes 27303936 | tf_op jit(solution)/shard_map/rgd,kd->rgk/dot_general | solution.py:43
  149.5 6.0 %fusion.28 = bf16[4224,128]{1,0:T(8,128)(2,1)S(1)} fusion(bf16[128,8,4224]{0,2,1:T(8,128)(2,1)} %fusion.19, bf16[128,2,8,128]{0,3,2,1:T(8,128)(2,1)S(1)} %bitcast.315), kind=kOutput, calls=%fused_computation.44 | convolution fusion | flops 1107836928 | bytes 9994240 | tf_op jit(solution)/shard_map/rgk,rgd->kd/dot_general | solution.py:51
  156.6 2.5 fusion.27
  160.1 1.5 pad_maximum_fusion.1
  161.6 5.9 %all-to-all-start.3 = ((bf16[8,512,256]{2,1,0:T(8,128)(2,1)}), bf16[8,512,256]{2,1,0:T(8,128)(2,1)S(1)}, u32[]{:S(2)}, u32[]{:S(2)}) async-start(bf16[8,512,256]{2,1,0:T(8,128)(2,1)} %pad_maximum_fusion.1), calls=%async_computation.3 | async-start | bytes 4194304 | tf_op jit(solution)/shard_map/all_to_all | solution.py:121
  168.4 4.9 %fusion.34 = bf16[128,1,8,128]{0,3,2,1:T(8,128)(2,1)S(1)} fusion(bf16[128,8,4224]{0,2,1:T(8,128)(2,1)} %fusion.3, bf16[128,128]{1,0:T(8,128)(2,1)S(1)} %get-tuple-element.92, bf16[4096,128]{1,0:T(8,128)(2,1)S(1)} %get-tuple-element.78), kind=kOutput, calls=%fused_computation.90 | convolution fusion | flops 1109721088 | bytes 9994240 | tf_op jit(solution)/shard_map/rgk,kd->rgd/dot_general | solution.py:118
  173.2 2.0 reduce
  175.4 17.5 %all-to-all-done.3 = bf16[8,512,256]{2,1,0:T(8,128)(2,1)S(1)} async-done(((bf16[8,512,256]{2,1,0:T(8,128)(2,1)}), bf16[8,512,256]{2,1,0:T(8,128)(2,1)S(1)}, u32[]{:S(2)}, u32[]{:S(2)}) %all-to-all-start.3) | async-done | bytes 2097184 | tf_op jit(solution)/shard_map/all_to_all | solution.py:121
  194.2 7.2 %all-to-all-start.4 = ((bf16[4,128,512]{2,1,0:T(8,128)(2,1)}), bf16[4,128,512]{2,1,0:T(8,128)(2,1)}, u32[]{:S(2)}, u32[]{:S(2)}) async-start(bf16[4,128,512]{2,1,0:T(8,128)(2,1)} %pad_maximum_fusion.4), calls=%async_computation.4 | async-start | bytes 1048576 | tf_op jit(solution)/shard_map/all_to_all | solution.py:129
  202.3 6.4 %fusion.9 = bf16[4,32,8192]{2,1,0:T(8,128)(2,1)S(1)} fusion(bf16[8192,2,256]{2,1,0:T(2,128)(2,1)} %bitcast.330, bf16[4,128,2,256]{3,1,0,2:T(8,128)(2,1)S(1)} %reshape.273), kind=kOutput, calls=%fused_computation.19 | convolution fusion | flops 1074790400 | bytes 10616832 | tf_op jit(solution)/shard_map/dot_general | solution.py:156
  208.7 1.2 copy.155
  211.0 1.0 dynamic-slice_bitcast_fusion.3
  212.3 4.9 %fusion.33 = bf16[128,1,8,128]{0,3,2,1:T(8,128)(2,1)S(1)} fusion(bf16[128,8,4224]{0,2,1:T(8,128)(2,1)} %fusion.2, bf16[128,128]{1,0:T(8,128)(2,1)S(1)} %get-tuple-element.93, bf16[4096,128]{1,0:T(8,128)(2,1)S(1)} %copy-done.2), kind=kOutput, calls=%fused_computation.89 | convolution fusion | flops 1109721088 | bytes 9994240 | tf_op jit(solution)/shard_map/rgk,kd->rgd/dot_general | solution.py:118
  221.1 1.1 fusion.104
  222.2 2.0 copy.161
  225.2 1.4 convert_add_fusion.3
  226.7 3.2 collective-permute-start.1
  229.9 6.4 %fusion.6 = bf16[4,32,8192]{2,1,0:T(8,128)(2,1)S(1)} fusion(bf16[4,32,2,256]{3,1,0,2:T(8,128)(2,1)S(1)} %get-tuple-element.28, bf16[8192,2,256,1]{2,1,0,3:T(2,128)(2,1)} %bitcast.331), kind=kOutput, calls=%fused_computation.16 | convolution fusion | flops 1074790400 | bytes 10616832 | tf_op jit(solution)/shard_map/dot_general | solution.py:156
  236.7 5.9 %collective-permute-done.1 = bf16[32,8192]{1,0:T(8,128)(2,1)S(1)} collective-permute-done((bf16[32,8192]{1,0:T(8,128)(2,1)S(1)}, bf16[32,8192]{1,0:T(8,128)(2,1)S(1)}, u32[]{:S(2)}, u32[]{:S(2)}) %collective-permute-start.1) | collective-permute-done | bytes 524320 | tf_op jit(solution)/shard_map/ppermute | solution.py:174
  243.6 1.3 collective-permute-start.3
  246.0 3.2 collective-permute-start.6
  249.2 2.8 fusion.7
  252.2 7.9 %collective-permute-done.3 = bf16[32,8192]{1,0:T(8,128)(2,1)S(1)} collective-permute-done((bf16[32,8192]{1,0:T(8,128)(2,1)S(1)}, bf16[32,8192]{1,0:T(8,128)(2,1)S(1)}, u32[]{:S(2)}, u32[]{:S(2)}) %collective-permute-start.3) | collective-permute-done | bytes 524320 | tf_op jit(solution)/shard_map/ppermute | solution.py:187
  260.3 2.9 collective-permute-start.4
  263.9 1.3 collective-permute-start.8
  265.9 8.9 %collective-permute-done.4 = bf16[32,8192]{1,0:T(8,128)(2,1)S(1)} collective-permute-done((bf16[32,8192]{1,0:T(8,128)(2,1)S(1)}, bf16[32,8192]{1,0:T(8,128)(2,1)S(1)}, u32[]{:S(2)}, u32[]{:S(2)}) %collective-permute-start.4) | collective-permute-done | bytes 524320 | tf_op jit(solution)/shard_map/ppermute | solution.py:193
  275.3 3.6 %collective-permute-start.11 = (bf16[32,8192]{1,0:T(8,128)(2,1)S(1)}, bf16[32,8192]{1,0:T(8,128)(2,1)S(1)}, u32[]{:S(2)}, u32[]{:S(2)}) collective-permute-start(bf16[32,8192]{1,0:T(8,128)(2,1)S(1)} %fusion.67), channel_id=1, source_target_pairs={{0,2},{1,3},{2,0},{3,1},{4,6},{5,7},{6,4},{7,5},{8,10},{9,11},{10,... | collective-permute-start | bytes 1572872 | tf_op jit(solution)/shard_map/ppermute | solution.py:174
  278.9 6.2 %fusion.8 = bf16[4,32,8192]{2,1,0:T(8,128)(2,1)S(1)} fusion(bf16[4,32,2,256]{3,1,0,2:T(8,128)(2,1)S(1)} %get-tuple-element.32, bf16[8192,2,256,1]{2,1,0,3:T(2,128)(2,1)} %bitcast.332), kind=kOutput, calls=%fused_computation.18 | convolution fusion | flops 1074790400 | bytes 10616832 | tf_op jit(solution)/shard_map/dot_general | solution.py:156
  285.5 2.9 collective-permute-start.9
  289.5 1.3 collective-permute-start.13
  291.8 3.3 collective-permute-start.16
  295.1 6.5 %collective-permute-done.9 = bf16[32,8192]{1,0:T(8,128)(2,1)S(1)} collective-permute-done((bf16[32,8192]{1,0:T(8,128)(2,1)S(1)}, bf16[32,8192]{1,0:T(8,128)(2,1)S(1)}, u32[]{:S(2)}, u32[]{:S(2)}) %collective-permute-start.9) | collective-permute-done | bytes 524320 | tf_op jit(solution)/shard_map/ppermute | solution.py:193
  301.9 5.1 %collective-permute-done.16 = bf16[32,8192]{1,0:T(8,128)(2,1)S(1)} collective-permute-done((bf16[32,8192]{1,0:T(8,128)(2,1)S(1)}, bf16[32,8192]{1,0:T(8,128)(2,1)S(1)}, u32[]{:S(2)}, u32[]{:S(2)}) %collective-permute-start.16) | collective-permute-done | bytes 524320 | tf_op jit(solution)/shard_map/ppermute | solution.py:174
  307.6 1.3 collective-permute-start.18
  309.9 3.0 collective-permute-start.14
  312.9 10.9 %collective-permute-done.18 = bf16[32,8192]{1,0:T(8,128)(2,1)S(1)} collective-permute-done((bf16[32,8192]{1,0:T(8,128)(2,1)S(1)}, bf16[32,8192]{1,0:T(8,128)(2,1)S(1)}, u32[]{:S(2)}, u32[]{:S(2)}) %collective-permute-start.18) | collective-permute-done | bytes 524320 | tf_op jit(solution)/shard_map/ppermute | solution.py:187
  324.0 2.5 collective-permute-start.19
  326.8 10.9 %collective-permute-done.19 = bf16[32,8192]{1,0:T(8,128)(2,1)S(1)} collective-permute-done((bf16[32,8192]{1,0:T(8,128)(2,1)S(1)}, bf16[32,8192]{1,0:T(8,128)(2,1)S(1)}, u32[]{:S(2)}, u32[]{:S(2)}) %collective-permute-start.19) | collective-permute-done | bytes 524320 | tf_op jit(solution)/shard_map/ppermute | solution.py:193
  338.0 2.4 maximum_bitcast_fusion
  (181 shorter events, 31.0 us)
Async XLA Ops:
  14.1 8.5 %copy-start.18 = (bf16[1,128,2048]{2,1,0:T(8,128)(2,1)S(1)}, bf16[1,128,2048]{2,1,0:T(8,128)(2,1)}, u32[]{:S(2)}) copy-start(bf16[1,128,2048]{2,1,0:T(8,128)(2,1)} %param.12) | copy-start | bytes 1572868
  14.1 9.6 %copy-start.19 = (bf16[1,128,2048]{2,1,0:T(8,128)(2,1)S(1)}, bf16[1,128,2048]{2,1,0:T(8,128)(2,1)}, u32[]{:S(2)}) copy-start(bf16[1,128,2048]{2,1,0:T(8,128)(2,1)} %param.15) | copy-start | bytes 1572868
  14.1 34.0 %all-to-all-start = ((bf16[32,128,256]{2,1,0:T(8,128)(2,1)}), bf16[32,128,256]{2,1,0:T(8,128)(2,1)}, u32[]{:S(2)}, u32[]{:S(2)}) async-start(bf16[32,128,256]{2,1,0:T(8,128)(2,1)} %bitcast.5), calls=%async_computation | async-start | bytes 4194304 | tf_op jit(solution)/shard_map/all_to_all | solution.py:88
  22.6 3.1 copy-start.25
  22.6 3.1 copy-start.27
  22.6 3.2 copy-start.26
  22.6 3.5 copy-start.22
  22.7 3.5 %copy-start.23 = (bf16[1,128,256]{2,1,0:T(8,128)(2,1)S(1)}, bf16[1,128,256]{2,1,0:T(8,128)(2,1)}, u32[]{:S(2)}) copy-start(bf16[1,128,256]{2,1,0:T(8,128)(2,1)} %param.14) | copy-start | bytes 196612
  23.9 24.2 %copy-start.6 = (bf16[1,128,2048]{1,2,0:T(8,128)(2,1)}, bf16[1,128,2048]{1,2,0:T(8,128)(2,1)S(1)}, u32[]{:S(2)}) copy-start(bf16[1,128,2048]{1,2,0:T(8,128)(2,1)S(1)} %copy.141) | copy-start | bytes 1572868
  48.1 10.4 %all-to-all-start.1 = ((bf16[1,4,128,256]{3,2,0,1:T(8,128)(2,1)}), bf16[1,4,128,256]{3,2,0,1:T(8,128)(2,1)S(1)}, u32[]{:S(2)}, u32[]{:S(2)}) async-start(bf16[1,4,128,256]{3,2,0,1:T(8,128)(2,1)} %get-tuple-element.89), calls=%async_computation.1 | async-start | bytes 524288 | tf_op jit(solution)/shard_map/all_to_all | solution.py:90
  54.2 55.5 %all-gather.2.cloned.1.call-start = ((), (), s32[]{:S(2)}) async-start(), calls=%async_computation.5 | async-start | bytes 2359296 | tf_op jit(solution)/shard_map/all_gather | solution.py:100
  73.0 6.8 %copy-start.7 = (bf16[1,128,2048]{1,2,0:T(8,128)(2,1)S(1)}, bf16[1,128,2048]{1,2,0:T(8,128)(2,1)}, u32[]{:S(2)}) copy-start(bf16[1,128,2048]{1,2,0:T(8,128)(2,1)} %copy-done.6) | copy-start | bytes 1572868
  79.9 4.6 %copy-start.16 = (bf16[4096,128]{1,0:T(8,128)(2,1)S(1)}, bf16[4096,128]{1,0:T(8,128)(2,1)}, u32[]{:S(2)}) copy-start(bf16[4096,128]{1,0:T(8,128)(2,1)} %get-tuple-element.77) | copy-start | bytes 3145732
  79.9 4.6 %copy-start.21 = (bf16[128,1,8,128]{3,0,2,1:T(8,128)(2,1)S(1)}, bf16[128,1,8,128]{3,0,2,1:T(8,128)(2,1)}, u32[]{:S(2)}) copy-start(bf16[128,1,8,128]{3,0,2,1:T(8,128)(2,1)} %copy.196) | copy-start | bytes 786436
  79.9 7.1 %slice-start = ((s8[17301504]{0:T(1024)(128)(4,1)}), s8[4194304]{0:T(1024)(128)(4,1)S(1)}, s32[]{:S(2)}) async-start(s8[17301504]{0:T(1024)(128)(4,1)} %bitcast.280), calls=%async_computation.6 | async-start | bytes 8388608
  79.9 7.1 %slice-start.1 = ((s8[17301504]{0:T(1024)(128)(4,1)}), s8[4194304]{0:T(1024)(128)(4,1)S(1)}, s32[]{:S(2)}) async-start(s8[17301504]{0:T(1024)(128)(4,1)} %bitcast.280), calls=%async_computation.7 | async-start | bytes 8388608
  79.9 7.1 %slice-start.2 = ((s8[17301504]{0:T(1024)(128)(4,1)}), s8[4194304]{0:T(1024)(128)(4,1)S(1)}, s32[]{:S(2)}) async-start(s8[17301504]{0:T(1024)(128)(4,1)} %bitcast.280), calls=%async_computation.8 | async-start | bytes 8388608
  82.4 1.0 copy-start.11
  84.5 2.7 slice-start.3
  84.5 2.7 slice-start.4
  101.5 1.2 copy-start.3
  104.3 57.4 %all-to-all-start.2 = ((bf16[8,512,256]{2,1,0:T(8,128)(2,1)}), bf16[8,512,256]{2,1,0:T(8,128)(2,1)}, u32[]{:S(2)}, u32[]{:S(2)}) async-start(bf16[8,512,256]{2,1,0:T(8,128)(2,1)} %pad_maximum_fusion), calls=%async_computation.2 | async-start | bytes 4194304 | tf_op jit(solution)/shard_map/all_to_all | solution.py:121
  109.7 3.7 %copy-start.4 = (bf16[1,128,2048]{1,2,0:T(8,128)(2,1)S(1)}, bf16[1,128,2048]{1,2,0:T(8,128)(2,1)}, u32[]{:S(2)}) copy-start(bf16[1,128,2048]{1,2,0:T(8,128)(2,1)} %copy.139) | copy-start | bytes 1572868
  112.4 1.0 copy-start.1
  126.0 10.3 %copy-start.17 = (bf16[4096,128]{1,0:T(8,128)(2,1)S(1)}, bf16[4096,128]{1,0:T(8,128)(2,1)}, u32[]{:S(2)}) copy-start(bf16[4096,128]{1,0:T(8,128)(2,1)} %get-tuple-element.79) | copy-start | bytes 3145732
  126.0 10.3 %copy-start.20 = (bf16[128,1,8,128]{3,0,2,1:T(8,128)(2,1)S(1)}, bf16[128,1,8,128]{3,0,2,1:T(8,128)(2,1)}, u32[]{:S(2)}) copy-start(bf16[128,1,8,128]{3,0,2,1:T(8,128)(2,1)} %copy.198) | copy-start | bytes 786436
  126.0 17.1 %slice-start.5 = ((s8[17301504]{0:T(1024)(128)(4,1)}), s8[4194304]{0:T(1024)(128)(4,1)S(1)}, s32[]{:S(2)}) async-start(s8[17301504]{0:T(1024)(128)(4,1)} %bitcast.282), calls=%async_computation.11 | async-start | bytes 8388608
  126.0 17.1 %slice-start.6 = ((s8[17301504]{0:T(1024)(128)(4,1)}), s8[4194304]{0:T(1024)(128)(4,1)S(1)}, s32[]{:S(2)}) async-start(s8[17301504]{0:T(1024)(128)(4,1)} %bitcast.282), calls=%async_computation.12 | async-start | bytes 8388608
  126.0 17.1 %slice-start.7 = ((s8[17301504]{0:T(1024)(128)(4,1)}), s8[4194304]{0:T(1024)(128)(4,1)S(1)}, s32[]{:S(2)}) async-start(s8[17301504]{0:T(1024)(128)(4,1)} %bitcast.282), calls=%async_computation.13 | async-start | bytes 8388608
  126.0 17.1 %slice-start.8 = ((s8[17301504]{0:T(1024)(128)(4,1)}), s8[4194304]{0:T(1024)(128)(4,1)S(1)}, s32[]{:S(2)}) async-start(s8[17301504]{0:T(1024)(128)(4,1)} %bitcast.282), calls=%async_computation.14 | async-start | bytes 8388608
  136.2 6.9 %slice-start.9 = ((s8[17301504]{0:T(1024)(128)(4,1)}), s8[524288]{0:T(1024)(128)(4,1)S(1)}, s32[]{:S(2)}) async-start(s8[17301504]{0:T(1024)(128)(4,1)} %bitcast.282), calls=%async_computation.15 | async-start | bytes 1048576
  136.2 6.9 %copy-start.8 = (bf16[1,128,2048]{1,2,0:T(8,128)(2,1)S(1)}, bf16[1,128,2048]{1,2,0:T(8,128)(2,1)}, u32[]{:S(2)}) copy-start(bf16[1,128,2048]{1,2,0:T(8,128)(2,1)} %copy-done.6) | copy-start | bytes 1572868
  149.5 7.1 %copy-start.5 = (bf16[1,128,2048]{1,2,0:T(8,128)(2,1)S(1)}, bf16[1,128,2048]{1,2,0:T(8,128)(2,1)}, u32[]{:S(2)}) copy-start(bf16[1,128,2048]{1,2,0:T(8,128)(2,1)} %copy.139) | copy-start | bytes 1572868
  149.5 7.1 %copy-start.28 = (bf16[128,8,4224]{0,2,1:T(8,128)(2,1)S(1)}, bf16[128,8,4224]{0,2,1:T(8,128)(2,1)}, u32[]{:S(2)}) copy-start(bf16[128,8,4224]{0,2,1:T(8,128)(2,1)} %fusion.2) | copy-start | bytes 25952260
  155.5 1.0 copy-start.13
  161.6 5.9 %copy-start.24 = (bf16[1,8192]{1,0:T(2,128)(2,1)S(1)}, bf16[1,8192]{1,0:T(2,128)(2,1)}, u32[]{:S(2)}) copy-start(bf16[1,8192]{1,0:T(2,128)(2,1)} %param.20) | copy-start | bytes 49156
  161.6 31.2 %all-to-all-start.3 = ((bf16[8,512,256]{2,1,0:T(8,128)(2,1)}), bf16[8,512,256]{2,1,0:T(8,128)(2,1)S(1)}, u32[]{:S(2)}, u32[]{:S(2)}) async-start(bf16[8,512,256]{2,1,0:T(8,128)(2,1)} %pad_maximum_fusion.1), calls=%async_computation.3 | async-start | bytes 4194304 | tf_op jit(solution)/shard_map/all_to_all | solution.py:121
  194.2 14.5 %all-to-all-start.4 = ((bf16[4,128,512]{2,1,0:T(8,128)(2,1)}), bf16[4,128,512]{2,1,0:T(8,128)(2,1)}, u32[]{:S(2)}, u32[]{:S(2)}) async-start(bf16[4,128,512]{2,1,0:T(8,128)(2,1)} %pad_maximum_fusion.4), calls=%async_computation.4 | async-start | bytes 1048576 | tf_op jit(solution)/shard_map/all_to_all | solution.py:129
  202.3 6.4 %copy-start.10 = (bf16[4,128,2,256]{3,1,0,2:T(8,128)(2,1)}, bf16[4,128,2,256]{3,1,0,2:T(8,128)(2,1)S(1)}, u32[]{:S(2)}) copy-start(bf16[4,128,2,256]{3,1,0,2:T(8,128)(2,1)S(1)} %reshape.273) | copy-start | bytes 1572868
  210.0 2.4 copy-start.2
  212.1 13.2 %collective-permute-start = (bf16[2,32,8192]{2,1,0:T(8,128)(2,1)}, bf16[2,32,8192]{2,1,0:T(8,128)(2,1)}, u32[]{:S(2)}, u32[]{:S(2)}) collective-permute-start(bf16[2,32,8192]{2,1,0:T(8,128)(2,1)} %dynamic-slice_bitcast_fusion.3), channel_id=1, source_target_pairs={{0,1},{1,0},{2,3},{3,2},{4,5},{5,4},{6,7},{7,6},{8,9},{9,8},{10,11... | collective-permute-start | bytes 3145736 | tf_op jit(solution)/shard_map/ppermute | solution.py:167
  217.2 7.0 %copy-start.9 = (f32[1,128,4,2,128]{1,4,0,3,2:T(8,128)S(1)}, f32[1,128,4,2,128]{1,4,0,3,2:T(8,128)}, u32[]{:S(2)}) copy-start(f32[1,128,4,2,128]{1,4,0,3,2:T(8,128)} %get-tuple-element.81) | copy-start | bytes 1572868
  226.7 15.8 %collective-permute-start.1 = (bf16[32,8192]{1,0:T(8,128)(2,1)S(1)}, bf16[32,8192]{1,0:T(8,128)(2,1)S(1)}, u32[]{:S(2)}, u32[]{:S(2)}) collective-permute-start(bf16[32,8192]{1,0:T(8,128)(2,1)S(1)} %fusion.65), channel_id=1, source_target_pairs={{0,2},{1,3},{2,0},{3,1},{4,6},{5,7},{6,4},{7,5},{8,10},{9,11},{10,... | collective-permute-start | bytes 1572872 | tf_op jit(solution)/shard_map/ppermute | solution.py:174
  229.9 19.3 %slice-start.10 = ((s8[8388608]{0:T(1024)(128)(4,1)}), s8[4194304]{0:T(1024)(128)(4,1)S(1)}, s32[]{:S(2)}) async-start(s8[8388608]{0:T(1024)(128)(4,1)} %bitcast.333), calls=%async_computation.16 | async-start | bytes 8388608
  236.3 6.3 %copy-start = (bf16[1,128,8192]{2,1,0:T(8,128)(2,1)S(1)}, bf16[1,128,8192]{2,1,0:T(8,128)(2,1)}, u32[]{:S(2)}) copy-start(bf16[1,128,8192]{2,1,0:T(8,128)(2,1)} %param.19) | copy-start | bytes 6291460
  236.3 12.9 %slice-start.11 = ((s8[8388608]{0:T(1024)(128)(4,1)}), s8[4194304]{0:T(1024)(128)(4,1)S(1)}, s32[]{:S(2)}) async-start(s8[8388608]{0:T(1024)(128)(4,1)} %bitcast.333), calls=%async_computation.17 | async-start | bytes 8388608
  236.4 9.3 %collective-permute-start.5 = (bf16[2,32,8192]{2,1,0:T(8,128)(2,1)S(1)}, bf16[2,32,8192]{2,1,0:T(8,128)(2,1)S(1)}, u32[]{:S(2)}, u32[]{:S(2)}) collective-permute-start(bf16[2,32,8192]{2,1,0:T(8,128)(2,1)S(1)} %dynamic-slice_bitcast_fusion.2), channel_id=1, source_target_pairs={{0,1},{1,0},{2,3},{3,2},{4,5},{5,4},{6,7},{7,6},{8,9},{9,8},{10,11... | collective-permute-start | bytes 3145736 | tf_op jit(solution)/shard_map/ppermute | solution.py:167
  243.6 16.5 %collective-permute-start.3 = (bf16[32,8192]{1,0:T(8,128)(2,1)S(1)}, bf16[32,8192]{1,0:T(8,128)(2,1)S(1)}, u32[]{:S(2)}, u32[]{:S(2)}) collective-permute-start(bf16[32,8192]{1,0:T(8,128)(2,1)S(1)} %get-tuple-element.75), channel_id=1, source_target_pairs={{96,0},{97,1},{98,2},{99,3},{100,4},{101,5},{102,6},{103,7},{104,8... | collective-permute-start | bytes 1572872 | tf_op jit(solution)/shard_map/ppermute | solution.py:187
  244.9 15.2 %collective-permute-start.2 = (bf16[32,8192]{1,0:T(8,128)(2,1)S(1)}, bf16[32,8192]{1,0:T(8,128)(2,1)S(1)}, u32[]{:S(2)}, u32[]{:S(2)}) collective-permute-start(bf16[32,8192]{1,0:T(8,128)(2,1)S(1)} %get-tuple-element.75), channel_id=1, source_target_pairs={{96,64},{64,32},{97,65},{65,33},{98,66},{66,34},{99,67},{67,35},{1... | collective-permute-start | bytes 1572872 | tf_op jit(solution)/shard_map/ppermute | solution.py:186
  246.0 17.2 %collective-permute-start.6 = (bf16[32,8192]{1,0:T(8,128)(2,1)S(1)}, bf16[32,8192]{1,0:T(8,128)(2,1)S(1)}, u32[]{:S(2)}, u32[]{:S(2)}) collective-permute-start(bf16[32,8192]{1,0:T(8,128)(2,1)S(1)} %fusion.66), channel_id=1, source_target_pairs={{0,2},{1,3},{2,0},{3,1},{4,6},{5,7},{6,4},{7,5},{8,10},{9,11},{10,... | collective-permute-start | bytes 1572872 | tf_op jit(solution)/shard_map/ppermute | solution.py:174
  252.1 22.8 %collective-permute-start.10 = (bf16[2,32,8192]{2,1,0:T(8,128)(2,1)S(1)}, bf16[2,32,8192]{2,1,0:T(8,128)(2,1)S(1)}, u32[]{:S(2)}, u32[]{:S(2)}) collective-permute-start(bf16[2,32,8192]{2,1,0:T(8,128)(2,1)S(1)} %dynamic-slice_bitcast_fusion.1), channel_id=1, source_target_pairs={{0,1},{1,0},{2,3},{3,2},{4,5},{5,4},{6,7},{7,6},{8,9},{9,8},{10,11... | collective-permute-start | bytes 3145736 | tf_op jit(solution)/shard_map/ppermute | solution.py:167
  260.3 14.4 %collective-permute-start.4 = (bf16[32,8192]{1,0:T(8,128)(2,1)S(1)}, bf16[32,8192]{1,0:T(8,128)(2,1)S(1)}, u32[]{:S(2)}, u32[]{:S(2)}) collective-permute-start(bf16[32,8192]{1,0:T(8,128)(2,1)S(1)} %fusion.36), channel_id=1, source_target_pairs={{32,0},{0,32},{33,1},{1,33},{34,2},{2,34},{35,3},{3,35},{36,4},{4,... | collective-permute-start | bytes 1572872 | tf_op jit(solution)/shard_map/ppermute | solution.py:193
  263.9 21.4 %collective-permute-start.8 = (bf16[32,8192]{1,0:T(8,128)(2,1)S(1)}, bf16[32,8192]{1,0:T(8,128)(2,1)S(1)}, u32[]{:S(2)}, u32[]{:S(2)}) collective-permute-start(bf16[32,8192]{1,0:T(8,128)(2,1)S(1)} %get-tuple-element.73), channel_id=1, source_target_pairs={{96,0},{97,1},{98,2},{99,3},{100,4},{101,5},{102,6},{103,7},{104,8... | collective-permute-start | bytes 1572872 | tf_op jit(solution)/shard_map/ppermute | solution.py:187
  265.2 20.1 %collective-permute-start.7 = (bf16[32,8192]{1,0:T(8,128)(2,1)S(1)}, bf16[32,8192]{1,0:T(8,128)(2,1)S(1)}, u32[]{:S(2)}, u32[]{:S(2)}) collective-permute-start(bf16[32,8192]{1,0:T(8,128)(2,1)S(1)} %get-tuple-element.73), channel_id=1, source_target_pairs={{96,64},{64,32},{97,65},{65,33},{98,66},{66,34},{99,67},{67,35},{1... | collective-permute-start | bytes 1572872 | tf_op jit(solution)/shard_map/ppermute | solution.py:186
  275.3 13.6 %collective-permute-start.11 = (bf16[32,8192]{1,0:T(8,128)(2,1)S(1)}, bf16[32,8192]{1,0:T(8,128)(2,1)S(1)}, u32[]{:S(2)}, u32[]{:S(2)}) collective-permute-start(bf16[32,8192]{1,0:T(8,128)(2,1)S(1)} %fusion.67), channel_id=1, source_target_pairs={{0,2},{1,3},{2,0},{3,1},{4,6},{5,7},{6,4},{7,5},{8,10},{9,11},{10,... | collective-permute-start | bytes 1572872 | tf_op jit(solution)/shard_map/ppermute | solution.py:174
  285.2 6.4 %collective-permute-start.15 = (bf16[2,32,8192]{2,1,0:T(8,128)(2,1)S(1)}, bf16[2,32,8192]{2,1,0:T(8,128)(2,1)S(1)}, u32[]{:S(2)}, u32[]{:S(2)}) collective-permute-start(bf16[2,32,8192]{2,1,0:T(8,128)(2,1)S(1)} %dynamic-slice_bitcast_fusion), channel_id=1, source_target_pairs={{0,1},{1,0},{2,3},{3,2},{4,5},{5,4},{6,7},{7,6},{8,9},{9,8},{10,11... | collective-permute-start | bytes 3145736 | tf_op jit(solution)/shard_map/ppermute | solution.py:167
  285.5 16.2 %collective-permute-start.9 = (bf16[32,8192]{1,0:T(8,128)(2,1)S(1)}, bf16[32,8192]{1,0:T(8,128)(2,1)S(1)}, u32[]{:S(2)}, u32[]{:S(2)}) collective-permute-start(bf16[32,8192]{1,0:T(8,128)(2,1)S(1)} %fusion.38), channel_id=1, source_target_pairs={{32,0},{0,32},{33,1},{1,33},{34,2},{2,34},{35,3},{3,35},{36,4},{4,... | collective-permute-start | bytes 1572872 | tf_op jit(solution)/shard_map/ppermute | solution.py:193
  289.5 20.1 %collective-permute-start.13 = (bf16[32,8192]{1,0:T(8,128)(2,1)S(1)}, bf16[32,8192]{1,0:T(8,128)(2,1)S(1)}, u32[]{:S(2)}, u32[]{:S(2)}) collective-permute-start(bf16[32,8192]{1,0:T(8,128)(2,1)S(1)} %get-tuple-element.71), channel_id=1, source_target_pairs={{96,0},{97,1},{98,2},{99,3},{100,4},{101,5},{102,6},{103,7},{104,8... | collective-permute-start | bytes 1572872 | tf_op jit(solution)/shard_map/ppermute | solution.py:187
  290.8 18.8 %collective-permute-start.12 = (bf16[32,8192]{1,0:T(8,128)(2,1)S(1)}, bf16[32,8192]{1,0:T(8,128)(2,1)S(1)}, u32[]{:S(2)}, u32[]{:S(2)}) collective-permute-start(bf16[32,8192]{1,0:T(8,128)(2,1)S(1)} %get-tuple-element.71), channel_id=1, source_target_pairs={{96,64},{64,32},{97,65},{65,33},{98,66},{66,34},{99,67},{67,35},{1... | collective-permute-start | bytes 1572872 | tf_op jit(solution)/shard_map/ppermute | solution.py:186
  291.8 15.1 %collective-permute-start.16 = (bf16[32,8192]{1,0:T(8,128)(2,1)S(1)}, bf16[32,8192]{1,0:T(8,128)(2,1)S(1)}, u32[]{:S(2)}, u32[]{:S(2)}) collective-permute-start(bf16[32,8192]{1,0:T(8,128)(2,1)S(1)} %fusion.68), channel_id=1, source_target_pairs={{0,2},{1,3},{2,0},{3,1},{4,6},{5,7},{6,4},{7,5},{8,10},{9,11},{10,... | collective-permute-start | bytes 1572872 | tf_op jit(solution)/shard_map/ppermute | solution.py:174
  307.6 16.2 %collective-permute-start.18 = (bf16[32,8192]{1,0:T(8,128)(2,1)S(1)}, bf16[32,8192]{1,0:T(8,128)(2,1)S(1)}, u32[]{:S(2)}, u32[]{:S(2)}) collective-permute-start(bf16[32,8192]{1,0:T(8,128)(2,1)S(1)} %get-tuple-element.69), channel_id=1, source_target_pairs={{96,0},{97,1},{98,2},{99,3},{100,4},{101,5},{102,6},{103,7},{104,8... | collective-permute-start | bytes 1572872 | tf_op jit(solution)/shard_map/ppermute | solution.py:187
  308.9 14.9 %collective-permute-start.17 = (bf16[32,8192]{1,0:T(8,128)(2,1)S(1)}, bf16[32,8192]{1,0:T(8,128)(2,1)S(1)}, u32[]{:S(2)}, u32[]{:S(2)}) collective-permute-start(bf16[32,8192]{1,0:T(8,128)(2,1)S(1)} %get-tuple-element.69), channel_id=1, source_target_pairs={{96,64},{64,32},{97,65},{65,33},{98,66},{66,34},{99,67},{67,35},{1... | collective-permute-start | bytes 1572872 | tf_op jit(solution)/shard_map/ppermute | solution.py:186
  309.9 16.7 %collective-permute-start.14 = (bf16[32,8192]{1,0:T(8,128)(2,1)S(1)}, bf16[32,8192]{1,0:T(8,128)(2,1)S(1)}, u32[]{:S(2)}, u32[]{:S(2)}) collective-permute-start(bf16[32,8192]{1,0:T(8,128)(2,1)S(1)} %fusion.40), channel_id=1, source_target_pairs={{32,0},{0,32},{33,1},{1,33},{34,2},{2,34},{35,3},{3,35},{36,4},{4,... | collective-permute-start | bytes 1572872 | tf_op jit(solution)/shard_map/ppermute | solution.py:193
  324.0 13.7 %collective-permute-start.19 = (bf16[32,8192]{1,0:T(8,128)(2,1)S(1)}, bf16[32,8192]{1,0:T(8,128)(2,1)S(1)}, u32[]{:S(2)}, u32[]{:S(2)}) collective-permute-start(bf16[32,8192]{1,0:T(8,128)(2,1)S(1)} %fusion.42), channel_id=1, source_target_pairs={{32,0},{0,32},{33,1},{1,33},{34,2},{2,34},{35,3},{3,35},{36,4},{4,... | collective-permute-start | bytes 1572872 | tf_op jit(solution)/shard_map/ppermute | solution.py:193
  (3 other events, 2.6 us)
Sparse Core Ops, SparseCore 0:
  59.4 50.2 all-gather.1

commit v6 on v4

--- a/solution.py
+++ b/solution.py
@@ -181,7 +181,13 @@
             )
             term_low = layer_term.astype(jnp.bfloat16)
             previous = term_low
-            if n_sec == 4:
+            if n_sec == 4 and c == len(sizes) - 1:
+                total = layer_term
+                for shift in range(1, n_sec):
+                    pairs = [(l + shift, l) for l in range(n_sec - shift)]
+                    total = total + lax.ppermute(term_low, "section", pairs).astype(jnp.float32)
+                outs.append(total)
+            elif n_sec == 4:
                 down = lax.ppermute(term_low, "section", [(3, 2), (2, 1)])
                 wrap = lax.ppermute(term_low, "section", [(3, 0)])
                 carry = (

time: 349 us -> 346 us (level)
  waiting for transfers between devices: 107 us -> 103 us
    ppermute x4 -> x3, waiting for transfers between devices: 14.7 us -> 5.35 us  [on_device(): wrap = lax.ppermute(term_low, 'section', [(3, 0)])]
    ppermute x0 -> x3, waiting for transfers between devices: none -> 4.97 us  [on_device(): total = total + lax.ppermute(term_low, 'section', pairs).astype(jnp.float32)]
    ppermute x0 -> x3, starting transfers between devices: none -> 3.88 us  [on_device(): total = total + lax.ppermute(term_low, 'section', pairs).astype(jnp.float32)]
    ppermute x4 -> x3, waiting for transfers between devices: 14.9 us -> 17.3 us  [on_device(): last = lax.ppermute(carry.astype(jnp.bfloat16), 'section', [(1, 0), (0, 1)])]
    ppermute x4 -> x3, starting transfers between devices: 11.7 us -> 10.4 us  [on_device(): last = lax.ppermute(carry.astype(jnp.bfloat16), 'section', [(1, 0), (0, 1)])]
  transfers between devices with their start and end apart: 26 -> 26, of which waited for: 16 -> 15; matrix products, arithmetic and copies ran while one was open for 41% -> 42% of each run, Pallas kernels for 0% -> 0%
where the time goes in v6:
time: 346 us; the launch traced here: 340 us
  waiting for transfers between devices  103 us (30%)
  matrix products  76.1 us (22%)
  other arithmetic  58.5 us (17%)
  starting transfers between devices  52.8 us (15%)
  local copies, waits for them, and re-layouts  34.3 us (10%)
  between operations  15.3 us (4%)
    ppermute x4, waiting for transfers between devices, on_device(): got2 = lax.ppermute(other, 'tensor', chip_pairs)  24.1 us
    all_to_all x1, waiting for transfers between devices, on_device(): lax.all_to_all(spread, 'sample', 0, 0, tiled=True).reshape(pooled_rows, -1)  22.1 us
    sub x2, other arithmetic, attend_group(): exponent = jnp.exp(scores - row_max)  21 us
    dot_general x4, matrix products, on_device(): lax.dot_general(grad_rows_c, weight_local, (((2, 3), (1, 2)), ((), ())),...  20 us
    ppermute x3, waiting for transfers between devices, on_device(): last = lax.ppermute(carry.astype(jnp.bfloat16), 'section', [(1, 0), (0, 1)])  17.3 us
    convert_element_type x2, other arithmetic, attend_group(): weights_low = softmax_w.astype(jnp.bfloat16)  17.1 us
    all_to_all x2, waiting for transfers between devices, on_device(): parts = lax.all_to_all(pool_grad, 'sample', 0, 0, tiled=False)  16.5 us
    dot_general x2, matrix products, attend_group(): jnp.einsum('rgd,kd->rgk', grad_grp, value_rows, preferred_element_type=jn...  13.6 us
  transfers between devices with their start and end apart: 26, of which 15 were waited for; matrix products, arithmetic and copies ran while one was open for 42% of the time, Pallas kernels for 0%

profile of v6, /device:TPU:0, one launch (start us, length us, event | category | flops | bytes accessed | tf_op | source)
XLA Modules:
  0.0 340.2 jit_solution(1510882118671815545)
XLA Ops:
  7.2 1.2 copy.108
  10.3 4.6 %all-to-all-start = ((bf16[4,128,512]{1,2,0:T(8,128)(2,1)}), bf16[4,128,512]{1,2,0:T(8,128)(2,1)S(1)}, u32[]{:S(2)}, u32[]{:S(2)}) async-start(bf16[4,128,512]{1,2,0:T(8,128)(2,1)} %bitcast.6), calls=%async_computation | async-start | bytes 1048576 | tf_op jit(solution)/shard_map/all_to_all | solution.py:85
  15.2 10.0 %all-to-all-done = bf16[4,128,512]{1,2,0:T(8,128)(2,1)S(1)} async-done(((bf16[4,128,512]{1,2,0:T(8,128)(2,1)}), bf16[4,128,512]{1,2,0:T(8,128)(2,1)S(1)}, u32[]{:S(2)}, u32[]{:S(2)}) %all-to-all-start) | async-done | bytes 524320 | tf_op jit(solution)/shard_map/all_to_all | solution.py:85
  26.4 1.5 broadcast_in_dim.93
  27.8 5.6 %all-to-all-start.1 = ((bf16[8,512,256]{2,1,0:T(8,128)(2,1)}), bf16[8,512,256]{2,1,0:T(8,128)(2,1)}, u32[]{:S(2)}, u32[]{:S(2)}) async-start(bf16[8,512,256]{2,1,0:T(8,128)(2,1)} %broadcast_in_dim.93), calls=%async_computation.1 | async-start | bytes 4194304 | tf_op jit(solution)/shard_map/all_to_all | solution.py:94
  38.1 22.1 %all-to-all-done.1 = bf16[8,512,256]{2,1,0:T(8,128)(2,1)} async-done(((bf16[8,512,256]{2,1,0:T(8,128)(2,1)}), bf16[8,512,256]{2,1,0:T(8,128)(2,1)}, u32[]{:S(2)}, u32[]{:S(2)}) %all-to-all-start.1) | async-done | bytes 2097184 | tf_op jit(solution)/shard_map/all_to_all | solution.py:94
  60.2 2.6 fusion.98
  62.9 3.2 fusion.58
  66.0 10.8 %fusion.107 = (f32[128,8]{0,1:T(8,128)S(1)}, f32[128,8,4224]{0,2,1:T(8,128)}) fusion(f32[4224,128,8]{1,0,2:T(8,128)S(1)} %fusion.58, pred[128,4224]{0,1:T(8,128)(4,1)S(1)} %pad_add_fusion), kind=kOutput, calls=%fused_computation.204 | output fusion | flops 17305728 | bytes 35147776 | tf_op jit(solution)/shard_map/sub | solution.py:36
  76.8 6.8 %fusion.18 = bf16[128,8,4224]{0,2,1:T(8,128)(2,1)S(1)} fusion(f32[128,8,4224]{0,2,1:T(8,128)} %get-tuple-element.98, f32[128,8]{0,1:T(8,128)S(1)} %get-tuple-element.97), kind=kLoop, calls=%fused_computation.30 | loop fusion | flops 8650752 | bytes 25956352 | tf_op jit(solution)/shard_map/convert_element_type | solution.py:38
  83.7 2.4 fusion.26
  86.2 2.5 fusion.38
  89.2 1.3 slice-done.3
  90.5 7.2 %fusion.3 = bf16[128,8,4224]{0,2,1:T(8,128)(2,1)} fusion(f32[128,8]{0,1:T(8,128)S(1)} %fusion.38, f32[128,8,4224]{0,2,1:T(8,128)S(1)} %bitcast.291, f32[128,8]{0,1:T(8,128)S(1)} %get-tuple-element.97, bf16[128,128]{1,0:T(8,128)(2,1)S(1)} %copy-done.30, bf16[4096,128]{1,0:T(8,128)(2,1)} %get-tuple-element.71, bf16[128,2,8,128]{0,3,2,1:T(8,128)(2,1)} %bitcast.321), kind=kOutput, calls=%fused_computation.6 | convolution fusion | flops 1126760448 | bytes 27303936 | tf_op jit(solution)/shard_map/rgd,kd->rgk/dot_general | solution.py:43
  97.7 5.9 %fusion.25 = bf16[4224,128]{1,0:T(8,128)(2,1)S(1)} fusion(bf16[128,8,4224]{0,2,1:T(8,128)(2,1)} %fusion.3, bf16[128,2,8,128]{0,3,2,1:T(8,128)(2,1)} %bitcast.313), kind=kOutput, calls=%fused_computation.41 | convolution fusion | flops 1108377600 | bytes 9994240 | tf_op jit(solution)/shard_map/rgk,rgd->kd/dot_general | solution.py:48
  105.9 1.5 pad_maximum_fusion
  107.4 4.4 %all-to-all-start.2 = ((bf16[8,512,256]{2,1,0:T(8,128)(2,1)}), bf16[8,512,256]{2,1,0:T(8,128)(2,1)}, u32[]{:S(2)}, u32[]{:S(2)}) async-start(bf16[8,512,256]{2,1,0:T(8,128)(2,1)} %pad_maximum_fusion), calls=%async_computation.2 | async-start | bytes 4194304 | tf_op jit(solution)/shard_map/all_to_all | solution.py:118
  111.8 1.6 all-gather.2.cloned.1.call-done
  113.4 2.7 fusion.99
  116.1 2.4 fusion.57
  118.5 10.2 %fusion.106 = (f32[128,8]{0,1:T(8,128)S(1)}, f32[128,8,4224]{0,2,1:T(8,128)}) fusion(f32[4224,128,8]{1,0,2:T(8,128)S(1)} %fusion.57, pred[128,4224]{0,1:T(8,128)(4,1)S(1)} %pad_add_fusion), kind=kOutput, calls=%fused_computation.203 | output fusion | flops 17305728 | bytes 35147776 | tf_op jit(solution)/shard_map/sub | solution.py:36
  128.8 10.2 %fusion.19 = bf16[128,8,4224]{0,2,1:T(8,128)(2,1)} fusion(f32[128,8,4224]{0,2,1:T(8,128)} %get-tuple-element.96, f32[128,8]{0,1:T(8,128)S(1)} %get-tuple-element.95), kind=kLoop, calls=%fused_computation.31 | loop fusion | flops 8650752 | bytes 25956352 | tf_op jit(solution)/shard_map/convert_element_type | solution.py:38
  139.0 6.8 %fusion.39 = f32[128,8]{0,1:T(8,128)S(1)} fusion(bf16[128,8,4224]{0,2,1:T(8,128)(2,1)} %fusion.19, bf16[128,128]{1,0:T(8,128)(2,1)S(1)} %copy-done.29, bf16[4096,128]{1,0:T(8,128)(2,1)S(1)} %copy-done.18, bf16[128,1,8,128]{3,0,2,1:T(8,128)(2,1)S(1)} %copy-done.21), kind=kOutput, calls=%fused_computation.90 | convolution fusion | flops 1109851136 | bytes 9998336 | tf_op jit(solution)/shard_map/rgk,kd->rgd/dot_general | solution.py:39
  145.9 6.4 %fusion.2 = bf16[128,8,4224]{0,2,1:T(8,128)(2,1)} fusion(f32[128,8]{0,1:T(8,128)S(1)} %fusion.39, f32[128,8,4224]{0,2,1:T(8,128)S(1)} %bitcast.293, f32[128,8]{0,1:T(8,128)S(1)} %get-tuple-element.95, bf16[128,128]{1,0:T(8,128)(2,1)S(1)} %copy-done.29, bf16[4096,128]{1,0:T(8,128)(2,1)} %get-tuple-element.73, bf16[128,2,8,128]{0,3,2,1:T(8,128)(2,1)S(1)} %bitcast.323), kind=kOutput, calls=%fused_computation.3 | convolution fusion | flops 1126760448 | bytes 27303936 | tf_op jit(solution)/shard_map/rgd,kd->rgk/dot_general | solution.py:43
  152.3 6.0 %fusion.28 = bf16[4224,128]{1,0:T(8,128)(2,1)S(1)} fusion(bf16[128,8,4224]{0,2,1:T(8,128)(2,1)} %fusion.19, bf16[128,2,8,128]{0,3,2,1:T(8,128)(2,1)S(1)} %bitcast.324), kind=kOutput, calls=%fused_computation.44 | convolution fusion | flops 1107836928 | bytes 9994240 | tf_op jit(solution)/shard_map/rgk,rgd->kd/dot_general | solution.py:51
  159.4 2.5 fusion.27
  163.0 1.5 pad_maximum_fusion.1
  164.6 4.2 %all-to-all-start.3 = ((bf16[8,512,256]{2,1,0:T(8,128)(2,1)}), bf16[8,512,256]{2,1,0:T(8,128)(2,1)S(1)}, u32[]{:S(2)}, u32[]{:S(2)}) async-start(bf16[8,512,256]{2,1,0:T(8,128)(2,1)} %pad_maximum_fusion.1), calls=%async_computation.3 | async-start | bytes 4194304 | tf_op jit(solution)/shard_map/all_to_all | solution.py:118
  169.6 5.8 %fusion.41 = bf16[128,1,8,128]{0,3,2,1:T(8,128)(2,1)} fusion(bf16[128,8,4224]{0,2,1:T(8,128)(2,1)} %fusion.3, bf16[128,128]{1,0:T(8,128)(2,1)S(1)} %copy-done.25, bf16[4096,128]{1,0:T(8,128)(2,1)} %copy-done.1), kind=kOutput, calls=%fused_computation.92 | convolution fusion | flops 1109721088 | bytes 9994240 | tf_op jit(solution)/shard_map/rgk,kd->rgd/dot_general | solution.py:115
  175.4 2.0 reduce
  178.3 16.5 %all-to-all-done.3 = bf16[8,512,256]{2,1,0:T(8,128)(2,1)S(1)} async-done(((bf16[8,512,256]{2,1,0:T(8,128)(2,1)}), bf16[8,512,256]{2,1,0:T(8,128)(2,1)S(1)}, u32[]{:S(2)}, u32[]{:S(2)}) %all-to-all-start.3) | async-done | bytes 2097184 | tf_op jit(solution)/shard_map/all_to_all | solution.py:118
  196.9 1.8 pad_maximum_fusion.4
  198.7 4.0 %all-to-all-start.4 = ((bf16[4,128,512]{2,1,0:T(8,128)(2,1)}), bf16[4,128,512]{2,1,0:T(8,128)(2,1)S(1)}, u32[]{:S(2)}, u32[]{:S(2)}) async-start(bf16[4,128,512]{2,1,0:T(8,128)(2,1)} %pad_maximum_fusion.4), calls=%async_computation.4 | async-start | bytes 1048576 | tf_op jit(solution)/shard_map/all_to_all | solution.py:126
  203.5 8.2 %fusion.6 = bf16[4,48,8192]{2,1,0:T(8,128)(2,1)} fusion(bf16[8192,2,256]{2,1,0:T(2,128)(2,1)} %bitcast.343, bf16[4,128,2,256]{3,1,0,2:T(8,128)(2,1)S(1)} %reshape.274), kind=kOutput, calls=%fused_computation.13 | convolution fusion | flops 1612185600 | bytes 11730944 | tf_op jit(solution)/shard_map/dot_general | solution.py:155
  211.7 1.3 all-to-all-done.4
  214.3 2.7 dynamic-slice_bitcast_fusion
  217.3 4.9 %fusion.40 = bf16[128,1,8,128]{0,3,2,1:T(8,128)(2,1)S(1)} fusion(bf16[128,8,4224]{0,2,1:T(8,128)(2,1)} %fusion.2, bf16[128,128]{1,0:T(8,128)(2,1)S(1)} %copy-done.24, bf16[4096,128]{1,0:T(8,128)(2,1)S(1)} %get-tuple-element.74), kind=kOutput, calls=%fused_computation.91 | convolution fusion | flops 1109721088 | bytes 9994240 | tf_op jit(solution)/shard_map/rgk,kd->rgd/dot_general | solution.py:115
  229.1 2.2 convert_add_fusion
  231.5 2.4 collective-permute-start.1
  233.9 6.4 %fusion.7 = bf16[4,32,8192]{2,1,0:T(8,128)(2,1)S(1)} fusion(bf16[4,32,2,256]{3,1,0,2:T(8,128)(2,1)S(1)} %get-tuple-element.28, bf16[8192,2,256,1]{2,1,0,3:T(2,128)(2,1)} %bitcast.344), kind=kOutput, calls=%fused_computation.16 | convolution fusion | flops 1074790400 | bytes 10616832 | tf_op jit(solution)/shard_map/dot_general | solution.py:155
  240.5 12.5 %collective-permute-done.1 = bf16[48,8192]{1,0:T(8,128)(2,1)S(1)} collective-permute-done((bf16[48,8192]{1,0:T(8,128)(2,1)S(1)}, bf16[48,8192]{1,0:T(8,128)(2,1)S(1)}, u32[]{:S(2)}, u32[]{:S(2)}) %collective-permute-start.1) | collective-permute-done | bytes 786464 | tf_op jit(solution)/shard_map/ppermute | solution.py:173
  254.0 1.3 collective-permute-start.3
  256.3 2.3 collective-permute-start.6
  258.6 2.8 fusion.8
  261.6 9.7 %collective-permute-done.6 = bf16[32,8192]{1,0:T(8,128)(2,1)S(1)} collective-permute-done((bf16[32,8192]{1,0:T(8,128)(2,1)S(1)}, bf16[32,8192]{1,0:T(8,128)(2,1)S(1)}, u32[]{:S(2)}, u32[]{:S(2)}) %collective-permute-start.6) | collective-permute-done | bytes 524320 | tf_op jit(solution)/shard_map/ppermute | solution.py:173
  272.3 1.3 collective-permute-start.8
  274.3 1.9 collective-permute-done.3
  276.5 3.0 collective-permute-start.4
  279.8 2.3 collective-permute-start.11
  282.2 2.6 fusion.9
  285.0 3.4 %collective-permute-done.8 = bf16[32,8192]{1,0:T(8,128)(2,1)S(1)} collective-permute-done((bf16[32,8192]{1,0:T(8,128)(2,1)S(1)}, bf16[32,8192]{1,0:T(8,128)(2,1)S(1)}, u32[]{:S(2)}, u32[]{:S(2)}) %collective-permute-start.8) | collective-permute-done | bytes 524320 | tf_op jit(solution)/shard_map/ppermute | solution.py:192
  288.6 2.8 collective-permute-start.9
  291.4 7.5 %collective-permute-done.4 = bf16[48,8192]{1,0:T(8,128)(2,1)S(1)} collective-permute-done((bf16[48,8192]{1,0:T(8,128)(2,1)S(1)}, bf16[48,8192]{1,0:T(8,128)(2,1)S(1)}, u32[]{:S(2)}, u32[]{:S(2)}) %collective-permute-start.4) | collective-permute-done | bytes 786464 | tf_op jit(solution)/shard_map/ppermute | solution.py:198
  300.0 1.3 collective-permute-start.13
  302.1 2.2 collective-permute-start.16
  304.3 3.7 %collective-permute-done.9 = bf16[32,8192]{1,0:T(8,128)(2,1)S(1)} collective-permute-done((bf16[32,8192]{1,0:T(8,128)(2,1)S(1)}, bf16[32,8192]{1,0:T(8,128)(2,1)S(1)}, u32[]{:S(2)}, u32[]{:S(2)}) %collective-permute-start.9) | collective-permute-done | bytes 524320 | tf_op jit(solution)/shard_map/ppermute | solution.py:198
  308.2 1.9 collective-permute-done.16
  310.6 1.3 collective-permute-start.19
  311.9 1.3 collective-permute-start.18
  313.2 1.3 collective-permute-start.17
  314.7 4.6 %collective-permute-start.14 = (bf16[32,8192]{1,0:T(8,128)(2,1)S(1)}, bf16[32,8192]{1,0:T(8,128)(2,1)S(1)}, u32[]{:S(2)}, u32[]{:S(2)}) collective-permute-start(bf16[32,8192]{1,0:T(8,128)(2,1)S(1)} %fusion.45), channel_id=1, source_target_pairs={{32,0},{0,32},{33,1},{1,33},{34,2},{2,34},{35,3},{3,35},{36,4},{4,... | collective-permute-start | bytes 1572872 | tf_op jit(solution)/shard_map/ppermute | solution.py:198
  319.3 4.6 %collective-permute-done.19 = bf16[16,8192]{1,0:T(8,128)(2,1)S(1)} collective-permute-done((bf16[16,8192]{1,0:T(8,128)(2,1)S(1)}, bf16[16,8192]{1,0:T(8,128)(2,1)S(1)}, u32[]{:S(2)}, u32[]{:S(2)}) %collective-permute-start.19) | collective-permute-done | bytes 262176 | tf_op jit(solution)/shard_map/ppermute | solution.py:188
  324.6 6.1 %collective-permute-done.14 = bf16[32,8192]{1,0:T(8,128)(2,1)S(1)} collective-permute-done((bf16[32,8192]{1,0:T(8,128)(2,1)S(1)}, bf16[32,8192]{1,0:T(8,128)(2,1)S(1)}, u32[]{:S(2)}, u32[]{:S(2)}) %collective-permute-start.14) | collective-permute-done | bytes 524320 | tf_op jit(solution)/shard_map/ppermute | solution.py:198
  330.9 2.3 maximum_bitcast_fusion
  (196 shorter events, 34.8 us)
Async XLA Ops:
  7.2 7.7 %copy-start.19 = (bf16[1,128,2048]{2,1,0:T(8,128)(2,1)S(1)}, bf16[1,128,2048]{2,1,0:T(8,128)(2,1)}, u32[]{:S(2)}) copy-start(bf16[1,128,2048]{2,1,0:T(8,128)(2,1)} %param.15) | copy-start | bytes 1572868
  10.3 14.9 %all-to-all-start = ((bf16[4,128,512]{1,2,0:T(8,128)(2,1)}), bf16[4,128,512]{1,2,0:T(8,128)(2,1)S(1)}, u32[]{:S(2)}, u32[]{:S(2)}) async-start(bf16[4,128,512]{1,2,0:T(8,128)(2,1)} %bitcast.6), calls=%async_computation | async-start | bytes 1048576 | tf_op jit(solution)/shard_map/all_to_all | solution.py:85
  15.2 18.3 %copy-start.7 = (bf16[1,128,2048]{1,2,0:T(8,128)(2,1)}, bf16[1,128,2048]{1,2,0:T(8,128)(2,1)S(1)}, u32[]{:S(2)}) copy-start(bf16[1,128,2048]{1,2,0:T(8,128)(2,1)S(1)} %copy.113) | copy-start | bytes 1572868
  27.8 5.7 %copy-start.20 = (bf16[1,128,2048]{2,1,0:T(8,128)(2,1)S(1)}, bf16[1,128,2048]{2,1,0:T(8,128)(2,1)}, u32[]{:S(2)}) copy-start(bf16[1,128,2048]{2,1,0:T(8,128)(2,1)} %param.12) | copy-start | bytes 1572868
  27.8 32.4 %all-to-all-start.1 = ((bf16[8,512,256]{2,1,0:T(8,128)(2,1)}), bf16[8,512,256]{2,1,0:T(8,128)(2,1)}, u32[]{:S(2)}, u32[]{:S(2)}) async-start(bf16[8,512,256]{2,1,0:T(8,128)(2,1)} %broadcast_in_dim.93), calls=%async_computation.1 | async-start | bytes 4194304 | tf_op jit(solution)/shard_map/all_to_all | solution.py:94
  33.4 3.1 copy-start.27
  33.4 79.9 %all-gather.2.cloned.1.call-start = ((), (), s32[]{:S(2)}) async-start(), calls=%async_computation.5 | async-start | bytes 2359296 | tf_op jit(solution)/shard_map/all_gather | solution.py:97
  33.8 29.0 %copy-start.4 = (bf16[1,128,2048]{1,2,0:T(8,128)(2,1)}, bf16[1,128,2048]{1,2,0:T(8,128)(2,1)S(1)}, u32[]{:S(2)}) copy-start(bf16[1,128,2048]{1,2,0:T(8,128)(2,1)S(1)} %copy.111) | copy-start | bytes 1572868
  62.8 3.2 copy-start.1
  76.8 6.8 %copy-start.8 = (bf16[1,128,2048]{1,2,0:T(8,128)(2,1)S(1)}, bf16[1,128,2048]{1,2,0:T(8,128)(2,1)}, u32[]{:S(2)}) copy-start(bf16[1,128,2048]{1,2,0:T(8,128)(2,1)} %copy-done.7) | copy-start | bytes 1572868
  83.7 5.1 %slice-start = ((s8[17301504]{0:T(1024)(128)(4,1)}), s8[4194304]{0:T(1024)(128)(4,1)S(1)}, s32[]{:S(2)}) async-start(s8[17301504]{0:T(1024)(128)(4,1)} %bitcast.290), calls=%async_computation.6 | async-start | bytes 8388608
  83.7 5.1 %slice-start.1 = ((s8[17301504]{0:T(1024)(128)(4,1)}), s8[4194304]{0:T(1024)(128)(4,1)S(1)}, s32[]{:S(2)}) async-start(s8[17301504]{0:T(1024)(128)(4,1)} %bitcast.290), calls=%async_computation.7 | async-start | bytes 8388608
  83.7 5.5 %slice-start.2 = ((s8[17301504]{0:T(1024)(128)(4,1)}), s8[4194304]{0:T(1024)(128)(4,1)S(1)}, s32[]{:S(2)}) async-start(s8[17301504]{0:T(1024)(128)(4,1)} %bitcast.290), calls=%async_computation.8 | async-start | bytes 8388608
  86.1 2.6 copy-start.2
  86.2 4.3 %slice-start.3 = ((s8[17301504]{0:T(1024)(128)(4,1)}), s8[4194304]{0:T(1024)(128)(4,1)S(1)}, s32[]{:S(2)}) async-start(s8[17301504]{0:T(1024)(128)(4,1)} %bitcast.290), calls=%async_computation.9 | async-start | bytes 8388608
  86.2 4.3 %slice-start.4 = ((s8[17301504]{0:T(1024)(128)(4,1)}), s8[524288]{0:T(1024)(128)(4,1)S(1)}, s32[]{:S(2)}) async-start(s8[17301504]{0:T(1024)(128)(4,1)} %bitcast.290), calls=%async_computation.10 | async-start | bytes 1048576
  107.4 57.2 %all-to-all-start.2 = ((bf16[8,512,256]{2,1,0:T(8,128)(2,1)}), bf16[8,512,256]{2,1,0:T(8,128)(2,1)}, u32[]{:S(2)}, u32[]{:S(2)}) async-start(bf16[8,512,256]{2,1,0:T(8,128)(2,1)} %pad_maximum_fusion), calls=%async_computation.2 | async-start | bytes 4194304 | tf_op jit(solution)/shard_map/all_to_all | solution.py:118
  111.8 4.3 %copy-start.24 = (bf16[128,128]{1,0:T(8,128)(2,1)S(1)}, bf16[128,128]{1,0:T(8,128)(2,1)}, u32[]{:S(2)}) copy-start(bf16[128,128]{1,0:T(8,128)(2,1)} %get-tuple-element.86) | copy-start | bytes 98308
  113.4 2.7 copy-start.5
  128.7 10.3 %copy-start.18 = (bf16[4096,128]{1,0:T(8,128)(2,1)S(1)}, bf16[4096,128]{1,0:T(8,128)(2,1)}, u32[]{:S(2)}) copy-start(bf16[4096,128]{1,0:T(8,128)(2,1)} %get-tuple-element.73) | copy-start | bytes 3145732
  128.7 10.3 %copy-start.21 = (bf16[128,1,8,128]{3,0,2,1:T(8,128)(2,1)S(1)}, bf16[128,1,8,128]{3,0,2,1:T(8,128)(2,1)}, u32[]{:S(2)}) copy-start(bf16[128,1,8,128]{3,0,2,1:T(8,128)(2,1)} %copy.173) | copy-start | bytes 786436
  128.7 10.3 %copy-start.29 = (bf16[128,128]{1,0:T(8,128)(2,1)S(1)}, bf16[128,128]{1,0:T(8,128)(2,1)}, u32[]{:S(2)}) copy-start(bf16[128,128]{1,0:T(8,128)(2,1)} %get-tuple-element.84) | copy-start | bytes 98308
  128.7 17.2 %slice-start.5 = ((s8[17301504]{0:T(1024)(128)(4,1)}), s8[4194304]{0:T(1024)(128)(4,1)S(1)}, s32[]{:S(2)}) async-start(s8[17301504]{0:T(1024)(128)(4,1)} %bitcast.292), calls=%async_computation.11 | async-start | bytes 8388608
  128.7 17.2 %slice-start.6 = ((s8[17301504]{0:T(1024)(128)(4,1)}), s8[4194304]{0:T(1024)(128)(4,1)S(1)}, s32[]{:S(2)}) async-start(s8[17301504]{0:T(1024)(128)(4,1)} %bitcast.292), calls=%async_computation.12 | async-start | bytes 8388608
  128.7 17.2 %slice-start.7 = ((s8[17301504]{0:T(1024)(128)(4,1)}), s8[4194304]{0:T(1024)(128)(4,1)S(1)}, s32[]{:S(2)}) async-start(s8[17301504]{0:T(1024)(128)(4,1)} %bitcast.292), calls=%async_computation.13 | async-start | bytes 8388608
  128.8 17.2 %slice-start.8 = ((s8[17301504]{0:T(1024)(128)(4,1)}), s8[4194304]{0:T(1024)(128)(4,1)S(1)}, s32[]{:S(2)}) async-start(s8[17301504]{0:T(1024)(128)(4,1)} %bitcast.292), calls=%async_computation.14 | async-start | bytes 8388608
  139.0 6.9 %slice-start.9 = ((s8[17301504]{0:T(1024)(128)(4,1)}), s8[524288]{0:T(1024)(128)(4,1)S(1)}, s32[]{:S(2)}) async-start(s8[17301504]{0:T(1024)(128)(4,1)} %bitcast.292), calls=%async_computation.15 | async-start | bytes 1048576
  139.0 6.9 %copy-start.9 = (bf16[1,128,2048]{1,2,0:T(8,128)(2,1)S(1)}, bf16[1,128,2048]{1,2,0:T(8,128)(2,1)}, u32[]{:S(2)}) copy-start(bf16[1,128,2048]{1,2,0:T(8,128)(2,1)} %copy-done.7) | copy-start | bytes 1572868
  152.3 7.1 %copy-start.6 = (bf16[1,128,2048]{1,2,0:T(8,128)(2,1)S(1)}, bf16[1,128,2048]{1,2,0:T(8,128)(2,1)}, u32[]{:S(2)}) copy-start(bf16[1,128,2048]{1,2,0:T(8,128)(2,1)} %copy-done.4) | copy-start | bytes 1572868
  152.3 7.1 %copy-start.34 = (bf16[128,8,4224]{0,2,1:T(8,128)(2,1)S(1)}, bf16[128,8,4224]{0,2,1:T(8,128)(2,1)}, u32[]{:S(2)}) copy-start(bf16[128,8,4224]{0,2,1:T(8,128)(2,1)} %fusion.2) | copy-start | bytes 25952260
  164.6 4.2 %copy-start.28 = (bf16[1,8192]{1,0:T(2,128)(2,1)S(1)}, bf16[1,8192]{1,0:T(2,128)(2,1)}, u32[]{:S(2)}) copy-start(bf16[1,8192]{1,0:T(2,128)(2,1)} %param.20) | copy-start | bytes 49156
  164.6 5.0 %copy-start.25 = (bf16[128,128]{1,0:T(8,128)(2,1)S(1)}, bf16[128,128]{1,0:T(8,128)(2,1)}, u32[]{:S(2)}) copy-start(bf16[128,128]{1,0:T(8,128)(2,1)} %get-tuple-element.85) | copy-start | bytes 98308
  164.6 30.2 %all-to-all-start.3 = ((bf16[8,512,256]{2,1,0:T(8,128)(2,1)}), bf16[8,512,256]{2,1,0:T(8,128)(2,1)S(1)}, u32[]{:S(2)}, u32[]{:S(2)}) async-start(bf16[8,512,256]{2,1,0:T(8,128)(2,1)} %pad_maximum_fusion.1), calls=%async_computation.3 | async-start | bytes 4194304 | tf_op jit(solution)/shard_map/all_to_all | solution.py:118
  195.8 6.9 %copy-start.16 = (bf16[512,256]{0,1:T(8,128)(2,1)S(1)}, bf16[512,256]{0,1:T(8,128)(2,1)}, u32[]{:S(2)}) copy-start(bf16[512,256]{0,1:T(8,128)(2,1)} %copy.129) | copy-start | bytes 786436
  198.7 14.3 %all-to-all-start.4 = ((bf16[4,128,512]{2,1,0:T(8,128)(2,1)}), bf16[4,128,512]{2,1,0:T(8,128)(2,1)S(1)}, u32[]{:S(2)}, u32[]{:S(2)}) async-start(bf16[4,128,512]{2,1,0:T(8,128)(2,1)} %pad_maximum_fusion.4), calls=%async_computation.4 | async-start | bytes 1048576 | tf_op jit(solution)/shard_map/all_to_all | solution.py:126
  203.5 8.2 %copy-start.12 = (bf16[4,128,2,256]{3,1,0,2:T(8,128)(2,1)}, bf16[4,128,2,256]{3,1,0,2:T(8,128)(2,1)S(1)}, u32[]{:S(2)}) copy-start(bf16[4,128,2,256]{3,1,0,2:T(8,128)(2,1)S(1)} %reshape.274) | copy-start | bytes 1572868
  216.9 5.3 %copy-start.23 = (bf16[128,1,8,128]{0,3,2,1:T(8,128)(2,1)S(1)}, bf16[128,1,8,128]{0,3,2,1:T(8,128)(2,1)}, u32[]{:S(2)}) copy-start(bf16[128,1,8,128]{0,3,2,1:T(8,128)(2,1)} %fusion.41) | copy-start | bytes 786436
  216.9 6.4 %copy-start.3 = (bf16[4224,128]{1,0:T(8,128)(2,1)S(1)}, bf16[4224,128]{1,0:T(8,128)(2,1)}, u32[]{:S(2)}) copy-start(bf16[4224,128]{1,0:T(8,128)(2,1)} %copy-done.2) | copy-start | bytes 3244036
  216.9 12.2 %collective-permute-start = (bf16[2,48,8192]{2,1,0:T(8,128)(2,1)}, bf16[2,48,8192]{2,1,0:T(8,128)(2,1)}, u32[]{:S(2)}, u32[]{:S(2)}) collective-permute-start(bf16[2,48,8192]{2,1,0:T(8,128)(2,1)} %dynamic-slice_bitcast_fusion), channel_id=1, source_target_pairs={{0,1},{1,0},{2,3},{3,2},{4,5},{5,4},{6,7},{7,6},{8,9},{9,8},{10,11... | collective-permute-start | bytes 4718600 | tf_op jit(solution)/shard_map/ppermute | solution.py:166
  222.2 4.9 %copy-start.11 = (f32[1,128,4,2,128]{1,4,0,3,2:T(8,128)S(1)}, f32[1,128,4,2,128]{1,4,0,3,2:T(8,128)}, u32[]{:S(2)}) copy-start(f32[1,128,4,2,128]{1,4,0,3,2:T(8,128)} %get-tuple-element.76) | copy-start | bytes 1572868
  222.2 5.9 %copy-start.10 = (f32[1,128,4,2,128]{1,4,0,3,2:T(8,128)S(1)}, f32[1,128,4,2,128]{1,4,0,3,2:T(8,128)}, u32[]{:S(2)}) copy-start(f32[1,128,4,2,128]{1,4,0,3,2:T(8,128)} %get-tuple-element.75) | copy-start | bytes 1572868
  231.5 21.5 %collective-permute-start.1 = (bf16[48,8192]{1,0:T(8,128)(2,1)S(1)}, bf16[48,8192]{1,0:T(8,128)(2,1)S(1)}, u32[]{:S(2)}, u32[]{:S(2)}) collective-permute-start(bf16[48,8192]{1,0:T(8,128)(2,1)S(1)} %fusion.56), channel_id=1, source_target_pairs={{0,2},{1,3},{2,0},{3,1},{4,6},{5,7},{6,4},{7,5},{8,10},{9,11},{10,... | collective-permute-start | bytes 2359304 | tf_op jit(solution)/shard_map/ppermute | solution.py:173
  233.8 24.8 %slice-start.12 = ((s8[8388608]{0:T(1024)(128)(4,1)}), s8[4194304]{0:T(1024)(128)(4,1)S(1)}, s32[]{:S(2)}) async-start(s8[8388608]{0:T(1024)(128)(4,1)} %bitcast.345), calls=%async_computation.18 | async-start | bytes 8388608
  240.2 12.8 %copy-start = (bf16[1,128,8192]{2,1,0:T(8,128)(2,1)S(1)}, bf16[1,128,8192]{2,1,0:T(8,128)(2,1)}, u32[]{:S(2)}) copy-start(bf16[1,128,8192]{2,1,0:T(8,128)(2,1)} %param.19) | copy-start | bytes 6291460
  240.2 18.4 %slice-start.13 = ((s8[8388608]{0:T(1024)(128)(4,1)}), s8[4194304]{0:T(1024)(128)(4,1)S(1)}, s32[]{:S(2)}) async-start(s8[8388608]{0:T(1024)(128)(4,1)} %bitcast.345), calls=%async_computation.19 | async-start | bytes 8388608
  240.3 15.7 %collective-permute-start.5 = (bf16[2,32,8192]{2,1,0:T(8,128)(2,1)S(1)}, bf16[2,32,8192]{2,1,0:T(8,128)(2,1)S(1)}, u32[]{:S(2)}, u32[]{:S(2)}) collective-permute-start(bf16[2,32,8192]{2,1,0:T(8,128)(2,1)S(1)} %dynamic-slice_bitcast_fusion.2), channel_id=1, source_target_pairs={{0,1},{1,0},{2,3},{3,2},{4,5},{5,4},{6,7},{7,6},{8,9},{9,8},{10,11... | collective-permute-start | bytes 3145736 | tf_op jit(solution)/shard_map/ppermute | solution.py:166
  254.0 22.2 %collective-permute-start.3 = (bf16[48,8192]{1,0:T(8,128)(2,1)S(1)}, bf16[48,8192]{1,0:T(8,128)(2,1)S(1)}, u32[]{:S(2)}, u32[]{:S(2)}) collective-permute-start(bf16[48,8192]{1,0:T(8,128)(2,1)S(1)} %get-tuple-element.69), channel_id=1, source_target_pairs={{96,0},{97,1},{98,2},{99,3},{100,4},{101,5},{102,6},{103,7},{104,8... | collective-permute-start | bytes 2359304 | tf_op jit(solution)/shard_map/ppermute | solution.py:192
  255.3 20.9 %collective-permute-start.2 = (bf16[48,8192]{1,0:T(8,128)(2,1)S(1)}, bf16[48,8192]{1,0:T(8,128)(2,1)S(1)}, u32[]{:S(2)}, u32[]{:S(2)}) collective-permute-start(bf16[48,8192]{1,0:T(8,128)(2,1)S(1)} %get-tuple-element.69), channel_id=1, source_target_pairs={{96,64},{64,32},{97,65},{65,33},{98,66},{66,34},{99,67},{67,35},{1... | collective-permute-start | bytes 2359304 | tf_op jit(solution)/shard_map/ppermute | solution.py:191
  256.3 15.1 %collective-permute-start.6 = (bf16[32,8192]{1,0:T(8,128)(2,1)S(1)}, bf16[32,8192]{1,0:T(8,128)(2,1)S(1)}, u32[]{:S(2)}, u32[]{:S(2)}) collective-permute-start(bf16[32,8192]{1,0:T(8,128)(2,1)S(1)} %fusion.63), channel_id=1, source_target_pairs={{0,2},{1,3},{2,0},{3,1},{4,6},{5,7},{6,4},{7,5},{8,10},{9,11},{10,... | collective-permute-start | bytes 1572872 | tf_op jit(solution)/shard_map/ppermute | solution.py:173
  261.6 18.0 %collective-permute-start.10 = (bf16[2,32,8192]{2,1,0:T(8,128)(2,1)S(1)}, bf16[2,32,8192]{2,1,0:T(8,128)(2,1)S(1)}, u32[]{:S(2)}, u32[]{:S(2)}) collective-permute-start(bf16[2,32,8192]{2,1,0:T(8,128)(2,1)S(1)} %dynamic-slice_bitcast_fusion.1), channel_id=1, source_target_pairs={{0,1},{1,0},{2,3},{3,2},{4,5},{5,4},{6,7},{7,6},{8,9},{9,8},{10,11... | collective-permute-start | bytes 3145736 | tf_op jit(solution)/shard_map/ppermute | solution.py:166
  272.3 16.1 %collective-permute-start.8 = (bf16[32,8192]{1,0:T(8,128)(2,1)S(1)}, bf16[32,8192]{1,0:T(8,128)(2,1)S(1)}, u32[]{:S(2)}, u32[]{:S(2)}) collective-permute-start(bf16[32,8192]{1,0:T(8,128)(2,1)S(1)} %get-tuple-element.67), channel_id=1, source_target_pairs={{96,0},{97,1},{98,2},{99,3},{100,4},{101,5},{102,6},{103,7},{104,8... | collective-permute-start | bytes 1572872 | tf_op jit(solution)/shard_map/ppermute | solution.py:192
  273.6 14.8 %collective-permute-start.7 = (bf16[32,8192]{1,0:T(8,128)(2,1)S(1)}, bf16[32,8192]{1,0:T(8,128)(2,1)S(1)}, u32[]{:S(2)}, u32[]{:S(2)}) collective-permute-start(bf16[32,8192]{1,0:T(8,128)(2,1)S(1)} %get-tuple-element.67), channel_id=1, source_target_pairs={{96,64},{64,32},{97,65},{65,33},{98,66},{66,34},{99,67},{67,35},{1... | collective-permute-start | bytes 1572872 | tf_op jit(solution)/shard_map/ppermute | solution.py:191
  276.5 5.7 %slice-start.11 = ((bf16[4,128,2,256]{3,1,0,2:T(8,128)(2,1)}), bf16[4,16,2,256]{3,1,0,2:T(8,128)(2,1)S(1)}, s32[]{:S(2)}) async-start(bf16[4,128,2,256]{3,1,0,2:T(8,128)(2,1)} %copy-done.12), calls=%async_computation.17 | async-start | bytes 131072 | tf_op jit(solution)/shard_map/slice | solution.py:152
  276.5 22.4 %collective-permute-start.4 = (bf16[48,8192]{1,0:T(8,128)(2,1)S(1)}, bf16[48,8192]{1,0:T(8,128)(2,1)S(1)}, u32[]{:S(2)}, u32[]{:S(2)}) collective-permute-start(bf16[48,8192]{1,0:T(8,128)(2,1)S(1)} %fusion.30), channel_id=1, source_target_pairs={{32,0},{0,32},{33,1},{1,33},{34,2},{2,34},{35,3},{3,35},{36,4},{4,... | collective-permute-start | bytes 2359304 | tf_op jit(solution)/shard_map/ppermute | solution.py:198
  279.8 19.4 %collective-permute-start.11 = (bf16[32,8192]{1,0:T(8,128)(2,1)S(1)}, bf16[32,8192]{1,0:T(8,128)(2,1)S(1)}, u32[]{:S(2)}, u32[]{:S(2)}) collective-permute-start(bf16[32,8192]{1,0:T(8,128)(2,1)S(1)} %fusion.64), channel_id=1, source_target_pairs={{0,2},{1,3},{2,0},{3,1},{4,6},{5,7},{6,4},{7,5},{8,10},{9,11},{10,... | collective-permute-start | bytes 1572872 | tf_op jit(solution)/shard_map/ppermute | solution.py:173
  284.9 17.1 %collective-permute-start.15 = (bf16[2,16,8192]{2,1,0:T(8,128)(2,1)S(1)}, bf16[2,16,8192]{2,1,0:T(8,128)(2,1)S(1)}, u32[]{:S(2)}, u32[]{:S(2)}) collective-permute-start(bf16[2,16,8192]{2,1,0:T(8,128)(2,1)S(1)} %dynamic-slice_bitcast_fusion.3), channel_id=1, source_target_pairs={{0,1},{1,0},{2,3},{3,2},{4,5},{5,4},{6,7},{7,6},{8,9},{9,8},{10,11... | collective-permute-start | bytes 1572872 | tf_op jit(solution)/shard_map/ppermute | solution.py:166
  288.6 19.4 %collective-permute-start.9 = (bf16[32,8192]{1,0:T(8,128)(2,1)S(1)}, bf16[32,8192]{1,0:T(8,128)(2,1)S(1)}, u32[]{:S(2)}, u32[]{:S(2)}) collective-permute-start(bf16[32,8192]{1,0:T(8,128)(2,1)S(1)} %fusion.43), channel_id=1, source_target_pairs={{32,0},{0,32},{33,1},{1,33},{34,2},{2,34},{35,3},{3,35},{36,4},{4,... | collective-permute-start | bytes 1572872 | tf_op jit(solution)/shard_map/ppermute | solution.py:198
  300.0 14.5 %collective-permute-start.13 = (bf16[32,8192]{1,0:T(8,128)(2,1)S(1)}, bf16[32,8192]{1,0:T(8,128)(2,1)S(1)}, u32[]{:S(2)}, u32[]{:S(2)}) collective-permute-start(bf16[32,8192]{1,0:T(8,128)(2,1)S(1)} %get-tuple-element.65), channel_id=1, source_target_pairs={{96,0},{97,1},{98,2},{99,3},{100,4},{101,5},{102,6},{103,7},{104,8... | collective-permute-start | bytes 1572872 | tf_op jit(solution)/shard_map/ppermute | solution.py:192
  301.3 13.3 %collective-permute-start.12 = (bf16[32,8192]{1,0:T(8,128)(2,1)S(1)}, bf16[32,8192]{1,0:T(8,128)(2,1)S(1)}, u32[]{:S(2)}, u32[]{:S(2)}) collective-permute-start(bf16[32,8192]{1,0:T(8,128)(2,1)S(1)} %get-tuple-element.65), channel_id=1, source_target_pairs={{96,64},{64,32},{97,65},{65,33},{98,66},{66,34},{99,67},{67,35},{1... | collective-permute-start | bytes 1572872 | tf_op jit(solution)/shard_map/ppermute | solution.py:191
  302.1 8.0 %collective-permute-start.16 = (bf16[16,8192]{1,0:T(8,128)(2,1)S(1)}, bf16[16,8192]{1,0:T(8,128)(2,1)S(1)}, u32[]{:S(2)}, u32[]{:S(2)}) collective-permute-start(bf16[16,8192]{1,0:T(8,128)(2,1)S(1)} %fusion.66), channel_id=1, source_target_pairs={{0,2},{1,3},{2,0},{3,1},{4,6},{5,7},{6,4},{7,5},{8,10},{9,11},{10,... | collective-permute-start | bytes 786440 | tf_op jit(solution)/shard_map/ppermute | solution.py:173
  310.6 13.3 %collective-permute-start.19 = (bf16[16,8192]{1,0:T(8,128)(2,1)S(1)}, bf16[16,8192]{1,0:T(8,128)(2,1)S(1)}, u32[]{:S(2)}, u32[]{:S(2)}) collective-permute-start(bf16[16,8192]{1,0:T(8,128)(2,1)S(1)} %fusion.91), channel_id=1, source_target_pairs={{96,0},{97,1},{98,2},{99,3},{100,4},{101,5},{102,6},{103,7},{104,8... | collective-permute-start | bytes 786440 | tf_op jit(solution)/shard_map/ppermute | solution.py:188
  311.9 12.0 %collective-permute-start.18 = (bf16[16,8192]{1,0:T(8,128)(2,1)S(1)}, bf16[16,8192]{1,0:T(8,128)(2,1)S(1)}, u32[]{:S(2)}, u32[]{:S(2)}) collective-permute-start(bf16[16,8192]{1,0:T(8,128)(2,1)S(1)} %fusion.91), channel_id=1, source_target_pairs={{64,0},{96,32},{65,1},{97,33},{66,2},{98,34},{67,3},{99,35},{68,4}... | collective-permute-start | bytes 786440 | tf_op jit(solution)/shard_map/ppermute | solution.py:188
  313.2 11.1 %collective-permute-start.17 = (bf16[16,8192]{1,0:T(8,128)(2,1)S(1)}, bf16[16,8192]{1,0:T(8,128)(2,1)S(1)}, u32[]{:S(2)}, u32[]{:S(2)}) collective-permute-start(bf16[16,8192]{1,0:T(8,128)(2,1)S(1)} %fusion.91), channel_id=1, source_target_pairs={{32,0},{64,32},{96,64},{33,1},{65,33},{97,65},{34,2},{66,34},{98,6... | collective-permute-start | bytes 786440 | tf_op jit(solution)/shard_map/ppermute | solution.py:188
  314.7 15.9 %collective-permute-start.14 = (bf16[32,8192]{1,0:T(8,128)(2,1)S(1)}, bf16[32,8192]{1,0:T(8,128)(2,1)S(1)}, u32[]{:S(2)}, u32[]{:S(2)}) collective-permute-start(bf16[32,8192]{1,0:T(8,128)(2,1)S(1)} %fusion.45), channel_id=1, source_target_pairs={{32,0},{0,32},{33,1},{1,33},{34,2},{2,34},{35,3},{3,35},{36,4},{4,... | collective-permute-start | bytes 1572872 | tf_op jit(solution)/shard_map/ppermute | solution.py:198
  (11 other events, 20.8 us)
Sparse Core Ops, SparseCore 0:
  63.0 50.3 all-gather.1

commit v7 on v6

--- a/solution.py
+++ b/solution.py
@@ -181,7 +181,7 @@
             )
             term_low = layer_term.astype(jnp.bfloat16)
             previous = term_low
-            if n_sec == 4 and c == len(sizes) - 1:
+            if n_sec == 4 and c >= len(sizes) - 2:
                 total = layer_term
                 for shift in range(1, n_sec):
                     pairs = [(l + shift, l) for l in range(n_sec - shift)]

time: 346 us -> 355 us (1.026)
  waiting for transfers between devices: 103 us -> 115 us
    ppermute x3 -> x6, waiting for transfers between devices: 4.97 us -> 22.5 us  [on_device(): total = total + lax.ppermute(term_low, 'section', pairs).astype(jnp.float32)]
    ppermute x3 -> x2, waiting for transfers between devices: 17.3 us -> 11.5 us  [on_device(): last = lax.ppermute(carry.astype(jnp.bfloat16), 'section', [(1, 0), (0, 1)])]
    ppermute x3 -> x2, starting transfers between devices: 10.4 us -> 5.84 us  [on_device(): last = lax.ppermute(carry.astype(jnp.bfloat16), 'section', [(1, 0), (0, 1)])]
    ppermute x3 -> x6, starting transfers between devices: 3.88 us -> 7.74 us  [on_device(): total = total + lax.ppermute(term_low, 'section', pairs).astype(jnp.float32)]
  transfers between devices with their start and end apart: 26 -> 26, of which waited for: 15 -> 15; matrix products, arithmetic and copies ran while one was open for 42% -> 41% of each run, Pallas kernels for 0% -> 0%
where the time goes in v7:
time: 355 us; the launch traced here: 349 us
  waiting for transfers between devices  115 us (32%)
  matrix products  76.2 us (21%)
  other arithmetic  58.6 us (17%)
  starting transfers between devices  50.2 us (14%)
  local copies, waits for them, and re-layouts  34.3 us (10%)
  between operations  15.3 us (4%)
    ppermute x4, waiting for transfers between devices, on_device(): got2 = lax.ppermute(other, 'tensor', chip_pairs)  23.7 us
    ppermute x6, waiting for transfers between devices, on_device(): total = total + lax.ppermute(term_low, 'section', pairs).astype(jnp.float32)  22.5 us
    all_to_all x1, waiting for transfers between devices, on_device(): lax.all_to_all(spread, 'sample', 0, 0, tiled=True).reshape(pooled_rows, -1)  22.1 us
    sub x2, other arithmetic, attend_group(): exponent = jnp.exp(scores - row_max)  21 us
    dot_general x4, matrix products, on_device(): lax.dot_general(grad_rows_c, weight_local, (((2, 3), (1, 2)), ((), ())),...  20.1 us
    convert_element_type x2, other arithmetic, attend_group(): weights_low = softmax_w.astype(jnp.bfloat16)  17.1 us
    all_to_all x2, waiting for transfers between devices, on_device(): parts = lax.all_to_all(pool_grad, 'sample', 0, 0, tiled=False)  16.5 us
    dot_general x2, matrix products, attend_group(): jnp.einsum('rgd,kd->rgk', grad_grp, value_rows, preferred_element_type=jn...  13.6 us
  transfers between devices with their start and end apart: 26, of which 15 were waited for; matrix products, arithmetic and copies ran while one was open for 41% of the time, Pallas kernels for 0%

profile of v7, /device:TPU:0, one launch (start us, length us, event | category | flops | bytes accessed | tf_op | source)
XLA Modules:
  0.0 349.1 jit_solution(8363076865553293443)
XLA Ops:
  10.3 4.6 %all-to-all-start = ((bf16[4,128,512]{1,2,0:T(8,128)(2,1)}), bf16[4,128,512]{1,2,0:T(8,128)(2,1)S(1)}, u32[]{:S(2)}, u32[]{:S(2)}) async-start(bf16[4,128,512]{1,2,0:T(8,128)(2,1)} %bitcast.6), calls=%async_computation | async-start | bytes 1048576 | tf_op jit(solution)/shard_map/all_to_all | solution.py:85
  15.2 10.0 %all-to-all-done = bf16[4,128,512]{1,2,0:T(8,128)(2,1)S(1)} async-done(((bf16[4,128,512]{1,2,0:T(8,128)(2,1)}), bf16[4,128,512]{1,2,0:T(8,128)(2,1)S(1)}, u32[]{:S(2)}, u32[]{:S(2)}) %all-to-all-start) | async-done | bytes 524320 | tf_op jit(solution)/shard_map/all_to_all | solution.py:85
  26.4 1.5 broadcast_in_dim.92
  27.8 5.6 %all-to-all-start.1 = ((bf16[8,512,256]{2,1,0:T(8,128)(2,1)}), bf16[8,512,256]{2,1,0:T(8,128)(2,1)}, u32[]{:S(2)}, u32[]{:S(2)}) async-start(bf16[8,512,256]{2,1,0:T(8,128)(2,1)} %broadcast_in_dim.92), calls=%async_computation.1 | async-start | bytes 4194304 | tf_op jit(solution)/shard_map/all_to_all | solution.py:94
  38.1 22.1 %all-to-all-done.1 = bf16[8,512,256]{2,1,0:T(8,128)(2,1)} async-done(((bf16[8,512,256]{2,1,0:T(8,128)(2,1)}), bf16[8,512,256]{2,1,0:T(8,128)(2,1)}, u32[]{:S(2)}, u32[]{:S(2)}) %all-to-all-start.1) | async-done | bytes 2097184 | tf_op jit(solution)/shard_map/all_to_all | solution.py:94
  60.2 2.6 fusion.95
  62.9 3.2 fusion.56
  66.0 10.8 %fusion.104 = (f32[128,8]{0,1:T(8,128)S(1)}, f32[128,8,4224]{0,2,1:T(8,128)}) fusion(f32[4224,128,8]{1,0,2:T(8,128)S(1)} %fusion.56, pred[128,4224]{0,1:T(8,128)(4,1)S(1)} %pad_add_fusion), kind=kOutput, calls=%fused_computation.199 | output fusion | flops 17305728 | bytes 35147776 | tf_op jit(solution)/shard_map/sub | solution.py:36
  76.8 6.8 %fusion.18 = bf16[128,8,4224]{0,2,1:T(8,128)(2,1)S(1)} fusion(f32[128,8,4224]{0,2,1:T(8,128)} %get-tuple-element.96, f32[128,8]{0,1:T(8,128)S(1)} %get-tuple-element.95), kind=kLoop, calls=%fused_computation.30 | loop fusion | flops 8650752 | bytes 25956352 | tf_op jit(solution)/shard_map/convert_element_type | solution.py:38
  83.7 2.4 fusion.26
  86.2 2.5 fusion.38
  89.2 1.3 slice-done.3
  90.5 7.2 %fusion.3 = bf16[128,8,4224]{0,2,1:T(8,128)(2,1)} fusion(f32[128,8]{0,1:T(8,128)S(1)} %fusion.38, f32[128,8,4224]{0,2,1:T(8,128)S(1)} %bitcast.297, f32[128,8]{0,1:T(8,128)S(1)} %get-tuple-element.95, bf16[128,128]{1,0:T(8,128)(2,1)S(1)} %copy-done.30, bf16[4096,128]{1,0:T(8,128)(2,1)} %get-tuple-element.69, bf16[128,2,8,128]{0,3,2,1:T(8,128)(2,1)} %bitcast.328), kind=kOutput, calls=%fused_computation.6 | convolution fusion | flops 1126760448 | bytes 27303936 | tf_op jit(solution)/shard_map/rgd,kd->rgk/dot_general | solution.py:43
  97.8 5.9 %fusion.25 = bf16[4224,128]{1,0:T(8,128)(2,1)S(1)} fusion(bf16[128,8,4224]{0,2,1:T(8,128)(2,1)} %fusion.3, bf16[128,2,8,128]{0,3,2,1:T(8,128)(2,1)} %bitcast.320), kind=kOutput, calls=%fused_computation.41 | convolution fusion | flops 1108377600 | bytes 9994240 | tf_op jit(solution)/shard_map/rgk,rgd->kd/dot_general | solution.py:48
  105.9 1.5 pad_maximum_fusion
  107.4 4.3 %all-to-all-start.2 = ((bf16[8,512,256]{2,1,0:T(8,128)(2,1)}), bf16[8,512,256]{2,1,0:T(8,128)(2,1)}, u32[]{:S(2)}, u32[]{:S(2)}) async-start(bf16[8,512,256]{2,1,0:T(8,128)(2,1)} %pad_maximum_fusion), calls=%async_computation.2 | async-start | bytes 4194304 | tf_op jit(solution)/shard_map/all_to_all | solution.py:118
  111.8 1.6 all-gather.2.cloned.1.call-done
  113.4 2.7 fusion.96
  116.1 2.4 fusion.55
  118.5 10.2 %fusion.103 = (f32[128,8]{0,1:T(8,128)S(1)}, f32[128,8,4224]{0,2,1:T(8,128)}) fusion(f32[4224,128,8]{1,0,2:T(8,128)S(1)} %fusion.55, pred[128,4224]{0,1:T(8,128)(4,1)S(1)} %pad_add_fusion), kind=kOutput, calls=%fused_computation.198 | output fusion | flops 17305728 | bytes 35147776 | tf_op jit(solution)/shard_map/sub | solution.py:36
  128.8 10.3 %fusion.19 = bf16[128,8,4224]{0,2,1:T(8,128)(2,1)} fusion(f32[128,8,4224]{0,2,1:T(8,128)} %get-tuple-element.94, f32[128,8]{0,1:T(8,128)S(1)} %get-tuple-element.93), kind=kLoop, calls=%fused_computation.31 | loop fusion | flops 8650752 | bytes 25956352 | tf_op jit(solution)/shard_map/convert_element_type | solution.py:38
  139.1 6.8 %fusion.39 = f32[128,8]{0,1:T(8,128)S(1)} fusion(bf16[128,8,4224]{0,2,1:T(8,128)(2,1)} %fusion.19, bf16[128,128]{1,0:T(8,128)(2,1)S(1)} %copy-done.29, bf16[4096,128]{1,0:T(8,128)(2,1)S(1)} %copy-done.18, bf16[128,1,8,128]{3,0,2,1:T(8,128)(2,1)S(1)} %copy-done.21), kind=kOutput, calls=%fused_computation.86 | convolution fusion | flops 1109851136 | bytes 9998336 | tf_op jit(solution)/shard_map/rgk,kd->rgd/dot_general | solution.py:39
  146.0 6.4 %fusion.2 = bf16[128,8,4224]{0,2,1:T(8,128)(2,1)} fusion(f32[128,8]{0,1:T(8,128)S(1)} %fusion.39, f32[128,8,4224]{0,2,1:T(8,128)S(1)} %bitcast.299, f32[128,8]{0,1:T(8,128)S(1)} %get-tuple-element.93, bf16[128,128]{1,0:T(8,128)(2,1)S(1)} %copy-done.29, bf16[4096,128]{1,0:T(8,128)(2,1)} %get-tuple-element.71, bf16[128,2,8,128]{0,3,2,1:T(8,128)(2,1)S(1)} %bitcast.330), kind=kOutput, calls=%fused_computation.3 | convolution fusion | flops 1126760448 | bytes 27303936 | tf_op jit(solution)/shard_map/rgd,kd->rgk/dot_general | solution.py:43
  152.3 6.0 %fusion.28 = bf16[4224,128]{1,0:T(8,128)(2,1)S(1)} fusion(bf16[128,8,4224]{0,2,1:T(8,128)(2,1)} %fusion.19, bf16[128,2,8,128]{0,3,2,1:T(8,128)(2,1)S(1)} %bitcast.331), kind=kOutput, calls=%fused_computation.44 | convolution fusion | flops 1107836928 | bytes 9994240 | tf_op jit(solution)/shard_map/rgk,rgd->kd/dot_general | solution.py:51
  159.4 2.5 fusion.27
  163.1 1.5 pad_maximum_fusion.1
  164.6 4.2 %all-to-all-start.3 = ((bf16[8,512,256]{2,1,0:T(8,128)(2,1)}), bf16[8,512,256]{2,1,0:T(8,128)(2,1)S(1)}, u32[]{:S(2)}, u32[]{:S(2)}) async-start(bf16[8,512,256]{2,1,0:T(8,128)(2,1)} %pad_maximum_fusion.1), calls=%async_computation.3 | async-start | bytes 4194304 | tf_op jit(solution)/shard_map/all_to_all | solution.py:118
  169.6 5.8 %fusion.41 = bf16[128,1,8,128]{0,3,2,1:T(8,128)(2,1)} fusion(bf16[128,8,4224]{0,2,1:T(8,128)(2,1)} %fusion.3, bf16[128,128]{1,0:T(8,128)(2,1)S(1)} %copy-done.25, bf16[4096,128]{1,0:T(8,128)(2,1)} %copy-done.1), kind=kOutput, calls=%fused_computation.88 | convolution fusion | flops 1109721088 | bytes 9994240 | tf_op jit(solution)/shard_map/rgk,kd->rgd/dot_general | solution.py:115
  175.5 2.0 reduce
  178.3 16.5 %all-to-all-done.3 = bf16[8,512,256]{2,1,0:T(8,128)(2,1)S(1)} async-done(((bf16[8,512,256]{2,1,0:T(8,128)(2,1)}), bf16[8,512,256]{2,1,0:T(8,128)(2,1)S(1)}, u32[]{:S(2)}, u32[]{:S(2)}) %all-to-all-start.3) | async-done | bytes 2097184 | tf_op jit(solution)/shard_map/all_to_all | solution.py:118
  197.0 1.8 pad_maximum_fusion.4
  198.7 4.0 %all-to-all-start.4 = ((bf16[4,128,512]{2,1,0:T(8,128)(2,1)}), bf16[4,128,512]{2,1,0:T(8,128)(2,1)S(1)}, u32[]{:S(2)}, u32[]{:S(2)}) async-start(bf16[4,128,512]{2,1,0:T(8,128)(2,1)} %pad_maximum_fusion.4), calls=%async_computation.4 | async-start | bytes 1048576 | tf_op jit(solution)/shard_map/all_to_all | solution.py:126
  203.6 8.2 %fusion.6 = bf16[4,48,8192]{2,1,0:T(8,128)(2,1)} fusion(bf16[8192,2,256]{2,1,0:T(2,128)(2,1)} %bitcast.350, bf16[4,128,2,256]{3,1,0,2:T(8,128)(2,1)S(1)} %reshape.274), kind=kOutput, calls=%fused_computation.13 | convolution fusion | flops 1612185600 | bytes 11730944 | tf_op jit(solution)/shard_map/dot_general | solution.py:155
  211.7 1.3 all-to-all-done.4
  214.3 2.7 dynamic-slice_bitcast_fusion
  217.4 4.9 %fusion.40 = bf16[128,1,8,128]{0,3,2,1:T(8,128)(2,1)S(1)} fusion(bf16[128,8,4224]{0,2,1:T(8,128)(2,1)} %fusion.2, bf16[128,128]{1,0:T(8,128)(2,1)S(1)} %copy-done.24, bf16[4096,128]{1,0:T(8,128)(2,1)S(1)} %get-tuple-element.72), kind=kOutput, calls=%fused_computation.87 | convolution fusion | flops 1109721088 | bytes 9994240 | tf_op jit(solution)/shard_map/rgk,kd->rgd/dot_general | solution.py:115
  229.1 2.2 convert_add_fusion
  231.5 2.4 collective-permute-start.1
  233.9 6.4 %fusion.7 = bf16[4,32,8192]{2,1,0:T(8,128)(2,1)S(1)} fusion(bf16[4,32,2,256]{3,1,0,2:T(8,128)(2,1)S(1)} %get-tuple-element.28, bf16[8192,2,256,1]{2,1,0,3:T(2,128)(2,1)} %bitcast.351), kind=kOutput, calls=%fused_computation.16 | convolution fusion | flops 1074790400 | bytes 10616832 | tf_op jit(solution)/shard_map/dot_general | solution.py:155
  240.6 12.5 %collective-permute-done.1 = bf16[48,8192]{1,0:T(8,128)(2,1)S(1)} collective-permute-done((bf16[48,8192]{1,0:T(8,128)(2,1)S(1)}, bf16[48,8192]{1,0:T(8,128)(2,1)S(1)}, u32[]{:S(2)}, u32[]{:S(2)}) %collective-permute-start.1) | collective-permute-done | bytes 786464 | tf_op jit(solution)/shard_map/ppermute | solution.py:173
  254.0 1.3 collective-permute-start.3
  256.4 2.3 collective-permute-start.6
  258.6 2.9 fusion.8
  261.7 9.7 %collective-permute-done.6 = bf16[32,8192]{1,0:T(8,128)(2,1)S(1)} collective-permute-done((bf16[32,8192]{1,0:T(8,128)(2,1)S(1)}, bf16[32,8192]{1,0:T(8,128)(2,1)S(1)}, u32[]{:S(2)}, u32[]{:S(2)}) %collective-permute-start.6) | collective-permute-done | bytes 524320 | tf_op jit(solution)/shard_map/ppermute | solution.py:173
  272.3 1.3 collective-permute-start.8
  274.3 1.9 collective-permute-done.3
  276.5 3.0 collective-permute-start.4
  279.8 2.4 collective-permute-start.11
  282.2 2.7 fusion.9
  285.0 3.4 collective-permute-done.8
  288.6 2.8 collective-permute-start.9
  291.4 7.5 %collective-permute-done.4 = bf16[48,8192]{1,0:T(8,128)(2,1)S(1)} collective-permute-done((bf16[48,8192]{1,0:T(8,128)(2,1)S(1)}, bf16[48,8192]{1,0:T(8,128)(2,1)S(1)}, u32[]{:S(2)}, u32[]{:S(2)}) %collective-permute-start.4) | collective-permute-done | bytes 786464 | tf_op jit(solution)/shard_map/ppermute | solution.py:198
  300.0 1.3 collective-permute-start.14
  301.3 1.3 collective-permute-start.13
  302.6 1.3 collective-permute-start.12
  304.0 2.2 collective-permute-start.16
  306.2 4.0 %collective-permute-done.9 = bf16[32,8192]{1,0:T(8,128)(2,1)S(1)} collective-permute-done((bf16[32,8192]{1,0:T(8,128)(2,1)S(1)}, bf16[32,8192]{1,0:T(8,128)(2,1)S(1)}, u32[]{:S(2)}, u32[]{:S(2)}) %collective-permute-start.9) | collective-permute-done | bytes 524320 | tf_op jit(solution)/shard_map/ppermute | solution.py:198
  310.4 1.6 collective-permute-done.16
  312.5 1.3 collective-permute-start.19
  313.8 1.3 collective-permute-start.18
  315.1 16.1 %collective-permute-done.14 = bf16[32,8192]{1,0:T(8,128)(2,1)S(1)} collective-permute-done((bf16[32,8192]{1,0:T(8,128)(2,1)S(1)}, bf16[32,8192]{1,0:T(8,128)(2,1)S(1)}, u32[]{:S(2)}, u32[]{:S(2)}) %collective-permute-start.14) | collective-permute-done | bytes 524320 | tf_op jit(solution)/shard_map/ppermute | solution.py:188
  333.0 2.1 collective-permute-done.19
  335.1 4.3 %collective-permute-done.17 = bf16[16,8192]{1,0:T(8,128)(2,1)S(1)} collective-permute-done((bf16[16,8192]{1,0:T(8,128)(2,1)S(1)}, bf16[16,8192]{1,0:T(8,128)(2,1)S(1)}, u32[]{:S(2)}, u32[]{:S(2)}) %collective-permute-start.17) | collective-permute-done | bytes 262176 | tf_op jit(solution)/shard_map/ppermute | solution.py:188
  339.7 2.3 maximum_bitcast_fusion
  (195 shorter events, 36.2 us)
Async XLA Ops:
  7.2 7.7 %copy-start.19 = (bf16[1,128,2048]{2,1,0:T(8,128)(2,1)S(1)}, bf16[1,128,2048]{2,1,0:T(8,128)(2,1)}, u32[]{:S(2)}) copy-start(bf16[1,128,2048]{2,1,0:T(8,128)(2,1)} %param.15) | copy-start | bytes 1572868
  10.3 14.9 %all-to-all-start = ((bf16[4,128,512]{1,2,0:T(8,128)(2,1)}), bf16[4,128,512]{1,2,0:T(8,128)(2,1)S(1)}, u32[]{:S(2)}, u32[]{:S(2)}) async-start(bf16[4,128,512]{1,2,0:T(8,128)(2,1)} %bitcast.6), calls=%async_computation | async-start | bytes 1048576 | tf_op jit(solution)/shard_map/all_to_all | solution.py:85
  15.2 18.3 %copy-start.7 = (bf16[1,128,2048]{1,2,0:T(8,128)(2,1)}, bf16[1,128,2048]{1,2,0:T(8,128)(2,1)S(1)}, u32[]{:S(2)}) copy-start(bf16[1,128,2048]{1,2,0:T(8,128)(2,1)S(1)} %copy.113) | copy-start | bytes 1572868
  27.8 5.7 %copy-start.20 = (bf16[1,128,2048]{2,1,0:T(8,128)(2,1)S(1)}, bf16[1,128,2048]{2,1,0:T(8,128)(2,1)}, u32[]{:S(2)}) copy-start(bf16[1,128,2048]{2,1,0:T(8,128)(2,1)} %param.12) | copy-start | bytes 1572868
  27.8 32.4 %all-to-all-start.1 = ((bf16[8,512,256]{2,1,0:T(8,128)(2,1)}), bf16[8,512,256]{2,1,0:T(8,128)(2,1)}, u32[]{:S(2)}, u32[]{:S(2)}) async-start(bf16[8,512,256]{2,1,0:T(8,128)(2,1)} %broadcast_in_dim.92), calls=%async_computation.1 | async-start | bytes 4194304 | tf_op jit(solution)/shard_map/all_to_all | solution.py:94
  33.4 3.1 copy-start.27
  33.4 79.9 %all-gather.2.cloned.1.call-start = ((), (), s32[]{:S(2)}) async-start(), calls=%async_computation.5 | async-start | bytes 2359296 | tf_op jit(solution)/shard_map/all_gather | solution.py:97
  33.8 29.0 %copy-start.4 = (bf16[1,128,2048]{1,2,0:T(8,128)(2,1)}, bf16[1,128,2048]{1,2,0:T(8,128)(2,1)S(1)}, u32[]{:S(2)}) copy-start(bf16[1,128,2048]{1,2,0:T(8,128)(2,1)S(1)} %copy.111) | copy-start | bytes 1572868
  62.8 3.2 copy-start.1
  76.8 6.8 %copy-start.8 = (bf16[1,128,2048]{1,2,0:T(8,128)(2,1)S(1)}, bf16[1,128,2048]{1,2,0:T(8,128)(2,1)}, u32[]{:S(2)}) copy-start(bf16[1,128,2048]{1,2,0:T(8,128)(2,1)} %copy-done.7) | copy-start | bytes 1572868
  83.7 5.1 %slice-start = ((s8[17301504]{0:T(1024)(128)(4,1)}), s8[4194304]{0:T(1024)(128)(4,1)S(1)}, s32[]{:S(2)}) async-start(s8[17301504]{0:T(1024)(128)(4,1)} %bitcast.296), calls=%async_computation.6 | async-start | bytes 8388608
  83.7 5.1 %slice-start.1 = ((s8[17301504]{0:T(1024)(128)(4,1)}), s8[4194304]{0:T(1024)(128)(4,1)S(1)}, s32[]{:S(2)}) async-start(s8[17301504]{0:T(1024)(128)(4,1)} %bitcast.296), calls=%async_computation.7 | async-start | bytes 8388608
  83.7 5.5 %slice-start.2 = ((s8[17301504]{0:T(1024)(128)(4,1)}), s8[4194304]{0:T(1024)(128)(4,1)S(1)}, s32[]{:S(2)}) async-start(s8[17301504]{0:T(1024)(128)(4,1)} %bitcast.296), calls=%async_computation.8 | async-start | bytes 8388608
  86.1 2.6 copy-start.2
  86.2 4.3 %slice-start.3 = ((s8[17301504]{0:T(1024)(128)(4,1)}), s8[4194304]{0:T(1024)(128)(4,1)S(1)}, s32[]{:S(2)}) async-start(s8[17301504]{0:T(1024)(128)(4,1)} %bitcast.296), calls=%async_computation.9 | async-start | bytes 8388608
  86.2 4.3 %slice-start.4 = ((s8[17301504]{0:T(1024)(128)(4,1)}), s8[524288]{0:T(1024)(128)(4,1)S(1)}, s32[]{:S(2)}) async-start(s8[17301504]{0:T(1024)(128)(4,1)} %bitcast.296), calls=%async_computation.10 | async-start | bytes 1048576
  107.4 57.2 %all-to-all-start.2 = ((bf16[8,512,256]{2,1,0:T(8,128)(2,1)}), bf16[8,512,256]{2,1,0:T(8,128)(2,1)}, u32[]{:S(2)}, u32[]{:S(2)}) async-start(bf16[8,512,256]{2,1,0:T(8,128)(2,1)} %pad_maximum_fusion), calls=%async_computation.2 | async-start | bytes 4194304 | tf_op jit(solution)/shard_map/all_to_all | solution.py:118
  111.8 4.3 %copy-start.24 = (bf16[128,128]{1,0:T(8,128)(2,1)S(1)}, bf16[128,128]{1,0:T(8,128)(2,1)}, u32[]{:S(2)}) copy-start(bf16[128,128]{1,0:T(8,128)(2,1)} %get-tuple-element.84) | copy-start | bytes 98308
  113.4 2.7 copy-start.5
  128.7 10.3 %copy-start.18 = (bf16[4096,128]{1,0:T(8,128)(2,1)S(1)}, bf16[4096,128]{1,0:T(8,128)(2,1)}, u32[]{:S(2)}) copy-start(bf16[4096,128]{1,0:T(8,128)(2,1)} %get-tuple-element.71) | copy-start | bytes 3145732
  128.7 10.3 %copy-start.21 = (bf16[128,1,8,128]{3,0,2,1:T(8,128)(2,1)S(1)}, bf16[128,1,8,128]{3,0,2,1:T(8,128)(2,1)}, u32[]{:S(2)}) copy-start(bf16[128,1,8,128]{3,0,2,1:T(8,128)(2,1)} %copy.173) | copy-start | bytes 786436
  128.7 10.3 %copy-start.29 = (bf16[128,128]{1,0:T(8,128)(2,1)S(1)}, bf16[128,128]{1,0:T(8,128)(2,1)}, u32[]{:S(2)}) copy-start(bf16[128,128]{1,0:T(8,128)(2,1)} %get-tuple-element.82) | copy-start | bytes 98308
  128.7 17.2 %slice-start.5 = ((s8[17301504]{0:T(1024)(128)(4,1)}), s8[4194304]{0:T(1024)(128)(4,1)S(1)}, s32[]{:S(2)}) async-start(s8[17301504]{0:T(1024)(128)(4,1)} %bitcast.298), calls=%async_computation.11 | async-start | bytes 8388608
  128.7 17.2 %slice-start.6 = ((s8[17301504]{0:T(1024)(128)(4,1)}), s8[4194304]{0:T(1024)(128)(4,1)S(1)}, s32[]{:S(2)}) async-start(s8[17301504]{0:T(1024)(128)(4,1)} %bitcast.298), calls=%async_computation.12 | async-start | bytes 8388608
  128.7 17.2 %slice-start.7 = ((s8[17301504]{0:T(1024)(128)(4,1)}), s8[4194304]{0:T(1024)(128)(4,1)S(1)}, s32[]{:S(2)}) async-start(s8[17301504]{0:T(1024)(128)(4,1)} %bitcast.298), calls=%async_computation.13 | async-start | bytes 8388608
  128.8 17.2 %slice-start.8 = ((s8[17301504]{0:T(1024)(128)(4,1)}), s8[4194304]{0:T(1024)(128)(4,1)S(1)}, s32[]{:S(2)}) async-start(s8[17301504]{0:T(1024)(128)(4,1)} %bitcast.298), calls=%async_computation.14 | async-start | bytes 8388608
  139.0 6.9 %slice-start.9 = ((s8[17301504]{0:T(1024)(128)(4,1)}), s8[524288]{0:T(1024)(128)(4,1)S(1)}, s32[]{:S(2)}) async-start(s8[17301504]{0:T(1024)(128)(4,1)} %bitcast.298), calls=%async_computation.15 | async-start | bytes 1048576
  139.0 6.9 %copy-start.9 = (bf16[1,128,2048]{1,2,0:T(8,128)(2,1)S(1)}, bf16[1,128,2048]{1,2,0:T(8,128)(2,1)}, u32[]{:S(2)}) copy-start(bf16[1,128,2048]{1,2,0:T(8,128)(2,1)} %copy-done.7) | copy-start | bytes 1572868
  152.3 7.1 %copy-start.6 = (bf16[1,128,2048]{1,2,0:T(8,128)(2,1)S(1)}, bf16[1,128,2048]{1,2,0:T(8,128)(2,1)}, u32[]{:S(2)}) copy-start(bf16[1,128,2048]{1,2,0:T(8,128)(2,1)} %copy-done.4) | copy-start | bytes 1572868
  152.3 7.1 %copy-start.34 = (bf16[128,8,4224]{0,2,1:T(8,128)(2,1)S(1)}, bf16[128,8,4224]{0,2,1:T(8,128)(2,1)}, u32[]{:S(2)}) copy-start(bf16[128,8,4224]{0,2,1:T(8,128)(2,1)} %fusion.2) | copy-start | bytes 25952260
  164.6 4.2 %copy-start.28 = (bf16[1,8192]{1,0:T(2,128)(2,1)S(1)}, bf16[1,8192]{1,0:T(2,128)(2,1)}, u32[]{:S(2)}) copy-start(bf16[1,8192]{1,0:T(2,128)(2,1)} %param.20) | copy-start | bytes 49156
  164.6 5.0 %copy-start.25 = (bf16[128,128]{1,0:T(8,128)(2,1)S(1)}, bf16[128,128]{1,0:T(8,128)(2,1)}, u32[]{:S(2)}) copy-start(bf16[128,128]{1,0:T(8,128)(2,1)} %get-tuple-element.83) | copy-start | bytes 98308
  164.6 30.1 %all-to-all-start.3 = ((bf16[8,512,256]{2,1,0:T(8,128)(2,1)}), bf16[8,512,256]{2,1,0:T(8,128)(2,1)S(1)}, u32[]{:S(2)}, u32[]{:S(2)}) async-start(bf16[8,512,256]{2,1,0:T(8,128)(2,1)} %pad_maximum_fusion.1), calls=%async_computation.3 | async-start | bytes 4194304 | tf_op jit(solution)/shard_map/all_to_all | solution.py:118
  195.8 6.9 %copy-start.16 = (bf16[512,256]{0,1:T(8,128)(2,1)S(1)}, bf16[512,256]{0,1:T(8,128)(2,1)}, u32[]{:S(2)}) copy-start(bf16[512,256]{0,1:T(8,128)(2,1)} %copy.129) | copy-start | bytes 786436
  198.7 14.3 %all-to-all-start.4 = ((bf16[4,128,512]{2,1,0:T(8,128)(2,1)}), bf16[4,128,512]{2,1,0:T(8,128)(2,1)S(1)}, u32[]{:S(2)}, u32[]{:S(2)}) async-start(bf16[4,128,512]{2,1,0:T(8,128)(2,1)} %pad_maximum_fusion.4), calls=%async_computation.4 | async-start | bytes 1048576 | tf_op jit(solution)/shard_map/all_to_all | solution.py:126
  203.5 8.2 %copy-start.12 = (bf16[4,128,2,256]{3,1,0,2:T(8,128)(2,1)}, bf16[4,128,2,256]{3,1,0,2:T(8,128)(2,1)S(1)}, u32[]{:S(2)}) copy-start(bf16[4,128,2,256]{3,1,0,2:T(8,128)(2,1)S(1)} %reshape.274) | copy-start | bytes 1572868
  217.0 5.3 %copy-start.23 = (bf16[128,1,8,128]{0,3,2,1:T(8,128)(2,1)S(1)}, bf16[128,1,8,128]{0,3,2,1:T(8,128)(2,1)}, u32[]{:S(2)}) copy-start(bf16[128,1,8,128]{0,3,2,1:T(8,128)(2,1)} %fusion.41) | copy-start | bytes 786436
  217.0 6.4 %copy-start.3 = (bf16[4224,128]{1,0:T(8,128)(2,1)S(1)}, bf16[4224,128]{1,0:T(8,128)(2,1)}, u32[]{:S(2)}) copy-start(bf16[4224,128]{1,0:T(8,128)(2,1)} %copy-done.2) | copy-start | bytes 3244036
  217.0 12.2 %collective-permute-start = (bf16[2,48,8192]{2,1,0:T(8,128)(2,1)}, bf16[2,48,8192]{2,1,0:T(8,128)(2,1)}, u32[]{:S(2)}, u32[]{:S(2)}) collective-permute-start(bf16[2,48,8192]{2,1,0:T(8,128)(2,1)} %dynamic-slice_bitcast_fusion), channel_id=1, source_target_pairs={{0,1},{1,0},{2,3},{3,2},{4,5},{5,4},{6,7},{7,6},{8,9},{9,8},{10,11... | collective-permute-start | bytes 4718600 | tf_op jit(solution)/shard_map/ppermute | solution.py:166
  222.3 4.9 %copy-start.11 = (f32[1,128,4,2,128]{1,4,0,3,2:T(8,128)S(1)}, f32[1,128,4,2,128]{1,4,0,3,2:T(8,128)}, u32[]{:S(2)}) copy-start(f32[1,128,4,2,128]{1,4,0,3,2:T(8,128)} %get-tuple-element.74) | copy-start | bytes 1572868
  222.3 5.9 %copy-start.10 = (f32[1,128,4,2,128]{1,4,0,3,2:T(8,128)S(1)}, f32[1,128,4,2,128]{1,4,0,3,2:T(8,128)}, u32[]{:S(2)}) copy-start(f32[1,128,4,2,128]{1,4,0,3,2:T(8,128)} %get-tuple-element.73) | copy-start | bytes 1572868
  231.5 21.5 %collective-permute-start.1 = (bf16[48,8192]{1,0:T(8,128)(2,1)S(1)}, bf16[48,8192]{1,0:T(8,128)(2,1)S(1)}, u32[]{:S(2)}, u32[]{:S(2)}) collective-permute-start(bf16[48,8192]{1,0:T(8,128)(2,1)S(1)} %fusion.54), channel_id=1, source_target_pairs={{0,2},{1,3},{2,0},{3,1},{4,6},{5,7},{6,4},{7,5},{8,10},{9,11},{10,... | collective-permute-start | bytes 2359304 | tf_op jit(solution)/shard_map/ppermute | solution.py:173
  233.9 24.8 %slice-start.12 = ((s8[8388608]{0:T(1024)(128)(4,1)}), s8[4194304]{0:T(1024)(128)(4,1)S(1)}, s32[]{:S(2)}) async-start(s8[8388608]{0:T(1024)(128)(4,1)} %bitcast.352), calls=%async_computation.18 | async-start | bytes 8388608
  240.2 12.8 %copy-start = (bf16[1,128,8192]{2,1,0:T(8,128)(2,1)S(1)}, bf16[1,128,8192]{2,1,0:T(8,128)(2,1)}, u32[]{:S(2)}) copy-start(bf16[1,128,8192]{2,1,0:T(8,128)(2,1)} %param.19) | copy-start | bytes 6291460
  240.3 18.4 %slice-start.13 = ((s8[8388608]{0:T(1024)(128)(4,1)}), s8[4194304]{0:T(1024)(128)(4,1)S(1)}, s32[]{:S(2)}) async-start(s8[8388608]{0:T(1024)(128)(4,1)} %bitcast.352), calls=%async_computation.19 | async-start | bytes 8388608
  240.4 15.7 %collective-permute-start.5 = (bf16[2,32,8192]{2,1,0:T(8,128)(2,1)S(1)}, bf16[2,32,8192]{2,1,0:T(8,128)(2,1)S(1)}, u32[]{:S(2)}, u32[]{:S(2)}) collective-permute-start(bf16[2,32,8192]{2,1,0:T(8,128)(2,1)S(1)} %dynamic-slice_bitcast_fusion.2), channel_id=1, source_target_pairs={{0,1},{1,0},{2,3},{3,2},{4,5},{5,4},{6,7},{7,6},{8,9},{9,8},{10,11... | collective-permute-start | bytes 3145736 | tf_op jit(solution)/shard_map/ppermute | solution.py:166
  254.0 22.2 %collective-permute-start.3 = (bf16[48,8192]{1,0:T(8,128)(2,1)S(1)}, bf16[48,8192]{1,0:T(8,128)(2,1)S(1)}, u32[]{:S(2)}, u32[]{:S(2)}) collective-permute-start(bf16[48,8192]{1,0:T(8,128)(2,1)S(1)} %get-tuple-element.67), channel_id=1, source_target_pairs={{96,0},{97,1},{98,2},{99,3},{100,4},{101,5},{102,6},{103,7},{104,8... | collective-permute-start | bytes 2359304 | tf_op jit(solution)/shard_map/ppermute | solution.py:192
  255.3 20.9 %collective-permute-start.2 = (bf16[48,8192]{1,0:T(8,128)(2,1)S(1)}, bf16[48,8192]{1,0:T(8,128)(2,1)S(1)}, u32[]{:S(2)}, u32[]{:S(2)}) collective-permute-start(bf16[48,8192]{1,0:T(8,128)(2,1)S(1)} %get-tuple-element.67), channel_id=1, source_target_pairs={{96,64},{64,32},{97,65},{65,33},{98,66},{66,34},{99,67},{67,35},{1... | collective-permute-start | bytes 2359304 | tf_op jit(solution)/shard_map/ppermute | solution.py:191
  256.4 15.0 %collective-permute-start.6 = (bf16[32,8192]{1,0:T(8,128)(2,1)S(1)}, bf16[32,8192]{1,0:T(8,128)(2,1)S(1)}, u32[]{:S(2)}, u32[]{:S(2)}) collective-permute-start(bf16[32,8192]{1,0:T(8,128)(2,1)S(1)} %fusion.61), channel_id=1, source_target_pairs={{0,2},{1,3},{2,0},{3,1},{4,6},{5,7},{6,4},{7,5},{8,10},{9,11},{10,... | collective-permute-start | bytes 1572872 | tf_op jit(solution)/shard_map/ppermute | solution.py:173
  261.6 17.9 %collective-permute-start.10 = (bf16[2,32,8192]{2,1,0:T(8,128)(2,1)S(1)}, bf16[2,32,8192]{2,1,0:T(8,128)(2,1)S(1)}, u32[]{:S(2)}, u32[]{:S(2)}) collective-permute-start(bf16[2,32,8192]{2,1,0:T(8,128)(2,1)S(1)} %dynamic-slice_bitcast_fusion.1), channel_id=1, source_target_pairs={{0,1},{1,0},{2,3},{3,2},{4,5},{5,4},{6,7},{7,6},{8,9},{9,8},{10,11... | collective-permute-start | bytes 3145736 | tf_op jit(solution)/shard_map/ppermute | solution.py:166
  272.3 16.1 %collective-permute-start.8 = (bf16[32,8192]{1,0:T(8,128)(2,1)S(1)}, bf16[32,8192]{1,0:T(8,128)(2,1)S(1)}, u32[]{:S(2)}, u32[]{:S(2)}) collective-permute-start(bf16[32,8192]{1,0:T(8,128)(2,1)S(1)} %get-tuple-element.65), channel_id=1, source_target_pairs={{96,0},{97,1},{98,2},{99,3},{100,4},{101,5},{102,6},{103,7},{104,8... | collective-permute-start | bytes 1572872 | tf_op jit(solution)/shard_map/ppermute | solution.py:192
  273.6 14.8 %collective-permute-start.7 = (bf16[32,8192]{1,0:T(8,128)(2,1)S(1)}, bf16[32,8192]{1,0:T(8,128)(2,1)S(1)}, u32[]{:S(2)}, u32[]{:S(2)}) collective-permute-start(bf16[32,8192]{1,0:T(8,128)(2,1)S(1)} %get-tuple-element.65), channel_id=1, source_target_pairs={{96,64},{64,32},{97,65},{65,33},{98,66},{66,34},{99,67},{67,35},{1... | collective-permute-start | bytes 1572872 | tf_op jit(solution)/shard_map/ppermute | solution.py:191
  276.5 5.7 %slice-start.11 = ((bf16[4,128,2,256]{3,1,0,2:T(8,128)(2,1)}), bf16[4,16,2,256]{3,1,0,2:T(8,128)(2,1)S(1)}, s32[]{:S(2)}) async-start(bf16[4,128,2,256]{3,1,0,2:T(8,128)(2,1)} %copy-done.12), calls=%async_computation.17 | async-start | bytes 131072 | tf_op jit(solution)/shard_map/slice | solution.py:152
  276.5 22.4 %collective-permute-start.4 = (bf16[48,8192]{1,0:T(8,128)(2,1)S(1)}, bf16[48,8192]{1,0:T(8,128)(2,1)S(1)}, u32[]{:S(2)}, u32[]{:S(2)}) collective-permute-start(bf16[48,8192]{1,0:T(8,128)(2,1)S(1)} %fusion.30), channel_id=1, source_target_pairs={{32,0},{0,32},{33,1},{1,33},{34,2},{2,34},{35,3},{3,35},{36,4},{4,... | collective-permute-start | bytes 2359304 | tf_op jit(solution)/shard_map/ppermute | solution.py:198
  279.8 19.4 %collective-permute-start.11 = (bf16[32,8192]{1,0:T(8,128)(2,1)S(1)}, bf16[32,8192]{1,0:T(8,128)(2,1)S(1)}, u32[]{:S(2)}, u32[]{:S(2)}) collective-permute-start(bf16[32,8192]{1,0:T(8,128)(2,1)S(1)} %fusion.62), channel_id=1, source_target_pairs={{0,2},{1,3},{2,0},{3,1},{4,6},{5,7},{6,4},{7,5},{8,10},{9,11},{10,... | collective-permute-start | bytes 1572872 | tf_op jit(solution)/shard_map/ppermute | solution.py:173
  284.9 18.9 %collective-permute-start.15 = (bf16[2,16,8192]{2,1,0:T(8,128)(2,1)S(1)}, bf16[2,16,8192]{2,1,0:T(8,128)(2,1)S(1)}, u32[]{:S(2)}, u32[]{:S(2)}) collective-permute-start(bf16[2,16,8192]{2,1,0:T(8,128)(2,1)S(1)} %dynamic-slice_bitcast_fusion.3), channel_id=1, source_target_pairs={{0,1},{1,0},{2,3},{3,2},{4,5},{5,4},{6,7},{7,6},{8,9},{9,8},{10,11... | collective-permute-start | bytes 1572872 | tf_op jit(solution)/shard_map/ppermute | solution.py:166
  288.6 21.6 %collective-permute-start.9 = (bf16[32,8192]{1,0:T(8,128)(2,1)S(1)}, bf16[32,8192]{1,0:T(8,128)(2,1)S(1)}, u32[]{:S(2)}, u32[]{:S(2)}) collective-permute-start(bf16[32,8192]{1,0:T(8,128)(2,1)S(1)} %fusion.43), channel_id=1, source_target_pairs={{32,0},{0,32},{33,1},{1,33},{34,2},{2,34},{35,3},{3,35},{36,4},{4,... | collective-permute-start | bytes 1572872 | tf_op jit(solution)/shard_map/ppermute | solution.py:198
  300.0 31.2 %collective-permute-start.14 = (bf16[32,8192]{1,0:T(8,128)(2,1)S(1)}, bf16[32,8192]{1,0:T(8,128)(2,1)S(1)}, u32[]{:S(2)}, u32[]{:S(2)}) collective-permute-start(bf16[32,8192]{1,0:T(8,128)(2,1)S(1)} %fusion.90), channel_id=1, source_target_pairs={{96,0},{97,1},{98,2},{99,3},{100,4},{101,5},{102,6},{103,7},{104,8... | collective-permute-start | bytes 1572872 | tf_op jit(solution)/shard_map/ppermute | solution.py:188
  301.3 31.2 %collective-permute-start.13 = (bf16[32,8192]{1,0:T(8,128)(2,1)S(1)}, bf16[32,8192]{1,0:T(8,128)(2,1)S(1)}, u32[]{:S(2)}, u32[]{:S(2)}) collective-permute-start(bf16[32,8192]{1,0:T(8,128)(2,1)S(1)} %fusion.90), channel_id=1, source_target_pairs={{64,0},{96,32},{65,1},{97,33},{66,2},{98,34},{67,3},{99,35},{68,4}... | collective-permute-start | bytes 1572872 | tf_op jit(solution)/shard_map/ppermute | solution.py:188
  302.6 29.9 %collective-permute-start.12 = (bf16[32,8192]{1,0:T(8,128)(2,1)S(1)}, bf16[32,8192]{1,0:T(8,128)(2,1)S(1)}, u32[]{:S(2)}, u32[]{:S(2)}) collective-permute-start(bf16[32,8192]{1,0:T(8,128)(2,1)S(1)} %fusion.90), channel_id=1, source_target_pairs={{32,0},{64,32},{96,64},{33,1},{65,33},{97,65},{34,2},{66,34},{98,6... | collective-permute-start | bytes 1572872 | tf_op jit(solution)/shard_map/ppermute | solution.py:188
  304.0 8.0 %collective-permute-start.16 = (bf16[16,8192]{1,0:T(8,128)(2,1)S(1)}, bf16[16,8192]{1,0:T(8,128)(2,1)S(1)}, u32[]{:S(2)}, u32[]{:S(2)}) collective-permute-start(bf16[16,8192]{1,0:T(8,128)(2,1)S(1)} %fusion.64), channel_id=1, source_target_pairs={{0,2},{1,3},{2,0},{3,1},{4,6},{5,7},{6,4},{7,5},{8,10},{9,11},{10,... | collective-permute-start | bytes 786440 | tf_op jit(solution)/shard_map/ppermute | solution.py:173
  312.5 22.6 %collective-permute-start.19 = (bf16[16,8192]{1,0:T(8,128)(2,1)S(1)}, bf16[16,8192]{1,0:T(8,128)(2,1)S(1)}, u32[]{:S(2)}, u32[]{:S(2)}) collective-permute-start(bf16[16,8192]{1,0:T(8,128)(2,1)S(1)} %fusion.89), channel_id=1, source_target_pairs={{96,0},{97,1},{98,2},{99,3},{100,4},{101,5},{102,6},{103,7},{104,8... | collective-permute-start | bytes 786440 | tf_op jit(solution)/shard_map/ppermute | solution.py:188
  313.8 21.3 %collective-permute-start.18 = (bf16[16,8192]{1,0:T(8,128)(2,1)S(1)}, bf16[16,8192]{1,0:T(8,128)(2,1)S(1)}, u32[]{:S(2)}, u32[]{:S(2)}) collective-permute-start(bf16[16,8192]{1,0:T(8,128)(2,1)S(1)} %fusion.89), channel_id=1, source_target_pairs={{64,0},{96,32},{65,1},{97,33},{66,2},{98,34},{67,3},{99,35},{68,4}... | collective-permute-start | bytes 786440 | tf_op jit(solution)/shard_map/ppermute | solution.py:188
  331.2 8.3 %collective-permute-start.17 = (bf16[16,8192]{1,0:T(8,128)(2,1)S(1)}, bf16[16,8192]{1,0:T(8,128)(2,1)S(1)}, u32[]{:S(2)}, u32[]{:S(2)}) collective-permute-start(bf16[16,8192]{1,0:T(8,128)(2,1)S(1)} %fusion.89), channel_id=1, source_target_pairs={{32,0},{64,32},{96,64},{33,1},{65,33},{97,65},{34,2},{66,34},{98,6... | collective-permute-start | bytes 786440 | tf_op jit(solution)/shard_map/ppermute | solution.py:188
  (11 other events, 20.8 us)
Sparse Core Ops, SparseCore 0:
  63.0 50.3 all-gather.1

commit v8 on v6

--- a/solution.py
+++ b/solution.py
@@ -142,7 +142,7 @@
         gain_wide = norm_gain[0].astype(jnp.float32)[None, :]
         sec = lax.axis_index("section")
         unit = rows_local // 8
-        sizes = [3 * unit, 2 * unit, 2 * unit, unit]
+        sizes = [4 * unit, 2 * unit, unit, unit]
         starts = [sum(sizes[:i]) for i in range(len(sizes))]
         outs = []
         previous = None

time: 346 us -> 369 us (1.066)
  waiting for transfers between devices: 103 us -> 131 us
  matrix products: 76.1 us -> 71.3 us
    ppermute x4, waiting for transfers between devices: 24.1 us -> 34.4 us  [on_device(): got2 = lax.ppermute(other, 'tensor', chip_pairs)]
    all_to_all x2, waiting for transfers between devices: 16.5 us -> 23.1 us  [on_device(): parts = lax.all_to_all(pool_grad, 'sample', 0, 0, tiled=False)]
    ppermute x3, waiting for transfers between devices: 17.3 us -> 23.7 us  [on_device(): last = lax.ppermute(carry.astype(jnp.bfloat16), 'section', [(1, 0), (0, 1)])]
    dot_general x2, matrix products: 10.7 us -> 6.47 us  [on_device(): jnp.einsum('rgk,kd->rgd', score_grad, key_rows, preferred_element_type=jn...]
    unnamed x103 -> x109, local copies, waits for them, and re-layouts: 11.3 us -> 11.3 us
  transfers between devices with their start and end apart: 26 -> 26, of which waited for: 15 -> 12; matrix products, arithmetic and copies ran while one was open for 42% -> 38% of each run, Pallas kernels for 0% -> 0%
where the time goes in v8:
time: 369 us; the launch traced here: 363 us
  waiting for transfers between devices  131 us (36%)
  matrix products  71.3 us (19%)
  other arithmetic  59.1 us (16%)
  starting transfers between devices  51 us (14%)
  local copies, waits for them, and re-layouts  34.8 us (9%)
  between operations  15.4 us (4%)
    ppermute x4, waiting for transfers between devices, on_device(): got2 = lax.ppermute(other, 'tensor', chip_pairs)  34.4 us
    ppermute x3, waiting for transfers between devices, on_device(): last = lax.ppermute(carry.astype(jnp.bfloat16), 'section', [(1, 0), (0, 1)])  23.7 us
    all_to_all x2, waiting for transfers between devices, on_device(): parts = lax.all_to_all(pool_grad, 'sample', 0, 0, tiled=False)  23.1 us
    all_to_all x1, waiting for transfers between devices, on_device(): lax.all_to_all(spread, 'sample', 0, 0, tiled=True).reshape(pooled_rows, -1)  22 us
    sub x2, other arithmetic, attend_group(): exponent = jnp.exp(scores - row_max)  21 us
    dot_general x4, matrix products, on_device(): lax.dot_general(grad_rows_c, weight_local, (((2, 3), (1, 2)), ((), ())),...  19.5 us
    convert_element_type x2, other arithmetic, attend_group(): weights_low = softmax_w.astype(jnp.bfloat16)  17.1 us
    dot_general x2, matrix products, attend_group(): jnp.einsum('rgd,kd->rgk', grad_grp, value_rows, preferred_element_type=jn...  13.5 us
  transfers between devices with their start and end apart: 26, of which 12 were waited for; matrix products, arithmetic and copies ran while one was open for 38% of the time, Pallas kernels for 0%

profile of v8, /device:TPU:0, one launch (start us, length us, event | category | flops | bytes accessed | tf_op | source)
XLA Modules:
  0.0 362.9 jit_solution(16451617503814623924)
XLA Ops:
  7.2 1.2 copy.108
  10.3 4.6 %all-to-all-start = ((bf16[4,128,512]{1,2,0:T(8,128)(2,1)}), bf16[4,128,512]{1,2,0:T(8,128)(2,1)S(1)}, u32[]{:S(2)}, u32[]{:S(2)}) async-start(bf16[4,128,512]{1,2,0:T(8,128)(2,1)} %bitcast.6), calls=%async_computation | async-start | bytes 1048576 | tf_op jit(solution)/shard_map/all_to_all | solution.py:85
  15.2 10.0 %all-to-all-done = bf16[4,128,512]{1,2,0:T(8,128)(2,1)S(1)} async-done(((bf16[4,128,512]{1,2,0:T(8,128)(2,1)}), bf16[4,128,512]{1,2,0:T(8,128)(2,1)S(1)}, u32[]{:S(2)}, u32[]{:S(2)}) %all-to-all-start) | async-done | bytes 524320 | tf_op jit(solution)/shard_map/all_to_all | solution.py:85
  26.4 1.5 broadcast_in_dim.96
  27.8 5.6 %all-to-all-start.1 = ((bf16[8,512,256]{2,1,0:T(8,128)(2,1)}), bf16[8,512,256]{2,1,0:T(8,128)(2,1)}, u32[]{:S(2)}, u32[]{:S(2)}) async-start(bf16[8,512,256]{2,1,0:T(8,128)(2,1)} %broadcast_in_dim.96), calls=%async_computation.1 | async-start | bytes 4194304 | tf_op jit(solution)/shard_map/all_to_all | solution.py:94
  38.2 22.0 %all-to-all-done.1 = bf16[8,512,256]{2,1,0:T(8,128)(2,1)} async-done(((bf16[8,512,256]{2,1,0:T(8,128)(2,1)}), bf16[8,512,256]{2,1,0:T(8,128)(2,1)}, u32[]{:S(2)}, u32[]{:S(2)}) %all-to-all-start.1) | async-done | bytes 2097184 | tf_op jit(solution)/shard_map/all_to_all | solution.py:94
  60.2 2.6 fusion.98
  62.8 3.2 fusion.51
  66.0 10.8 %fusion.107 = (f32[128,8]{0,1:T(8,128)S(1)}, f32[128,8,4224]{0,2,1:T(8,128)}) fusion(f32[4224,128,8]{1,0,2:T(8,128)S(1)} %fusion.51, pred[128,4224]{0,1:T(8,128)(4,1)S(1)} %pad_add_fusion), kind=kOutput, calls=%fused_computation.204 | output fusion | flops 17305728 | bytes 35147776 | tf_op jit(solution)/shard_map/sub | solution.py:36
  76.8 6.8 %fusion.18 = bf16[128,8,4224]{0,2,1:T(8,128)(2,1)S(1)} fusion(f32[128,8,4224]{0,2,1:T(8,128)} %get-tuple-element.98, f32[128,8]{0,1:T(8,128)S(1)} %get-tuple-element.97), kind=kLoop, calls=%fused_computation.30 | loop fusion | flops 8650752 | bytes 25956352 | tf_op jit(solution)/shard_map/convert_element_type | solution.py:38
  83.7 2.4 fusion.26
  86.2 2.5 fusion.38
  89.2 1.3 slice-done.3
  90.5 7.2 %fusion.3 = bf16[128,8,4224]{0,2,1:T(8,128)(2,1)} fusion(f32[128,8]{0,1:T(8,128)S(1)} %fusion.38, f32[128,8,4224]{0,2,1:T(8,128)S(1)} %bitcast.291, f32[128,8]{0,1:T(8,128)S(1)} %get-tuple-element.97, bf16[128,128]{1,0:T(8,128)(2,1)S(1)} %copy-done.30, bf16[4096,128]{1,0:T(8,128)(2,1)} %get-tuple-element.71, bf16[128,2,8,128]{0,3,2,1:T(8,128)(2,1)} %bitcast.319), kind=kOutput, calls=%fused_computation.6 | convolution fusion | flops 1126760448 | bytes 27303936 | tf_op jit(solution)/shard_map/rgd,kd->rgk/dot_general | solution.py:43
  97.7 5.9 %fusion.25 = bf16[4224,128]{1,0:T(8,128)(2,1)S(1)} fusion(bf16[128,8,4224]{0,2,1:T(8,128)(2,1)} %fusion.3, bf16[128,2,8,128]{0,3,2,1:T(8,128)(2,1)} %bitcast.313), kind=kOutput, calls=%fused_computation.41 | convolution fusion | flops 1108377600 | bytes 9994240 | tf_op jit(solution)/shard_map/rgk,rgd->kd/dot_general | solution.py:48
  104.7 1.2 slice-done.10
  105.9 1.6 pad_maximum_fusion
  107.4 4.4 %all-to-all-start.2 = ((bf16[8,512,256]{2,1,0:T(8,128)(2,1)}), bf16[8,512,256]{2,1,0:T(8,128)(2,1)}, u32[]{:S(2)}, u32[]{:S(2)}) async-start(bf16[8,512,256]{2,1,0:T(8,128)(2,1)} %pad_maximum_fusion), calls=%async_computation.2 | async-start | bytes 4194304 | tf_op jit(solution)/shard_map/all_to_all | solution.py:118
  111.8 1.5 all-gather.2.cloned.1.call-done
  113.4 2.7 fusion.99
  116.1 2.4 fusion.50
  118.5 10.2 %fusion.106 = (f32[128,8]{0,1:T(8,128)S(1)}, f32[128,8,4224]{0,2,1:T(8,128)}) fusion(f32[4224,128,8]{1,0,2:T(8,128)S(1)} %fusion.50, pred[128,4224]{0,1:T(8,128)(4,1)S(1)} %pad_add_fusion), kind=kOutput, calls=%fused_computation.203 | output fusion | flops 17305728 | bytes 35147776 | tf_op jit(solution)/shard_map/sub | solution.py:36
  128.8 10.2 %fusion.19 = bf16[128,8,4224]{0,2,1:T(8,128)(2,1)} fusion(f32[128,8,4224]{0,2,1:T(8,128)} %get-tuple-element.96, f32[128,8]{0,1:T(8,128)S(1)} %get-tuple-element.95), kind=kLoop, calls=%fused_computation.31 | loop fusion | flops 8650752 | bytes 25956352 | tf_op jit(solution)/shard_map/convert_element_type | solution.py:38
  139.0 6.8 %fusion.39 = f32[128,8]{0,1:T(8,128)S(1)} fusion(bf16[128,8,4224]{0,2,1:T(8,128)(2,1)} %fusion.19, bf16[128,128]{1,0:T(8,128)(2,1)S(1)} %copy-done.29, bf16[4096,128]{1,0:T(8,128)(2,1)S(1)} %copy-done.19, bf16[128,1,8,128]{3,0,2,1:T(8,128)(2,1)S(1)} %copy-done.22), kind=kOutput, calls=%fused_computation.82 | convolution fusion | flops 1109851136 | bytes 9998336 | tf_op jit(solution)/shard_map/rgk,kd->rgd/dot_general | solution.py:39
  145.9 6.3 %fusion.2 = bf16[128,8,4224]{0,2,1:T(8,128)(2,1)} fusion(f32[128,8]{0,1:T(8,128)S(1)} %fusion.39, f32[128,8,4224]{0,2,1:T(8,128)S(1)} %bitcast.293, f32[128,8]{0,1:T(8,128)S(1)} %get-tuple-element.95, bf16[128,128]{1,0:T(8,128)(2,1)S(1)} %copy-done.29, bf16[4096,128]{1,0:T(8,128)(2,1)} %get-tuple-element.73, bf16[128,2,8,128]{0,3,2,1:T(8,128)(2,1)S(1)} %bitcast.321), kind=kOutput, calls=%fused_computation.3 | convolution fusion | flops 1126760448 | bytes 27303936 | tf_op jit(solution)/shard_map/rgd,kd->rgk/dot_general | solution.py:43
  152.3 6.0 %fusion.28 = bf16[4224,128]{1,0:T(8,128)(2,1)S(1)} fusion(bf16[128,8,4224]{0,2,1:T(8,128)(2,1)} %fusion.19, bf16[128,2,8,128]{0,3,2,1:T(8,128)(2,1)S(1)} %bitcast.322), kind=kOutput, calls=%fused_computation.44 | convolution fusion | flops 1107836928 | bytes 9994240 | tf_op jit(solution)/shard_map/rgk,rgd->kd/dot_general | solution.py:51
  159.4 2.5 fusion.27
  163.0 1.5 pad_maximum_fusion.1
  164.5 4.2 %all-to-all-start.3 = ((bf16[8,512,256]{2,1,0:T(8,128)(2,1)}), bf16[8,512,256]{2,1,0:T(8,128)(2,1)S(1)}, u32[]{:S(2)}, u32[]{:S(2)}) async-start(bf16[8,512,256]{2,1,0:T(8,128)(2,1)} %pad_maximum_fusion.1), calls=%async_computation.3 | async-start | bytes 4194304 | tf_op jit(solution)/shard_map/all_to_all | solution.py:118
  168.8 2.0 reduce
  171.6 23.1 %all-to-all-done.3 = bf16[8,512,256]{2,1,0:T(8,128)(2,1)S(1)} async-done(((bf16[8,512,256]{2,1,0:T(8,128)(2,1)}), bf16[8,512,256]{2,1,0:T(8,128)(2,1)S(1)}, u32[]{:S(2)}, u32[]{:S(2)}) %all-to-all-start.3) | async-done | bytes 2097184 | tf_op jit(solution)/shard_map/all_to_all | solution.py:118
  195.7 1.1 copy.130
  196.9 1.8 pad_maximum_fusion.4
  198.7 4.0 %all-to-all-start.4 = ((bf16[4,128,512]{2,1,0:T(8,128)(2,1)}), bf16[4,128,512]{2,1,0:T(8,128)(2,1)S(1)}, u32[]{:S(2)}, u32[]{:S(2)}) async-start(bf16[4,128,512]{2,1,0:T(8,128)(2,1)} %pad_maximum_fusion.4), calls=%async_computation.4 | async-start | bytes 1048576 | tf_op jit(solution)/shard_map/all_to_all | solution.py:126
  203.5 8.0 %fusion.6 = bf16[4,64,8192]{2,1,0:T(8,128)(2,1)} fusion(bf16[8192,2,256]{2,1,0:T(2,128)(2,1)} %bitcast.343, bf16[4,128,2,256]{3,1,0,2:T(8,128)(2,1)S(1)} %reshape.274), kind=kOutput, calls=%fused_computation.13 | convolution fusion | flops 2149580800 | bytes 12845056 | tf_op jit(solution)/shard_map/dot_general | solution.py:155
  211.4 1.5 all-to-all-done.4
  214.2 3.3 dynamic-slice_bitcast_fusion
  217.9 5.0 %fusion.41 = bf16[128,1,8,128]{0,3,2,1:T(8,128)(2,1)S(1)} fusion(bf16[128,8,4224]{0,2,1:T(8,128)(2,1)} %fusion.3, bf16[128,128]{1,0:T(8,128)(2,1)S(1)} %copy-done.25, bf16[4096,128]{1,0:T(8,128)(2,1)S(1)} %copy-done.2), kind=kOutput, calls=%fused_computation.84 | convolution fusion | flops 1109721088 | bytes 9994240 | tf_op jit(solution)/shard_map/rgk,kd->rgd/dot_general | solution.py:115
  223.7 1.4 fusion.40
  232.0 2.8 convert_add_fusion
  234.9 2.2 collective-permute-start.1
  237.1 6.2 %fusion.7 = bf16[4,32,8192]{2,1,0:T(8,128)(2,1)S(1)} fusion(bf16[4,32,2,256]{3,1,0,2:T(8,128)(2,1)S(1)} %slice-done.11, bf16[8192,2,256,1]{2,1,0,3:T(2,128)(2,1)} %bitcast.344), kind=kOutput, calls=%fused_computation.15 | convolution fusion | flops 1074790400 | bytes 10616832 | tf_op jit(solution)/shard_map/dot_general | solution.py:155
  243.7 18.1 %collective-permute-done.1 = bf16[64,8192]{1,0:T(8,128)(2,1)S(1)} collective-permute-done((bf16[64,8192]{1,0:T(8,128)(2,1)S(1)}, bf16[64,8192]{1,0:T(8,128)(2,1)S(1)}, u32[]{:S(2)}, u32[]{:S(2)}) %collective-permute-start.1) | collective-permute-done | bytes 1048608 | tf_op jit(solution)/shard_map/ppermute | solution.py:173
  263.1 1.4 collective-permute-start.3
  265.6 2.4 collective-permute-start.6
  268.0 2.6 fusion.8
  270.8 9.7 %collective-permute-done.6 = bf16[32,8192]{1,0:T(8,128)(2,1)S(1)} collective-permute-done((bf16[32,8192]{1,0:T(8,128)(2,1)S(1)}, bf16[32,8192]{1,0:T(8,128)(2,1)S(1)}, u32[]{:S(2)}, u32[]{:S(2)}) %collective-permute-start.6) | collective-permute-done | bytes 524320 | tf_op jit(solution)/shard_map/ppermute | solution.py:173
  281.3 1.5 collective-permute-start.8
  283.6 2.6 collective-permute-start.11
  286.2 2.6 fusion.9
  288.9 3.1 collective-permute-done.11
  292.6 1.3 collective-permute-start.13
  295.0 8.6 %collective-permute-done.8 = bf16[32,8192]{1,0:T(8,128)(2,1)S(1)} collective-permute-done((bf16[32,8192]{1,0:T(8,128)(2,1)S(1)}, bf16[32,8192]{1,0:T(8,128)(2,1)S(1)}, u32[]{:S(2)}, u32[]{:S(2)}) %collective-permute-start.8) | collective-permute-done | bytes 524320 | tf_op jit(solution)/shard_map/ppermute | solution.py:192
  303.6 1.9 collective-permute-start.4
  305.8 3.9 %collective-permute-start.9 = (bf16[32,8192]{1,0:T(8,128)(2,1)S(1)}, bf16[32,8192]{1,0:T(8,128)(2,1)S(1)}, u32[]{:S(2)}, u32[]{:S(2)}) collective-permute-start(bf16[32,8192]{1,0:T(8,128)(2,1)S(1)} %fusion.43), channel_id=1, source_target_pairs={{32,0},{0,32},{33,1},{1,33},{34,2},{2,34},{35,3},{3,35},{36,4},{4,... | collective-permute-start | bytes 1572872 | tf_op jit(solution)/shard_map/ppermute | solution.py:198
  309.9 2.4 collective-permute-start.16
  312.4 1.9 collective-permute-start.14
  314.3 3.5 collective-permute-done.16
  318.2 1.3 collective-permute-start.19
  319.5 1.3 collective-permute-start.18
  320.8 23.7 %collective-permute-done.14 = bf16[16,8192]{1,0:T(8,128)(2,1)S(1)} collective-permute-done((bf16[16,8192]{1,0:T(8,128)(2,1)S(1)}, bf16[16,8192]{1,0:T(8,128)(2,1)S(1)}, u32[]{:S(2)}, u32[]{:S(2)}) %collective-permute-start.14) | collective-permute-done | bytes 262176 | tf_op jit(solution)/shard_map/ppermute | solution.py:198
  344.5 1.3 collective-permute-start.17
  346.2 6.6 %collective-permute-done.17 = bf16[16,8192]{1,0:T(8,128)(2,1)S(1)} collective-permute-done((bf16[16,8192]{1,0:T(8,128)(2,1)S(1)}, bf16[16,8192]{1,0:T(8,128)(2,1)S(1)}, u32[]{:S(2)}, u32[]{:S(2)}) %collective-permute-start.17) | collective-permute-done | bytes 262176 | tf_op jit(solution)/shard_map/ppermute | solution.py:188
  353.5 2.3 maximum_bitcast_fusion
  (203 shorter events, 32.0 us)
Async XLA Ops:
  7.2 7.7 %copy-start.20 = (bf16[1,128,2048]{2,1,0:T(8,128)(2,1)S(1)}, bf16[1,128,2048]{2,1,0:T(8,128)(2,1)}, u32[]{:S(2)}) copy-start(bf16[1,128,2048]{2,1,0:T(8,128)(2,1)} %param.15) | copy-start | bytes 1572868
  10.3 14.9 %all-to-all-start = ((bf16[4,128,512]{1,2,0:T(8,128)(2,1)}), bf16[4,128,512]{1,2,0:T(8,128)(2,1)S(1)}, u32[]{:S(2)}, u32[]{:S(2)}) async-start(bf16[4,128,512]{1,2,0:T(8,128)(2,1)} %bitcast.6), calls=%async_computation | async-start | bytes 1048576 | tf_op jit(solution)/shard_map/all_to_all | solution.py:85
  15.2 18.3 %copy-start.8 = (bf16[1,128,2048]{1,2,0:T(8,128)(2,1)}, bf16[1,128,2048]{1,2,0:T(8,128)(2,1)S(1)}, u32[]{:S(2)}) copy-start(bf16[1,128,2048]{1,2,0:T(8,128)(2,1)S(1)} %copy.113) | copy-start | bytes 1572868
  27.8 5.7 %copy-start.21 = (bf16[1,128,2048]{2,1,0:T(8,128)(2,1)S(1)}, bf16[1,128,2048]{2,1,0:T(8,128)(2,1)}, u32[]{:S(2)}) copy-start(bf16[1,128,2048]{2,1,0:T(8,128)(2,1)} %param.12) | copy-start | bytes 1572868
  27.8 32.3 %all-to-all-start.1 = ((bf16[8,512,256]{2,1,0:T(8,128)(2,1)}), bf16[8,512,256]{2,1,0:T(8,128)(2,1)}, u32[]{:S(2)}, u32[]{:S(2)}) async-start(bf16[8,512,256]{2,1,0:T(8,128)(2,1)} %broadcast_in_dim.96), calls=%async_computation.1 | async-start | bytes 4194304 | tf_op jit(solution)/shard_map/all_to_all | solution.py:94
  33.4 3.2 copy-start.27
  33.4 79.9 %all-gather.2.cloned.1.call-start = ((), (), s32[]{:S(2)}) async-start(), calls=%async_computation.5 | async-start | bytes 2359296 | tf_op jit(solution)/shard_map/all_gather | solution.py:97
  33.8 29.0 %copy-start.5 = (bf16[1,128,2048]{1,2,0:T(8,128)(2,1)}, bf16[1,128,2048]{1,2,0:T(8,128)(2,1)S(1)}, u32[]{:S(2)}) copy-start(bf16[1,128,2048]{1,2,0:T(8,128)(2,1)S(1)} %copy.111) | copy-start | bytes 1572868
  62.8 3.2 copy-start.1
  76.8 6.8 %copy-start.9 = (bf16[1,128,2048]{1,2,0:T(8,128)(2,1)S(1)}, bf16[1,128,2048]{1,2,0:T(8,128)(2,1)}, u32[]{:S(2)}) copy-start(bf16[1,128,2048]{1,2,0:T(8,128)(2,1)} %copy-done.8) | copy-start | bytes 1572868
  83.7 5.1 %slice-start = ((s8[17301504]{0:T(1024)(128)(4,1)}), s8[4194304]{0:T(1024)(128)(4,1)S(1)}, s32[]{:S(2)}) async-start(s8[17301504]{0:T(1024)(128)(4,1)} %bitcast.290), calls=%async_computation.6 | async-start | bytes 8388608
  83.7 5.1 %slice-start.1 = ((s8[17301504]{0:T(1024)(128)(4,1)}), s8[4194304]{0:T(1024)(128)(4,1)S(1)}, s32[]{:S(2)}) async-start(s8[17301504]{0:T(1024)(128)(4,1)} %bitcast.290), calls=%async_computation.7 | async-start | bytes 8388608
  83.7 5.5 %slice-start.2 = ((s8[17301504]{0:T(1024)(128)(4,1)}), s8[4194304]{0:T(1024)(128)(4,1)S(1)}, s32[]{:S(2)}) async-start(s8[17301504]{0:T(1024)(128)(4,1)} %bitcast.290), calls=%async_computation.8 | async-start | bytes 8388608
  86.2 4.3 %slice-start.3 = ((s8[17301504]{0:T(1024)(128)(4,1)}), s8[4194304]{0:T(1024)(128)(4,1)S(1)}, s32[]{:S(2)}) async-start(s8[17301504]{0:T(1024)(128)(4,1)} %bitcast.290), calls=%async_computation.9 | async-start | bytes 8388608
  86.2 4.3 %slice-start.4 = ((s8[17301504]{0:T(1024)(128)(4,1)}), s8[524288]{0:T(1024)(128)(4,1)S(1)}, s32[]{:S(2)}) async-start(s8[17301504]{0:T(1024)(128)(4,1)} %bitcast.290), calls=%async_computation.10 | async-start | bytes 1048576
  107.4 57.1 %all-to-all-start.2 = ((bf16[8,512,256]{2,1,0:T(8,128)(2,1)}), bf16[8,512,256]{2,1,0:T(8,128)(2,1)}, u32[]{:S(2)}, u32[]{:S(2)}) async-start(bf16[8,512,256]{2,1,0:T(8,128)(2,1)} %pad_maximum_fusion), calls=%async_computation.2 | async-start | bytes 4194304 | tf_op jit(solution)/shard_map/all_to_all | solution.py:118
  111.8 4.3 %copy-start.24 = (bf16[128,128]{1,0:T(8,128)(2,1)S(1)}, bf16[128,128]{1,0:T(8,128)(2,1)}, u32[]{:S(2)}) copy-start(bf16[128,128]{1,0:T(8,128)(2,1)} %get-tuple-element.86) | copy-start | bytes 98308
  128.7 10.3 %copy-start.19 = (bf16[4096,128]{1,0:T(8,128)(2,1)S(1)}, bf16[4096,128]{1,0:T(8,128)(2,1)}, u32[]{:S(2)}) copy-start(bf16[4096,128]{1,0:T(8,128)(2,1)} %get-tuple-element.73) | copy-start | bytes 3145732
  128.7 10.3 %copy-start.22 = (bf16[128,1,8,128]{3,0,2,1:T(8,128)(2,1)S(1)}, bf16[128,1,8,128]{3,0,2,1:T(8,128)(2,1)}, u32[]{:S(2)}) copy-start(bf16[128,1,8,128]{3,0,2,1:T(8,128)(2,1)} %copy.173) | copy-start | bytes 786436
  128.7 10.3 %copy-start.29 = (bf16[128,128]{1,0:T(8,128)(2,1)S(1)}, bf16[128,128]{1,0:T(8,128)(2,1)}, u32[]{:S(2)}) copy-start(bf16[128,128]{1,0:T(8,128)(2,1)} %get-tuple-element.84) | copy-start | bytes 98308
  128.7 17.1 %slice-start.5 = ((s8[17301504]{0:T(1024)(128)(4,1)}), s8[4194304]{0:T(1024)(128)(4,1)S(1)}, s32[]{:S(2)}) async-start(s8[17301504]{0:T(1024)(128)(4,1)} %bitcast.292), calls=%async_computation.11 | async-start | bytes 8388608
  128.7 17.1 %slice-start.6 = ((s8[17301504]{0:T(1024)(128)(4,1)}), s8[4194304]{0:T(1024)(128)(4,1)S(1)}, s32[]{:S(2)}) async-start(s8[17301504]{0:T(1024)(128)(4,1)} %bitcast.292), calls=%async_computation.12 | async-start | bytes 8388608
  128.8 17.1 %slice-start.7 = ((s8[17301504]{0:T(1024)(128)(4,1)}), s8[4194304]{0:T(1024)(128)(4,1)S(1)}, s32[]{:S(2)}) async-start(s8[17301504]{0:T(1024)(128)(4,1)} %bitcast.292), calls=%async_computation.13 | async-start | bytes 8388608
  128.8 17.1 %slice-start.8 = ((s8[17301504]{0:T(1024)(128)(4,1)}), s8[4194304]{0:T(1024)(128)(4,1)S(1)}, s32[]{:S(2)}) async-start(s8[17301504]{0:T(1024)(128)(4,1)} %bitcast.292), calls=%async_computation.14 | async-start | bytes 8388608
  139.0 6.9 %slice-start.9 = ((s8[17301504]{0:T(1024)(128)(4,1)}), s8[524288]{0:T(1024)(128)(4,1)S(1)}, s32[]{:S(2)}) async-start(s8[17301504]{0:T(1024)(128)(4,1)} %bitcast.292), calls=%async_computation.15 | async-start | bytes 1048576
  139.0 6.9 %copy-start.10 = (bf16[1,128,2048]{1,2,0:T(8,128)(2,1)S(1)}, bf16[1,128,2048]{1,2,0:T(8,128)(2,1)}, u32[]{:S(2)}) copy-start(bf16[1,128,2048]{1,2,0:T(8,128)(2,1)} %copy-done.8) | copy-start | bytes 1572868
  152.3 7.1 %copy-start.7 = (bf16[1,128,2048]{1,2,0:T(8,128)(2,1)S(1)}, bf16[1,128,2048]{1,2,0:T(8,128)(2,1)}, u32[]{:S(2)}) copy-start(bf16[1,128,2048]{1,2,0:T(8,128)(2,1)} %copy-done.5) | copy-start | bytes 1572868
  152.3 7.1 %copy-start.34 = (bf16[128,8,4224]{0,2,1:T(8,128)(2,1)S(1)}, bf16[128,8,4224]{0,2,1:T(8,128)(2,1)}, u32[]{:S(2)}) copy-start(bf16[128,8,4224]{0,2,1:T(8,128)(2,1)} %fusion.2) | copy-start | bytes 25952260
  164.5 4.2 %copy-start.28 = (bf16[1,8192]{1,0:T(2,128)(2,1)S(1)}, bf16[1,8192]{1,0:T(2,128)(2,1)}, u32[]{:S(2)}) copy-start(bf16[1,8192]{1,0:T(2,128)(2,1)} %param.20) | copy-start | bytes 49156
  164.5 30.1 %all-to-all-start.3 = ((bf16[8,512,256]{2,1,0:T(8,128)(2,1)}), bf16[8,512,256]{2,1,0:T(8,128)(2,1)S(1)}, u32[]{:S(2)}, u32[]{:S(2)}) async-start(bf16[8,512,256]{2,1,0:T(8,128)(2,1)} %pad_maximum_fusion.1), calls=%async_computation.3 | async-start | bytes 4194304 | tf_op jit(solution)/shard_map/all_to_all | solution.py:118
  195.7 6.9 %copy-start.17 = (bf16[512,256]{0,1:T(8,128)(2,1)S(1)}, bf16[512,256]{0,1:T(8,128)(2,1)}, u32[]{:S(2)}) copy-start(bf16[512,256]{0,1:T(8,128)(2,1)} %copy.129) | copy-start | bytes 786436
  198.7 14.3 %all-to-all-start.4 = ((bf16[4,128,512]{2,1,0:T(8,128)(2,1)}), bf16[4,128,512]{2,1,0:T(8,128)(2,1)S(1)}, u32[]{:S(2)}, u32[]{:S(2)}) async-start(bf16[4,128,512]{2,1,0:T(8,128)(2,1)} %pad_maximum_fusion.4), calls=%async_computation.4 | async-start | bytes 1048576 | tf_op jit(solution)/shard_map/all_to_all | solution.py:126
  203.5 8.0 %copy-start.13 = (bf16[4,128,2,256]{3,1,0,2:T(8,128)(2,1)}, bf16[4,128,2,256]{3,1,0,2:T(8,128)(2,1)S(1)}, u32[]{:S(2)}) copy-start(bf16[4,128,2,256]{3,1,0,2:T(8,128)(2,1)S(1)} %reshape.274) | copy-start | bytes 1572868
  214.2 3.7 %copy-start.2 = (bf16[4096,128]{1,0:T(8,128)(2,1)S(1)}, bf16[4096,128]{1,0:T(8,128)(2,1)}, u32[]{:S(2)}) copy-start(bf16[4096,128]{1,0:T(8,128)(2,1)} %copy-done.1) | copy-start | bytes 3145732
  214.2 3.7 %copy-start.25 = (bf16[128,128]{1,0:T(8,128)(2,1)S(1)}, bf16[128,128]{1,0:T(8,128)(2,1)}, u32[]{:S(2)}) copy-start(bf16[128,128]{1,0:T(8,128)(2,1)} %get-tuple-element.85) | copy-start | bytes 98308
  214.2 9.5 %slice-start.14 = ((s8[8650752]{0:T(1024)(128)(4,1)}), s8[4194304]{0:T(1024)(128)(4,1)S(1)}, s32[]{:S(2)}) async-start(s8[8650752]{0:T(1024)(128)(4,1)} %bitcast.350), calls=%async_computation.20 | async-start | bytes 8388608
  217.5 6.2 %slice-start.15 = ((s8[8650752]{0:T(1024)(128)(4,1)}), s8[4194304]{0:T(1024)(128)(4,1)S(1)}, s32[]{:S(2)}) async-start(s8[8650752]{0:T(1024)(128)(4,1)} %bitcast.350), calls=%async_computation.21 | async-start | bytes 8388608
  217.5 6.2 %slice-start.16 = ((s8[8650752]{0:T(1024)(128)(4,1)}), s8[262144]{0:T(1024)(128)(4,1)S(1)}, s32[]{:S(2)}) async-start(s8[8650752]{0:T(1024)(128)(4,1)} %bitcast.350), calls=%async_computation.22 | async-start | bytes 524288
  217.5 14.5 %collective-permute-start = (bf16[2,64,8192]{2,1,0:T(8,128)(2,1)}, bf16[2,64,8192]{2,1,0:T(8,128)(2,1)}, u32[]{:S(2)}, u32[]{:S(2)}) collective-permute-start(bf16[2,64,8192]{2,1,0:T(8,128)(2,1)} %dynamic-slice_bitcast_fusion), channel_id=1, source_target_pairs={{0,1},{1,0},{2,3},{3,2},{4,5},{5,4},{6,7},{7,6},{8,9},{9,8},{10,11... | collective-permute-start | bytes 6291464 | tf_op jit(solution)/shard_map/ppermute | solution.py:166
  225.2 4.8 %copy-start.12 = (f32[1,128,4,2,128]{1,4,0,3,2:T(8,128)S(1)}, f32[1,128,4,2,128]{1,4,0,3,2:T(8,128)}, u32[]{:S(2)}) copy-start(f32[1,128,4,2,128]{1,4,0,3,2:T(8,128)} %get-tuple-element.76) | copy-start | bytes 1572868
  225.2 5.8 %copy-start.11 = (f32[1,128,4,2,128]{1,4,0,3,2:T(8,128)S(1)}, f32[1,128,4,2,128]{1,4,0,3,2:T(8,128)}, u32[]{:S(2)}) copy-start(f32[1,128,4,2,128]{1,4,0,3,2:T(8,128)} %get-tuple-element.75) | copy-start | bytes 1572868
  232.0 5.1 %slice-start.11 = ((bf16[4,128,2,256]{3,1,0,2:T(8,128)(2,1)}), bf16[4,32,2,256]{3,1,0,2:T(8,128)(2,1)S(1)}, s32[]{:S(2)}) async-start(bf16[4,128,2,256]{3,1,0,2:T(8,128)(2,1)} %copy-done.13), calls=%async_computation.17 | async-start | bytes 262144 | tf_op jit(solution)/shard_map/slice | solution.py:152
  234.9 27.0 %collective-permute-start.1 = (bf16[64,8192]{1,0:T(8,128)(2,1)S(1)}, bf16[64,8192]{1,0:T(8,128)(2,1)S(1)}, u32[]{:S(2)}, u32[]{:S(2)}) collective-permute-start(bf16[64,8192]{1,0:T(8,128)(2,1)S(1)} %fusion.48), channel_id=1, source_target_pairs={{0,2},{1,3},{2,0},{3,1},{4,6},{5,7},{6,4},{7,5},{8,10},{9,11},{10,... | collective-permute-start | bytes 3145736 | tf_op jit(solution)/shard_map/ppermute | solution.py:173
  243.3 18.5 %copy-start = (bf16[1,128,8192]{2,1,0:T(8,128)(2,1)S(1)}, bf16[1,128,8192]{2,1,0:T(8,128)(2,1)}, u32[]{:S(2)}) copy-start(bf16[1,128,8192]{2,1,0:T(8,128)(2,1)} %param.19) | copy-start | bytes 6291460
  243.3 24.7 %slice-start.12 = ((s8[8388608]{0:T(1024)(128)(4,1)}), s8[4194304]{0:T(1024)(128)(4,1)S(1)}, s32[]{:S(2)}) async-start(s8[8388608]{0:T(1024)(128)(4,1)} %bitcast.345), calls=%async_computation.18 | async-start | bytes 8388608
  243.4 21.9 %collective-permute-start.5 = (bf16[2,32,8192]{2,1,0:T(8,128)(2,1)S(1)}, bf16[2,32,8192]{2,1,0:T(8,128)(2,1)S(1)}, u32[]{:S(2)}, u32[]{:S(2)}) collective-permute-start(bf16[2,32,8192]{2,1,0:T(8,128)(2,1)S(1)} %dynamic-slice_bitcast_fusion.1), channel_id=1, source_target_pairs={{0,1},{1,0},{2,3},{3,2},{4,5},{5,4},{6,7},{7,6},{8,9},{9,8},{10,11... | collective-permute-start | bytes 3145736 | tf_op jit(solution)/shard_map/ppermute | solution.py:166
  262.5 5.5 %slice-start.13 = ((s8[8388608]{0:T(1024)(128)(4,1)}), s8[4194304]{0:T(1024)(128)(4,1)S(1)}, s32[]{:S(2)}) async-start(s8[8388608]{0:T(1024)(128)(4,1)} %bitcast.345), calls=%async_computation.19 | async-start | bytes 8388608
  263.1 29.5 %collective-permute-start.3 = (bf16[64,8192]{1,0:T(8,128)(2,1)S(1)}, bf16[64,8192]{1,0:T(8,128)(2,1)S(1)}, u32[]{:S(2)}, u32[]{:S(2)}) collective-permute-start(bf16[64,8192]{1,0:T(8,128)(2,1)S(1)} %get-tuple-element.69), channel_id=1, source_target_pairs={{96,0},{97,1},{98,2},{99,3},{100,4},{101,5},{102,6},{103,7},{104,8... | collective-permute-start | bytes 3145736 | tf_op jit(solution)/shard_map/ppermute | solution.py:192
  264.6 29.4 %collective-permute-start.2 = (bf16[64,8192]{1,0:T(8,128)(2,1)S(1)}, bf16[64,8192]{1,0:T(8,128)(2,1)S(1)}, u32[]{:S(2)}, u32[]{:S(2)}) collective-permute-start(bf16[64,8192]{1,0:T(8,128)(2,1)S(1)} %get-tuple-element.69), channel_id=1, source_target_pairs={{96,64},{64,32},{97,65},{65,33},{98,66},{66,34},{99,67},{67,35},{1... | collective-permute-start | bytes 3145736 | tf_op jit(solution)/shard_map/ppermute | solution.py:191
  265.6 14.9 %collective-permute-start.6 = (bf16[32,8192]{1,0:T(8,128)(2,1)S(1)}, bf16[32,8192]{1,0:T(8,128)(2,1)S(1)}, u32[]{:S(2)}, u32[]{:S(2)}) collective-permute-start(bf16[32,8192]{1,0:T(8,128)(2,1)S(1)} %fusion.62), channel_id=1, source_target_pairs={{0,2},{1,3},{2,0},{3,1},{4,6},{5,7},{6,4},{7,5},{8,10},{9,11},{10,... | collective-permute-start | bytes 1572872 | tf_op jit(solution)/shard_map/ppermute | solution.py:173
  270.7 12.8 %collective-permute-start.10 = (bf16[2,16,8192]{2,1,0:T(8,128)(2,1)S(1)}, bf16[2,16,8192]{2,1,0:T(8,128)(2,1)S(1)}, u32[]{:S(2)}, u32[]{:S(2)}) collective-permute-start(bf16[2,16,8192]{2,1,0:T(8,128)(2,1)S(1)} %dynamic-slice_bitcast_fusion.3), channel_id=1, source_target_pairs={{0,1},{1,0},{2,3},{3,2},{4,5},{5,4},{6,7},{7,6},{8,9},{9,8},{10,11... | collective-permute-start | bytes 1572872 | tf_op jit(solution)/shard_map/ppermute | solution.py:166
  281.3 22.3 %collective-permute-start.8 = (bf16[32,8192]{1,0:T(8,128)(2,1)S(1)}, bf16[32,8192]{1,0:T(8,128)(2,1)S(1)}, u32[]{:S(2)}, u32[]{:S(2)}) collective-permute-start(bf16[32,8192]{1,0:T(8,128)(2,1)S(1)} %get-tuple-element.67), channel_id=1, source_target_pairs={{96,0},{97,1},{98,2},{99,3},{100,4},{101,5},{102,6},{103,7},{104,8... | collective-permute-start | bytes 1572872 | tf_op jit(solution)/shard_map/ppermute | solution.py:192
  282.8 22.8 %collective-permute-start.7 = (bf16[32,8192]{1,0:T(8,128)(2,1)S(1)}, bf16[32,8192]{1,0:T(8,128)(2,1)S(1)}, u32[]{:S(2)}, u32[]{:S(2)}) collective-permute-start(bf16[32,8192]{1,0:T(8,128)(2,1)S(1)} %get-tuple-element.67), channel_id=1, source_target_pairs={{96,64},{64,32},{97,65},{65,33},{98,66},{66,34},{99,67},{67,35},{1... | collective-permute-start | bytes 1572872 | tf_op jit(solution)/shard_map/ppermute | solution.py:191
  283.6 8.4 %collective-permute-start.11 = (bf16[16,8192]{1,0:T(8,128)(2,1)S(1)}, bf16[16,8192]{1,0:T(8,128)(2,1)S(1)}, u32[]{:S(2)}, u32[]{:S(2)}) collective-permute-start(bf16[16,8192]{1,0:T(8,128)(2,1)S(1)} %fusion.65), channel_id=1, source_target_pairs={{0,2},{1,3},{2,0},{3,1},{4,6},{5,7},{6,4},{7,5},{8,10},{9,11},{10,... | collective-permute-start | bytes 786440 | tf_op jit(solution)/shard_map/ppermute | solution.py:173
  292.0 17.7 %collective-permute-start.15 = (bf16[2,16,8192]{2,1,0:T(8,128)(2,1)S(1)}, bf16[2,16,8192]{2,1,0:T(8,128)(2,1)S(1)}, u32[]{:S(2)}, u32[]{:S(2)}) collective-permute-start(bf16[2,16,8192]{2,1,0:T(8,128)(2,1)S(1)} %dynamic-slice_bitcast_fusion.2), channel_id=1, source_target_pairs={{0,1},{1,0},{2,3},{3,2},{4,5},{5,4},{6,7},{7,6},{8,9},{9,8},{10,11... | collective-permute-start | bytes 1572872 | tf_op jit(solution)/shard_map/ppermute | solution.py:166
  292.6 19.6 %collective-permute-start.13 = (bf16[16,8192]{1,0:T(8,128)(2,1)S(1)}, bf16[16,8192]{1,0:T(8,128)(2,1)S(1)}, u32[]{:S(2)}, u32[]{:S(2)}) collective-permute-start(bf16[16,8192]{1,0:T(8,128)(2,1)S(1)} %get-tuple-element.65), channel_id=1, source_target_pairs={{96,0},{97,1},{98,2},{99,3},{100,4},{101,5},{102,6},{103,7},{104,8... | collective-permute-start | bytes 786440 | tf_op jit(solution)/shard_map/ppermute | solution.py:192
  293.9 18.3 %collective-permute-start.12 = (bf16[16,8192]{1,0:T(8,128)(2,1)S(1)}, bf16[16,8192]{1,0:T(8,128)(2,1)S(1)}, u32[]{:S(2)}, u32[]{:S(2)}) collective-permute-start(bf16[16,8192]{1,0:T(8,128)(2,1)S(1)} %get-tuple-element.65), channel_id=1, source_target_pairs={{96,64},{64,32},{97,65},{65,33},{98,66},{66,34},{99,67},{67,35},{1... | collective-permute-start | bytes 786440 | tf_op jit(solution)/shard_map/ppermute | solution.py:191
  303.6 49.5 %collective-permute-start.4 = (bf16[64,8192]{1,0:T(8,128)(2,1)S(1)}, bf16[64,8192]{1,0:T(8,128)(2,1)S(1)}, u32[]{:S(2)}, u32[]{:S(2)}) collective-permute-start(bf16[64,8192]{1,0:T(8,128)(2,1)S(1)} %fusion.30), channel_id=1, source_target_pairs={{32,0},{0,32},{33,1},{1,33},{34,2},{2,34},{35,3},{3,35},{36,4},{4,... | collective-permute-start | bytes 3145736 | tf_op jit(solution)/shard_map/ppermute | solution.py:198
  305.8 40.2 %collective-permute-start.9 = (bf16[32,8192]{1,0:T(8,128)(2,1)S(1)}, bf16[32,8192]{1,0:T(8,128)(2,1)S(1)}, u32[]{:S(2)}, u32[]{:S(2)}) collective-permute-start(bf16[32,8192]{1,0:T(8,128)(2,1)S(1)} %fusion.43), channel_id=1, source_target_pairs={{32,0},{0,32},{33,1},{1,33},{34,2},{2,34},{35,3},{3,35},{36,4},{4,... | collective-permute-start | bytes 1572872 | tf_op jit(solution)/shard_map/ppermute | solution.py:198
  309.9 8.0 %collective-permute-start.16 = (bf16[16,8192]{1,0:T(8,128)(2,1)S(1)}, bf16[16,8192]{1,0:T(8,128)(2,1)S(1)}, u32[]{:S(2)}, u32[]{:S(2)}) collective-permute-start(bf16[16,8192]{1,0:T(8,128)(2,1)S(1)} %fusion.66), channel_id=1, source_target_pairs={{0,2},{1,3},{2,0},{3,1},{4,6},{5,7},{6,4},{7,5},{8,10},{9,11},{10,... | collective-permute-start | bytes 786440 | tf_op jit(solution)/shard_map/ppermute | solution.py:173
  312.4 32.1 %collective-permute-start.14 = (bf16[16,8192]{1,0:T(8,128)(2,1)S(1)}, bf16[16,8192]{1,0:T(8,128)(2,1)S(1)}, u32[]{:S(2)}, u32[]{:S(2)}) collective-permute-start(bf16[16,8192]{1,0:T(8,128)(2,1)S(1)} %fusion.53), channel_id=1, source_target_pairs={{32,0},{0,32},{33,1},{1,33},{34,2},{2,34},{35,3},{3,35},{36,4},{4,... | collective-permute-start | bytes 786440 | tf_op jit(solution)/shard_map/ppermute | solution.py:198
  318.2 27.9 %collective-permute-start.19 = (bf16[16,8192]{1,0:T(8,128)(2,1)S(1)}, bf16[16,8192]{1,0:T(8,128)(2,1)S(1)}, u32[]{:S(2)}, u32[]{:S(2)}) collective-permute-start(bf16[16,8192]{1,0:T(8,128)(2,1)S(1)} %fusion.91), channel_id=1, source_target_pairs={{96,0},{97,1},{98,2},{99,3},{100,4},{101,5},{102,6},{103,7},{104,8... | collective-permute-start | bytes 786440 | tf_op jit(solution)/shard_map/ppermute | solution.py:188
  319.5 26.6 %collective-permute-start.18 = (bf16[16,8192]{1,0:T(8,128)(2,1)S(1)}, bf16[16,8192]{1,0:T(8,128)(2,1)S(1)}, u32[]{:S(2)}, u32[]{:S(2)}) collective-permute-start(bf16[16,8192]{1,0:T(8,128)(2,1)S(1)} %fusion.91), channel_id=1, source_target_pairs={{64,0},{96,32},{65,1},{97,33},{66,2},{98,34},{67,3},{99,35},{68,4}... | collective-permute-start | bytes 786440 | tf_op jit(solution)/shard_map/ppermute | solution.py:188
  344.5 8.3 %collective-permute-start.17 = (bf16[16,8192]{1,0:T(8,128)(2,1)S(1)}, bf16[16,8192]{1,0:T(8,128)(2,1)S(1)}, u32[]{:S(2)}, u32[]{:S(2)}) collective-permute-start(bf16[16,8192]{1,0:T(8,128)(2,1)S(1)} %fusion.91), channel_id=1, source_target_pairs={{32,0},{64,32},{96,64},{33,1},{65,33},{97,65},{34,2},{66,34},{98,6... | collective-permute-start | bytes 786440 | tf_op jit(solution)/shard_map/ppermute | solution.py:188
  (14 other events, 28.7 us)
Sparse Core Ops, SparseCore 0:
  63.0 50.3 all-gather.1
